TPU v7x, 32 devices: a whole 2x2x4 slice. The times are simulated.
32 devices in a mesh: slab: 2 (over x), curve: 16 (over z, y, core).
Axes of the slice: x: 2, y: 2, z: 4, core: 2. Of those that a mesh axis runs over, the one named last changes fastest.
Arguments:
- state: float32 [512, 8, 512], P(('slab', 'curve')), may hold values from -6 to 6
- velocity: bfloat16 [3, 64, 512], P(None, None, ('slab', 'curve')), may hold values from -4 to 4
- pre_exp: float32 [512], P(('slab', 'curve')), may hold values from 0.5 to 5
- stoich: float32 [8], replicated, may hold values from -3 to 3
- neighbours: int32 [512, 6], P(('slab', 'curve')), may hold values from 0 to 511, as said below
- switch: int32 [512], P(('slab', 'curve')), may hold values from 0 to 1
- new_owner: int32 [512], P(('slab', 'curve')), may hold values from 0 to 15, as said below
Outputs:
- state7_out: float32 [384, 8, 512], P(('slab', 'curve'))
- state3_out: float32 [512, 512], P(('slab', 'curve'))
Inputs may be any that keep to these rules, and one draw needn't show every extreme that they name: Element g lives on device g // 16 of the mesh flattened slab first. The neighbour across face 0 (1) is on the same device or on the previous (next) curve index with wrap, same slab; across faces 2 and 3 on the same device; across face 4 (5) on the same device or the previous (next) slab with wrap, same curve index. The relation is symmetric: the neighbour of neighbours[g, s] across face s xor 1 is g, and face nodes match in the stated order. Each device has exactly 8 faces 0, 8 faces 1, 16 faces 4 and 16 faces 5 whose neighbour lies on another device. `new_owner`: the new owner is in the same slab: the element's own curve index or one next to it with wrap; elements with switch 1 keep their own. From one device at most 2 elements go to each of its two neighbours, and afterwards a device holds at most 12 elements with switch 0; both bounds are reached in every draw.
All inputs are finite; a program needn't handle non-finite values.
Results may differ from a plain program's by a relative error of at most 0.0005.
Values may be sent and summed in bfloat16 or wider, within the bound.
No kernel may reach another device: no remote copies, remote signals or barrier semaphores. Data moves between devices by JAX's collectives and lax.ppermute only.
A program may use at most 64 MiB of HBM per device.

v0:
```python
import functools

import jax
import jax.numpy as jnp
import ml_dtypes
import numpy as np
from jax import lax
from jax.experimental import pallas as pl
from jax.experimental.pallas import tpu as pltpu
from jax.sharding import PartitionSpec as P

P7 = 8
P3 = 4
MOVE_CAP = 2
HOLD7 = 12
LANE = 128

TIME_STEP = 0.002
ACTIVATION = 1.5
SIDE_SIGNS = (-1.0, 1.0, -1.0, 1.0, -1.0, 1.0)
OPPOSITE = (1, 0, 3, 2, 5, 4)
SEND_FACES = (0, 1, 4, 5)
missing_id = 1 << 30

f32 = jnp.float32
bf16 = jnp.bfloat16


def shifted(value, axis, steps):
    count = lax.axis_size(axis)
    pairs = [(source, (source + steps) % count) for source in range(count)]
    return lax.ppermute(value, axis, pairs)


def lobatto_points(number):
    return -np.cos(np.pi * np.arange(number) / (number - 1))


def lagrange_weights(points):
    weights = np.ones(points.shape[0])
    for row_id in range(points.shape[0]):
        for col_id in range(points.shape[0]):
            if col_id != row_id:
                weights[row_id] = weights[row_id] / (points[row_id] - points[col_id])
    return weights


def derivative_matrix(points):
    weights = lagrange_weights(points)
    number = points.shape[0]
    matrix = np.zeros((number, number))
    for row_id in range(number):
        for col_id in range(number):
            if col_id != row_id:
                matrix[row_id, col_id] = (
                    weights[col_id] / weights[row_id] / (points[row_id] - points[col_id])
                )
        matrix[row_id, row_id] = -np.sum(matrix[row_id])
    return matrix


def interpolation_matrix(source, target):
    matrix = np.ones((target.shape[0], source.shape[0]))
    for col_id in range(source.shape[0]):
        for other_id in range(source.shape[0]):
            if other_id != col_id:
                matrix[:, col_id] = (
                    matrix[:, col_id]
                    * (target - source[other_id])
                    / (source[col_id] - source[other_id])
                )
    return matrix


def spread_three(matrix, identity):
    return (
        np.kron(matrix, np.kron(identity, identity)),
        np.kron(identity, np.kron(matrix, identity)),
        np.kron(identity, np.kron(identity, matrix)),
    )


def face_nodes(extent):
    grid = np.arange(extent**3).reshape(extent, extent, extent)
    last = extent - 1
    pieces = (grid[0], grid[last], grid[:, 0], grid[:, last], grid[:, :, 0], grid[:, :, last])
    return [piece.reshape(-1) for piece in pieces]


def to_bf16(x):
    return np.asarray(np.asarray(x, np.float32).astype(ml_dtypes.bfloat16))


def split_parts(x):
    x = np.asarray(x, np.float32)
    hi = x.astype(ml_dtypes.bfloat16)
    rest = x - hi.astype(np.float32)
    mid = rest.astype(ml_dtypes.bfloat16)
    lo = (rest - mid.astype(np.float32)).astype(ml_dtypes.bfloat16)
    return np.stack([hi, mid, lo])


def make_tables():
    fine_points = lobatto_points(P7)
    coarse_points = lobatto_points(P3)
    fine_derivs = spread_three(derivative_matrix(fine_points), np.eye(P7))
    coarse_derivs = spread_three(derivative_matrix(coarse_points), np.eye(P3))
    downward = interpolation_matrix(fine_points, coarse_points)
    upward = interpolation_matrix(coarse_points, fine_points)
    d7t = np.stack([to_bf16(m.T) for m in fine_derivs])
    d3t = np.stack([to_bf16(m).T for m in coarse_derivs])
    lift_table = to_bf16(np.kron(upward, np.kron(upward, upward)))
    projection = np.asarray(np.kron(downward, np.kron(downward, downward)), np.float32)
    mortar_up = np.asarray(np.kron(upward, upward), np.float32)
    mortar_down = np.asarray(np.kron(downward, downward), np.float32)
    nodes7 = face_nodes(P7)
    nodes3 = face_nodes(P3)
    n7 = P7**3
    n3 = P3**3
    g7 = np.zeros((n7, 6 * LANE), np.float32)
    tm = np.zeros((n3, 6 * LANE), np.float32)
    mds = np.zeros((6 * LANE, n3), np.float32)
    for side in range(6):
        for q, node in enumerate(nodes7[side]):
            g7[node, side * LANE + q] = 1.0
        for k, node in enumerate(nodes3[side]):
            tm[node, side * LANE : side * LANE + P7 * P7] = mortar_up[:, k]
            mds[side * LANE : side * LANE + P7 * P7, node] = mortar_down[k, :]
    send_cols = np.concatenate([np.arange(s * LANE, (s + 1) * LANE) for s in SEND_FACES])
    tables = {
        "d7t": to_bf16(d7t),
        "d3t": to_bf16(d3t),
        "lift": lift_table,
        "mortar_up": mortar_up,
        "g7": to_bf16(g7),
        "s7": to_bf16(g7.T),
        "g7s": to_bf16(g7[:, send_cols]),
        "tm": split_parts(tm),
        "tms": split_parts(tm[:, send_cols]),
        "mds": split_parts(mds),
        "pjt": split_parts(projection.T),
        "nodes7": nodes7,
        "nodes3": nodes3,
    }
    return tables


def _dot(a, b):
    return jnp.dot(a, b, preferred_element_type=f32)


def _split(x):
    hi = x.astype(bf16)
    rest = x - hi.astype(f32)
    mid = rest.astype(bf16)
    lo = (rest - mid.astype(f32)).astype(bf16)
    return hi, mid, lo


def _exact_left(x, table):
    hi, mid, lo = _split(x)
    return (_dot(hi, table) + _dot(mid, table)) + _dot(lo, table)


def _exact_right(table, x):
    hi, mid, lo = _split(x)
    return (_dot(table, hi) + _dot(table, mid)) + _dot(table, lo)


def _full(x, parts_ref):
    xh, xm, xl = _split(x)
    bh = parts_ref[0]
    bm = parts_ref[1]
    bl = parts_ref[2]
    return _dot(xh, bh) + (_dot(xh, bm) + _dot(xm, bh)) + (
        _dot(xh, bl) + _dot(xm, bm) + _dot(xl, bh)
    )


def _rate_source(values, pre, stc, bc, sel, local):
    picked = _exact_right(sel, values)
    v0 = picked[0:local]
    v1 = picked[local : 2 * local]
    v2 = picked[2 * local : 3 * local]
    rate = pre * jnp.exp(-ACTIVATION * jnp.exp(-v0)) * v1 * v2
    return stc * _exact_right(bc, rate)


def stage_kernel(coarse, second, project, sends, local, *refs):
    refs = list(refs)

    def take():
        return refs.pop(0)

    u_ref = take()
    c_ref = take() if coarse else None
    bu_ref = take() if second else None
    bc_ref = take() if (second and coarse) else None
    recv = {s: take() for s in SEND_FACES}
    pl_ref = take()
    pr_ref = take()
    v7_ref = take()
    m7_ref = take()
    pre_ref = take()
    stc_ref = take()
    bc_tab = take()
    sel_tab = take()
    d7_ref = take()
    g7_ref = take()
    s7_ref = take()
    if coarse:
        v3_ref = take()
        m3_ref = take()
        d3_ref = take()
        mds_ref = take()
    if coarse or project:
        tm_ref = take()
        sw_ref = take()
    if sends:
        g7s_ref = take()
        if coarse or project:
            tms_ref = take()
    if project:
        pj_ref = take()
    out_u = take()
    out_c = take() if (coarse or project) else None
    out_send = [take() for _ in SEND_FACES] if sends else None

    pre = pre_ref[...]
    stc = stc_ref[...]
    bcast = bc_tab[...]
    sel = sel_tab[...]
    u = u_ref[...]
    trace7 = _dot(u.astype(bf16), g7_ref[...])
    if coarse:
        c = c_ref[...]
        trace3 = _full(c, tm_ref).astype(bf16).astype(f32)
        switched = sw_ref[...] > 0.5
        own = jnp.where(switched, trace3, trace7)
    else:
        own = trace7
    own_b = own.astype(bf16)
    near_blocks = []
    for side in range(6):
        other = OPPOSITE[side]
        block = own_b[:, other * LANE : (other + 1) * LANE]
        near = _dot(pl_ref[side], block)
        if side in SEND_FACES:
            k = SEND_FACES.index(side)
            near = near + _dot(pr_ref[k], recv[side][...])
        near_blocks.append(near)
    near = jnp.concatenate(near_blocks, axis=1)

    divergence = None
    for d in range(3):
        flux = (v7_ref[d].astype(f32) * u).astype(bf16)
        term = _dot(flux, d7_ref[d])
        divergence = term if divergence is None else divergence + term
    result = _rate_source(u, pre, stc, bcast, sel, local) - divergence
    jump = (P7 * (P7 - 1) / 2.0) * (m7_ref[...] * (trace7 - near))
    rate7 = result + _exact_left(jump, s7_ref[...])

    if coarse:
        div3 = None
        for d in range(3):
            flux3 = (v3_ref[d] * c).astype(bf16)
            term = _dot(flux3, d3_ref[d])
            div3 = term if div3 is None else div3 + term
        result3 = _rate_source(c, pre, stc, bcast, sel, local) - div3
        jump3 = m3_ref[...] * (trace3 - near)
        rate3 = result3 + (P3 * (P3 - 1) / 2.0) * _full(jump3, mds_ref)

    if second:
        new_u = 0.5 * (bu_ref[...] + u + TIME_STEP * rate7)
    else:
        new_u = u + TIME_STEP * rate7
    out_u[...] = new_u
    new_c = None
    if coarse:
        if second:
            new_c = 0.5 * (bc_ref[...] + c + TIME_STEP * rate3)
        else:
            new_c = c + TIME_STEP * rate3
        out_c[...] = new_c
    if project:
        new_c = _full(new_u, pj_ref)
        out_c[...] = new_c
    if sends:
        send7 = _dot(new_u.astype(bf16), g7s_ref[...])
        if new_c is not None:
            send3 = _full(new_c, tms_ref).astype(bf16).astype(f32)
            send = jnp.where(sw_ref[...] > 0.5, send3, send7)
        else:
            send = send7
        send = send.astype(bf16)
        for k in range(len(SEND_FACES)):
            out_send[k][...] = send[:, k * LANE : (k + 1) * LANE]


def _vmem():
    return pl.BlockSpec(memory_space=pltpu.VMEM)


def run_stage(flags, inputs, out_shapes):
    coarse, second, project, sends, local = flags
    kernel = functools.partial(stage_kernel, coarse, second, project, sends, local)
    return pl.pallas_call(
        kernel,
        out_shape=out_shapes,
        in_specs=[_vmem() for _ in inputs],
        out_specs=[_vmem() for _ in out_shapes],
        compiler_params=pltpu.CompilerParams(vmem_limit_bytes=48 * 1024 * 1024),
    )(*inputs)


def trace_kernel(u_ref, g7s_ref, *out_refs):
    send = _dot(u_ref[...].astype(bf16), g7s_ref[...]).astype(bf16)
    for k in range(len(SEND_FACES)):
        out_refs[k][...] = send[:, k * LANE : (k + 1) * LANE]


def per_device(state, velocity, pre_exp, stoich, neighbours, switch, new_owner):
    tab = make_tables()
    local_count = state.shape[0]
    field_count = state.shape[1]
    rows = local_count * field_count
    curve_count = lax.axis_size("curve")
    curve_pos = lax.axis_index("curve")
    device_id = lax.axis_index("slab") * curve_count + curve_pos
    first_global = device_id * local_count
    positions = jnp.arange(local_count, dtype=jnp.int32)

    lift = jnp.asarray(tab["lift"])
    fine_vel = jnp.einsum("nm,dme->edn", lift, velocity, preferred_element_type=f32).astype(bf16)
    v7 = jnp.broadcast_to(
        jnp.transpose(fine_vel, (1, 0, 2))[:, :, None, :], (3, local_count, field_count, P7**3)
    ).reshape(3, rows, P7**3)
    fvf = fine_vel.astype(f32)
    m7_parts = []
    for side in range(6):
        vals = SIDE_SIGNS[side] * fvf[:, side // 2, tab["nodes7"][side]]
        m7_parts.append(jnp.pad(jnp.minimum(vals, 0.0), ((0, 0), (0, LANE - P7 * P7))))
    m7 = jnp.repeat(jnp.concatenate(m7_parts, axis=1), field_count, axis=0)
    coarse_vel = jnp.transpose(velocity, (0, 2, 1)).astype(f32)
    v3 = jnp.broadcast_to(
        coarse_vel[:, :, None, :], (3, local_count, field_count, P3**3)
    ).reshape(3, rows, P3**3)
    normal3 = jnp.stack(
        [SIDE_SIGNS[s] * coarse_vel[s // 2][:, tab["nodes3"][s]] for s in range(6)], axis=1
    )
    mortar_vel = jnp.einsum(
        "mk,esk->esm", jnp.asarray(tab["mortar_up"]), normal3, precision=lax.Precision.HIGHEST
    )
    m3 = jnp.pad(jnp.minimum(mortar_vel, 0.0), ((0, 0), (0, 0), (0, LANE - P7 * P7)))
    m3 = jnp.repeat(m3.reshape(local_count, 6 * LANE), field_count, axis=0)

    near_device = neighbours // local_count
    near_local = neighbours - near_device * local_count
    remote = near_device != device_id
    row_elem = jnp.arange(rows, dtype=jnp.int32) // field_count
    row_field = jnp.arange(rows, dtype=jnp.int32) % field_count
    col = jnp.arange(rows, dtype=jnp.int32)
    src_row = near_local[row_elem] * field_count + row_field[:, None]
    hit = src_row[:, :, None] == col[None, None, :]
    rem = remote[row_elem]
    p_local = jnp.transpose(hit & ~rem[:, :, None], (1, 0, 2)).astype(bf16)
    p_remote = jnp.transpose(hit & rem[:, :, None], (1, 0, 2))[np.array(SEND_FACES)].astype(bf16)

    pre = pre_exp.reshape(local_count, 1)
    stc = jnp.tile(stoich, local_count).reshape(rows, 1)
    bcast = (row_elem[:, None] == positions[None, :]).astype(bf16)
    pick_rows = (jnp.arange(3, dtype=jnp.int32)[:, None] + field_count * positions[None, :]).reshape(-1)
    sel = (pick_rows[:, None] == col[None, :]).astype(bf16)
    sw = jnp.repeat(switch.astype(f32), field_count).reshape(rows, 1)

    d7t = jnp.asarray(tab["d7t"])
    g7 = jnp.asarray(tab["g7"])
    s7 = jnp.asarray(tab["s7"])
    g7s = jnp.asarray(tab["g7s"])
    d3t = jnp.asarray(tab["d3t"])
    tm = jnp.asarray(tab["tm"])
    tms = jnp.asarray(tab["tms"])
    mds = jnp.asarray(tab["mds"])
    pjt = jnp.asarray(tab["pjt"])

    send_shape = jax.ShapeDtypeStruct((rows, LANE), bf16)
    u_shape = jax.ShapeDtypeStruct((rows, P7**3), f32)
    c_shape = jax.ShapeDtypeStruct((rows, P3**3), f32)

    def exchange(sends):
        out = dict(zip(SEND_FACES, sends))
        return [
            shifted(out[1], "curve", 1),
            shifted(out[0], "curve", -1),
            shifted(out[5], "slab", 1),
            shifted(out[4], "slab", -1),
        ]

    common = [p_local, p_remote, v7, m7, pre, stc, bcast, sel, d7t, g7, s7]
    u0 = state.reshape(rows, P7**3)
    sends = pl.pallas_call(
        trace_kernel,
        out_shape=[send_shape] * 4,
        in_specs=[_vmem(), _vmem()],
        out_specs=[_vmem()] * 4,
    )(u0, g7s)
    recv = exchange(sends)
    res = run_stage(
        (False, False, False, True, local_count),
        [u0] + recv + common + [g7s],
        [u_shape] + [send_shape] * 4,
    )
    first, sends = res[0], res[1:]
    recv = exchange(sends)
    res = run_stage(
        (False, True, True, True, local_count),
        [first, u0] + recv + common + [tm, sw, g7s, tms, pjt],
        [u_shape, c_shape] + [send_shape] * 4,
    )
    after, coarse, sends = res[0], res[1], res[2:]
    recv = exchange(sends)
    mixed_tail = [v3, m3, d3t, mds, tm, sw]
    res = run_stage(
        (True, False, False, True, local_count),
        [after, coarse] + recv + common + mixed_tail + [g7s, tms],
        [u_shape, c_shape] + [send_shape] * 4,
    )
    first7, first3, sends = res[0], res[1], res[2:]
    recv = exchange(sends)
    res = run_stage(
        (True, True, False, False, local_count),
        [first7, first3, after, coarse] + recv + common + mixed_tail,
        [u_shape, c_shape],
    )
    final7 = res[0].reshape(local_count, field_count, P7**3)
    final3 = res[1].reshape(local_count, field_count * P3**3)

    switched = switch == 1
    left_pos = (curve_pos + curve_count - 1) % curve_count
    right_pos = (curve_pos + 1) % curve_count
    to_left = (new_owner == left_pos) & ~switched
    to_right = (new_owner == right_pos) & ~switched
    stays_home = ~switched & ~to_left & ~to_right

    def first_rows(mask):
        rank = jnp.cumsum(mask.astype(jnp.int32)) - 1
        slot = jnp.arange(MOVE_CAP, dtype=jnp.int32)
        chosen = mask[None, :] & (rank[None, :] == slot[:, None])
        live = jnp.any(chosen, axis=1)
        row = jnp.sum(jnp.where(chosen, positions[None, :], 0), axis=1)
        return row, live

    left_rows, left_live = first_rows(to_left)
    right_rows, right_live = first_rows(to_right)
    left_ids = jnp.where(left_live, first_global + left_rows, missing_id)
    right_ids = jnp.where(right_live, first_global + right_rows, missing_id)
    home_ids = jnp.where(stays_home, first_global + positions, missing_id)
    from_right_ids = shifted(left_ids, "curve", -1)
    from_left_ids = shifted(right_ids, "curve", 1)
    from_right = shifted(final7[left_rows], "curve", -1)
    from_left = shifted(final7[right_rows], "curve", 1)
    cand_ids = jnp.concatenate([home_ids, from_left_ids, from_right_ids])
    cand_count = cand_ids.shape[0]
    rank = jnp.sum((cand_ids[None, :] < cand_ids[:, None]).astype(jnp.int32), axis=1)
    slot = jnp.arange(HOLD7, dtype=jnp.int32)
    pick = (rank[None, :] == slot[:, None]) & (cand_ids[None, :] < missing_id)
    order = jnp.sum(jnp.where(pick, jnp.arange(cand_count, dtype=jnp.int32)[None, :], 0), axis=1)
    slot_live = jnp.any(pick, axis=1)
    held = jnp.concatenate([final7, from_left, from_right], axis=0)[order]
    state7_out = jnp.where(slot_live[:, None, None], held, 0.0)
    state3_out = jnp.where(switched[:, None], final3, 0.0)
    return (state7_out, state3_out)


def solution(mesh):
    return jax.shard_map(
        per_device,
        mesh=mesh,
        in_specs=(
            P(("slab", "curve"), None, None),
            P(None, None, ("slab", "curve")),
            P(("slab", "curve")),
            P(),
            P(("slab", "curve"), None),
            P(("slab", "curve")),
            P(("slab", "curve")),
        ),
        out_specs=(P(("slab", "curve"), None, None), P(("slab", "curve"), None)),
        check_vma=False,
    )
```

profile of v0, /device:TPU:0, one launch (start us, length us, event | category | flops | bytes accessed | tf_op | source)
XLA Modules:
  0.0 149.8 jit_solution(1969659811457939678)
XLA Ops:
  0.7 2.0 %shard_map.419 = (bf16[128,128]{1,0:T(8,128)(2,1)}, bf16[128,128]{1,0:T(8,128)(2,1)}, bf16[128,128]{1,0:T(8,128)(2,1)}, bf16[128,128]{1,0:T(8,128)(2,1)}) custom-call(f32[128,512]{1,0:T(8,128)} %bitcast.94, bf16[512,512]{1,0:T(8,128)(2,1)} %constant.186.clone.g7s_ref.refs_16_.refs_19_.refs_23_), custom_call_target="tpu_custom_call" | custom-call | tf_op jit(solution)/shard_map/pallas_call | solution.py:401
  3.2 5.0 %collective-permute-start.3 = (bf16[128,128]{1,0:T(8,128)(2,1)}, bf16[128,128]{1,0:T(8,128)(2,1)}, u32[]{:S(2)}, u32[]{:S(2)}) collective-permute-start(bf16[128,128]{1,0:T(8,128)(2,1)} %get-tuple-element.26), channel_id=1, source_target_pairs={{0,15},{1,0},{2,1},{3,2},{4,3},{5,4},{6,5},{7,6},{8,7},{9,8},{10,9... | collective-permute-start | bytes 98312 | tf_op jit(solution)/shard_map/ppermute | solution.py:32
  8.2 1.9 %collective-permute-start.4 = (bf16[128,128]{1,0:T(8,128)(2,1)}, bf16[128,128]{1,0:T(8,128)(2,1)}, u32[]{:S(2)}, u32[]{:S(2)}) collective-permute-start(bf16[128,128]{1,0:T(8,128)(2,1)} %get-tuple-element.27), channel_id=1, source_target_pairs={{0,16},{16,0},{1,17},{17,1},{2,18},{18,2},{3,19},{19,3},{4,20},{20... | collective-permute-start | bytes 98312 | tf_op jit(solution)/shard_map/ppermute | solution.py:32
  31.1 1.7 %add_bitcast_fusion = s32[6,128]{0,1:T(8,128)} fusion(s32[128,6]{1,0:T(8,128)} %gather_fusion, s32[128]{0:T(128)S(1)} %and_select_fusion.1), kind=kLoop, calls=%fused_computation.31 | loop fusion | flops 1536 | bytes 6656 | tf_op jit(solution)/shard_map/add | solution.py:363
  34.9 2.1 %gather_fusion.2 = pred[4,128,128]{2,1,0:T(8,128)(4,1)} fusion(pred[6,128,128]{2,1,0:T(8,128)(4,1)} %get-tuple-element.58, s32[1024]{0:T(1024)S(1)} %get-tuple-element.67), kind=kCustom, calls=%fused_computation.2 | custom fusion | bytes 131088 | tf_op jit(solution)/shard_map/gather | solution.py:367
  37.0 1.5 %convert_element_type.60.refs_6_.refs_7_.refs_9_ = bf16[4,128,128]{2,1,0:T(8,128)(2,1)} convert(pred[4,128,128]{2,1,0:T(8,128)(4,1)} %gather_fusion.2) | non-fusion elementwise | flops 65536 | bytes 196608 | tf_op jit(solution)/shard_map/convert_element_type | solution.py:367
  38.5 1.6 %broadcast_bitcast_fusion.2.refs_7_.refs_8_.refs_10_ = bf16[3,128,512]{2,1,0:T(8,128)(2,1)} fusion(bf16[3,16,512]{2,1,0:T(8,128)(2,1)} %get-tuple-element.54), kind=kLoop, calls=%fused_computation.26 | loop fusion | bytes 442368 | tf_op jit(solution)/shard_map/reshape | solution.py:337
  44.9 1.4 copy.229
  47.5 2.0 %gather_fusion.9 = f32[16,16]{1,0:T(8,128)} fusion(f32[16,64]{0,1:T(8,128)} %copy.229, s32[1024]{0:T(1024)} %get-tuple-element.66), kind=kCustom, calls=%fused_computation.9 | custom fusion | bytes 2112 | tf_op jit(solution)/shard_map/gather | solution.py:349
  52.2 1.9 %gather_fusion.10 = f32[16,16]{1,0:T(8,128)} fusion(f32[16,64]{0,1:T(8,128)} %copy.229, s32[1024]{0:T(1024)S(1)} %get-tuple-element.65), kind=kCustom, calls=%fused_computation.10 | custom fusion | bytes 2112 | tf_op jit(solution)/shard_map/gather | solution.py:349
  55.5 1.4 copy.233
  58.1 2.0 %gather_fusion.11 = f32[16,16]{1,0:T(8,128)} fusion(f32[16,64]{0,1:T(8,128)} %copy.233, s32[1024]{0:T(1024)} %get-tuple-element.64), kind=kCustom, calls=%fused_computation.11 | custom fusion | bytes 2112 | tf_op jit(solution)/shard_map/gather | solution.py:349
  61.5 1.9 %gather_fusion.12 = f32[16,16]{1,0:T(8,128)} fusion(f32[16,64]{0,1:T(8,128)} %copy.233, s32[1024]{0:T(1024)S(1)} %get-tuple-element.63), kind=kCustom, calls=%fused_computation.12 | custom fusion | bytes 2112 | tf_op jit(solution)/shard_map/gather | solution.py:349
  67.4 2.0 %gather_fusion.13 = f32[16,16]{1,0:T(8,128)} fusion(f32[16,64]{0,1:T(8,128)} %copy.237, s32[1024]{0:T(1024)} %get-tuple-element.62), kind=kCustom, calls=%fused_computation.13 | custom fusion | bytes 2112 | tf_op jit(solution)/shard_map/gather | solution.py:349
  70.8 1.9 %gather_fusion.14 = f32[16,16]{1,0:T(8,128)} fusion(f32[16,64]{0,1:T(8,128)} %copy.237, s32[1024]{0:T(1024)S(1)} %get-tuple-element.61), kind=kCustom, calls=%fused_computation.14 | custom fusion | bytes 2112 | tf_op jit(solution)/shard_map/gather | solution.py:349
  84.2 4.4 %collective-permute-start.1 = (s32[2]{0:T(128)S(1)}, s32[2]{0:T(128)S(1)}, u32[]{:S(2)}, u32[]{:S(2)}) collective-permute-start(s32[2]{0:T(128)S(1)} %add_select_fusion.1), channel_id=1, source_target_pairs={{0,15},{1,0},{2,1},{3,2},{4,3},{5,4},{6,5},{7,6},{8,7},{9,8},{10,9... | collective-permute-start | bytes 32 | tf_op jit(solution)/shard_map/ppermute | solution.py:32
  98.2 2.5 %shard_map.420 = (f32[128,512]{1,0:T(8,128)S(1)}, bf16[128,128]{1,0:T(8,128)(2,1)S(1)}, bf16[128,128]{1,0:T(8,128)(2,1)S(1)}, bf16[128,128]{1,0:T(8,128)(2,1)S(1)}, bf16[128,128]{1,0:T(8,128)(2,1)S(1)}) custom-call(f32[128,512]{1,0:T(8,128)S(1)} %bitcast.95, bf16[128,128]{1,0:T(8,128)(2,1)} %collective-permute-done.2.refs_1_, ...), custom_call_target="tpu_custom_call" | custom-call | tf_op jit(solution)/shard_map/pallas_call | solution.py:307
  100.7 4.4 %collective-permute-start.7 = (bf16[128,128]{1,0:T(8,128)(2,1)S(1)}, bf16[128,128]{1,0:T(8,128)(2,1)S(1)}, u32[]{:S(2)}, u32[]{:S(2)}) collective-permute-start(bf16[128,128]{1,0:T(8,128)(2,1)S(1)} %get-tuple-element.31), channel_id=1, source_target_pairs={{0,15},{1,0},{2,1},{3,2},{4,3},{5,4},{6,5},{7,6},{8,7},{9,8},{10,9... | collective-permute-start | bytes 98312 | tf_op jit(solution)/shard_map/ppermute | solution.py:32
  105.2 1.9 %collective-permute-start.8 = (bf16[128,128]{1,0:T(8,128)(2,1)S(1)}, bf16[128,128]{1,0:T(8,128)(2,1)S(1)}, u32[]{:S(2)}, u32[]{:S(2)}) collective-permute-start(bf16[128,128]{1,0:T(8,128)(2,1)S(1)} %get-tuple-element.32), channel_id=1, source_target_pairs={{0,16},{16,0},{1,17},{17,1},{2,18},{18,2},{3,19},{19,3},{4,20},{20... | collective-permute-start | bytes 98312 | tf_op jit(solution)/shard_map/ppermute | solution.py:32
  107.2 1.9 %collective-permute-done.8.refs_4_ = bf16[128,128]{1,0:T(8,128)(2,1)S(1)} collective-permute-done((bf16[128,128]{1,0:T(8,128)(2,1)S(1)}, bf16[128,128]{1,0:T(8,128)(2,1)S(1)}, u32[]{:S(2)}, u32[]{:S(2)}) %collective-permute-start.8) | collective-permute-done | bytes 32800 | tf_op jit(solution)/shard_map/ppermute | solution.py:32
  109.1 1.9 %collective-permute-done.9.refs_5_ = bf16[128,128]{1,0:T(8,128)(2,1)S(1)} collective-permute-done((bf16[128,128]{1,0:T(8,128)(2,1)S(1)}, bf16[128,128]{1,0:T(8,128)(2,1)S(1)}, u32[]{:S(2)}, u32[]{:S(2)}) %collective-permute-start.9) | collective-permute-done | bytes 32800 | tf_op jit(solution)/shard_map/ppermute | solution.py:32
  111.1 3.5 %shard_map.421 = (f32[128,512]{1,0:T(8,128)S(1)}, f32[128,64]{1,0:T(8,128)S(1)}, bf16[128,128]{1,0:T(8,128)(2,1)S(1)}, bf16[128,128]{1,0:T(8,128)(2,1)S(1)}, bf1...) custom-call(f32[128,512]{1,0:T(8,128)S(1)} %get-tuple-element.29.refs_0_, f32[128,512]{1,0:T(8,128)S(1)} %bitcast.96, ...), custom_call_target="tpu_custom_call" | custom-call | tf_op jit(solution)/shard_map/pallas_call | solution.py:307
  114.7 4.4 %collective-permute-start.11 = (bf16[128,128]{1,0:T(8,128)(2,1)S(1)}, bf16[128,128]{1,0:T(8,128)(2,1)S(1)}, u32[]{:S(2)}, u32[]{:S(2)}) collective-permute-start(bf16[128,128]{1,0:T(8,128)(2,1)S(1)} %get-tuple-element.37), channel_id=1, source_target_pairs={{0,15},{1,0},{2,1},{3,2},{4,3},{5,4},{6,5},{7,6},{8,7},{9,8},{10,9... | collective-permute-start | bytes 98312 | tf_op jit(solution)/shard_map/ppermute | solution.py:32
  119.5 1.7 %collective-permute-start.13 = (bf16[128,128]{1,0:T(8,128)(2,1)S(1)}, bf16[128,128]{1,0:T(8,128)(2,1)S(1)}, u32[]{:S(2)}, u32[]{:S(2)}) collective-permute-start(bf16[128,128]{1,0:T(8,128)(2,1)S(1)} %get-tuple-element.39), channel_id=1, source_target_pairs={{0,16},{16,0},{1,17},{17,1},{2,18},{18,2},{3,19},{19,3},{4,20},{20... | collective-permute-start | bytes 98312 | tf_op jit(solution)/shard_map/ppermute | solution.py:32
  121.3 1.8 %collective-permute-done.12.refs_4_ = bf16[128,128]{1,0:T(8,128)(2,1)S(1)} collective-permute-done((bf16[128,128]{1,0:T(8,128)(2,1)S(1)}, bf16[128,128]{1,0:T(8,128)(2,1)S(1)}, u32[]{:S(2)}, u32[]{:S(2)}) %collective-permute-start.12) | collective-permute-done | bytes 32800 | tf_op jit(solution)/shard_map/ppermute | solution.py:32
  123.4 4.0 %shard_map.422 = (f32[128,512]{1,0:T(8,128)S(1)}, f32[128,64]{1,0:T(8,128)S(1)}, bf16[128,128]{1,0:T(8,128)(2,1)S(1)}, bf16[128,128]{1,0:T(8,128)(2,1)S(1)}, bf1...) custom-call(f32[128,512]{1,0:T(8,128)S(1)} %get-tuple-element.34.refs_0_.refs_2_, ...), custom_call_target="tpu_custom_call" | custom-call | tf_op jit(solution)/shard_map/pallas_call | solution.py:307
  127.5 4.4 %collective-permute-start.15 = (bf16[128,128]{1,0:T(8,128)(2,1)S(1)}, bf16[128,128]{1,0:T(8,128)(2,1)S(1)}, u32[]{:S(2)}, u32[]{:S(2)}) collective-permute-start(bf16[128,128]{1,0:T(8,128)(2,1)S(1)} %get-tuple-element.43), channel_id=1, source_target_pairs={{0,15},{1,0},{2,1},{3,2},{4,3},{5,4},{6,5},{7,6},{8,7},{9,8},{10,9... | collective-permute-start | bytes 98312 | tf_op jit(solution)/shard_map/ppermute | solution.py:32
  131.9 1.7 %collective-permute-start.16 = (bf16[128,128]{1,0:T(8,128)(2,1)S(1)}, bf16[128,128]{1,0:T(8,128)(2,1)S(1)}, u32[]{:S(2)}, u32[]{:S(2)}) collective-permute-start(bf16[128,128]{1,0:T(8,128)(2,1)S(1)} %get-tuple-element.44), channel_id=1, source_target_pairs={{0,16},{16,0},{1,17},{17,1},{2,18},{18,2},{3,19},{19,3},{4,20},{20... | collective-permute-start | bytes 98312 | tf_op jit(solution)/shard_map/ppermute | solution.py:32
  133.9 1.9 %collective-permute-done.16.refs_6_ = bf16[128,128]{1,0:T(8,128)(2,1)S(1)} collective-permute-done((bf16[128,128]{1,0:T(8,128)(2,1)S(1)}, bf16[128,128]{1,0:T(8,128)(2,1)S(1)}, u32[]{:S(2)}, u32[]{:S(2)}) %collective-permute-start.16) | collective-permute-done | bytes 32800 | tf_op jit(solution)/shard_map/ppermute | solution.py:32
  135.8 1.7 %collective-permute-done.17.refs_7_ = bf16[128,128]{1,0:T(8,128)(2,1)S(1)} collective-permute-done((bf16[128,128]{1,0:T(8,128)(2,1)S(1)}, bf16[128,128]{1,0:T(8,128)(2,1)S(1)}, u32[]{:S(2)}, u32[]{:S(2)}) %collective-permute-start.17) | collective-permute-done | bytes 32800 | tf_op jit(solution)/shard_map/ppermute | solution.py:32
  137.5 3.6 %shard_map.423 = (f32[128,512]{1,0:T(8,128)S(1)}, f32[128,64]{1,0:T(8,128)S(1)}) custom-call(f32[128,512]{1,0:T(8,128)S(1)} %get-tuple-element.40.refs_0_, f32[128,64]{1,0:T(8,128)S(1)} %get-tuple-element.41.refs_1_, f32[128,512]{1,0:T(8,128)S(1)} %get-tuple-element.34.refs_0_.refs_2_, f32[128,64]{1,0:T(8,128)S(1)} %get-tuple-element.35.refs_1_.refs_3_, ...), custom_call_target="tpu_custom_call" | custom-call | tf_op jit(solution)/shard_map/pallas_call | solution.py:307
  142.4 4.5 %collective-permute-start.19 = (f32[2,8,512]{2,1,0:T(8,128)S(1)}, f32[2,8,512]{2,1,0:T(8,128)S(1)}, u32[]{:S(2)}, u32[]{:S(2)}) collective-permute-start(f32[2,8,512]{2,1,0:T(8,128)S(1)} %gather_fusion.16), channel_id=1, source_target_pairs={{0,15},{1,0},{2,1},{3,2},{4,3},{5,4},{6,5},{7,6},{8,7},{9,8},{10,9... | collective-permute-start | bytes 98312 | tf_op jit(solution)/shard_map/ppermute | solution.py:32
  (195 shorter events, 68.2 us)
Async XLA Ops:
  0.6 23.5 %copy-start.26 = (s32[64]{0:T(128)S(1)}, s32[64]{0:T(128)}, u32[]{:S(2)}) copy-start(s32[64]{0:T(128)} %constant.332) | copy-start | bytes 772
  0.6 24.5 %copy-start.25 = (s32[64]{0:T(128)S(1)}, s32[64]{0:T(128)}, u32[]{:S(2)}) copy-start(s32[64]{0:T(128)} %constant.340) | copy-start | bytes 772
  0.7 25.4 %copy-start.24 = (s32[64]{0:T(128)S(1)}, s32[64]{0:T(128)}, u32[]{:S(2)}) copy-start(s32[64]{0:T(128)} %constant.348) | copy-start | bytes 772
  2.7 25.3 %copy-start.23 = (s32[64]{0:T(128)S(1)}, s32[64]{0:T(128)}, u32[]{:S(2)}) copy-start(s32[64]{0:T(128)} %constant.358) | copy-start | bytes 772
  2.7 88.3 %collective-permute-start.2 = (bf16[128,128]{1,0:T(8,128)(2,1)}, bf16[128,128]{1,0:T(8,128)(2,1)}, u32[]{:S(2)}, u32[]{:S(2)}) collective-permute-start(bf16[128,128]{1,0:T(8,128)(2,1)} %get-tuple-element.25), channel_id=1, source_target_pairs={{0,1},{1,2},{2,3},{3,4},{4,5},{5,6},{6,7},{7,8},{8,9},{9,10},{10,1... | collective-permute-start | bytes 98312 | tf_op jit(solution)/shard_map/ppermute | solution.py:32
  3.2 87.8 %collective-permute-start.3 = (bf16[128,128]{1,0:T(8,128)(2,1)}, bf16[128,128]{1,0:T(8,128)(2,1)}, u32[]{:S(2)}, u32[]{:S(2)}) collective-permute-start(bf16[128,128]{1,0:T(8,128)(2,1)} %get-tuple-element.26), channel_id=1, source_target_pairs={{0,15},{1,0},{2,1},{3,2},{4,3},{5,4},{6,5},{7,6},{8,7},{9,8},{10,9... | collective-permute-start | bytes 98312 | tf_op jit(solution)/shard_map/ppermute | solution.py:32
  8.2 82.8 %collective-permute-start.4 = (bf16[128,128]{1,0:T(8,128)(2,1)}, bf16[128,128]{1,0:T(8,128)(2,1)}, u32[]{:S(2)}, u32[]{:S(2)}) collective-permute-start(bf16[128,128]{1,0:T(8,128)(2,1)} %get-tuple-element.27), channel_id=1, source_target_pairs={{0,16},{16,0},{1,17},{17,1},{2,18},{18,2},{3,19},{19,3},{4,20},{20... | collective-permute-start | bytes 98312 | tf_op jit(solution)/shard_map/ppermute | solution.py:32
  10.1 80.9 %collective-permute-start.5 = (bf16[128,128]{1,0:T(8,128)(2,1)}, bf16[128,128]{1,0:T(8,128)(2,1)}, u32[]{:S(2)}, u32[]{:S(2)}) collective-permute-start(bf16[128,128]{1,0:T(8,128)(2,1)} %get-tuple-element.28), channel_id=1, source_target_pairs={{0,16},{16,0},{1,17},{17,1},{2,18},{18,2},{3,19},{19,3},{4,20},{20... | collective-permute-start | bytes 98312 | tf_op jit(solution)/shard_map/ppermute | solution.py:32
  12.6 71.7 %collective-permute-start = (s32[2]{0:T(128)}, s32[2]{0:T(128)}, u32[]{:S(2)}, u32[]{:S(2)}) collective-permute-start(s32[2]{0:T(128)} %add_select_fusion.2), channel_id=1, source_target_pairs={{0,1},{1,2},{2,3},{3,4},{4,5},{5,6},{6,7},{7,8},{8,9},{9,10},{10,1... | collective-permute-start | bytes 32 | tf_op jit(solution)/shard_map/ppermute | solution.py:32
  31.1 59.9 %copy-start = (bf16[3,512,512]{2,1,0:T(8,128)(2,1)S(1)}, bf16[3,512,512]{2,1,0:T(8,128)(2,1)}, u32[]{:S(2)}) copy-start(bf16[3,512,512]{2,1,0:T(8,128)(2,1)} %constant.183.clone.refs_13_.refs_14_.refs_16_) | copy-start | bytes 4718596
  31.1 59.9 %copy-start.1 = (bf16[512,768]{1,0:T(8,128)(2,1)S(1)}, bf16[512,768]{1,0:T(8,128)(2,1)}, u32[]{:S(2)}) copy-start(bf16[512,768]{1,0:T(8,128)(2,1)} %constant.184.clone.refs_14_.refs_15_.refs_17_) | copy-start | bytes 2359300
  31.1 59.9 %copy-start.2 = (bf16[768,512]{1,0:T(8,128)(2,1)S(1)}, bf16[768,512]{1,0:T(8,128)(2,1)}, u32[]{:S(2)}) copy-start(bf16[768,512]{1,0:T(8,128)(2,1)} %constant.185.clone.refs_15_.refs_16_.refs_18_) | copy-start | bytes 2359300
  84.2 5.7 %collective-permute-start.1 = (s32[2]{0:T(128)S(1)}, s32[2]{0:T(128)S(1)}, u32[]{:S(2)}, u32[]{:S(2)}) collective-permute-start(s32[2]{0:T(128)S(1)} %add_select_fusion.1), channel_id=1, source_target_pairs={{0,15},{1,0},{2,1},{3,2},{4,3},{5,4},{6,5},{7,6},{8,7},{9,8},{10,9... | collective-permute-start | bytes 32 | tf_op jit(solution)/shard_map/ppermute | solution.py:32
  98.1 12.9 %copy-start.16 = (f32[128,1]{1,0:T(8,128)S(1)}, f32[128,1]{1,0:T(8,128)}, u32[]{:S(2)}) copy-start(f32[128,1]{1,0:T(8,128)} %reshape_reshape.4.refs_18_.refs_22_.refs_24_) | copy-start | bytes 1540
  98.1 12.9 %copy-start.18 = (bf16[128,16]{1,0:T(8,128)(2,1)S(1)}, bf16[128,16]{1,0:T(8,128)(2,1)}, u32[]{:S(2)}) copy-start(bf16[128,16]{1,0:T(8,128)(2,1)} %fusion.3.refs_11_.refs_12_.refs_14_) | copy-start | bytes 12292
  98.2 12.9 %copy-start.19 = (bf16[3,64,512]{2,1,0:T(8,128)(2,1)S(1)}, bf16[3,64,512]{2,1,0:T(8,128)(2,1)}, u32[]{:S(2)}) copy-start(bf16[3,64,512]{2,1,0:T(8,128)(2,1)} %constant.189.clone.refs_20_.refs_24_) | copy-start | bytes 589828
  98.2 12.9 %copy-start.20 = (bf16[3,512,64]{2,1,0:T(8,128)(2,1)S(1)}, bf16[3,512,64]{2,1,0:T(8,128)(2,1)}, u32[]{:S(2)}) copy-start(bf16[3,512,64]{2,1,0:T(8,128)(2,1)} %constant.191.clone.refs_21_) | copy-start | bytes 589828
  100.7 6.5 %collective-permute-start.6 = (bf16[128,128]{1,0:T(8,128)(2,1)S(1)}, bf16[128,128]{1,0:T(8,128)(2,1)S(1)}, u32[]{:S(2)}, u32[]{:S(2)}) collective-permute-start(bf16[128,128]{1,0:T(8,128)(2,1)S(1)} %get-tuple-element.30), channel_id=1, source_target_pairs={{0,1},{1,2},{2,3},{3,4},{4,5},{5,6},{6,7},{7,8},{8,9},{9,10},{10,1... | collective-permute-start | bytes 98312 | tf_op jit(solution)/shard_map/ppermute | solution.py:32
  100.7 6.5 %collective-permute-start.7 = (bf16[128,128]{1,0:T(8,128)(2,1)S(1)}, bf16[128,128]{1,0:T(8,128)(2,1)S(1)}, u32[]{:S(2)}, u32[]{:S(2)}) collective-permute-start(bf16[128,128]{1,0:T(8,128)(2,1)S(1)} %get-tuple-element.31), channel_id=1, source_target_pairs={{0,15},{1,0},{2,1},{3,2},{4,3},{5,4},{6,5},{7,6},{8,7},{9,8},{10,9... | collective-permute-start | bytes 98312 | tf_op jit(solution)/shard_map/ppermute | solution.py:32
  105.2 3.9 %collective-permute-start.8 = (bf16[128,128]{1,0:T(8,128)(2,1)S(1)}, bf16[128,128]{1,0:T(8,128)(2,1)S(1)}, u32[]{:S(2)}, u32[]{:S(2)}) collective-permute-start(bf16[128,128]{1,0:T(8,128)(2,1)S(1)} %get-tuple-element.32), channel_id=1, source_target_pairs={{0,16},{16,0},{1,17},{17,1},{2,18},{18,2},{3,19},{19,3},{4,20},{20... | collective-permute-start | bytes 98312 | tf_op jit(solution)/shard_map/ppermute | solution.py:32
  107.1 3.9 %collective-permute-start.9 = (bf16[128,128]{1,0:T(8,128)(2,1)S(1)}, bf16[128,128]{1,0:T(8,128)(2,1)S(1)}, u32[]{:S(2)}, u32[]{:S(2)}) collective-permute-start(bf16[128,128]{1,0:T(8,128)(2,1)S(1)} %get-tuple-element.33), channel_id=1, source_target_pairs={{0,16},{16,0},{1,17},{17,1},{2,18},{18,2},{3,19},{19,3},{4,20},{20... | collective-permute-start | bytes 98312 | tf_op jit(solution)/shard_map/ppermute | solution.py:32
  114.6 6.6 %collective-permute-start.10 = (bf16[128,128]{1,0:T(8,128)(2,1)S(1)}, bf16[128,128]{1,0:T(8,128)(2,1)S(1)}, u32[]{:S(2)}, u32[]{:S(2)}) collective-permute-start(bf16[128,128]{1,0:T(8,128)(2,1)S(1)} %get-tuple-element.36), channel_id=1, source_target_pairs={{0,1},{1,2},{2,3},{3,4},{4,5},{5,6},{6,7},{7,8},{8,9},{9,10},{10,1... | collective-permute-start | bytes 98312 | tf_op jit(solution)/shard_map/ppermute | solution.py:32
  114.7 6.6 %collective-permute-start.11 = (bf16[128,128]{1,0:T(8,128)(2,1)S(1)}, bf16[128,128]{1,0:T(8,128)(2,1)S(1)}, u32[]{:S(2)}, u32[]{:S(2)}) collective-permute-start(bf16[128,128]{1,0:T(8,128)(2,1)S(1)} %get-tuple-element.37), channel_id=1, source_target_pairs={{0,15},{1,0},{2,1},{3,2},{4,3},{5,4},{6,5},{7,6},{8,7},{9,8},{10,9... | collective-permute-start | bytes 98312 | tf_op jit(solution)/shard_map/ppermute | solution.py:32
  119.1 3.9 %collective-permute-start.12 = (bf16[128,128]{1,0:T(8,128)(2,1)S(1)}, bf16[128,128]{1,0:T(8,128)(2,1)S(1)}, u32[]{:S(2)}, u32[]{:S(2)}) collective-permute-start(bf16[128,128]{1,0:T(8,128)(2,1)S(1)} %get-tuple-element.38), channel_id=1, source_target_pairs={{0,16},{16,0},{1,17},{17,1},{2,18},{18,2},{3,19},{19,3},{4,20},{20... | collective-permute-start | bytes 98312 | tf_op jit(solution)/shard_map/ppermute | solution.py:32
  119.5 3.9 %collective-permute-start.13 = (bf16[128,128]{1,0:T(8,128)(2,1)S(1)}, bf16[128,128]{1,0:T(8,128)(2,1)S(1)}, u32[]{:S(2)}, u32[]{:S(2)}) collective-permute-start(bf16[128,128]{1,0:T(8,128)(2,1)S(1)} %get-tuple-element.39), channel_id=1, source_target_pairs={{0,16},{16,0},{1,17},{17,1},{2,18},{18,2},{3,19},{19,3},{4,20},{20... | collective-permute-start | bytes 98312 | tf_op jit(solution)/shard_map/ppermute | solution.py:32
  123.4 14.1 %copy-start.9 = (bf16[4,128,128]{2,1,0:T(8,128)(2,1)S(1)}, bf16[4,128,128]{2,1,0:T(8,128)(2,1)}, u32[]{:S(2)}) copy-start(bf16[4,128,128]{2,1,0:T(8,128)(2,1)} %convert_element_type.60.refs_6_.refs_7_.refs_9_) | copy-start | bytes 393220
  127.4 6.5 %collective-permute-start.14 = (bf16[128,128]{1,0:T(8,128)(2,1)S(1)}, bf16[128,128]{1,0:T(8,128)(2,1)S(1)}, u32[]{:S(2)}, u32[]{:S(2)}) collective-permute-start(bf16[128,128]{1,0:T(8,128)(2,1)S(1)} %get-tuple-element.42), channel_id=1, source_target_pairs={{0,1},{1,2},{2,3},{3,4},{4,5},{5,6},{6,7},{7,8},{8,9},{9,10},{10,1... | collective-permute-start | bytes 98312 | tf_op jit(solution)/shard_map/ppermute | solution.py:32
  127.5 6.5 %collective-permute-start.15 = (bf16[128,128]{1,0:T(8,128)(2,1)S(1)}, bf16[128,128]{1,0:T(8,128)(2,1)S(1)}, u32[]{:S(2)}, u32[]{:S(2)}) collective-permute-start(bf16[128,128]{1,0:T(8,128)(2,1)S(1)} %get-tuple-element.43), channel_id=1, source_target_pairs={{0,15},{1,0},{2,1},{3,2},{4,3},{5,4},{6,5},{7,6},{8,7},{9,8},{10,9... | collective-permute-start | bytes 98312 | tf_op jit(solution)/shard_map/ppermute | solution.py:32
  131.9 3.9 %collective-permute-start.16 = (bf16[128,128]{1,0:T(8,128)(2,1)S(1)}, bf16[128,128]{1,0:T(8,128)(2,1)S(1)}, u32[]{:S(2)}, u32[]{:S(2)}) collective-permute-start(bf16[128,128]{1,0:T(8,128)(2,1)S(1)} %get-tuple-element.44), channel_id=1, source_target_pairs={{0,16},{16,0},{1,17},{17,1},{2,18},{18,2},{3,19},{19,3},{4,20},{20... | collective-permute-start | bytes 98312 | tf_op jit(solution)/shard_map/ppermute | solution.py:32
  133.6 3.9 %collective-permute-start.17 = (bf16[128,128]{1,0:T(8,128)(2,1)S(1)}, bf16[128,128]{1,0:T(8,128)(2,1)S(1)}, u32[]{:S(2)}, u32[]{:S(2)}) collective-permute-start(bf16[128,128]{1,0:T(8,128)(2,1)S(1)} %get-tuple-element.45), channel_id=1, source_target_pairs={{0,16},{16,0},{1,17},{17,1},{2,18},{18,2},{3,19},{19,3},{4,20},{20... | collective-permute-start | bytes 98312 | tf_op jit(solution)/shard_map/ppermute | solution.py:32
  141.8 6.1 %collective-permute-start.18 = (f32[2,8,512]{2,1,0:T(8,128)S(1)}, f32[2,8,512]{2,1,0:T(8,128)S(1)}, u32[]{:S(2)}, u32[]{:S(2)}) collective-permute-start(f32[2,8,512]{2,1,0:T(8,128)S(1)} %gather_fusion.15), channel_id=1, source_target_pairs={{0,1},{1,2},{2,3},{3,4},{4,5},{5,6},{6,7},{7,8},{8,9},{9,10},{10,1... | collective-permute-start | bytes 98312 | tf_op jit(solution)/shard_map/ppermute | solution.py:32
  142.4 6.1 %collective-permute-start.19 = (f32[2,8,512]{2,1,0:T(8,128)S(1)}, f32[2,8,512]{2,1,0:T(8,128)S(1)}, u32[]{:S(2)}, u32[]{:S(2)}) collective-permute-start(f32[2,8,512]{2,1,0:T(8,128)S(1)} %gather_fusion.16), channel_id=1, source_target_pairs={{0,15},{1,0},{2,1},{3,2},{4,3},{5,4},{6,5},{7,6},{8,7},{9,8},{10,9... | collective-permute-start | bytes 98312 | tf_op jit(solution)/shard_map/ppermute | solution.py:32
  (17 other events, 112.3 us)
where the time goes:
time: 152 us; the launch traced here: 150 us
  local copies, waits for them, and re-layouts  55.5 us (37%)
  starting transfers between devices  36.1 us (24%)
  other arithmetic  27.9 us (18%)
  Pallas kernels  15.6 us (10%)
  waiting for transfers between devices  11.6 us (8%)
  matrix products  1.96 us (1%)
    ppermute x20, starting transfers between devices, shifted(): return lax.ppermute(value, axis, pairs)  36.1 us
    gather x12, local copies, waits for them, and re-layouts, per_device(): coarse_vel[s // 2][:, tab['nodes3'][s]]  20 us
    pallas_call x4, Pallas kernels, run_stage(): pl.pallas_call(kernel, out_shape=out_shapes, in_specs=[_vmem() for _ in i...  13.6 us
    ppermute x20, waiting for transfers between devices, shifted(): return lax.ppermute(value, axis, pairs)  11.6 us
    unnamed x74, local copies, waits for them, and re-layouts  11 us
    gather x6, local copies, waits for them, and re-layouts, per_device(): vals = SIDE_SIGNS[side] * fvf[:, side // 2, tab['nodes7'][side]]  5.34 us
    squeeze x4, local copies, waits for them, and re-layouts, per_device(): coarse_vel[s // 2][:, tab['nodes3'][s]]  4.75 us
    unnamed x3, other arithmetic  3.87 us
  transfers between devices with their start and end apart: 20, of which 9 were waited for; matrix products, arithmetic and copies ran while one was open for 51% of the time, Pallas kernels for 0%

commit v1 on v0

--- a/solution.py
+++ b/solution.py
@@ -319,6 +319,57 @@
         out_refs[k][...] = send[:, k * LANE : (k + 1) * LANE]
 
 
+def setup_kernel(local, fields, u_ref, vt_ref, packed_ref, lift_ref, g7_ref, tm_ref, bc_ref,
+                 g7s_ref, pre_ref, sto_ref, v7_out, m7_out, v3_out, m3_out, pl_out, pr_out,
+                 pre_out, stc_out, sw_out, *send_refs):
+    rows = local * fields
+    bcast = bc_ref[...]
+    lanes = lax.broadcasted_iota(jnp.int32, (local, 6 * LANE), 1) // LANE
+    sign = jnp.where(lanes % 2 == 0, -1.0, 1.0)
+    fvg = []
+    mvg = []
+    for d in range(3):
+        vt = vt_ref[d]
+        fv = _dot(vt, lift_ref[...]).astype(bf16)
+        v7_out[d] = _dot(bcast, fv).astype(bf16)
+        v3_out[d] = _dot(bcast, vt)
+        fvg.append(_dot(fv, g7_ref[...]))
+        mvg.append((_dot(vt, tm_ref[0]) + _dot(vt, tm_ref[1])) + _dot(vt, tm_ref[2]))
+
+    def by_block(parts):
+        return jnp.where(lanes < 2, parts[0], jnp.where(lanes < 4, parts[1], parts[2]))
+
+    m7 = jnp.minimum(sign * by_block(fvg), 0.0)
+    m7_out[...] = _dot(bcast, m7.astype(bf16))
+    m3 = jnp.minimum(sign * by_block(mvg), 0.0)
+    m3_out[...] = _exact_right(bcast, m3)
+    rep = _dot(bcast, packed_ref[...].astype(bf16))
+    row_f = (lax.broadcasted_iota(jnp.int32, (rows, 1), 0) % fields).astype(f32)
+    cols = lax.broadcasted_iota(jnp.int32, (rows, rows), 1).astype(f32)
+    for side in range(6):
+        code = rep[:, side : side + 1]
+        far = code >= local
+        target = (code - jnp.where(far, float(local), 0.0)) * fields + row_f
+        hit = cols == target
+        pl_out[side] = jnp.where(hit & ~far, 1.0, 0.0).astype(bf16)
+        if side in SEND_FACES:
+            pr_out[SEND_FACES.index(side)] = jnp.where(hit & far, 1.0, 0.0).astype(bf16)
+    sw_out[...] = rep[:, 6:7]
+    elem = lax.broadcasted_iota(jnp.int32, (local, 1), 0)
+    pre = jnp.zeros((local, 1), f32)
+    for e in range(local):
+        pre = jnp.where(elem == e, pre_ref[e], pre)
+    pre_out[...] = pre
+    row_fi = lax.broadcasted_iota(jnp.int32, (rows, 1), 0) % fields
+    stc = jnp.zeros((rows, 1), f32)
+    for f in range(fields):
+        stc = jnp.where(row_fi == f, sto_ref[f], stc)
+    stc_out[...] = stc
+    send = _dot(u_ref[...].astype(bf16), g7s_ref[...]).astype(bf16)
+    for k in range(len(SEND_FACES)):
+        send_refs[k][...] = send[:, k * LANE : (k + 1) * LANE]
+
+
 def per_device(state, velocity, pre_exp, stoich, neighbours, switch, new_owner):
     tab = make_tables()
     local_count = state.shape[0]
@@ -330,49 +381,19 @@
     first_global = device_id * local_count
     positions = jnp.arange(local_count, dtype=jnp.int32)
 
-    lift = jnp.asarray(tab["lift"])
-    fine_vel = jnp.einsum("nm,dme->edn", lift, velocity, preferred_element_type=f32).astype(bf16)
-    v7 = jnp.broadcast_to(
-        jnp.transpose(fine_vel, (1, 0, 2))[:, :, None, :], (3, local_count, field_count, P7**3)
-    ).reshape(3, rows, P7**3)
-    fvf = fine_vel.astype(f32)
-    m7_parts = []
-    for side in range(6):
-        vals = SIDE_SIGNS[side] * fvf[:, side // 2, tab["nodes7"][side]]
-        m7_parts.append(jnp.pad(jnp.minimum(vals, 0.0), ((0, 0), (0, LANE - P7 * P7))))
-    m7 = jnp.repeat(jnp.concatenate(m7_parts, axis=1), field_count, axis=0)
-    coarse_vel = jnp.transpose(velocity, (0, 2, 1)).astype(f32)
-    v3 = jnp.broadcast_to(
-        coarse_vel[:, :, None, :], (3, local_count, field_count, P3**3)
-    ).reshape(3, rows, P3**3)
-    normal3 = jnp.stack(
-        [SIDE_SIGNS[s] * coarse_vel[s // 2][:, tab["nodes3"][s]] for s in range(6)], axis=1
-    )
-    mortar_vel = jnp.einsum(
-        "mk,esk->esm", jnp.asarray(tab["mortar_up"]), normal3, precision=lax.Precision.HIGHEST
-    )
-    m3 = jnp.pad(jnp.minimum(mortar_vel, 0.0), ((0, 0), (0, 0), (0, LANE - P7 * P7)))
-    m3 = jnp.repeat(m3.reshape(local_count, 6 * LANE), field_count, axis=0)
-
     near_device = neighbours // local_count
     near_local = neighbours - near_device * local_count
     remote = near_device != device_id
-    row_elem = jnp.arange(rows, dtype=jnp.int32) // field_count
-    row_field = jnp.arange(rows, dtype=jnp.int32) % field_count
-    col = jnp.arange(rows, dtype=jnp.int32)
-    src_row = near_local[row_elem] * field_count + row_field[:, None]
-    hit = src_row[:, :, None] == col[None, None, :]
-    rem = remote[row_elem]
-    p_local = jnp.transpose(hit & ~rem[:, :, None], (1, 0, 2)).astype(bf16)
-    p_remote = jnp.transpose(hit & rem[:, :, None], (1, 0, 2))[np.array(SEND_FACES)].astype(bf16)
-
-    pre = pre_exp.reshape(local_count, 1)
-    stc = jnp.tile(stoich, local_count).reshape(rows, 1)
-    bcast = (row_elem[:, None] == positions[None, :]).astype(bf16)
-    pick_rows = (jnp.arange(3, dtype=jnp.int32)[:, None] + field_count * positions[None, :]).reshape(-1)
-    sel = (pick_rows[:, None] == col[None, :]).astype(bf16)
-    sw = jnp.repeat(switch.astype(f32), field_count).reshape(rows, 1)
-
+    codes = (near_local + local_count * remote.astype(jnp.int32)).astype(f32)
+    packed = jnp.concatenate(
+        [codes, switch.astype(f32)[:, None], jnp.zeros((local_count, LANE - 7), f32)], axis=1
+    )
+    vt = jnp.transpose(velocity, (0, 2, 1))
+    row_elem = np.arange(rows) // field_count
+    bcast = jnp.asarray(to_bf16(row_elem[:, None] == np.arange(local_count)[None, :]))
+    pick_rows = (np.arange(3)[:, None] + field_count * np.arange(local_count)[None, :]).reshape(-1)
+    sel = jnp.asarray(to_bf16(pick_rows[:, None] == np.arange(rows)[None, :]))
+    lift_t = jnp.asarray(to_bf16(tab["lift"].astype(np.float32).T))
     d7t = jnp.asarray(tab["d7t"])
     g7 = jnp.asarray(tab["g7"])
     s7 = jnp.asarray(tab["s7"])
@@ -396,14 +417,29 @@
             shifted(out[4], "slab", -1),
         ]
 
+    setup_out = [
+        jax.ShapeDtypeStruct((3, rows, P7**3), bf16),
+        jax.ShapeDtypeStruct((rows, 6 * LANE), f32),
+        jax.ShapeDtypeStruct((3, rows, P3**3), f32),
+        jax.ShapeDtypeStruct((rows, 6 * LANE), f32),
+        jax.ShapeDtypeStruct((6, rows, rows), bf16),
+        jax.ShapeDtypeStruct((len(SEND_FACES), rows, rows), bf16),
+        jax.ShapeDtypeStruct((local_count, 1), f32),
+        jax.ShapeDtypeStruct((rows, 1), f32),
+        jax.ShapeDtypeStruct((rows, 1), f32),
+    ] + [send_shape] * 4
+    u0 = state.reshape(rows, P7**3)
+    smem = pl.BlockSpec(memory_space=pltpu.SMEM)
+    res = pl.pallas_call(
+        functools.partial(setup_kernel, local_count, field_count),
+        out_shape=setup_out,
+        in_specs=[_vmem()] * 8 + [smem, smem],
+        out_specs=[_vmem() for _ in setup_out],
+        compiler_params=pltpu.CompilerParams(vmem_limit_bytes=48 * 1024 * 1024),
+    )(u0, vt, packed, lift_t, g7, tm, bcast, g7s, pre_exp, stoich)
+    v7, m7, v3, m3, p_local, p_remote, pre, stc, sw = res[:9]
+    sends = res[9:]
     common = [p_local, p_remote, v7, m7, pre, stc, bcast, sel, d7t, g7, s7]
-    u0 = state.reshape(rows, P7**3)
-    sends = pl.pallas_call(
-        trace_kernel,
-        out_shape=[send_shape] * 4,
-        in_specs=[_vmem(), _vmem()],
-        out_specs=[_vmem()] * 4,
-    )(u0, g7s)
     recv = exchange(sends)
     res = run_stage(
         (False, False, False, True, local_count),

time: 152 us -> 88.6 us (0.58)
  local copies, waits for them, and re-layouts: 55.5 us -> 15.2 us
  other arithmetic: 27.9 us -> 7.36 us
  waiting for transfers between devices: 11.6 us -> 15.5 us
  starting transfers between devices: 36.1 us -> 32.2 us
  matrix products: 1.96 us -> 0 us
    gather x22 -> x0, local copies, waits for them, and re-layouts: 29.4 us -> none  [the longest x12 20 us: per_device(): coarse_vel[s // 2][:, tab['nodes3'][s]]]
    squeeze x4 -> x0, local copies, waits for them, and re-layouts: 4.75 us -> none  [per_device(): coarse_vel[s // 2][:, tab['nodes3'][s]]]
    convert_element_type x5 -> x1, other arithmetic: 4.24 us -> 0.02 us  [per_device(): codes = (near_local + local_count * remote.astype(jnp.int32)).astype(f32)]
    ppermute x20, waiting for transfers between devices: 11.6 us -> 15.5 us  [shifted(): return lax.ppermute(value, axis, pairs)]
    ppermute x20, starting transfers between devices: 36.1 us -> 32.2 us  [shifted(): return lax.ppermute(value, axis, pairs)]
    unnamed x3 -> x0, other arithmetic: 3.87 us -> none
    gather x4 -> x0, other arithmetic: 3.76 us -> none  [the longest x3 3.75 us: per_device(): coarse_vel[s // 2][:, tab['nodes3'][s]]]
    reshape x5 -> x0, local copies, waits for them, and re-layouts: 3.68 us -> none  [the longest x1 1.6 us: per_device(): v7 = jnp.broadcast_to(jnp.transpose(fine_vel, (1, 0, 2))[:, :, None, :],...]
  transfers between devices with their start and end apart: 20 -> 20, of which waited for: 9 -> 10; matrix products, arithmetic and copies ran while one was open for 51% -> 7% of each run, Pallas kernels for 0% -> 0%
where the time goes in v1:
time: 88.6 us; the launch traced here: 87.8 us
  starting transfers between devices  32.2 us (36%)
  Pallas kernels  16.6 us (19%)
  waiting for transfers between devices  15.5 us (17%)
  local copies, waits for them, and re-layouts  15.2 us (17%)
  other arithmetic  7.36 us (8%)
  between operations  1 us (1%)
    ppermute x20, starting transfers between devices, shifted(): return lax.ppermute(value, axis, pairs)  32.2 us
    ppermute x20, waiting for transfers between devices, shifted(): return lax.ppermute(value, axis, pairs)  15.5 us
    pallas_call x4, Pallas kernels, run_stage(): pl.pallas_call(kernel, out_shape=out_shapes, in_specs=[_vmem() for _ in i...  13.8 us
    unnamed x59, local copies, waits for them, and re-layouts  13.1 us
    pallas_call x1, Pallas kernels, per_device(): pl.pallas_call(functools.partial(setup_kernel, local_count, field_count),...  2.82 us
  transfers between devices with their start and end apart: 20, of which 10 were waited for; matrix products, arithmetic and copies ran while one was open for 7% of the time, Pallas kernels for 0%

profile of v1, /device:TPU:0, one launch (start us, length us, event | category | flops | bytes accessed | tf_op | source)
XLA Modules:
  0.0 87.8 jit_solution(16041427624345880724)
XLA Ops:
  0.7 0.8 and_select_fusion
  1.6 0.8 copy.43
  2.5 1.1 %copy-done.1 = bf16[512,768]{1,0:T(8,128)(2,1)S(1)} copy-done((bf16[512,768]{1,0:T(8,128)(2,1)S(1)}, bf16[512,768]{1,0:T(8,128)(2,1)}, u32[]{:S(2)}) %copy-start.1) | copy-done | bytes 786456
  3.6 1.0 %copy-done.6 = bf16[512,512]{1,0:T(8,128)(2,1)S(1)} copy-done((bf16[512,512]{1,0:T(8,128)(2,1)S(1)}, bf16[512,512]{1,0:T(8,128)(2,1)}, u32[]{:S(2)}) %copy-start.6) | copy-done | bytes 524312
  4.7 1.0 %copy-done.8 = bf16[3,64,768]{2,1,0:T(8,128)(2,1)S(1)} copy-done((bf16[3,64,768]{2,1,0:T(8,128)(2,1)S(1)}, bf16[3,64,768]{2,1,0:T(8,128)(2,1)}, u32[]{:S(2)}) %copy-start.8) | copy-done | bytes 294936
  5.6 0.9 %copy-done.11 = f32[16,8,512]{2,1,0:T(8,128)S(1)} copy-done((f32[16,8,512]{2,1,0:T(8,128)S(1)}, f32[16,8,512]{2,1,0:T(8,128)}, u32[]{:S(2)}) %copy-start.11) | copy-done | bytes 262168
  7.4 0.8 copy-done.23
  10.2 2.8 %shard_map.194 = (bf16[3,128,512]{2,1,0:T(8,128)(2,1)S(1)}, f32[128,768]{1,0:T(8,128)S(1)}, f32[3,128,64]{2,1,0:T(8,128)S(1)}, f32[128,768]{1,0:T(8,128)S(1)}, b...) custom-call(f32[128,512]{1,0:T(8,128)S(1)} %bitcast.21, ...), custom_call_target="tpu_custom_call" | custom-call | tf_op jit(solution)/shard_map/pallas_call | solution.py:433
  14.9 5.0 %collective-permute-start.3 = (bf16[128,128]{1,0:T(8,128)(2,1)}, bf16[128,128]{1,0:T(8,128)(2,1)}, u32[]{:S(2)}, u32[]{:S(2)}) collective-permute-start(bf16[128,128]{1,0:T(8,128)(2,1)} %get-tuple-element.35), channel_id=1, source_target_pairs={{0,15},{1,0},{2,1},{3,2},{4,3},{5,4},{6,5},{7,6},{8,7},{9,8},{10,9... | collective-permute-start | bytes 98312 | tf_op jit(solution)/shard_map/ppermute | solution.py:32
  19.9 1.9 %collective-permute-start.4 = (bf16[128,128]{1,0:T(8,128)(2,1)}, bf16[128,128]{1,0:T(8,128)(2,1)}, u32[]{:S(2)}, u32[]{:S(2)}) collective-permute-start(bf16[128,128]{1,0:T(8,128)(2,1)} %get-tuple-element.36), channel_id=1, source_target_pairs={{0,16},{16,0},{1,17},{17,1},{2,18},{18,2},{3,19},{19,3},{4,20},{20... | collective-permute-start | bytes 98312 | tf_op jit(solution)/shard_map/ppermute | solution.py:32
  25.9 3.9 %collective-permute-done = s32[2]{0:T(128)} collective-permute-done((s32[2]{0:T(128)}, s32[2]{0:T(128)}, u32[]{:S(2)}, u32[]{:S(2)}) %collective-permute-start) | collective-permute-done | bytes 40 | tf_op jit(solution)/shard_map/ppermute | solution.py:32
  30.4 1.3 %collective-permute-done.1 = s32[2]{0:T(128)S(1)} collective-permute-done((s32[2]{0:T(128)S(1)}, s32[2]{0:T(128)S(1)}, u32[]{:S(2)}, u32[]{:S(2)}) %collective-permute-start.1) | collective-permute-done | bytes 40 | tf_op jit(solution)/shard_map/ppermute | solution.py:32
  32.9 1.1 %copy-done.2 = bf16[512,768]{1,0:T(8,128)(2,1)S(1)} copy-done((bf16[512,768]{1,0:T(8,128)(2,1)S(1)}, bf16[512,768]{1,0:T(8,128)(2,1)}, u32[]{:S(2)}) %copy-start.2) | copy-done | bytes 786456
  34.0 1.1 %copy-done.4 = bf16[768,512]{1,0:T(8,128)(2,1)S(1)} copy-done((bf16[768,512]{1,0:T(8,128)(2,1)S(1)}, bf16[768,512]{1,0:T(8,128)(2,1)}, u32[]{:S(2)}) %copy-start.4) | copy-done | bytes 786456
  35.1 0.9 %copy-done.12 = f32[16,8,512]{2,1,0:T(8,128)S(1)} copy-done((f32[16,8,512]{2,1,0:T(8,128)S(1)}, f32[16,8,512]{2,1,0:T(8,128)}, u32[]{:S(2)}) %copy-start.12) | copy-done | bytes 262168
  36.1 2.5 %shard_map.195 = (f32[128,512]{1,0:T(8,128)S(1)}, bf16[128,128]{1,0:T(8,128)(2,1)S(1)}, bf16[128,128]{1,0:T(8,128)(2,1)S(1)}, bf16[128,128]{1,0:T(8,128)(2,1)S(1)}, bf16[128,128]{1,0:T(8,128)(2,1)S(1)}) custom-call(f32[128,512]{1,0:T(8,128)S(1)} %bitcast.22, bf16[128,128]{1,0:T(8,128)(2,1)} %collective-permute-done.2.refs_1_, ...), custom_call_target="tpu_custom_call" | custom-call | tf_op jit(solution)/shard_map/pallas_call | solution.py:307
  38.6 4.4 %collective-permute-start.7 = (bf16[128,128]{1,0:T(8,128)(2,1)S(1)}, bf16[128,128]{1,0:T(8,128)(2,1)S(1)}, u32[]{:S(2)}, u32[]{:S(2)}) collective-permute-start(bf16[128,128]{1,0:T(8,128)(2,1)S(1)} %get-tuple-element.46), channel_id=1, source_target_pairs={{0,15},{1,0},{2,1},{3,2},{4,3},{5,4},{6,5},{7,6},{8,7},{9,8},{10,9... | collective-permute-start | bytes 98312 | tf_op jit(solution)/shard_map/ppermute | solution.py:32
  43.1 1.9 %collective-permute-start.8 = (bf16[128,128]{1,0:T(8,128)(2,1)S(1)}, bf16[128,128]{1,0:T(8,128)(2,1)S(1)}, u32[]{:S(2)}, u32[]{:S(2)}) collective-permute-start(bf16[128,128]{1,0:T(8,128)(2,1)S(1)} %get-tuple-element.47), channel_id=1, source_target_pairs={{0,16},{16,0},{1,17},{17,1},{2,18},{18,2},{3,19},{19,3},{4,20},{20... | collective-permute-start | bytes 98312 | tf_op jit(solution)/shard_map/ppermute | solution.py:32
  45.1 1.9 %collective-permute-done.8.refs_4_ = bf16[128,128]{1,0:T(8,128)(2,1)S(1)} collective-permute-done((bf16[128,128]{1,0:T(8,128)(2,1)S(1)}, bf16[128,128]{1,0:T(8,128)(2,1)S(1)}, u32[]{:S(2)}, u32[]{:S(2)}) %collective-permute-start.8) | collective-permute-done | bytes 32800 | tf_op jit(solution)/shard_map/ppermute | solution.py:32
  47.0 1.9 %collective-permute-done.9.refs_5_ = bf16[128,128]{1,0:T(8,128)(2,1)S(1)} collective-permute-done((bf16[128,128]{1,0:T(8,128)(2,1)S(1)}, bf16[128,128]{1,0:T(8,128)(2,1)S(1)}, u32[]{:S(2)}, u32[]{:S(2)}) %collective-permute-start.9) | collective-permute-done | bytes 32800 | tf_op jit(solution)/shard_map/ppermute | solution.py:32
  49.0 3.6 %shard_map.196 = (f32[128,512]{1,0:T(8,128)S(1)}, f32[128,64]{1,0:T(8,128)S(1)}, bf16[128,128]{1,0:T(8,128)(2,1)S(1)}, bf16[128,128]{1,0:T(8,128)(2,1)S(1)}, bf1...) custom-call(f32[128,512]{1,0:T(8,128)S(1)} %get-tuple-element.44.refs_0_, f32[128,512]{1,0:T(8,128)S(1)} %bitcast.23, ...), custom_call_target="tpu_custom_call" | custom-call | tf_op jit(solution)/shard_map/pallas_call | solution.py:307
  52.7 4.4 %collective-permute-start.11 = (bf16[128,128]{1,0:T(8,128)(2,1)S(1)}, bf16[128,128]{1,0:T(8,128)(2,1)S(1)}, u32[]{:S(2)}, u32[]{:S(2)}) collective-permute-start(bf16[128,128]{1,0:T(8,128)(2,1)S(1)} %get-tuple-element.53), channel_id=1, source_target_pairs={{0,15},{1,0},{2,1},{3,2},{4,3},{5,4},{6,5},{7,6},{8,7},{9,8},{10,9... | collective-permute-start | bytes 98312 | tf_op jit(solution)/shard_map/ppermute | solution.py:32
  57.5 1.7 %collective-permute-start.13 = (bf16[128,128]{1,0:T(8,128)(2,1)S(1)}, bf16[128,128]{1,0:T(8,128)(2,1)S(1)}, u32[]{:S(2)}, u32[]{:S(2)}) collective-permute-start(bf16[128,128]{1,0:T(8,128)(2,1)S(1)} %get-tuple-element.55), channel_id=1, source_target_pairs={{0,16},{16,0},{1,17},{17,1},{2,18},{18,2},{3,19},{19,3},{4,20},{20... | collective-permute-start | bytes 98312 | tf_op jit(solution)/shard_map/ppermute | solution.py:32
  59.3 1.8 %collective-permute-done.12.refs_4_ = bf16[128,128]{1,0:T(8,128)(2,1)S(1)} collective-permute-done((bf16[128,128]{1,0:T(8,128)(2,1)S(1)}, bf16[128,128]{1,0:T(8,128)(2,1)S(1)}, u32[]{:S(2)}, u32[]{:S(2)}) %collective-permute-start.12) | collective-permute-done | bytes 32800 | tf_op jit(solution)/shard_map/ppermute | solution.py:32
  61.4 4.0 %shard_map.197 = (f32[128,512]{1,0:T(8,128)S(1)}, f32[128,64]{1,0:T(8,128)S(1)}, bf16[128,128]{1,0:T(8,128)(2,1)S(1)}, bf16[128,128]{1,0:T(8,128)(2,1)S(1)}, bf1...) custom-call(f32[128,512]{1,0:T(8,128)S(1)} %get-tuple-element.50.refs_0_.refs_2_, ...), custom_call_target="tpu_custom_call" | custom-call | tf_op jit(solution)/shard_map/pallas_call | solution.py:307
  65.5 4.4 %collective-permute-start.15 = (bf16[128,128]{1,0:T(8,128)(2,1)S(1)}, bf16[128,128]{1,0:T(8,128)(2,1)S(1)}, u32[]{:S(2)}, u32[]{:S(2)}) collective-permute-start(bf16[128,128]{1,0:T(8,128)(2,1)S(1)} %get-tuple-element.61), channel_id=1, source_target_pairs={{0,15},{1,0},{2,1},{3,2},{4,3},{5,4},{6,5},{7,6},{8,7},{9,8},{10,9... | collective-permute-start | bytes 98312 | tf_op jit(solution)/shard_map/ppermute | solution.py:32
  69.9 1.7 %collective-permute-start.16 = (bf16[128,128]{1,0:T(8,128)(2,1)S(1)}, bf16[128,128]{1,0:T(8,128)(2,1)S(1)}, u32[]{:S(2)}, u32[]{:S(2)}) collective-permute-start(bf16[128,128]{1,0:T(8,128)(2,1)S(1)} %get-tuple-element.62), channel_id=1, source_target_pairs={{0,16},{16,0},{1,17},{17,1},{2,18},{18,2},{3,19},{19,3},{4,20},{20... | collective-permute-start | bytes 98312 | tf_op jit(solution)/shard_map/ppermute | solution.py:32
  72.0 1.9 %collective-permute-done.16.refs_6_ = bf16[128,128]{1,0:T(8,128)(2,1)S(1)} collective-permute-done((bf16[128,128]{1,0:T(8,128)(2,1)S(1)}, bf16[128,128]{1,0:T(8,128)(2,1)S(1)}, u32[]{:S(2)}, u32[]{:S(2)}) %collective-permute-start.16) | collective-permute-done | bytes 32800 | tf_op jit(solution)/shard_map/ppermute | solution.py:32
  73.9 1.7 %collective-permute-done.17.refs_7_ = bf16[128,128]{1,0:T(8,128)(2,1)S(1)} collective-permute-done((bf16[128,128]{1,0:T(8,128)(2,1)S(1)}, bf16[128,128]{1,0:T(8,128)(2,1)S(1)}, u32[]{:S(2)}, u32[]{:S(2)}) %collective-permute-start.17) | collective-permute-done | bytes 32800 | tf_op jit(solution)/shard_map/ppermute | solution.py:32
  75.5 3.7 %shard_map.198 = (f32[128,512]{1,0:T(8,128)S(1)}, f32[128,64]{1,0:T(8,128)S(1)}) custom-call(f32[128,512]{1,0:T(8,128)S(1)} %get-tuple-element.58.refs_0_, f32[128,64]{1,0:T(8,128)S(1)} %get-tuple-element.59.refs_1_, f32[128,512]{1,0:T(8,128)S(1)} %get-tuple-element.50.refs_0_.refs_2_, f32[128,64]{1,0:T(8,128)S(1)} %get-tuple-element.51.refs_1_.refs_3_, ...), custom_call_target="tpu_custom_call" | custom-call | tf_op jit(solution)/shard_map/pallas_call | solution.py:307
  80.4 4.5 %collective-permute-start.19 = (f32[2,8,512]{2,1,0:T(8,128)S(1)}, f32[2,8,512]{2,1,0:T(8,128)S(1)}, u32[]{:S(2)}, u32[]{:S(2)}) collective-permute-start(f32[2,8,512]{2,1,0:T(8,128)S(1)} %gather_fusion.1), channel_id=1, source_target_pairs={{0,15},{1,0},{2,1},{3,2},{4,3},{5,4},{6,5},{7,6},{8,7},{9,8},{10,9... | collective-permute-start | bytes 98312 | tf_op jit(solution)/shard_map/ppermute | solution.py:32
  87.1 0.8 broadcast_select_fusion
  (110 shorter events, 15.5 us)
Async XLA Ops:
  0.6 32.2 %copy-start = (bf16[3,512,512]{2,1,0:T(8,128)(2,1)S(1)}, bf16[3,512,512]{2,1,0:T(8,128)(2,1)}, u32[]{:S(2)}) copy-start(bf16[3,512,512]{2,1,0:T(8,128)(2,1)} %constant.92.clone.refs_13_.refs_14_.refs_16_) | copy-start | bytes 4718596
  1.5 20.5 %copy-start.28 = (pred[16]{0:T(512)(128)(4,1)}, pred[16]{0:T(512)(128)(4,1)S(1)}, u32[]{:S(2)}) copy-start(pred[16]{0:T(512)(128)(4,1)S(1)} %get-tuple-element.69) | copy-start | bytes 52
  10.2 15.0 %copy-start.27 = (s32[16]{0:T(128)S(1)}, s32[16]{0:T(128)}, u32[]{:S(2)}) copy-start(s32[16]{0:T(128)} %param.24) | copy-start | bytes 196
  10.2 22.6 %copy-start.7 = (bf16[512,512]{1,0:T(8,128)(2,1)S(1)}, bf16[512,512]{1,0:T(8,128)(2,1)}, u32[]{:S(2)}) copy-start(bf16[512,512]{1,0:T(8,128)(2,1)} %constant.95.clone.g7s_ref.refs_16_.refs_19_.refs_23_) | copy-start | bytes 1572868
  10.2 22.6 %copy-start.16 = (bf16[128,16]{1,0:T(8,128)(2,1)S(1)}, bf16[128,16]{1,0:T(8,128)(2,1)}, u32[]{:S(2)}) copy-start(bf16[128,16]{1,0:T(8,128)(2,1)} %constant.89.clone.bc_ref.refs_11_.refs_12_.refs_14_) | copy-start | bytes 12292
  10.2 22.6 %copy-start.22 = (bf16[48,128]{1,0:T(8,128)(2,1)S(1)}, bf16[48,128]{1,0:T(8,128)(2,1)}, u32[]{:S(2)}) copy-start(bf16[48,128]{1,0:T(8,128)(2,1)} %constant.90.clone.refs_12_.refs_13_.refs_15_) | copy-start | bytes 36868
  14.4 18.4 %collective-permute-start.2 = (bf16[128,128]{1,0:T(8,128)(2,1)}, bf16[128,128]{1,0:T(8,128)(2,1)}, u32[]{:S(2)}, u32[]{:S(2)}) collective-permute-start(bf16[128,128]{1,0:T(8,128)(2,1)} %get-tuple-element.34), channel_id=1, source_target_pairs={{0,1},{1,2},{2,3},{3,4},{4,5},{5,6},{6,7},{7,8},{8,9},{9,10},{10,1... | collective-permute-start | bytes 98312 | tf_op jit(solution)/shard_map/ppermute | solution.py:32
  14.9 17.9 %collective-permute-start.3 = (bf16[128,128]{1,0:T(8,128)(2,1)}, bf16[128,128]{1,0:T(8,128)(2,1)}, u32[]{:S(2)}, u32[]{:S(2)}) collective-permute-start(bf16[128,128]{1,0:T(8,128)(2,1)} %get-tuple-element.35), channel_id=1, source_target_pairs={{0,15},{1,0},{2,1},{3,2},{4,3},{5,4},{6,5},{7,6},{8,7},{9,8},{10,9... | collective-permute-start | bytes 98312 | tf_op jit(solution)/shard_map/ppermute | solution.py:32
  19.9 12.9 %collective-permute-start.4 = (bf16[128,128]{1,0:T(8,128)(2,1)}, bf16[128,128]{1,0:T(8,128)(2,1)}, u32[]{:S(2)}, u32[]{:S(2)}) collective-permute-start(bf16[128,128]{1,0:T(8,128)(2,1)} %get-tuple-element.36), channel_id=1, source_target_pairs={{0,16},{16,0},{1,17},{17,1},{2,18},{18,2},{3,19},{19,3},{4,20},{20... | collective-permute-start | bytes 98312 | tf_op jit(solution)/shard_map/ppermute | solution.py:32
  21.8 11.0 %collective-permute-start.5 = (bf16[128,128]{1,0:T(8,128)(2,1)}, bf16[128,128]{1,0:T(8,128)(2,1)}, u32[]{:S(2)}, u32[]{:S(2)}) collective-permute-start(bf16[128,128]{1,0:T(8,128)(2,1)} %get-tuple-element.37), channel_id=1, source_target_pairs={{0,16},{16,0},{1,17},{17,1},{2,18},{18,2},{3,19},{19,3},{4,20},{20... | collective-permute-start | bytes 98312 | tf_op jit(solution)/shard_map/ppermute | solution.py:32
  24.1 5.7 %collective-permute-start = (s32[2]{0:T(128)}, s32[2]{0:T(128)}, u32[]{:S(2)}, u32[]{:S(2)}) collective-permute-start(s32[2]{0:T(128)} %add_select_fusion.2), channel_id=1, source_target_pairs={{0,1},{1,2},{2,3},{3,4},{4,5},{5,6},{6,7},{7,8},{8,9},{9,10},{10,1... | collective-permute-start | bytes 32 | tf_op jit(solution)/shard_map/ppermute | solution.py:32
  29.8 1.9 %collective-permute-start.1 = (s32[2]{0:T(128)S(1)}, s32[2]{0:T(128)S(1)}, u32[]{:S(2)}, u32[]{:S(2)}) collective-permute-start(s32[2]{0:T(128)S(1)} %add_select_fusion.1), channel_id=1, source_target_pairs={{0,15},{1,0},{2,1},{3,2},{4,3},{5,4},{6,5},{7,6},{8,7},{9,8},{10,9... | collective-permute-start | bytes 32 | tf_op jit(solution)/shard_map/ppermute | solution.py:32
  36.1 12.9 %copy-start.5 = (bf16[768,512]{1,0:T(8,128)(2,1)S(1)}, bf16[768,512]{1,0:T(8,128)(2,1)}, u32[]{:S(2)}) copy-start(bf16[768,512]{1,0:T(8,128)(2,1)} %constant.94.clone.refs_15_.refs_16_.refs_18_) | copy-start | bytes 2359300
  36.1 12.9 %copy-start.9 = (bf16[3,64,768]{2,1,0:T(8,128)(2,1)S(1)}, bf16[3,64,768]{2,1,0:T(8,128)(2,1)}, u32[]{:S(2)}) copy-start(bf16[3,64,768]{2,1,0:T(8,128)(2,1)} %constant.97.clone.tm_ref.refs_17_.refs_21_.refs_23_) | copy-start | bytes 884740
  36.1 12.9 %copy-start.17 = (bf16[3,64,512]{2,1,0:T(8,128)(2,1)S(1)}, bf16[3,64,512]{2,1,0:T(8,128)(2,1)}, u32[]{:S(2)}) copy-start(bf16[3,64,512]{2,1,0:T(8,128)(2,1)} %constant.98.clone.refs_20_.refs_24_) | copy-start | bytes 589828
  36.1 12.9 %copy-start.19 = (f32[128,1]{1,0:T(8,128)S(1)}, f32[128,1]{1,0:T(8,128)}, u32[]{:S(2)}) copy-start(f32[128,1]{1,0:T(8,128)} %copy-done.18) | copy-start | bytes 1540
  36.1 12.9 %copy-start.20 = (bf16[3,512,64]{2,1,0:T(8,128)(2,1)S(1)}, bf16[3,512,64]{2,1,0:T(8,128)(2,1)}, u32[]{:S(2)}) copy-start(bf16[3,512,64]{2,1,0:T(8,128)(2,1)} %constant.100.clone.refs_21_) | copy-start | bytes 589828
  38.6 6.5 %collective-permute-start.6 = (bf16[128,128]{1,0:T(8,128)(2,1)S(1)}, bf16[128,128]{1,0:T(8,128)(2,1)S(1)}, u32[]{:S(2)}, u32[]{:S(2)}) collective-permute-start(bf16[128,128]{1,0:T(8,128)(2,1)S(1)} %get-tuple-element.45), channel_id=1, source_target_pairs={{0,1},{1,2},{2,3},{3,4},{4,5},{5,6},{6,7},{7,8},{8,9},{9,10},{10,1... | collective-permute-start | bytes 98312 | tf_op jit(solution)/shard_map/ppermute | solution.py:32
  38.6 6.5 %collective-permute-start.7 = (bf16[128,128]{1,0:T(8,128)(2,1)S(1)}, bf16[128,128]{1,0:T(8,128)(2,1)S(1)}, u32[]{:S(2)}, u32[]{:S(2)}) collective-permute-start(bf16[128,128]{1,0:T(8,128)(2,1)S(1)} %get-tuple-element.46), channel_id=1, source_target_pairs={{0,15},{1,0},{2,1},{3,2},{4,3},{5,4},{6,5},{7,6},{8,7},{9,8},{10,9... | collective-permute-start | bytes 98312 | tf_op jit(solution)/shard_map/ppermute | solution.py:32
  43.1 3.9 %collective-permute-start.8 = (bf16[128,128]{1,0:T(8,128)(2,1)S(1)}, bf16[128,128]{1,0:T(8,128)(2,1)S(1)}, u32[]{:S(2)}, u32[]{:S(2)}) collective-permute-start(bf16[128,128]{1,0:T(8,128)(2,1)S(1)} %get-tuple-element.47), channel_id=1, source_target_pairs={{0,16},{16,0},{1,17},{17,1},{2,18},{18,2},{3,19},{19,3},{4,20},{20... | collective-permute-start | bytes 98312 | tf_op jit(solution)/shard_map/ppermute | solution.py:32
  45.0 3.9 %collective-permute-start.9 = (bf16[128,128]{1,0:T(8,128)(2,1)S(1)}, bf16[128,128]{1,0:T(8,128)(2,1)S(1)}, u32[]{:S(2)}, u32[]{:S(2)}) collective-permute-start(bf16[128,128]{1,0:T(8,128)(2,1)S(1)} %get-tuple-element.48), channel_id=1, source_target_pairs={{0,16},{16,0},{1,17},{17,1},{2,18},{18,2},{3,19},{19,3},{4,20},{20... | collective-permute-start | bytes 98312 | tf_op jit(solution)/shard_map/ppermute | solution.py:32
  49.0 12.4 %copy-start.3 = (bf16[512,768]{1,0:T(8,128)(2,1)S(1)}, bf16[512,768]{1,0:T(8,128)(2,1)}, u32[]{:S(2)}) copy-start(bf16[512,768]{1,0:T(8,128)(2,1)} %constant.93.clone.g7_ref.refs_14_.refs_15_.refs_17_) | copy-start | bytes 2359300
  52.6 6.6 %collective-permute-start.10 = (bf16[128,128]{1,0:T(8,128)(2,1)S(1)}, bf16[128,128]{1,0:T(8,128)(2,1)S(1)}, u32[]{:S(2)}, u32[]{:S(2)}) collective-permute-start(bf16[128,128]{1,0:T(8,128)(2,1)S(1)} %get-tuple-element.52), channel_id=1, source_target_pairs={{0,1},{1,2},{2,3},{3,4},{4,5},{5,6},{6,7},{7,8},{8,9},{9,10},{10,1... | collective-permute-start | bytes 98312 | tf_op jit(solution)/shard_map/ppermute | solution.py:32
  52.7 6.6 %collective-permute-start.11 = (bf16[128,128]{1,0:T(8,128)(2,1)S(1)}, bf16[128,128]{1,0:T(8,128)(2,1)S(1)}, u32[]{:S(2)}, u32[]{:S(2)}) collective-permute-start(bf16[128,128]{1,0:T(8,128)(2,1)S(1)} %get-tuple-element.53), channel_id=1, source_target_pairs={{0,15},{1,0},{2,1},{3,2},{4,3},{5,4},{6,5},{7,6},{8,7},{9,8},{10,9... | collective-permute-start | bytes 98312 | tf_op jit(solution)/shard_map/ppermute | solution.py:32
  57.1 3.9 %collective-permute-start.12 = (bf16[128,128]{1,0:T(8,128)(2,1)S(1)}, bf16[128,128]{1,0:T(8,128)(2,1)S(1)}, u32[]{:S(2)}, u32[]{:S(2)}) collective-permute-start(bf16[128,128]{1,0:T(8,128)(2,1)S(1)} %get-tuple-element.54), channel_id=1, source_target_pairs={{0,16},{16,0},{1,17},{17,1},{2,18},{18,2},{3,19},{19,3},{4,20},{20... | collective-permute-start | bytes 98312 | tf_op jit(solution)/shard_map/ppermute | solution.py:32
  57.5 3.9 %collective-permute-start.13 = (bf16[128,128]{1,0:T(8,128)(2,1)S(1)}, bf16[128,128]{1,0:T(8,128)(2,1)S(1)}, u32[]{:S(2)}, u32[]{:S(2)}) collective-permute-start(bf16[128,128]{1,0:T(8,128)(2,1)S(1)} %get-tuple-element.55), channel_id=1, source_target_pairs={{0,16},{16,0},{1,17},{17,1},{2,18},{18,2},{3,19},{19,3},{4,20},{20... | collective-permute-start | bytes 98312 | tf_op jit(solution)/shard_map/ppermute | solution.py:32
  65.4 6.5 %collective-permute-start.14 = (bf16[128,128]{1,0:T(8,128)(2,1)S(1)}, bf16[128,128]{1,0:T(8,128)(2,1)S(1)}, u32[]{:S(2)}, u32[]{:S(2)}) collective-permute-start(bf16[128,128]{1,0:T(8,128)(2,1)S(1)} %get-tuple-element.60), channel_id=1, source_target_pairs={{0,1},{1,2},{2,3},{3,4},{4,5},{5,6},{6,7},{7,8},{8,9},{9,10},{10,1... | collective-permute-start | bytes 98312 | tf_op jit(solution)/shard_map/ppermute | solution.py:32
  65.5 6.5 %collective-permute-start.15 = (bf16[128,128]{1,0:T(8,128)(2,1)S(1)}, bf16[128,128]{1,0:T(8,128)(2,1)S(1)}, u32[]{:S(2)}, u32[]{:S(2)}) collective-permute-start(bf16[128,128]{1,0:T(8,128)(2,1)S(1)} %get-tuple-element.61), channel_id=1, source_target_pairs={{0,15},{1,0},{2,1},{3,2},{4,3},{5,4},{6,5},{7,6},{8,7},{9,8},{10,9... | collective-permute-start | bytes 98312 | tf_op jit(solution)/shard_map/ppermute | solution.py:32
  69.9 3.9 %collective-permute-start.16 = (bf16[128,128]{1,0:T(8,128)(2,1)S(1)}, bf16[128,128]{1,0:T(8,128)(2,1)S(1)}, u32[]{:S(2)}, u32[]{:S(2)}) collective-permute-start(bf16[128,128]{1,0:T(8,128)(2,1)S(1)} %get-tuple-element.62), channel_id=1, source_target_pairs={{0,16},{16,0},{1,17},{17,1},{2,18},{18,2},{3,19},{19,3},{4,20},{20... | collective-permute-start | bytes 98312 | tf_op jit(solution)/shard_map/ppermute | solution.py:32
  71.6 3.9 %collective-permute-start.17 = (bf16[128,128]{1,0:T(8,128)(2,1)S(1)}, bf16[128,128]{1,0:T(8,128)(2,1)S(1)}, u32[]{:S(2)}, u32[]{:S(2)}) collective-permute-start(bf16[128,128]{1,0:T(8,128)(2,1)S(1)} %get-tuple-element.63), channel_id=1, source_target_pairs={{0,16},{16,0},{1,17},{17,1},{2,18},{18,2},{3,19},{19,3},{4,20},{20... | collective-permute-start | bytes 98312 | tf_op jit(solution)/shard_map/ppermute | solution.py:32
  79.8 6.1 %collective-permute-start.18 = (f32[2,8,512]{2,1,0:T(8,128)S(1)}, f32[2,8,512]{2,1,0:T(8,128)S(1)}, u32[]{:S(2)}, u32[]{:S(2)}) collective-permute-start(f32[2,8,512]{2,1,0:T(8,128)S(1)} %gather_fusion), channel_id=1, source_target_pairs={{0,1},{1,2},{2,3},{3,4},{4,5},{5,6},{6,7},{7,8},{8,9},{9,10},{10,1... | collective-permute-start | bytes 98312 | tf_op jit(solution)/shard_map/ppermute | solution.py:32
  80.4 6.1 %collective-permute-start.19 = (f32[2,8,512]{2,1,0:T(8,128)S(1)}, f32[2,8,512]{2,1,0:T(8,128)S(1)}, u32[]{:S(2)}, u32[]{:S(2)}) collective-permute-start(f32[2,8,512]{2,1,0:T(8,128)S(1)} %gather_fusion.1), channel_id=1, source_target_pairs={{0,15},{1,0},{2,1},{3,2},{4,3},{5,4},{6,5},{7,6},{8,7},{9,8},{10,9... | collective-permute-start | bytes 98312 | tf_op jit(solution)/shard_map/ppermute | solution.py:32
  (17 other events, 49.5 us)

commit v2 on v1

--- a/solution.py
+++ b/solution.py
@@ -126,17 +126,13 @@
         for k, node in enumerate(nodes3[side]):
             tm[node, side * LANE : side * LANE + P7 * P7] = mortar_up[:, k]
             mds[side * LANE : side * LANE + P7 * P7, node] = mortar_down[k, :]
-    send_cols = np.concatenate([np.arange(s * LANE, (s + 1) * LANE) for s in SEND_FACES])
     tables = {
         "d7t": to_bf16(d7t),
         "d3t": to_bf16(d3t),
         "lift": lift_table,
         "mortar_up": mortar_up,
         "g7": to_bf16(g7),
-        "s7": to_bf16(g7.T),
-        "g7s": to_bf16(g7[:, send_cols]),
         "tm": split_parts(tm),
-        "tms": split_parts(tm[:, send_cols]),
         "mds": split_parts(mds),
         "pjt": split_parts(projection.T),
         "nodes7": nodes7,
@@ -160,6 +156,15 @@
 def _exact_left(x, table):
     hi, mid, lo = _split(x)
     return (_dot(hi, table) + _dot(mid, table)) + _dot(lo, table)
+
+
+def _dot_t(a, b):
+    return lax.dot_general(a, b, (((1,), (1,)), ((), ())), preferred_element_type=f32)
+
+
+def _exact_left_t(x, table):
+    hi, mid, lo = _split(x)
+    return (_dot_t(hi, table) + _dot_t(mid, table)) + _dot_t(lo, table)
 
 
 def _exact_right(table, x):
@@ -207,7 +212,6 @@
     sel_tab = take()
     d7_ref = take()
     g7_ref = take()
-    s7_ref = take()
     if coarse:
         v3_ref = take()
         m3_ref = take()
@@ -216,10 +220,6 @@
     if coarse or project:
         tm_ref = take()
         sw_ref = take()
-    if sends:
-        g7s_ref = take()
-        if coarse or project:
-            tms_ref = take()
     if project:
         pj_ref = take()
     out_u = take()
@@ -258,7 +258,7 @@
         divergence = term if divergence is None else divergence + term
     result = _rate_source(u, pre, stc, bcast, sel, local) - divergence
     jump = (P7 * (P7 - 1) / 2.0) * (m7_ref[...] * (trace7 - near))
-    rate7 = result + _exact_left(jump, s7_ref[...])
+    rate7 = result + _exact_left_t(jump, g7_ref[...])
 
     if coarse:
         div3 = None
@@ -286,15 +286,15 @@
         new_c = _full(new_u, pj_ref)
         out_c[...] = new_c
     if sends:
-        send7 = _dot(new_u.astype(bf16), g7s_ref[...])
+        send7 = _dot(new_u.astype(bf16), g7_ref[...])
         if new_c is not None:
-            send3 = _full(new_c, tms_ref).astype(bf16).astype(f32)
+            send3 = _full(new_c, tm_ref).astype(bf16).astype(f32)
             send = jnp.where(sw_ref[...] > 0.5, send3, send7)
         else:
             send = send7
         send = send.astype(bf16)
-        for k in range(len(SEND_FACES)):
-            out_send[k][...] = send[:, k * LANE : (k + 1) * LANE]
+        for k, side in enumerate(SEND_FACES):
+            out_send[k][...] = send[:, side * LANE : (side + 1) * LANE]
 
 
 def _vmem():
@@ -313,14 +313,8 @@
     )(*inputs)
 
 
-def trace_kernel(u_ref, g7s_ref, *out_refs):
-    send = _dot(u_ref[...].astype(bf16), g7s_ref[...]).astype(bf16)
-    for k in range(len(SEND_FACES)):
-        out_refs[k][...] = send[:, k * LANE : (k + 1) * LANE]
-
-
 def setup_kernel(local, fields, u_ref, vt_ref, packed_ref, lift_ref, g7_ref, tm_ref, bc_ref,
-                 g7s_ref, pre_ref, sto_ref, v7_out, m7_out, v3_out, m3_out, pl_out, pr_out,
+                 fsel_ref, v7_out, m7_out, v3_out, m3_out, pl_out, pr_out,
                  pre_out, stc_out, sw_out, *send_refs):
     rows = local * fields
     bcast = bc_ref[...]
@@ -355,19 +349,26 @@
         if side in SEND_FACES:
             pr_out[SEND_FACES.index(side)] = jnp.where(hit & far, 1.0, 0.0).astype(bf16)
     sw_out[...] = rep[:, 6:7]
-    elem = lax.broadcasted_iota(jnp.int32, (local, 1), 0)
-    pre = jnp.zeros((local, 1), f32)
-    for e in range(local):
-        pre = jnp.where(elem == e, pre_ref[e], pre)
-    pre_out[...] = pre
-    row_fi = lax.broadcasted_iota(jnp.int32, (rows, 1), 0) % fields
-    stc = jnp.zeros((rows, 1), f32)
-    for f in range(fields):
-        stc = jnp.where(row_fi == f, sto_ref[f], stc)
-    stc_out[...] = stc
-    send = _dot(u_ref[...].astype(bf16), g7s_ref[...]).astype(bf16)
-    for k in range(len(SEND_FACES)):
-        send_refs[k][...] = send[:, k * LANE : (k + 1) * LANE]
+    pre_out[...] = packed_ref[:, 7:8]
+    stc_out[...] = _exact_right(fsel_ref[...], packed_ref[...])[:, 8:9]
+    send = _dot(u_ref[...].astype(bf16), g7_ref[...]).astype(bf16)
+    for k, side in enumerate(SEND_FACES):
+        send_refs[k][...] = send[:, side * LANE : (side + 1) * LANE]
+
+
+def setup_entry(local, fields, n_in, n_out, *refs):
+    sources = refs[:n_in]
+    outs = refs[n_in : n_in + n_out]
+    buffers = refs[n_in + n_out : 2 * n_in + n_out]
+    sems = refs[2 * n_in + n_out]
+    copies = [
+        pltpu.make_async_copy(sources[i], buffers[i], sems.at[i]) for i in range(n_in)
+    ]
+    for copy in copies:
+        copy.start()
+    for copy in copies:
+        copy.wait()
+    setup_kernel(local, fields, *buffers, *outs)
 
 
 def per_device(state, velocity, pre_exp, stoich, neighbours, switch, new_owner):
@@ -385,9 +386,18 @@
     near_local = neighbours - near_device * local_count
     remote = near_device != device_id
     codes = (near_local + local_count * remote.astype(jnp.int32)).astype(f32)
+    sto_col = jnp.zeros((local_count,), f32).at[:field_count].set(stoich)
     packed = jnp.concatenate(
-        [codes, switch.astype(f32)[:, None], jnp.zeros((local_count, LANE - 7), f32)], axis=1
-    )
+        [
+            codes,
+            switch.astype(f32)[:, None],
+            pre_exp[:, None],
+            sto_col[:, None],
+            jnp.zeros((local_count, LANE - 9), f32),
+        ],
+        axis=1,
+    )
+    fsel = jnp.asarray(to_bf16(np.arange(rows)[:, None] % field_count == np.arange(local_count)[None, :]))
     vt = jnp.transpose(velocity, (0, 2, 1))
     row_elem = np.arange(rows) // field_count
     bcast = jnp.asarray(to_bf16(row_elem[:, None] == np.arange(local_count)[None, :]))
@@ -396,11 +406,8 @@
     lift_t = jnp.asarray(to_bf16(tab["lift"].astype(np.float32).T))
     d7t = jnp.asarray(tab["d7t"])
     g7 = jnp.asarray(tab["g7"])
-    s7 = jnp.asarray(tab["s7"])
-    g7s = jnp.asarray(tab["g7s"])
     d3t = jnp.asarray(tab["d3t"])
     tm = jnp.asarray(tab["tm"])
-    tms = jnp.asarray(tab["tms"])
     mds = jnp.asarray(tab["mds"])
     pjt = jnp.asarray(tab["pjt"])
 
@@ -429,28 +436,30 @@
         jax.ShapeDtypeStruct((rows, 1), f32),
     ] + [send_shape] * 4
     u0 = state.reshape(rows, P7**3)
-    smem = pl.BlockSpec(memory_space=pltpu.SMEM)
+    setup_in = [u0, vt, packed, lift_t, g7, tm, bcast, fsel]
     res = pl.pallas_call(
-        functools.partial(setup_kernel, local_count, field_count),
+        functools.partial(setup_entry, local_count, field_count, len(setup_in), len(setup_out)),
         out_shape=setup_out,
-        in_specs=[_vmem()] * 8 + [smem, smem],
+        in_specs=[pl.BlockSpec(memory_space=pl.ANY) for _ in setup_in],
         out_specs=[_vmem() for _ in setup_out],
+        scratch_shapes=[pltpu.VMEM(x.shape, x.dtype) for x in setup_in]
+        + [pltpu.SemaphoreType.DMA((len(setup_in),))],
         compiler_params=pltpu.CompilerParams(vmem_limit_bytes=48 * 1024 * 1024),
-    )(u0, vt, packed, lift_t, g7, tm, bcast, g7s, pre_exp, stoich)
+    )(*setup_in)
     v7, m7, v3, m3, p_local, p_remote, pre, stc, sw = res[:9]
     sends = res[9:]
-    common = [p_local, p_remote, v7, m7, pre, stc, bcast, sel, d7t, g7, s7]
+    common = [p_local, p_remote, v7, m7, pre, stc, bcast, sel, d7t, g7]
     recv = exchange(sends)
     res = run_stage(
         (False, False, False, True, local_count),
-        [u0] + recv + common + [g7s],
+        [u0] + recv + common,
         [u_shape] + [send_shape] * 4,
     )
     first, sends = res[0], res[1:]
     recv = exchange(sends)
     res = run_stage(
         (False, True, True, True, local_count),
-        [first, u0] + recv + common + [tm, sw, g7s, tms, pjt],
+        [first, u0] + recv + common + [tm, sw, pjt],
         [u_shape, c_shape] + [send_shape] * 4,
     )
     after, coarse, sends = res[0], res[1], res[2:]
@@ -458,7 +467,7 @@
     mixed_tail = [v3, m3, d3t, mds, tm, sw]
     res = run_stage(
         (True, False, False, True, local_count),
-        [after, coarse] + recv + common + mixed_tail + [g7s, tms],
+        [after, coarse] + recv + common + mixed_tail,
         [u_shape, c_shape] + [send_shape] * 4,
     )
     first7, first3, sends = res[0], res[1], res[2:]

time: 88.6 us -> 94.2 us (1.063)
  other arithmetic: 7.36 us -> 15.2 us
  waiting for transfers between devices: 15.5 us -> 11.6 us
  starting transfers between devices: 32.2 us -> 36.1 us
  Pallas kernels: 16.6 us -> 14.5 us
    ppermute x20, waiting for transfers between devices: 15.5 us -> 11.6 us  [shifted(): return lax.ppermute(value, axis, pairs)]
    ppermute x20, starting transfers between devices: 32.2 us -> 36.1 us  [shifted(): return lax.ppermute(value, axis, pairs)]
    another operation x4, other arithmetic: 0.08 us -> 3.55 us
    unnamed x59 -> x41, local copies, waits for them, and re-layouts: 13.1 us -> 10.2 us
    pallas_call x4, Pallas kernels: 13.8 us -> 11.8 us  [run_stage(): pl.pallas_call(kernel, out_shape=out_shapes, in_specs=[_vmem() for _ in i...]
    broadcast_in_dim x1 -> x3, local copies, waits for them, and re-layouts: 0.01 us -> 1.46 us  [the longest x1 0.73 us: per_device(): pre_exp[:, None]]
    sub x2, other arithmetic: 0.23 us -> 1.62 us  [first_rows(): rank = jnp.cumsum(mask.astype(jnp.int32)) - 1]
    another operation x2, local copies, waits for them, and re-layouts: 0.17 us -> 1.37 us
  transfers between devices with their start and end apart: 20 -> 20, of which waited for: 10 -> 9; matrix products, arithmetic and copies ran while one was open for 7% -> 16% of each run, Pallas kernels for 0% -> 0%
where the time goes in v2:
time: 94.2 us; the launch traced here: 93.3 us
  starting transfers between devices  36.1 us (38%)
  other arithmetic  15.2 us (16%)
  local copies, waits for them, and re-layouts  14.9 us (16%)
  Pallas kernels  14.5 us (15%)
  waiting for transfers between devices  11.6 us (12%)
    ppermute x20, starting transfers between devices, shifted(): return lax.ppermute(value, axis, pairs)  36.1 us
    pallas_call x4, Pallas kernels, run_stage(): pl.pallas_call(kernel, out_shape=out_shapes, in_specs=[_vmem() for _ in i...  11.8 us
    ppermute x20, waiting for transfers between devices, shifted(): return lax.ppermute(value, axis, pairs)  11.6 us
    unnamed x41, local copies, waits for them, and re-layouts  10.2 us
    another operation x4, other arithmetic  3.55 us
    pallas_call x1, Pallas kernels, per_device(): pl.pallas_call(functools.partial(setup_entry, local_count, field_count, l...  2.71 us
  transfers between devices with their start and end apart: 20, of which 9 were waited for; matrix products, arithmetic and copies ran while one was open for 16% of the time, Pallas kernels for 0%

profile of v2, /device:TPU:0, one launch (start us, length us, event | category | flops | bytes accessed | tf_op | source)
XLA Modules:
  0.0 93.3 jit_solution(2538823580134176434)
XLA Ops:
  0.7 1.4 %and_select_fusion = (s32[16]{0:T(128)}, pred[16]{0:T(512)(128)(4,1)}, pred[16]{0:T(512)(128)(4,1)}, f32[16,1]{0,1:T(1,128)S(1)}) fusion(s32[]{:T(128)S(6)} %mul.13, s32[16]{0:T(128)} %param.24, s32[16]{0:T(128)} %param.25, s32[]{:T(128)S(6)} %select_n.77, s32[]{:T(128)S(6)} %select_n.76), kind=kLoop, calls=%fused_computation.29 | loop fusion | flops 208 | bytes 300 | tf_op jit(solution)/shard_map/jit(_where)/select_n | solution.py:502
  4.5 1.1 %copy-done.1 = bf16[512,768]{1,0:T(8,128)(2,1)S(1)} copy-done((bf16[512,768]{1,0:T(8,128)(2,1)S(1)}, bf16[512,768]{1,0:T(8,128)(2,1)}, u32[]{:S(2)}) %copy-start.1) | copy-done | bytes 786456
  5.6 1.0 %copy-done.4 = bf16[3,64,768]{2,1,0:T(8,128)(2,1)S(1)} copy-done((bf16[3,64,768]{2,1,0:T(8,128)(2,1)S(1)}, bf16[3,64,768]{2,1,0:T(8,128)(2,1)}, u32[]{:S(2)}) %copy-start.4) | copy-done | bytes 294936
  6.6 0.9 %copy-done.7 = f32[16,8,512]{2,1,0:T(8,128)S(1)} copy-done((f32[16,8,512]{2,1,0:T(8,128)S(1)}, f32[16,8,512]{2,1,0:T(8,128)}, u32[]{:S(2)}) %copy-start.7) | copy-done | bytes 262168
  8.3 0.8 copy-done.16
  10.6 2.7 %shard_map.176 = (bf16[3,128,512]{2,1,0:T(8,128)(2,1)S(1)}, f32[128,768]{1,0:T(8,128)S(1)}, f32[3,128,64]{2,1,0:T(8,128)S(1)}, f32[128,768]{1,0:T(8,128)S(1)}, b...) custom-call(f32[128,512]{1,0:T(8,128)S(1)} %bitcast.23, ...), custom_call_target="tpu_custom_call" | custom-call | tf_op jit(solution)/shard_map/pallas_call | solution.py:440
  14.5 5.0 %collective-permute-start.3 = (bf16[128,128]{1,0:T(8,128)(2,1)}, bf16[128,128]{1,0:T(8,128)(2,1)S(1)}, u32[]{:S(2)}, u32[]{:S(2)}) collective-permute-start(bf16[128,128]{1,0:T(8,128)(2,1)} %get-tuple-element.47), channel_id=1, source_target_pairs={{0,15},{1,0},{2,1},{3,2},{4,3},{5,4},{6,5},{7,6},{8,7},{9,8},{10,9... | collective-permute-start | bytes 98312 | tf_op jit(solution)/shard_map/ppermute | solution.py:32
  19.5 1.9 %collective-permute-start.4 = (bf16[128,128]{1,0:T(8,128)(2,1)}, bf16[128,128]{1,0:T(8,128)(2,1)}, u32[]{:S(2)}, u32[]{:S(2)}) collective-permute-start(bf16[128,128]{1,0:T(8,128)(2,1)} %get-tuple-element.48), channel_id=1, source_target_pairs={{0,16},{16,0},{1,17},{17,1},{2,18},{18,2},{3,19},{19,3},{4,20},{20... | collective-permute-start | bytes 98312 | tf_op jit(solution)/shard_map/ppermute | solution.py:32
  21.5 1.2 %convert_bitcast_fusion.1 = s32[16,1]{0,1:T(1,128)} fusion(pred[16]{0:T(512)(128)(4,1)} %get-tuple-element.81), kind=kLoop, calls=%fused_computation.41 | loop fusion | flops 16 | bytes 80 | tf_op jit(solution)/shard_map/convert
  24.0 0.8 add_reduce_fusion.1
  27.5 1.1 %convert_bitcast_fusion = s32[16,1]{0,1:T(1,128)} fusion(pred[16]{0:T(512)(128)(4,1)} %get-tuple-element.82), kind=kLoop, calls=%fused_computation.40 | loop fusion | flops 16 | bytes 80 | tf_op jit(solution)/shard_map/convert.1
  29.9 0.8 add_reduce_fusion
  32.2 1.2 %broadcast_compare_fusion.1 = pred[16]{0:T(512)(128)(4,1)} fusion(s32[16]{0:T(128)} %param.24), kind=kLoop, calls=%fused_computation.46 | loop fusion | flops 16 | bytes 80 | tf_op jit(solution)/shard_map/eq | solution.py:483
  34.0 4.5 %collective-permute-start.1 = (s32[2]{0:T(128)S(1)}, s32[2]{0:T(128)S(1)}, u32[]{:S(2)}, u32[]{:S(2)}) collective-permute-start(s32[2]{0:T(128)S(1)} %add_select_fusion.1), channel_id=1, source_target_pairs={{0,15},{1,0},{2,1},{3,2},{4,3},{5,4},{6,5},{7,6},{8,7},{9,8},{10,9... | collective-permute-start | bytes 32 | tf_op jit(solution)/shard_map/ppermute | solution.py:32
  38.5 1.3 %collective-permute-done.1 = s32[2]{0:T(128)S(1)} collective-permute-done((s32[2]{0:T(128)S(1)}, s32[2]{0:T(128)S(1)}, u32[]{:S(2)}, u32[]{:S(2)}) %collective-permute-start.1) | collective-permute-done | bytes 40 | tf_op jit(solution)/shard_map/ppermute | solution.py:32
  41.0 1.1 %copy-done.2 = bf16[512,768]{1,0:T(8,128)(2,1)S(1)} copy-done((bf16[512,768]{1,0:T(8,128)(2,1)S(1)}, bf16[512,768]{1,0:T(8,128)(2,1)}, u32[]{:S(2)}) %copy-start.2) | copy-done | bytes 786456
  43.6 2.7 %shard_map.177 = (f32[128,512]{1,0:T(8,128)S(1)}, bf16[128,128]{1,0:T(8,128)(2,1)S(1)}, bf16[128,128]{1,0:T(8,128)(2,1)S(1)}, bf16[128,128]{1,0:T(8,128)(2,1)S(1)}, bf16[128,128]{1,0:T(8,128)(2,1)S(1)}) custom-call(f32[128,512]{1,0:T(8,128)S(1)} %bitcast.24, bf16[128,128]{1,0:T(8,128)(2,1)S(1)} %collective-permute-done.2.refs_1_, ...), custom_call_target="tpu_custom_call" | custom-call | tf_op jit(solution)/shard_map/pallas_call | solution.py:307
  46.3 4.4 %collective-permute-start.7 = (bf16[128,128]{1,0:T(8,128)(2,1)S(1)}, bf16[128,128]{1,0:T(8,128)(2,1)S(1)}, u32[]{:S(2)}, u32[]{:S(2)}) collective-permute-start(bf16[128,128]{1,0:T(8,128)(2,1)S(1)} %get-tuple-element.58), channel_id=1, source_target_pairs={{0,15},{1,0},{2,1},{3,2},{4,3},{5,4},{6,5},{7,6},{8,7},{9,8},{10,9... | collective-permute-start | bytes 98312 | tf_op jit(solution)/shard_map/ppermute | solution.py:32
  50.8 1.9 %collective-permute-start.8 = (bf16[128,128]{1,0:T(8,128)(2,1)S(1)}, bf16[128,128]{1,0:T(8,128)(2,1)S(1)}, u32[]{:S(2)}, u32[]{:S(2)}) collective-permute-start(bf16[128,128]{1,0:T(8,128)(2,1)S(1)} %get-tuple-element.59), channel_id=1, source_target_pairs={{0,16},{16,0},{1,17},{17,1},{2,18},{18,2},{3,19},{19,3},{4,20},{20... | collective-permute-start | bytes 98312 | tf_op jit(solution)/shard_map/ppermute | solution.py:32
  52.8 1.9 %collective-permute-done.8.refs_4_ = bf16[128,128]{1,0:T(8,128)(2,1)S(1)} collective-permute-done((bf16[128,128]{1,0:T(8,128)(2,1)S(1)}, bf16[128,128]{1,0:T(8,128)(2,1)S(1)}, u32[]{:S(2)}, u32[]{:S(2)}) %collective-permute-start.8) | collective-permute-done | bytes 32800 | tf_op jit(solution)/shard_map/ppermute | solution.py:32
  54.7 1.9 %collective-permute-done.9.refs_5_ = bf16[128,128]{1,0:T(8,128)(2,1)S(1)} collective-permute-done((bf16[128,128]{1,0:T(8,128)(2,1)S(1)}, bf16[128,128]{1,0:T(8,128)(2,1)S(1)}, u32[]{:S(2)}, u32[]{:S(2)}) %collective-permute-start.9) | collective-permute-done | bytes 32800 | tf_op jit(solution)/shard_map/ppermute | solution.py:32
  56.7 2.4 %shard_map.178 = (f32[128,512]{1,0:T(8,128)S(1)}, f32[128,64]{1,0:T(8,128)S(1)}, bf16[128,128]{1,0:T(8,128)(2,1)S(1)}, bf16[128,128]{1,0:T(8,128)(2,1)S(1)}, bf1...) custom-call(f32[128,512]{1,0:T(8,128)S(1)} %get-tuple-element.56.refs_0_, f32[128,512]{1,0:T(8,128)S(1)} %bitcast.25, ...), custom_call_target="tpu_custom_call" | custom-call | tf_op jit(solution)/shard_map/pallas_call | solution.py:307
  59.1 4.4 %collective-permute-start.11 = (bf16[128,128]{1,0:T(8,128)(2,1)S(1)}, bf16[128,128]{1,0:T(8,128)(2,1)S(1)}, u32[]{:S(2)}, u32[]{:S(2)}) collective-permute-start(bf16[128,128]{1,0:T(8,128)(2,1)S(1)} %get-tuple-element.65), channel_id=1, source_target_pairs={{0,15},{1,0},{2,1},{3,2},{4,3},{5,4},{6,5},{7,6},{8,7},{9,8},{10,9... | collective-permute-start | bytes 98312 | tf_op jit(solution)/shard_map/ppermute | solution.py:32
  63.9 1.7 %collective-permute-start.13 = (bf16[128,128]{1,0:T(8,128)(2,1)S(1)}, bf16[128,128]{1,0:T(8,128)(2,1)S(1)}, u32[]{:S(2)}, u32[]{:S(2)}) collective-permute-start(bf16[128,128]{1,0:T(8,128)(2,1)S(1)} %get-tuple-element.67), channel_id=1, source_target_pairs={{0,16},{16,0},{1,17},{17,1},{2,18},{18,2},{3,19},{19,3},{4,20},{20... | collective-permute-start | bytes 98312 | tf_op jit(solution)/shard_map/ppermute | solution.py:32
  65.7 1.8 %collective-permute-done.12.refs_4_ = bf16[128,128]{1,0:T(8,128)(2,1)S(1)} collective-permute-done((bf16[128,128]{1,0:T(8,128)(2,1)S(1)}, bf16[128,128]{1,0:T(8,128)(2,1)S(1)}, u32[]{:S(2)}, u32[]{:S(2)}) %collective-permute-start.12) | collective-permute-done | bytes 32800 | tf_op jit(solution)/shard_map/ppermute | solution.py:32
  67.9 2.8 %shard_map.179 = (f32[128,512]{1,0:T(8,128)S(1)}, f32[128,64]{1,0:T(8,128)S(1)}, bf16[128,128]{1,0:T(8,128)(2,1)S(1)}, bf16[128,128]{1,0:T(8,128)(2,1)S(1)}, bf1...) custom-call(f32[128,512]{1,0:T(8,128)S(1)} %get-tuple-element.62.refs_0_.refs_2_, ...), custom_call_target="tpu_custom_call" | custom-call | tf_op jit(solution)/shard_map/pallas_call | solution.py:307
  70.8 4.4 %collective-permute-start.15 = (bf16[128,128]{1,0:T(8,128)(2,1)S(1)}, bf16[128,128]{1,0:T(8,128)(2,1)S(1)}, u32[]{:S(2)}, u32[]{:S(2)}) collective-permute-start(bf16[128,128]{1,0:T(8,128)(2,1)S(1)} %get-tuple-element.73), channel_id=1, source_target_pairs={{0,15},{1,0},{2,1},{3,2},{4,3},{5,4},{6,5},{7,6},{8,7},{9,8},{10,9... | collective-permute-start | bytes 98312 | tf_op jit(solution)/shard_map/ppermute | solution.py:32
  75.2 1.7 %collective-permute-start.16 = (bf16[128,128]{1,0:T(8,128)(2,1)S(1)}, bf16[128,128]{1,0:T(8,128)(2,1)S(1)}, u32[]{:S(2)}, u32[]{:S(2)}) collective-permute-start(bf16[128,128]{1,0:T(8,128)(2,1)S(1)} %get-tuple-element.74), channel_id=1, source_target_pairs={{0,16},{16,0},{1,17},{17,1},{2,18},{18,2},{3,19},{19,3},{4,20},{20... | collective-permute-start | bytes 98312 | tf_op jit(solution)/shard_map/ppermute | solution.py:32
  77.2 1.9 %collective-permute-done.16.refs_6_ = bf16[128,128]{1,0:T(8,128)(2,1)S(1)} collective-permute-done((bf16[128,128]{1,0:T(8,128)(2,1)S(1)}, bf16[128,128]{1,0:T(8,128)(2,1)S(1)}, u32[]{:S(2)}, u32[]{:S(2)}) %collective-permute-start.16) | collective-permute-done | bytes 32800 | tf_op jit(solution)/shard_map/ppermute | solution.py:32
  79.1 1.7 %collective-permute-done.17.refs_7_ = bf16[128,128]{1,0:T(8,128)(2,1)S(1)} collective-permute-done((bf16[128,128]{1,0:T(8,128)(2,1)S(1)}, bf16[128,128]{1,0:T(8,128)(2,1)S(1)}, u32[]{:S(2)}, u32[]{:S(2)}) %collective-permute-start.17) | collective-permute-done | bytes 32800 | tf_op jit(solution)/shard_map/ppermute | solution.py:32
  80.8 3.9 %shard_map.180 = (f32[128,512]{1,0:T(8,128)S(1)}, f32[128,64]{1,0:T(8,128)S(1)}) custom-call(f32[128,512]{1,0:T(8,128)S(1)} %get-tuple-element.70.refs_0_, f32[128,64]{1,0:T(8,128)S(1)} %get-tuple-element.71.refs_1_, f32[128,512]{1,0:T(8,128)S(1)} %get-tuple-element.62.refs_0_.refs_2_, f32[128,64]{1,0:T(8,128)S(1)} %get-tuple-element.63.refs_1_.refs_3_, ...), custom_call_target="tpu_custom_call" | custom-call | tf_op jit(solution)/shard_map/pallas_call | solution.py:307
  85.9 4.5 %collective-permute-start.19 = (f32[2,8,512]{2,1,0:T(8,128)S(1)}, f32[2,8,512]{2,1,0:T(8,128)S(1)}, u32[]{:S(2)}, u32[]{:S(2)}) collective-permute-start(f32[2,8,512]{2,1,0:T(8,128)S(1)} %gather_fusion.1), channel_id=1, source_target_pairs={{0,15},{1,0},{2,1},{3,2},{4,3},{5,4},{6,5},{7,6},{8,7},{9,8},{10,9... | collective-permute-start | bytes 98312 | tf_op jit(solution)/shard_map/ppermute | solution.py:32
  (94 shorter events, 21.4 us)
Async XLA Ops:
  0.6 40.3 %copy-start = (bf16[3,512,512]{2,1,0:T(8,128)(2,1)S(1)}, bf16[3,512,512]{2,1,0:T(8,128)(2,1)}, u32[]{:S(2)}) copy-start(bf16[3,512,512]{2,1,0:T(8,128)(2,1)} %constant.114.clone.refs_13_.refs_14_.refs_16_) | copy-start | bytes 4718596
  4.5 1.1 %copy-start.1 = (bf16[512,768]{1,0:T(8,128)(2,1)S(1)}, bf16[512,768]{1,0:T(8,128)(2,1)}, u32[]{:S(2)}) copy-start(bf16[512,768]{1,0:T(8,128)(2,1)} %constant.115.clone.refs_4_.refs_14_.refs_15_.refs_17_) | copy-start | bytes 2359300
  5.6 1.0 %copy-start.4 = (bf16[3,64,768]{2,1,0:T(8,128)(2,1)S(1)}, bf16[3,64,768]{2,1,0:T(8,128)(2,1)}, u32[]{:S(2)}) copy-start(bf16[3,64,768]{2,1,0:T(8,128)(2,1)} %constant.117.clone.refs_5_.refs_16_.refs_20_.refs_22_) | copy-start | bytes 884740
  10.6 30.4 %copy-start.8 = (f32[16,8,512]{2,1,0:T(8,128)S(1)}, f32[16,8,512]{2,1,0:T(8,128)}, u32[]{:S(2)}) copy-start(f32[16,8,512]{2,1,0:T(8,128)} %param.19) | copy-start | bytes 786436
  14.0 26.9 %collective-permute-start.2 = (bf16[128,128]{1,0:T(8,128)(2,1)}, bf16[128,128]{1,0:T(8,128)(2,1)S(1)}, u32[]{:S(2)}, u32[]{:S(2)}) collective-permute-start(bf16[128,128]{1,0:T(8,128)(2,1)} %get-tuple-element.46), channel_id=1, source_target_pairs={{0,1},{1,2},{2,3},{3,4},{4,5},{5,6},{6,7},{7,8},{8,9},{9,10},{10,1... | collective-permute-start | bytes 98312 | tf_op jit(solution)/shard_map/ppermute | solution.py:32
  14.5 26.4 %collective-permute-start.3 = (bf16[128,128]{1,0:T(8,128)(2,1)}, bf16[128,128]{1,0:T(8,128)(2,1)S(1)}, u32[]{:S(2)}, u32[]{:S(2)}) collective-permute-start(bf16[128,128]{1,0:T(8,128)(2,1)} %get-tuple-element.47), channel_id=1, source_target_pairs={{0,15},{1,0},{2,1},{3,2},{4,3},{5,4},{6,5},{7,6},{8,7},{9,8},{10,9... | collective-permute-start | bytes 98312 | tf_op jit(solution)/shard_map/ppermute | solution.py:32
  19.5 21.4 %collective-permute-start.4 = (bf16[128,128]{1,0:T(8,128)(2,1)}, bf16[128,128]{1,0:T(8,128)(2,1)}, u32[]{:S(2)}, u32[]{:S(2)}) collective-permute-start(bf16[128,128]{1,0:T(8,128)(2,1)} %get-tuple-element.48), channel_id=1, source_target_pairs={{0,16},{16,0},{1,17},{17,1},{2,18},{18,2},{3,19},{19,3},{4,20},{20... | collective-permute-start | bytes 98312 | tf_op jit(solution)/shard_map/ppermute | solution.py:32
  21.4 19.5 %collective-permute-start.5 = (bf16[128,128]{1,0:T(8,128)(2,1)}, bf16[128,128]{1,0:T(8,128)(2,1)}, u32[]{:S(2)}, u32[]{:S(2)}) collective-permute-start(bf16[128,128]{1,0:T(8,128)(2,1)} %get-tuple-element.49), channel_id=1, source_target_pairs={{0,16},{16,0},{1,17},{17,1},{2,18},{18,2},{3,19},{19,3},{4,20},{20... | collective-permute-start | bytes 98312 | tf_op jit(solution)/shard_map/ppermute | solution.py:32
  27.0 7.1 %collective-permute-start = (s32[2]{0:T(128)}, s32[2]{0:T(128)}, u32[]{:S(2)}, u32[]{:S(2)}) collective-permute-start(s32[2]{0:T(128)} %add_select_fusion.2), channel_id=1, source_target_pairs={{0,1},{1,2},{2,3},{3,4},{4,5},{5,6},{6,7},{7,8},{8,9},{9,10},{10,1... | collective-permute-start | bytes 32 | tf_op jit(solution)/shard_map/ppermute | solution.py:32
  34.0 5.8 %collective-permute-start.1 = (s32[2]{0:T(128)S(1)}, s32[2]{0:T(128)S(1)}, u32[]{:S(2)}, u32[]{:S(2)}) collective-permute-start(s32[2]{0:T(128)S(1)} %add_select_fusion.1), channel_id=1, source_target_pairs={{0,15},{1,0},{2,1},{3,2},{4,3},{5,4},{6,5},{7,6},{8,7},{9,8},{10,9... | collective-permute-start | bytes 32 | tf_op jit(solution)/shard_map/ppermute | solution.py:32
  41.0 1.1 %copy-start.2 = (bf16[512,768]{1,0:T(8,128)(2,1)S(1)}, bf16[512,768]{1,0:T(8,128)(2,1)}, u32[]{:S(2)}) copy-start(bf16[512,768]{1,0:T(8,128)(2,1)} %constant.115.clone.refs_4_.refs_14_.refs_15_.refs_17_) | copy-start | bytes 2359300
  43.6 13.1 %copy-start.5 = (bf16[3,64,768]{2,1,0:T(8,128)(2,1)S(1)}, bf16[3,64,768]{2,1,0:T(8,128)(2,1)}, u32[]{:S(2)}) copy-start(bf16[3,64,768]{2,1,0:T(8,128)(2,1)} %constant.117.clone.refs_5_.refs_16_.refs_20_.refs_22_) | copy-start | bytes 884740
  43.6 13.1 %copy-start.13 = (bf16[3,512,64]{2,1,0:T(8,128)(2,1)S(1)}, bf16[3,512,64]{2,1,0:T(8,128)(2,1)}, u32[]{:S(2)}) copy-start(bf16[3,512,64]{2,1,0:T(8,128)(2,1)} %constant.119.clone.refs_18_) | copy-start | bytes 589828
  46.3 6.5 %collective-permute-start.6 = (bf16[128,128]{1,0:T(8,128)(2,1)S(1)}, bf16[128,128]{1,0:T(8,128)(2,1)S(1)}, u32[]{:S(2)}, u32[]{:S(2)}) collective-permute-start(bf16[128,128]{1,0:T(8,128)(2,1)S(1)} %get-tuple-element.57), channel_id=1, source_target_pairs={{0,1},{1,2},{2,3},{3,4},{4,5},{5,6},{6,7},{7,8},{8,9},{9,10},{10,1... | collective-permute-start | bytes 98312 | tf_op jit(solution)/shard_map/ppermute | solution.py:32
  46.3 6.5 %collective-permute-start.7 = (bf16[128,128]{1,0:T(8,128)(2,1)S(1)}, bf16[128,128]{1,0:T(8,128)(2,1)S(1)}, u32[]{:S(2)}, u32[]{:S(2)}) collective-permute-start(bf16[128,128]{1,0:T(8,128)(2,1)S(1)} %get-tuple-element.58), channel_id=1, source_target_pairs={{0,15},{1,0},{2,1},{3,2},{4,3},{5,4},{6,5},{7,6},{8,7},{9,8},{10,9... | collective-permute-start | bytes 98312 | tf_op jit(solution)/shard_map/ppermute | solution.py:32
  50.8 3.9 %collective-permute-start.8 = (bf16[128,128]{1,0:T(8,128)(2,1)S(1)}, bf16[128,128]{1,0:T(8,128)(2,1)S(1)}, u32[]{:S(2)}, u32[]{:S(2)}) collective-permute-start(bf16[128,128]{1,0:T(8,128)(2,1)S(1)} %get-tuple-element.59), channel_id=1, source_target_pairs={{0,16},{16,0},{1,17},{17,1},{2,18},{18,2},{3,19},{19,3},{4,20},{20... | collective-permute-start | bytes 98312 | tf_op jit(solution)/shard_map/ppermute | solution.py:32
  52.7 3.9 %collective-permute-start.9 = (bf16[128,128]{1,0:T(8,128)(2,1)S(1)}, bf16[128,128]{1,0:T(8,128)(2,1)S(1)}, u32[]{:S(2)}, u32[]{:S(2)}) collective-permute-start(bf16[128,128]{1,0:T(8,128)(2,1)S(1)} %get-tuple-element.60), channel_id=1, source_target_pairs={{0,16},{16,0},{1,17},{17,1},{2,18},{18,2},{3,19},{19,3},{4,20},{20... | collective-permute-start | bytes 98312 | tf_op jit(solution)/shard_map/ppermute | solution.py:32
  56.6 11.2 %copy-start.3 = (bf16[512,768]{1,0:T(8,128)(2,1)S(1)}, bf16[512,768]{1,0:T(8,128)(2,1)}, u32[]{:S(2)}) copy-start(bf16[512,768]{1,0:T(8,128)(2,1)} %constant.115.clone.refs_4_.refs_14_.refs_15_.refs_17_) | copy-start | bytes 2359300
  56.6 11.2 %copy-start.6 = (bf16[3,768,64]{2,1,0:T(8,128)(2,1)S(1)}, bf16[3,768,64]{2,1,0:T(8,128)(2,1)}, u32[]{:S(2)}) copy-start(bf16[3,768,64]{2,1,0:T(8,128)(2,1)} %constant.118.clone.refs_19_.refs_21_) | copy-start | bytes 884740
  56.6 11.2 %copy-start.12 = (f32[3,128,64]{2,1,0:T(8,128)S(1)}, f32[3,128,64]{2,1,0:T(8,128)}, u32[]{:S(2)}) copy-start(f32[3,128,64]{2,1,0:T(8,128)} %copy-done.11) | copy-start | bytes 294916
  56.6 11.2 %copy-start.14 = (bf16[3,64,64]{2,1,0:T(8,128)(2,1)S(1)}, bf16[3,64,64]{2,1,0:T(8,128)(2,1)}, u32[]{:S(2)}) copy-start(bf16[3,64,64]{2,1,0:T(8,128)(2,1)} %constant.116.clone.refs_18_.refs_20_) | copy-start | bytes 73732
  59.1 6.6 %collective-permute-start.10 = (bf16[128,128]{1,0:T(8,128)(2,1)S(1)}, bf16[128,128]{1,0:T(8,128)(2,1)S(1)}, u32[]{:S(2)}, u32[]{:S(2)}) collective-permute-start(bf16[128,128]{1,0:T(8,128)(2,1)S(1)} %get-tuple-element.64), channel_id=1, source_target_pairs={{0,1},{1,2},{2,3},{3,4},{4,5},{5,6},{6,7},{7,8},{8,9},{9,10},{10,1... | collective-permute-start | bytes 98312 | tf_op jit(solution)/shard_map/ppermute | solution.py:32
  59.1 6.6 %collective-permute-start.11 = (bf16[128,128]{1,0:T(8,128)(2,1)S(1)}, bf16[128,128]{1,0:T(8,128)(2,1)S(1)}, u32[]{:S(2)}, u32[]{:S(2)}) collective-permute-start(bf16[128,128]{1,0:T(8,128)(2,1)S(1)} %get-tuple-element.65), channel_id=1, source_target_pairs={{0,15},{1,0},{2,1},{3,2},{4,3},{5,4},{6,5},{7,6},{8,7},{9,8},{10,9... | collective-permute-start | bytes 98312 | tf_op jit(solution)/shard_map/ppermute | solution.py:32
  63.6 3.9 %collective-permute-start.12 = (bf16[128,128]{1,0:T(8,128)(2,1)S(1)}, bf16[128,128]{1,0:T(8,128)(2,1)S(1)}, u32[]{:S(2)}, u32[]{:S(2)}) collective-permute-start(bf16[128,128]{1,0:T(8,128)(2,1)S(1)} %get-tuple-element.66), channel_id=1, source_target_pairs={{0,16},{16,0},{1,17},{17,1},{2,18},{18,2},{3,19},{19,3},{4,20},{20... | collective-permute-start | bytes 98312 | tf_op jit(solution)/shard_map/ppermute | solution.py:32
  63.9 3.9 %collective-permute-start.13 = (bf16[128,128]{1,0:T(8,128)(2,1)S(1)}, bf16[128,128]{1,0:T(8,128)(2,1)S(1)}, u32[]{:S(2)}, u32[]{:S(2)}) collective-permute-start(bf16[128,128]{1,0:T(8,128)(2,1)S(1)} %get-tuple-element.67), channel_id=1, source_target_pairs={{0,16},{16,0},{1,17},{17,1},{2,18},{18,2},{3,19},{19,3},{4,20},{20... | collective-permute-start | bytes 98312 | tf_op jit(solution)/shard_map/ppermute | solution.py:32
  70.7 6.5 %collective-permute-start.14 = (bf16[128,128]{1,0:T(8,128)(2,1)S(1)}, bf16[128,128]{1,0:T(8,128)(2,1)S(1)}, u32[]{:S(2)}, u32[]{:S(2)}) collective-permute-start(bf16[128,128]{1,0:T(8,128)(2,1)S(1)} %get-tuple-element.72), channel_id=1, source_target_pairs={{0,1},{1,2},{2,3},{3,4},{4,5},{5,6},{6,7},{7,8},{8,9},{9,10},{10,1... | collective-permute-start | bytes 98312 | tf_op jit(solution)/shard_map/ppermute | solution.py:32
  70.8 6.5 %collective-permute-start.15 = (bf16[128,128]{1,0:T(8,128)(2,1)S(1)}, bf16[128,128]{1,0:T(8,128)(2,1)S(1)}, u32[]{:S(2)}, u32[]{:S(2)}) collective-permute-start(bf16[128,128]{1,0:T(8,128)(2,1)S(1)} %get-tuple-element.73), channel_id=1, source_target_pairs={{0,15},{1,0},{2,1},{3,2},{4,3},{5,4},{6,5},{7,6},{8,7},{9,8},{10,9... | collective-permute-start | bytes 98312 | tf_op jit(solution)/shard_map/ppermute | solution.py:32
  75.2 3.9 %collective-permute-start.16 = (bf16[128,128]{1,0:T(8,128)(2,1)S(1)}, bf16[128,128]{1,0:T(8,128)(2,1)S(1)}, u32[]{:S(2)}, u32[]{:S(2)}) collective-permute-start(bf16[128,128]{1,0:T(8,128)(2,1)S(1)} %get-tuple-element.74), channel_id=1, source_target_pairs={{0,16},{16,0},{1,17},{17,1},{2,18},{18,2},{3,19},{19,3},{4,20},{20... | collective-permute-start | bytes 98312 | tf_op jit(solution)/shard_map/ppermute | solution.py:32
  76.9 3.9 %collective-permute-start.17 = (bf16[128,128]{1,0:T(8,128)(2,1)S(1)}, bf16[128,128]{1,0:T(8,128)(2,1)S(1)}, u32[]{:S(2)}, u32[]{:S(2)}) collective-permute-start(bf16[128,128]{1,0:T(8,128)(2,1)S(1)} %get-tuple-element.75), channel_id=1, source_target_pairs={{0,16},{16,0},{1,17},{17,1},{2,18},{18,2},{3,19},{19,3},{4,20},{20... | collective-permute-start | bytes 98312 | tf_op jit(solution)/shard_map/ppermute | solution.py:32
  80.8 9.6 %copy-start.19 = (pred[16]{0:T(512)(128)(4,1)S(1)}, pred[16]{0:T(512)(128)(4,1)}, u32[]{:S(2)}) copy-start(pred[16]{0:T(512)(128)(4,1)} %broadcast_compare_fusion.1) | copy-start | bytes 52
  85.2 6.1 %collective-permute-start.18 = (f32[2,8,512]{2,1,0:T(8,128)S(1)}, f32[2,8,512]{2,1,0:T(8,128)S(1)}, u32[]{:S(2)}, u32[]{:S(2)}) collective-permute-start(f32[2,8,512]{2,1,0:T(8,128)S(1)} %gather_fusion), channel_id=1, source_target_pairs={{0,1},{1,2},{2,3},{3,4},{4,5},{5,6},{6,7},{7,8},{8,9},{9,10},{10,1... | collective-permute-start | bytes 98312 | tf_op jit(solution)/shard_map/ppermute | solution.py:32
  85.9 6.1 %collective-permute-start.19 = (f32[2,8,512]{2,1,0:T(8,128)S(1)}, f32[2,8,512]{2,1,0:T(8,128)S(1)}, u32[]{:S(2)}, u32[]{:S(2)}) collective-permute-start(f32[2,8,512]{2,1,0:T(8,128)S(1)} %gather_fusion.1), channel_id=1, source_target_pairs={{0,15},{1,0},{2,1},{3,2},{4,3},{5,4},{6,5},{7,6},{8,7},{9,8},{10,9... | collective-permute-start | bytes 98312 | tf_op jit(solution)/shard_map/ppermute | solution.py:32
  (8 other events, 6.2 us)

commit v3 on v2

--- a/solution.py
+++ b/solution.py
@@ -222,9 +222,16 @@
         sw_ref = take()
     if project:
         pj_ref = take()
+    last = coarse and not sends
+    if last:
+        sel_l_ref = take()
+        sel_r_ref = take()
     out_u = take()
     out_c = take() if (coarse or project) else None
     out_send = [take() for _ in SEND_FACES] if sends else None
+    if last:
+        pay_l_ref = take()
+        pay_r_ref = take()
 
     pre = pre_ref[...]
     stc = stc_ref[...]
@@ -281,7 +288,12 @@
             new_c = 0.5 * (bc_ref[...] + c + TIME_STEP * rate3)
         else:
             new_c = c + TIME_STEP * rate3
-        out_c[...] = new_c
+        if last:
+            out_c[...] = jnp.where(sw_ref[...] > 0.5, new_c, 0.0)
+            pay_l_ref[...] = _exact_right(sel_l_ref[...], new_u)
+            pay_r_ref[...] = _exact_right(sel_r_ref[...], new_u)
+        else:
+            out_c[...] = new_c
     if project:
         new_c = _full(new_u, pj_ref)
         out_c[...] = new_c
@@ -315,7 +327,8 @@
 
 def setup_kernel(local, fields, u_ref, vt_ref, packed_ref, lift_ref, g7_ref, tm_ref, bc_ref,
                  fsel_ref, v7_out, m7_out, v3_out, m3_out, pl_out, pr_out,
-                 pre_out, stc_out, sw_out, *send_refs):
+                 pre_out, stc_out, sw_out, hinfo_out, cnt_l_out, cnt_r_out, sel_l_out,
+                 sel_r_out, *send_refs):
     rows = local * fields
     bcast = bc_ref[...]
     lanes = lax.broadcasted_iota(jnp.int32, (local, 6 * LANE), 1) // LANE
@@ -349,11 +362,82 @@
         if side in SEND_FACES:
             pr_out[SEND_FACES.index(side)] = jnp.where(hit & far, 1.0, 0.0).astype(bf16)
     sw_out[...] = rep[:, 6:7]
+    packed = packed_ref[...]
+    stay_sw = packed[:, 6:7] < 0.5
+    go_left = (packed[:, 9:10] == packed[:, 10:11]) & stay_sw
+    go_right = (packed[:, 9:10] == packed[:, 11:12]) & stay_sw
+    stays = stay_sw & ~go_left & ~go_right
+    lane16 = lax.broadcasted_iota(jnp.int32, (local, LANE), 1)
+    marks = jnp.where(
+        lane16 == 0, go_left.astype(f32),
+        jnp.where(lane16 == 1, go_right.astype(f32), jnp.where(lane16 == 2, stays.astype(f32), 0.0)),
+    ).astype(bf16)
+    er = lax.broadcasted_iota(jnp.int32, (local, local), 0)
+    ec = lax.broadcasted_iota(jnp.int32, (local, local), 1)
+    before = _dot(jnp.where(ec < er, 1.0, 0.0).astype(bf16), marks)
+    totals = _dot(jnp.ones((local, local), bf16), marks)
+    info = jnp.where(lane16 < 3, marks.astype(f32), 0.0)
+    for k in range(3):
+        info = jnp.where(lane16 == 3 + k, before[:, k : k + 1], info)
+    info = jnp.where(lane16 == 6, totals[:, 2:3], info)
+    info = jnp.where(lane16 == 7, packed[:, 12:13], info)
+    info = jnp.where(lane16 == 8, packed[:, 13:14], info)
+    hinfo = _dot(bcast, info.astype(bf16))
+    hinfo_out[...] = hinfo
+    cnt_l_out[...] = jnp.broadcast_to(totals[0:1, 0:1], cnt_l_out.shape)
+    cnt_r_out[...] = jnp.broadcast_to(totals[0:1, 1:2], cnt_r_out.shape)
+    rf = lax.broadcasted_iota(jnp.int32, (rows, LANE), 0) % fields
+    cc = lax.broadcasted_iota(jnp.int32, (rows, LANE), 1)
+    eye = jnp.where(
+        lax.broadcasted_iota(jnp.int32, (MOVE_CAP * fields, LANE), 0)
+        == lax.broadcasted_iota(jnp.int32, (MOVE_CAP * fields, LANE), 1), 1.0, 0.0
+    ).astype(bf16)
+    for mark_lane, rank_lane, out in ((0, 3, sel_l_out), (1, 4, sel_r_out)):
+        hit = (
+            (hinfo[:, mark_lane : mark_lane + 1] > 0.5)
+            & (hinfo[:, rank_lane : rank_lane + 1] == (cc // fields).astype(f32))
+            & (rf == cc % fields)
+            & (cc < MOVE_CAP * fields)
+        )
+        out[...] = _dot_t(eye, jnp.where(hit, 1.0, 0.0).astype(bf16)).astype(bf16)
     pre_out[...] = packed_ref[:, 7:8]
     stc_out[...] = _exact_right(fsel_ref[...], packed_ref[...])[:, 8:9]
     send = _dot(u_ref[...].astype(bf16), g7_ref[...]).astype(bf16)
     for k, side in enumerate(SEND_FACES):
         send_refs[k][...] = send[:, side * LANE : (side + 1) * LANE]
+
+
+def final_kernel(fields, hold, home_ref, from_l_ref, from_r_ref, n_l_ref, n_r_ref, hinfo_ref,
+                 out_ref):
+    hinfo = hinfo_ref[...]
+    n_l = n_l_ref[0:1, 0:1]
+    n_r = n_r_ref[0:1, 0:1]
+    n_h = hinfo[0:1, 6:7]
+    first = hinfo[0:1, 7:8] > 0.5
+    final = hinfo[0:1, 8:9] > 0.5
+    off_l = jnp.where(first, n_h + n_r, jnp.where(final, n_r, 0.0))
+    off_h = jnp.where(first, 0.0, jnp.where(final, n_r + n_l, n_l))
+    off_r = jnp.where(first, n_h, jnp.where(final, 0.0, n_l + n_h))
+    width = hold * fields
+    eye = jnp.where(
+        lax.broadcasted_iota(jnp.int32, (width, LANE), 0)
+        == lax.broadcasted_iota(jnp.int32, (width, LANE), 1), 1.0, 0.0
+    ).astype(bf16)
+
+    def gather(values, valid, pos):
+        count = values.shape[0]
+        rf = lax.broadcasted_iota(jnp.int32, (count, LANE), 0) % fields
+        cc = lax.broadcasted_iota(jnp.int32, (count, LANE), 1)
+        hit = valid & (pos == (cc // fields).astype(f32)) & (rf == cc % fields) & (cc < width)
+        pick = _dot_t(eye, jnp.where(hit, 1.0, 0.0).astype(bf16)).astype(bf16)
+        return _exact_right(pick, values)
+
+    total = gather(home_ref[...], hinfo[:, 2:3] > 0.5, off_h + hinfo[:, 5:6])
+    moved = from_l_ref.shape[0]
+    slot = (lax.broadcasted_iota(jnp.int32, (moved, 1), 0) // fields).astype(f32)
+    total = total + gather(from_l_ref[...], slot < n_l, off_l + slot)
+    total = total + gather(from_r_ref[...], slot < n_r, off_r + slot)
+    out_ref[...] = total
 
 
 def setup_entry(local, fields, n_in, n_out, *refs):
@@ -387,13 +471,21 @@
     remote = near_device != device_id
     codes = (near_local + local_count * remote.astype(jnp.int32)).astype(f32)
     sto_col = jnp.zeros((local_count,), f32).at[:field_count].set(stoich)
+    left_pos = (curve_pos + curve_count - 1) % curve_count
+    right_pos = (curve_pos + 1) % curve_count
+    ones = jnp.ones((local_count, 1), f32)
     packed = jnp.concatenate(
         [
             codes,
             switch.astype(f32)[:, None],
             pre_exp[:, None],
             sto_col[:, None],
-            jnp.zeros((local_count, LANE - 9), f32),
+            new_owner.astype(f32)[:, None],
+            ones * left_pos.astype(f32),
+            ones * right_pos.astype(f32),
+            ones * (curve_pos == 0).astype(f32),
+            ones * (curve_pos == curve_count - 1).astype(f32),
+            jnp.zeros((local_count, LANE - 14), f32),
         ],
         axis=1,
     )
@@ -434,20 +526,28 @@
         jax.ShapeDtypeStruct((local_count, 1), f32),
         jax.ShapeDtypeStruct((rows, 1), f32),
         jax.ShapeDtypeStruct((rows, 1), f32),
+        jax.ShapeDtypeStruct((rows, LANE), f32),
+        jax.ShapeDtypeStruct((8, LANE), f32),
+        jax.ShapeDtypeStruct((8, LANE), f32),
+        jax.ShapeDtypeStruct((MOVE_CAP * field_count, rows), bf16),
+        jax.ShapeDtypeStruct((MOVE_CAP * field_count, rows), bf16),
     ] + [send_shape] * 4
     u0 = state.reshape(rows, P7**3)
     setup_in = [u0, vt, packed, lift_t, g7, tm, bcast, fsel]
     res = pl.pallas_call(
         functools.partial(setup_entry, local_count, field_count, len(setup_in), len(setup_out)),
         out_shape=setup_out,
-        in_specs=[pl.BlockSpec(memory_space=pl.ANY) for _ in setup_in],
+        in_specs=[pl.BlockSpec(memory_space=pltpu.HBM) for _ in setup_in],
         out_specs=[_vmem() for _ in setup_out],
         scratch_shapes=[pltpu.VMEM(x.shape, x.dtype) for x in setup_in]
         + [pltpu.SemaphoreType.DMA((len(setup_in),))],
-        compiler_params=pltpu.CompilerParams(vmem_limit_bytes=48 * 1024 * 1024),
+        compiler_params=pltpu.CompilerParams(vmem_limit_bytes=63 * 1024 * 1024),
     )(*setup_in)
     v7, m7, v3, m3, p_local, p_remote, pre, stc, sw = res[:9]
-    sends = res[9:]
+    hinfo, cnt_l, cnt_r, sel_l, sel_r = res[9:14]
+    sends = res[14:]
+    n_from_right = shifted(cnt_l, "curve", -1)
+    n_from_left = shifted(cnt_r, "curve", 1)
     common = [p_local, p_remote, v7, m7, pre, stc, bcast, sel, d7t, g7]
     recv = exchange(sends)
     res = run_stage(
@@ -472,48 +572,23 @@
     )
     first7, first3, sends = res[0], res[1], res[2:]
     recv = exchange(sends)
+    pay_shape = jax.ShapeDtypeStruct((MOVE_CAP * field_count, P7**3), f32)
     res = run_stage(
         (True, True, False, False, local_count),
-        [first7, first3, after, coarse] + recv + common + mixed_tail,
-        [u_shape, c_shape],
-    )
-    final7 = res[0].reshape(local_count, field_count, P7**3)
-    final3 = res[1].reshape(local_count, field_count * P3**3)
-
-    switched = switch == 1
-    left_pos = (curve_pos + curve_count - 1) % curve_count
-    right_pos = (curve_pos + 1) % curve_count
-    to_left = (new_owner == left_pos) & ~switched
-    to_right = (new_owner == right_pos) & ~switched
-    stays_home = ~switched & ~to_left & ~to_right
-
-    def first_rows(mask):
-        rank = jnp.cumsum(mask.astype(jnp.int32)) - 1
-        slot = jnp.arange(MOVE_CAP, dtype=jnp.int32)
-        chosen = mask[None, :] & (rank[None, :] == slot[:, None])
-        live = jnp.any(chosen, axis=1)
-        row = jnp.sum(jnp.where(chosen, positions[None, :], 0), axis=1)
-        return row, live
-
-    left_rows, left_live = first_rows(to_left)
-    right_rows, right_live = first_rows(to_right)
-    left_ids = jnp.where(left_live, first_global + left_rows, missing_id)
-    right_ids = jnp.where(right_live, first_global + right_rows, missing_id)
-    home_ids = jnp.where(stays_home, first_global + positions, missing_id)
-    from_right_ids = shifted(left_ids, "curve", -1)
-    from_left_ids = shifted(right_ids, "curve", 1)
-    from_right = shifted(final7[left_rows], "curve", -1)
-    from_left = shifted(final7[right_rows], "curve", 1)
-    cand_ids = jnp.concatenate([home_ids, from_left_ids, from_right_ids])
-    cand_count = cand_ids.shape[0]
-    rank = jnp.sum((cand_ids[None, :] < cand_ids[:, None]).astype(jnp.int32), axis=1)
-    slot = jnp.arange(HOLD7, dtype=jnp.int32)
-    pick = (rank[None, :] == slot[:, None]) & (cand_ids[None, :] < missing_id)
-    order = jnp.sum(jnp.where(pick, jnp.arange(cand_count, dtype=jnp.int32)[None, :], 0), axis=1)
-    slot_live = jnp.any(pick, axis=1)
-    held = jnp.concatenate([final7, from_left, from_right], axis=0)[order]
-    state7_out = jnp.where(slot_live[:, None, None], held, 0.0)
-    state3_out = jnp.where(switched[:, None], final3, 0.0)
+        [first7, first3, after, coarse] + recv + common + mixed_tail + [sel_l, sel_r],
+        [u_shape, c_shape, pay_shape, pay_shape],
+    )
+    final7, final3, pay_l, pay_r = res
+    from_right = shifted(pay_l, "curve", -1)
+    from_left = shifted(pay_r, "curve", 1)
+    held = pl.pallas_call(
+        functools.partial(final_kernel, field_count, HOLD7),
+        out_shape=jax.ShapeDtypeStruct((HOLD7 * field_count, P7**3), f32),
+        in_specs=[_vmem() for _ in range(6)],
+        out_specs=_vmem(),
+    )(final7, from_left, from_right, n_from_left, n_from_right, hinfo)
+    state7_out = held.reshape(HOLD7, field_count, P7**3)
+    state3_out = final3.reshape(local_count, field_count * P3**3)
     return (state7_out, state3_out)
 
 

time: 94.2 us -> 82.7 us (0.88)
  other arithmetic: 15.2 us -> 1.39 us
  Pallas kernels: 14.5 us -> 18.2 us
  local copies, waits for them, and re-layouts: 14.9 us -> 12.9 us
  waiting for transfers between devices: 11.6 us -> 12.7 us
    select_n x8 -> x0, other arithmetic: 4 us -> none  [the longest x1 1.41 us: per_device(): home_ids = jnp.where(stays_home, first_global + positions, missing_id)]
    another operation x4 -> x0, other arithmetic: 3.55 us -> none
    pallas_call x0 -> x1, Pallas kernels: none -> 2.73 us  [per_device(): pl.pallas_call(functools.partial(final_kernel, field_count, HOLD7), out_s...]
    reduce_sum x4 -> x0, other arithmetic: 1.81 us -> none  [the longest x2 1.51 us: first_rows(): row = jnp.sum(jnp.where(chosen, positions[None, :], 0), axis=1)]
    gather x3 -> x0, local copies, waits for them, and re-layouts: 1.66 us -> none  [the longest x1 0.56 us: per_device(): held = jnp.concatenate([final7, from_left, from_right], axis=0)[order]]
    reduce_or x3 -> x0, other arithmetic: 1.63 us -> none  [the longest x2 1.51 us: first_rows(): live = jnp.any(chosen, axis=1)]
    sub x2 -> x0, other arithmetic: 1.62 us -> none  [first_rows(): rank = jnp.cumsum(mask.astype(jnp.int32)) - 1]
    pallas_call x1, Pallas kernels: 2.71 us -> 4.31 us  [per_device(): pl.pallas_call(functools.partial(setup_entry, local_count, field_count, l...]
  transfers between devices with their start and end apart: 20 -> 20, of which waited for: 9 -> 9; matrix products, arithmetic and copies ran while one was open for 16% -> 1% of each run, Pallas kernels for 0% -> 0%
where the time goes in v3:
time: 82.7 us; the launch traced here: 82.2 us
  starting transfers between devices  36 us (44%)
  Pallas kernels  18.2 us (22%)
  local copies, waits for them, and re-layouts  12.9 us (16%)
  waiting for transfers between devices  12.7 us (15%)
  other arithmetic  1.39 us (2%)
  between operations  0.99 us (1%)
    ppermute x20, starting transfers between devices, shifted(): return lax.ppermute(value, axis, pairs)  36 us
    ppermute x20, waiting for transfers between devices, shifted(): return lax.ppermute(value, axis, pairs)  12.7 us
    pallas_call x4, Pallas kernels, run_stage(): pl.pallas_call(kernel, out_shape=out_shapes, in_specs=[_vmem() for _ in i...  11.2 us
    unnamed x65, local copies, waits for them, and re-layouts  9.88 us
    pallas_call x1, Pallas kernels, per_device(): pl.pallas_call(functools.partial(setup_entry, local_count, field_count, l...  4.31 us
    pallas_call x1, Pallas kernels, per_device(): pl.pallas_call(functools.partial(final_kernel, field_count, HOLD7), out_s...  2.73 us
  transfers between devices with their start and end apart: 20, of which 9 were waited for; matrix products, arithmetic and copies ran while one was open for 1% of the time, Pallas kernels for 0%

profile of v3, /device:TPU:0, one launch (start us, length us, event | category | flops | bytes accessed | tf_op | source)
XLA Modules:
  0.0 82.2 jit_solution(14306969137959543117)
XLA Ops:
  2.1 0.7 copy.33
  3.0 0.7 copy.35
  3.7 0.8 copy.32
  5.2 4.3 %shard_map.176 = (bf16[3,128,512]{2,1,0:T(8,128)(2,1)}, f32[128,768]{1,0:T(8,128)}, f32[3,128,64]{2,1,0:T(8,128)}, f32[128,768]{1,0:T(8,128)}, bf16[6,128,128]{2...) custom-call(f32[128,512]{1,0:T(8,128)} %bitcast.9, ...), custom_call_target="tpu_custom_call" | custom-call | tf_op jit(solution)/shard_map/pallas_call | solution.py:537
  10.1 5.0 %collective-permute-start.1 = (bf16[128,128]{1,0:T(8,128)(2,1)}, bf16[128,128]{1,0:T(8,128)(2,1)S(1)}, u32[]{:S(2)}, u32[]{:S(2)}) collective-permute-start(bf16[128,128]{1,0:T(8,128)(2,1)} %get-tuple-element.54), channel_id=1, source_target_pairs={{0,15},{1,0},{2,1},{3,2},{4,3},{5,4},{6,5},{7,6},{8,7},{9,8},{10,9... | collective-permute-start | bytes 98312 | tf_op jit(solution)/shard_map/ppermute | solution.py:32
  15.1 1.9 %collective-permute-start.2 = (bf16[128,128]{1,0:T(8,128)(2,1)}, bf16[128,128]{1,0:T(8,128)(2,1)S(1)}, u32[]{:S(2)}, u32[]{:S(2)}) collective-permute-start(bf16[128,128]{1,0:T(8,128)(2,1)} %get-tuple-element.55), channel_id=1, source_target_pairs={{0,16},{16,0},{1,17},{17,1},{2,18},{18,2},{3,19},{19,3},{4,20},{20... | collective-permute-start | bytes 98312 | tf_op jit(solution)/shard_map/ppermute | solution.py:32
  17.2 2.1 %collective-permute-done.2.refs_3_ = bf16[128,128]{1,0:T(8,128)(2,1)S(1)} collective-permute-done((bf16[128,128]{1,0:T(8,128)(2,1)}, bf16[128,128]{1,0:T(8,128)(2,1)S(1)}, u32[]{:S(2)}, u32[]{:S(2)}) %collective-permute-start.2) | collective-permute-done | bytes 32800 | tf_op jit(solution)/shard_map/ppermute | solution.py:32
  19.3 1.9 %collective-permute-done.3.refs_4_ = bf16[128,128]{1,0:T(8,128)(2,1)S(1)} collective-permute-done((bf16[128,128]{1,0:T(8,128)(2,1)}, bf16[128,128]{1,0:T(8,128)(2,1)S(1)}, u32[]{:S(2)}, u32[]{:S(2)}) %collective-permute-start.3) | collective-permute-done | bytes 32800 | tf_op jit(solution)/shard_map/ppermute | solution.py:32
  21.2 1.4 %copy-done = bf16[3,512,512]{2,1,0:T(8,128)(2,1)S(1)} copy-done((bf16[3,512,512]{2,1,0:T(8,128)(2,1)S(1)}, bf16[3,512,512]{2,1,0:T(8,128)(2,1)}, u32[]{:S(2)}) %copy-start) | copy-done | bytes 1572888
  22.6 1.0 %copy-done.3 = bf16[3,128,512]{2,1,0:T(8,128)(2,1)S(1)} copy-done((bf16[3,128,512]{2,1,0:T(8,128)(2,1)S(1)}, bf16[3,128,512]{2,1,0:T(8,128)(2,1)}, u32[]{:S(2)}) %copy-start.3) | copy-done | bytes 393240
  23.6 1.0 %copy-done.5 = f32[128,768]{1,0:T(8,128)S(1)} copy-done((f32[128,768]{1,0:T(8,128)S(1)}, f32[128,768]{1,0:T(8,128)}, u32[]{:S(2)}) %copy-start.5) | copy-done | bytes 393240
  24.6 0.9 %copy-done.8 = bf16[6,128,128]{2,1,0:T(8,128)(2,1)S(1)} copy-done((bf16[6,128,128]{2,1,0:T(8,128)(2,1)S(1)}, bf16[6,128,128]{2,1,0:T(8,128)(2,1)}, u32[]{:S(2)}) %copy-start.8) | copy-done | bytes 196632
  25.5 0.9 %copy-done.11 = f32[16,8,512]{2,1,0:T(8,128)S(1)} copy-done((f32[16,8,512]{2,1,0:T(8,128)S(1)}, f32[16,8,512]{2,1,0:T(8,128)}, u32[]{:S(2)}) %copy-start.11) | copy-done | bytes 262168
  26.4 0.9 %copy-done.12 = bf16[4,128,128]{2,1,0:T(8,128)(2,1)S(1)} copy-done((bf16[4,128,128]{2,1,0:T(8,128)(2,1)S(1)}, bf16[4,128,128]{2,1,0:T(8,128)(2,1)}, u32[]{:S(2)}) %copy-start.12) | copy-done | bytes 131096
  27.3 0.8 %copy-done.15 = f32[128,1]{1,0:T(8,128)S(1)} copy-done((f32[128,1]{1,0:T(8,128)S(1)}, f32[128,1]{1,0:T(8,128)}, u32[]{:S(2)}) %copy-start.15) | copy-done | bytes 536
  28.9 1.9 %shard_map.177 = (f32[128,512]{1,0:T(8,128)S(1)}, bf16[128,128]{1,0:T(8,128)(2,1)S(1)}, bf16[128,128]{1,0:T(8,128)(2,1)S(1)}, bf16[128,128]{1,0:T(8,128)(2,1)S(1)}, bf16[128,128]{1,0:T(8,128)(2,1)S(1)}) custom-call(f32[128,512]{1,0:T(8,128)S(1)} %bitcast.10, bf16[128,128]{1,0:T(8,128)(2,1)S(1)} %collective-permute-done.refs_1_, ...), custom_call_target="tpu_custom_call" | custom-call | tf_op jit(solution)/shard_map/pallas_call | solution.py:319
  30.9 4.4 %collective-permute-start.5 = (bf16[128,128]{1,0:T(8,128)(2,1)S(1)}, bf16[128,128]{1,0:T(8,128)(2,1)S(1)}, u32[]{:S(2)}, u32[]{:S(2)}) collective-permute-start(bf16[128,128]{1,0:T(8,128)(2,1)S(1)} %get-tuple-element.65), channel_id=1, source_target_pairs={{0,15},{1,0},{2,1},{3,2},{4,3},{5,4},{6,5},{7,6},{8,7},{9,8},{10,9... | collective-permute-start | bytes 98312 | tf_op jit(solution)/shard_map/ppermute | solution.py:32
  35.6 1.7 %collective-permute-start.7 = (bf16[128,128]{1,0:T(8,128)(2,1)S(1)}, bf16[128,128]{1,0:T(8,128)(2,1)S(1)}, u32[]{:S(2)}, u32[]{:S(2)}) collective-permute-start(bf16[128,128]{1,0:T(8,128)(2,1)S(1)} %get-tuple-element.67), channel_id=1, source_target_pairs={{0,16},{16,0},{1,17},{17,1},{2,18},{18,2},{3,19},{19,3},{4,20},{20... | collective-permute-start | bytes 98312 | tf_op jit(solution)/shard_map/ppermute | solution.py:32
  37.3 1.9 %collective-permute-done.6.refs_4_ = bf16[128,128]{1,0:T(8,128)(2,1)S(1)} collective-permute-done((bf16[128,128]{1,0:T(8,128)(2,1)S(1)}, bf16[128,128]{1,0:T(8,128)(2,1)S(1)}, u32[]{:S(2)}, u32[]{:S(2)}) %collective-permute-start.6) | collective-permute-done | bytes 32800 | tf_op jit(solution)/shard_map/ppermute | solution.py:32
  39.7 2.4 %shard_map.178 = (f32[128,512]{1,0:T(8,128)S(1)}, f32[128,64]{1,0:T(8,128)S(1)}, bf16[128,128]{1,0:T(8,128)(2,1)S(1)}, bf16[128,128]{1,0:T(8,128)(2,1)S(1)}, bf1...) custom-call(f32[128,512]{1,0:T(8,128)S(1)} %get-tuple-element.63.refs_0_, f32[128,512]{1,0:T(8,128)S(1)} %bitcast.11, ...), custom_call_target="tpu_custom_call" | custom-call | tf_op jit(solution)/shard_map/pallas_call | solution.py:319
  42.2 4.4 %collective-permute-start.9 = (bf16[128,128]{1,0:T(8,128)(2,1)S(1)}, bf16[128,128]{1,0:T(8,128)(2,1)S(1)}, u32[]{:S(2)}, u32[]{:S(2)}) collective-permute-start(bf16[128,128]{1,0:T(8,128)(2,1)S(1)} %get-tuple-element.72), channel_id=1, source_target_pairs={{0,15},{1,0},{2,1},{3,2},{4,3},{5,4},{6,5},{7,6},{8,7},{9,8},{10,9... | collective-permute-start | bytes 98312 | tf_op jit(solution)/shard_map/ppermute | solution.py:32
  46.6 1.7 %collective-permute-start.10 = (bf16[128,128]{1,0:T(8,128)(2,1)S(1)}, bf16[128,128]{1,0:T(8,128)(2,1)S(1)}, u32[]{:S(2)}, u32[]{:S(2)}) collective-permute-start(bf16[128,128]{1,0:T(8,128)(2,1)S(1)} %get-tuple-element.73), channel_id=1, source_target_pairs={{0,16},{16,0},{1,17},{17,1},{2,18},{18,2},{3,19},{19,3},{4,20},{20... | collective-permute-start | bytes 98312 | tf_op jit(solution)/shard_map/ppermute | solution.py:32
  48.6 1.9 %collective-permute-done.10.refs_4_ = bf16[128,128]{1,0:T(8,128)(2,1)S(1)} collective-permute-done((bf16[128,128]{1,0:T(8,128)(2,1)S(1)}, bf16[128,128]{1,0:T(8,128)(2,1)S(1)}, u32[]{:S(2)}, u32[]{:S(2)}) %collective-permute-start.10) | collective-permute-done | bytes 32800 | tf_op jit(solution)/shard_map/ppermute | solution.py:32
  50.5 1.7 %collective-permute-done.11.refs_5_ = bf16[128,128]{1,0:T(8,128)(2,1)S(1)} collective-permute-done((bf16[128,128]{1,0:T(8,128)(2,1)S(1)}, bf16[128,128]{1,0:T(8,128)(2,1)S(1)}, u32[]{:S(2)}, u32[]{:S(2)}) %collective-permute-start.11) | collective-permute-done | bytes 32800 | tf_op jit(solution)/shard_map/ppermute | solution.py:32
  52.3 2.9 %shard_map.179 = (f32[128,512]{1,0:T(8,128)S(1)}, f32[128,64]{1,0:T(8,128)S(1)}, bf16[128,128]{1,0:T(8,128)(2,1)S(1)}, bf16[128,128]{1,0:T(8,128)(2,1)S(1)}, bf1...) custom-call(f32[128,512]{1,0:T(8,128)S(1)} %get-tuple-element.69.refs_0_.refs_2_, ...), custom_call_target="tpu_custom_call" | custom-call | tf_op jit(solution)/shard_map/pallas_call | solution.py:319
  55.2 4.4 %collective-permute-start.13 = (bf16[128,128]{1,0:T(8,128)(2,1)S(1)}, bf16[128,128]{1,0:T(8,128)(2,1)S(1)}, u32[]{:S(2)}, u32[]{:S(2)}) collective-permute-start(bf16[128,128]{1,0:T(8,128)(2,1)S(1)} %get-tuple-element.80), channel_id=1, source_target_pairs={{0,15},{1,0},{2,1},{3,2},{4,3},{5,4},{6,5},{7,6},{8,7},{9,8},{10,9... | collective-permute-start | bytes 98312 | tf_op jit(solution)/shard_map/ppermute | solution.py:32
  60.0 1.7 %collective-permute-start.15 = (bf16[128,128]{1,0:T(8,128)(2,1)S(1)}, bf16[128,128]{1,0:T(8,128)(2,1)S(1)}, u32[]{:S(2)}, u32[]{:S(2)}) collective-permute-start(bf16[128,128]{1,0:T(8,128)(2,1)S(1)} %get-tuple-element.82), channel_id=1, source_target_pairs={{0,16},{16,0},{1,17},{17,1},{2,18},{18,2},{3,19},{19,3},{4,20},{20... | collective-permute-start | bytes 98312 | tf_op jit(solution)/shard_map/ppermute | solution.py:32
  61.6 1.9 %collective-permute-done.14.refs_6_ = bf16[128,128]{1,0:T(8,128)(2,1)S(1)} collective-permute-done((bf16[128,128]{1,0:T(8,128)(2,1)S(1)}, bf16[128,128]{1,0:T(8,128)(2,1)S(1)}, u32[]{:S(2)}, u32[]{:S(2)}) %collective-permute-start.14) | collective-permute-done | bytes 32800 | tf_op jit(solution)/shard_map/ppermute | solution.py:32
  63.9 4.0 %shard_map.180 = (f32[128,512]{1,0:T(8,128)S(1)}, f32[128,64]{1,0:T(8,128)S(1)}, f32[16,512]{1,0:T(8,128)S(1)}, f32[16,512]{1,0:T(8,128)S(1)}) custom-call(f32[128,512]{1,0:T(8,128)S(1)} %get-tuple-element.77.refs_0_, f32[128,64]{1,0:T(8,128)S(1)} %get-tuple-element.78.refs_1_, f32[128,512]{1,0:T(8,128)S(1)} %get-tuple-element.69.refs_0_.refs_2_, ...), custom_call_target="tpu_custom_call" | custom-call | tf_op jit(solution)/shard_map/pallas_call | solution.py:319
  68.6 4.4 %collective-permute-start.17 = (f32[16,512]{1,0:T(8,128)S(1)}, f32[16,512]{1,0:T(8,128)S(1)}, u32[]{:S(2)}, u32[]{:S(2)}) collective-permute-start(f32[16,512]{1,0:T(8,128)S(1)} %get-tuple-element.87), channel_id=1, source_target_pairs={{0,15},{1,0},{2,1},{3,2},{4,3},{5,4},{6,5},{7,6},{8,7},{9,8},{10,9... | collective-permute-start | bytes 98312 | tf_op jit(solution)/shard_map/ppermute | solution.py:32
  73.1 4.4 %collective-permute-start.19 = (f32[8,128]{1,0:T(8,128)S(1)}, f32[8,128]{1,0:T(8,128)S(1)}, u32[]{:S(2)}, u32[]{:S(2)}) collective-permute-start(f32[8,128]{1,0:T(8,128)S(1)} %copy-done.30), channel_id=1, source_target_pairs={{0,15},{1,0},{2,1},{3,2},{4,3},{5,4},{6,5},{7,6},{8,7},{9,8},{10,9... | collective-permute-start | bytes 12296 | tf_op jit(solution)/shard_map/ppermute | solution.py:32
  79.5 2.7 %shard_map.181 = f32[96,512]{1,0:T(8,128)} custom-call(f32[128,512]{1,0:T(8,128)} %copy-done.20, f32[16,512]{1,0:T(8,128)} %copy-done.26, f32[16,512]{1,0:T(8,128)} %copy-done.27, f32[8,128]{1,0:T(8,128)} %copy-done.28, f32[8,128]{1,0:T(8,128)} %copy-done.29, f32[128,128]{1,0:T(8,128)} %get-tuple-element.90.hinfo_ref), custom_call_target="tpu_custom_call" | custom-call | tf_op jit(solution)/shard_map/pallas_call | solution.py:584
  (94 shorter events, 8.4 us)
Async XLA Ops:
  0.6 20.5 %copy-start.2 = (bf16[512,768]{1,0:T(8,128)(2,1)S(1)}, bf16[512,768]{1,0:T(8,128)(2,1)}, u32[]{:S(2)}) copy-start(bf16[512,768]{1,0:T(8,128)(2,1)} %constant.98.clone.refs_4_.refs_14_.refs_15_.refs_17_) | copy-start | bytes 2359300
  0.6 20.5 %copy-start.16 = (bf16[128,16]{1,0:T(8,128)(2,1)S(1)}, bf16[128,16]{1,0:T(8,128)(2,1)}, u32[]{:S(2)}) copy-start(bf16[128,16]{1,0:T(8,128)(2,1)} %constant.94.clone.refs_6_.refs_11_.refs_12_.refs_14_) | copy-start | bytes 12292
  0.7 20.5 %copy-start.22 = (bf16[48,128]{1,0:T(8,128)(2,1)S(1)}, bf16[48,128]{1,0:T(8,128)(2,1)}, u32[]{:S(2)}) copy-start(bf16[48,128]{1,0:T(8,128)(2,1)} %constant.95.clone.refs_12_.refs_13_.refs_15_) | copy-start | bytes 36868
  9.5 7.6 %collective-permute-start = (bf16[128,128]{1,0:T(8,128)(2,1)}, bf16[128,128]{1,0:T(8,128)(2,1)S(1)}, u32[]{:S(2)}, u32[]{:S(2)}) collective-permute-start(bf16[128,128]{1,0:T(8,128)(2,1)} %get-tuple-element.53), channel_id=1, source_target_pairs={{0,1},{1,2},{2,3},{3,4},{4,5},{5,6},{6,7},{7,8},{8,9},{9,10},{10,1... | collective-permute-start | bytes 98312 | tf_op jit(solution)/shard_map/ppermute | solution.py:32
  10.1 7.1 %collective-permute-start.1 = (bf16[128,128]{1,0:T(8,128)(2,1)}, bf16[128,128]{1,0:T(8,128)(2,1)S(1)}, u32[]{:S(2)}, u32[]{:S(2)}) collective-permute-start(bf16[128,128]{1,0:T(8,128)(2,1)} %get-tuple-element.54), channel_id=1, source_target_pairs={{0,15},{1,0},{2,1},{3,2},{4,3},{5,4},{6,5},{7,6},{8,7},{9,8},{10,9... | collective-permute-start | bytes 98312 | tf_op jit(solution)/shard_map/ppermute | solution.py:32
  15.1 4.1 %collective-permute-start.2 = (bf16[128,128]{1,0:T(8,128)(2,1)}, bf16[128,128]{1,0:T(8,128)(2,1)S(1)}, u32[]{:S(2)}, u32[]{:S(2)}) collective-permute-start(bf16[128,128]{1,0:T(8,128)(2,1)} %get-tuple-element.55), channel_id=1, source_target_pairs={{0,16},{16,0},{1,17},{17,1},{2,18},{18,2},{3,19},{19,3},{4,20},{20... | collective-permute-start | bytes 98312 | tf_op jit(solution)/shard_map/ppermute | solution.py:32
  17.0 4.1 %collective-permute-start.3 = (bf16[128,128]{1,0:T(8,128)(2,1)}, bf16[128,128]{1,0:T(8,128)(2,1)S(1)}, u32[]{:S(2)}, u32[]{:S(2)}) collective-permute-start(bf16[128,128]{1,0:T(8,128)(2,1)} %get-tuple-element.56), channel_id=1, source_target_pairs={{0,16},{16,0},{1,17},{17,1},{2,18},{18,2},{3,19},{19,3},{4,20},{20... | collective-permute-start | bytes 98312 | tf_op jit(solution)/shard_map/ppermute | solution.py:32
  30.8 6.5 %collective-permute-start.4 = (bf16[128,128]{1,0:T(8,128)(2,1)S(1)}, bf16[128,128]{1,0:T(8,128)(2,1)S(1)}, u32[]{:S(2)}, u32[]{:S(2)}) collective-permute-start(bf16[128,128]{1,0:T(8,128)(2,1)S(1)} %get-tuple-element.64), channel_id=1, source_target_pairs={{0,1},{1,2},{2,3},{3,4},{4,5},{5,6},{6,7},{7,8},{8,9},{9,10},{10,1... | collective-permute-start | bytes 98312 | tf_op jit(solution)/shard_map/ppermute | solution.py:32
  30.9 6.5 %collective-permute-start.5 = (bf16[128,128]{1,0:T(8,128)(2,1)S(1)}, bf16[128,128]{1,0:T(8,128)(2,1)S(1)}, u32[]{:S(2)}, u32[]{:S(2)}) collective-permute-start(bf16[128,128]{1,0:T(8,128)(2,1)S(1)} %get-tuple-element.65), channel_id=1, source_target_pairs={{0,15},{1,0},{2,1},{3,2},{4,3},{5,4},{6,5},{7,6},{8,7},{9,8},{10,9... | collective-permute-start | bytes 98312 | tf_op jit(solution)/shard_map/ppermute | solution.py:32
  35.3 3.9 %collective-permute-start.6 = (bf16[128,128]{1,0:T(8,128)(2,1)S(1)}, bf16[128,128]{1,0:T(8,128)(2,1)S(1)}, u32[]{:S(2)}, u32[]{:S(2)}) collective-permute-start(bf16[128,128]{1,0:T(8,128)(2,1)S(1)} %get-tuple-element.66), channel_id=1, source_target_pairs={{0,16},{16,0},{1,17},{17,1},{2,18},{18,2},{3,19},{19,3},{4,20},{20... | collective-permute-start | bytes 98312 | tf_op jit(solution)/shard_map/ppermute | solution.py:32
  35.6 3.9 %collective-permute-start.7 = (bf16[128,128]{1,0:T(8,128)(2,1)S(1)}, bf16[128,128]{1,0:T(8,128)(2,1)S(1)}, u32[]{:S(2)}, u32[]{:S(2)}) collective-permute-start(bf16[128,128]{1,0:T(8,128)(2,1)S(1)} %get-tuple-element.67), channel_id=1, source_target_pairs={{0,16},{16,0},{1,17},{17,1},{2,18},{18,2},{3,19},{19,3},{4,20},{20... | collective-permute-start | bytes 98312 | tf_op jit(solution)/shard_map/ppermute | solution.py:32
  39.6 12.6 %copy-start.6 = (f32[128,768]{1,0:T(8,128)S(1)}, f32[128,768]{1,0:T(8,128)}, u32[]{:S(2)}) copy-start(f32[128,768]{1,0:T(8,128)} %get-tuple-element.60.refs_8_.refs_9_.refs_11_) | copy-start | bytes 1179652
  39.6 12.6 %copy-start.9 = (bf16[6,128,128]{2,1,0:T(8,128)(2,1)S(1)}, bf16[6,128,128]{2,1,0:T(8,128)(2,1)}, u32[]{:S(2)}) copy-start(bf16[6,128,128]{2,1,0:T(8,128)(2,1)} %get-tuple-element.57.refs_5_.refs_6_.refs_8_) | copy-start | bytes 589828
  39.6 12.6 %copy-start.10 = (bf16[3,768,64]{2,1,0:T(8,128)(2,1)S(1)}, bf16[3,768,64]{2,1,0:T(8,128)(2,1)}, u32[]{:S(2)}) copy-start(bf16[3,768,64]{2,1,0:T(8,128)(2,1)} %constant.101.clone.refs_19_.refs_21_) | copy-start | bytes 884740
  39.6 12.6 %copy-start.13 = (bf16[4,128,128]{2,1,0:T(8,128)(2,1)S(1)}, bf16[4,128,128]{2,1,0:T(8,128)(2,1)}, u32[]{:S(2)}) copy-start(bf16[4,128,128]{2,1,0:T(8,128)(2,1)} %get-tuple-element.58.refs_6_.refs_7_.refs_9_) | copy-start | bytes 393220
  39.6 12.6 %copy-start.14 = (f32[128,768]{1,0:T(8,128)S(1)}, f32[128,768]{1,0:T(8,128)}, u32[]{:S(2)}) copy-start(f32[128,768]{1,0:T(8,128)} %get-tuple-element.76.refs_17_.refs_19_) | copy-start | bytes 1179652
  39.7 12.6 %copy-start.17 = (f32[3,128,64]{2,1,0:T(8,128)S(1)}, f32[3,128,64]{2,1,0:T(8,128)}, u32[]{:S(2)}) copy-start(f32[3,128,64]{2,1,0:T(8,128)} %get-tuple-element.75.refs_16_.refs_18_) | copy-start | bytes 294916
  39.7 12.6 %copy-start.21 = (bf16[3,64,64]{2,1,0:T(8,128)(2,1)S(1)}, bf16[3,64,64]{2,1,0:T(8,128)(2,1)}, u32[]{:S(2)}) copy-start(bf16[3,64,64]{2,1,0:T(8,128)(2,1)} %constant.99.clone.refs_18_.refs_20_) | copy-start | bytes 73732
  42.1 6.5 %collective-permute-start.8 = (bf16[128,128]{1,0:T(8,128)(2,1)S(1)}, bf16[128,128]{1,0:T(8,128)(2,1)S(1)}, u32[]{:S(2)}, u32[]{:S(2)}) collective-permute-start(bf16[128,128]{1,0:T(8,128)(2,1)S(1)} %get-tuple-element.71), channel_id=1, source_target_pairs={{0,1},{1,2},{2,3},{3,4},{4,5},{5,6},{6,7},{7,8},{8,9},{9,10},{10,1... | collective-permute-start | bytes 98312 | tf_op jit(solution)/shard_map/ppermute | solution.py:32
  42.2 6.5 %collective-permute-start.9 = (bf16[128,128]{1,0:T(8,128)(2,1)S(1)}, bf16[128,128]{1,0:T(8,128)(2,1)S(1)}, u32[]{:S(2)}, u32[]{:S(2)}) collective-permute-start(bf16[128,128]{1,0:T(8,128)(2,1)S(1)} %get-tuple-element.72), channel_id=1, source_target_pairs={{0,15},{1,0},{2,1},{3,2},{4,3},{5,4},{6,5},{7,6},{8,7},{9,8},{10,9... | collective-permute-start | bytes 98312 | tf_op jit(solution)/shard_map/ppermute | solution.py:32
  46.6 3.9 %collective-permute-start.10 = (bf16[128,128]{1,0:T(8,128)(2,1)S(1)}, bf16[128,128]{1,0:T(8,128)(2,1)S(1)}, u32[]{:S(2)}, u32[]{:S(2)}) collective-permute-start(bf16[128,128]{1,0:T(8,128)(2,1)S(1)} %get-tuple-element.73), channel_id=1, source_target_pairs={{0,16},{16,0},{1,17},{17,1},{2,18},{18,2},{3,19},{19,3},{4,20},{20... | collective-permute-start | bytes 98312 | tf_op jit(solution)/shard_map/ppermute | solution.py:32
  48.3 3.9 %collective-permute-start.11 = (bf16[128,128]{1,0:T(8,128)(2,1)S(1)}, bf16[128,128]{1,0:T(8,128)(2,1)S(1)}, u32[]{:S(2)}, u32[]{:S(2)}) collective-permute-start(bf16[128,128]{1,0:T(8,128)(2,1)S(1)} %get-tuple-element.74), channel_id=1, source_target_pairs={{0,16},{16,0},{1,17},{17,1},{2,18},{18,2},{3,19},{19,3},{4,20},{20... | collective-permute-start | bytes 98312 | tf_op jit(solution)/shard_map/ppermute | solution.py:32
  52.2 11.7 %copy-start.24 = (bf16[16,128]{1,0:T(8,128)(2,1)S(1)}, bf16[16,128]{1,0:T(8,128)(2,1)}, u32[]{:S(2)}) copy-start(bf16[16,128]{1,0:T(8,128)(2,1)} %get-tuple-element.83.refs_24_) | copy-start | bytes 12292
  52.2 11.7 %copy-start.25 = (bf16[16,128]{1,0:T(8,128)(2,1)S(1)}, bf16[16,128]{1,0:T(8,128)(2,1)}, u32[]{:S(2)}) copy-start(bf16[16,128]{1,0:T(8,128)(2,1)} %get-tuple-element.84.refs_25_) | copy-start | bytes 12292
  55.1 6.5 %collective-permute-start.12 = (bf16[128,128]{1,0:T(8,128)(2,1)S(1)}, bf16[128,128]{1,0:T(8,128)(2,1)S(1)}, u32[]{:S(2)}, u32[]{:S(2)}) collective-permute-start(bf16[128,128]{1,0:T(8,128)(2,1)S(1)} %get-tuple-element.79), channel_id=1, source_target_pairs={{0,1},{1,2},{2,3},{3,4},{4,5},{5,6},{6,7},{7,8},{8,9},{9,10},{10,1... | collective-permute-start | bytes 98312 | tf_op jit(solution)/shard_map/ppermute | solution.py:32
  55.2 6.5 %collective-permute-start.13 = (bf16[128,128]{1,0:T(8,128)(2,1)S(1)}, bf16[128,128]{1,0:T(8,128)(2,1)S(1)}, u32[]{:S(2)}, u32[]{:S(2)}) collective-permute-start(bf16[128,128]{1,0:T(8,128)(2,1)S(1)} %get-tuple-element.80), channel_id=1, source_target_pairs={{0,15},{1,0},{2,1},{3,2},{4,3},{5,4},{6,5},{7,6},{8,7},{9,8},{10,9... | collective-permute-start | bytes 98312 | tf_op jit(solution)/shard_map/ppermute | solution.py:32
  59.6 3.9 %collective-permute-start.14 = (bf16[128,128]{1,0:T(8,128)(2,1)S(1)}, bf16[128,128]{1,0:T(8,128)(2,1)S(1)}, u32[]{:S(2)}, u32[]{:S(2)}) collective-permute-start(bf16[128,128]{1,0:T(8,128)(2,1)S(1)} %get-tuple-element.81), channel_id=1, source_target_pairs={{0,16},{16,0},{1,17},{17,1},{2,18},{18,2},{3,19},{19,3},{4,20},{20... | collective-permute-start | bytes 98312 | tf_op jit(solution)/shard_map/ppermute | solution.py:32
  60.0 3.9 %collective-permute-start.15 = (bf16[128,128]{1,0:T(8,128)(2,1)S(1)}, bf16[128,128]{1,0:T(8,128)(2,1)S(1)}, u32[]{:S(2)}, u32[]{:S(2)}) collective-permute-start(bf16[128,128]{1,0:T(8,128)(2,1)S(1)} %get-tuple-element.82), channel_id=1, source_target_pairs={{0,16},{16,0},{1,17},{17,1},{2,18},{18,2},{3,19},{19,3},{4,20},{20... | collective-permute-start | bytes 98312 | tf_op jit(solution)/shard_map/ppermute | solution.py:32
  68.6 10.2 %collective-permute-start.16 = (f32[16,512]{1,0:T(8,128)S(1)}, f32[16,512]{1,0:T(8,128)S(1)}, u32[]{:S(2)}, u32[]{:S(2)}) collective-permute-start(f32[16,512]{1,0:T(8,128)S(1)} %get-tuple-element.86), channel_id=1, source_target_pairs={{0,1},{1,2},{2,3},{3,4},{4,5},{5,6},{6,7},{7,8},{8,9},{9,10},{10,1... | collective-permute-start | bytes 98312 | tf_op jit(solution)/shard_map/ppermute | solution.py:32
  68.6 10.2 %collective-permute-start.17 = (f32[16,512]{1,0:T(8,128)S(1)}, f32[16,512]{1,0:T(8,128)S(1)}, u32[]{:S(2)}, u32[]{:S(2)}) collective-permute-start(f32[16,512]{1,0:T(8,128)S(1)} %get-tuple-element.87), channel_id=1, source_target_pairs={{0,15},{1,0},{2,1},{3,2},{4,3},{5,4},{6,5},{7,6},{8,7},{9,8},{10,9... | collective-permute-start | bytes 98312 | tf_op jit(solution)/shard_map/ppermute | solution.py:32
  73.0 5.7 %collective-permute-start.18 = (f32[8,128]{1,0:T(8,128)S(1)}, f32[8,128]{1,0:T(8,128)S(1)}, u32[]{:S(2)}, u32[]{:S(2)}) collective-permute-start(f32[8,128]{1,0:T(8,128)S(1)} %copy-done.31), channel_id=1, source_target_pairs={{0,1},{1,2},{2,3},{3,4},{4,5},{5,6},{6,7},{7,8},{8,9},{9,10},{10,1... | collective-permute-start | bytes 12296 | tf_op jit(solution)/shard_map/ppermute | solution.py:32
  73.1 5.8 %collective-permute-start.19 = (f32[8,128]{1,0:T(8,128)S(1)}, f32[8,128]{1,0:T(8,128)S(1)}, u32[]{:S(2)}, u32[]{:S(2)}) collective-permute-start(f32[8,128]{1,0:T(8,128)S(1)} %copy-done.30), channel_id=1, source_target_pairs={{0,15},{1,0},{2,1},{3,2},{4,3},{5,4},{6,5},{7,6},{8,7},{9,8},{10,9... | collective-permute-start | bytes 12296 | tf_op jit(solution)/shard_map/ppermute | solution.py:32
  (20 other events, 82.7 us)

commit v4 on v3

--- a/solution.py
+++ b/solution.py
@@ -172,6 +172,54 @@
     return (_dot(table, hi) + _dot(table, mid)) + _dot(table, lo)
 
 
+def _full_t(x, parts_ref):
+    xh, xm, xl = _split(x)
+    bh = parts_ref[0]
+    bm = parts_ref[1]
+    bl = parts_ref[2]
+    return _dot_t(xh, bh) + (_dot_t(xh, bm) + _dot_t(xm, bh)) + (
+        _dot_t(xh, bl) + _dot_t(xm, bm) + _dot_t(xl, bh)
+    )
+
+
+class View:
+    def __init__(self, ref, start, rows, width):
+        self.ref = ref
+        self.start = start
+        self.rows = rows
+        self.width = width
+
+    def __getitem__(self, k):
+        if k is Ellipsis:
+            k = 0
+        top = self.start + k * self.rows
+        return self.ref[top : top + self.rows, 0 : self.width]
+
+
+def table_layout(rows, local):
+    n7 = P7**3
+    n3 = P3**3
+    wide = {"g7": (0, n7, 6 * LANE), "tm": (n7, n3, 6 * LANE), "mdst": (n7 + 3 * n3, n3, 6 * LANE)}
+    mid = {"d7t": (0, n7, n7), "lift_t": (3 * n7, n3, n7), "pj": (3 * n7 + n3, n3, n7)}
+    narrow = {
+        "bcast": (0, rows, local),
+        "sel": (rows, 3 * local, rows),
+        "fsel": (rows + 3 * local, rows, local),
+        "d3t": (2 * rows + 3 * local, n3, n3),
+    }
+    return wide, mid, narrow
+
+
+def table_views(wide_ref, mid_ref, narrow_ref, local):
+    rows = narrow_ref.shape[1]
+    layouts = table_layout(rows, local)
+    views = {}
+    for ref, layout in zip((wide_ref, mid_ref, narrow_ref), layouts):
+        for name, (start, count, width) in layout.items():
+            views[name] = View(ref, start, count, width)
+    return views
+
+
 def _full(x, parts_ref):
     xh, xm, xl = _split(x)
     bh = parts_ref[0]
@@ -208,24 +256,26 @@
     m7_ref = take()
     pre_ref = take()
     stc_ref = take()
-    bc_tab = take()
-    sel_tab = take()
-    d7_ref = take()
-    g7_ref = take()
+    views = table_views(take(), take(), take(), local)
+    bc_tab = views["bcast"]
+    sel_tab = views["sel"]
+    d7_ref = views["d7t"]
+    g7_ref = views["g7"]
+    d3_ref = views["d3t"]
+    mds_ref = views["mdst"]
+    tm_ref = views["tm"]
+    pj_ref = views["pj"]
     if coarse:
         v3_ref = take()
         m3_ref = take()
-        d3_ref = take()
-        mds_ref = take()
     if coarse or project:
-        tm_ref = take()
         sw_ref = take()
-    if project:
-        pj_ref = take()
     last = coarse and not sends
     if last:
         sel_l_ref = take()
         sel_r_ref = take()
+        cnt_l_ref = take()
+        cnt_r_ref = take()
     out_u = take()
     out_c = take() if (coarse or project) else None
     out_send = [take() for _ in SEND_FACES] if sends else None
@@ -275,7 +325,7 @@
             div3 = term if div3 is None else div3 + term
         result3 = _rate_source(c, pre, stc, bcast, sel, local) - div3
         jump3 = m3_ref[...] * (trace3 - near)
-        rate3 = result3 + (P3 * (P3 - 1) / 2.0) * _full(jump3, mds_ref)
+        rate3 = result3 + (P3 * (P3 - 1) / 2.0) * _full_t(jump3, mds_ref)
 
     if second:
         new_u = 0.5 * (bu_ref[...] + u + TIME_STEP * rate7)
@@ -290,12 +340,16 @@
             new_c = c + TIME_STEP * rate3
         if last:
             out_c[...] = jnp.where(sw_ref[...] > 0.5, new_c, 0.0)
-            pay_l_ref[...] = _exact_right(sel_l_ref[...], new_u)
-            pay_r_ref[...] = _exact_right(sel_r_ref[...], new_u)
+            moved = sel_l_ref.shape[0]
+            pay_l_ref[0:moved, :] = _exact_right(sel_l_ref[...], new_u)
+            pay_r_ref[0:moved, :] = _exact_right(sel_r_ref[...], new_u)
+            tail = (pay_l_ref.shape[0] - moved, pay_l_ref.shape[1])
+            pay_l_ref[moved:, :] = jnp.broadcast_to(cnt_l_ref[0:1, 0:1], tail)
+            pay_r_ref[moved:, :] = jnp.broadcast_to(cnt_r_ref[0:1, 0:1], tail)
         else:
             out_c[...] = new_c
     if project:
-        new_c = _full(new_u, pj_ref)
+        new_c = _full_t(new_u, pj_ref)
         out_c[...] = new_c
     if sends:
         send7 = _dot(new_u.astype(bf16), g7_ref[...])
@@ -325,12 +379,16 @@
     )(*inputs)
 
 
-def setup_kernel(local, fields, u_ref, vt_ref, packed_ref, lift_ref, g7_ref, tm_ref, bc_ref,
-                 fsel_ref, v7_out, m7_out, v3_out, m3_out, pl_out, pr_out,
+def setup_kernel(local, fields, u_ref, vt_ref, packed_ref, wide_ref, mid_ref, narrow_ref, v7_out, m7_out, v3_out, m3_out, pl_out, pr_out,
                  pre_out, stc_out, sw_out, hinfo_out, cnt_l_out, cnt_r_out, sel_l_out,
                  sel_r_out, *send_refs):
     rows = local * fields
-    bcast = bc_ref[...]
+    views = table_views(wide_ref, mid_ref, narrow_ref, local)
+    lift_ref = views["lift_t"]
+    g7_ref = views["g7"]
+    tm_ref = views["tm"]
+    fsel_ref = views["fsel"]
+    bcast = views["bcast"][...]
     lanes = lax.broadcasted_iota(jnp.int32, (local, 6 * LANE), 1) // LANE
     sign = jnp.where(lanes % 2 == 0, -1.0, 1.0)
     fvg = []
@@ -407,11 +465,11 @@
         send_refs[k][...] = send[:, side * LANE : (side + 1) * LANE]
 
 
-def final_kernel(fields, hold, home_ref, from_l_ref, from_r_ref, n_l_ref, n_r_ref, hinfo_ref,
-                 out_ref):
+def final_kernel(fields, hold, home_ref, from_l_ref, from_r_ref, hinfo_ref, out_ref):
     hinfo = hinfo_ref[...]
-    n_l = n_l_ref[0:1, 0:1]
-    n_r = n_r_ref[0:1, 0:1]
+    moved = MOVE_CAP * fields
+    n_l = from_l_ref[moved : moved + 1, 0:1]
+    n_r = from_r_ref[moved : moved + 1, 0:1]
     n_h = hinfo[0:1, 6:7]
     first = hinfo[0:1, 7:8] > 0.5
     final = hinfo[0:1, 8:9] > 0.5
@@ -433,26 +491,28 @@
         return _exact_right(pick, values)
 
     total = gather(home_ref[...], hinfo[:, 2:3] > 0.5, off_h + hinfo[:, 5:6])
-    moved = from_l_ref.shape[0]
     slot = (lax.broadcasted_iota(jnp.int32, (moved, 1), 0) // fields).astype(f32)
-    total = total + gather(from_l_ref[...], slot < n_l, off_l + slot)
-    total = total + gather(from_r_ref[...], slot < n_r, off_r + slot)
+    total = total + gather(from_l_ref[0:moved, :], slot < n_l, off_l + slot)
+    total = total + gather(from_r_ref[0:moved, :], slot < n_r, off_r + slot)
     out_ref[...] = total
 
 
 def setup_entry(local, fields, n_in, n_out, *refs):
     sources = refs[:n_in]
     outs = refs[n_in : n_in + n_out]
-    buffers = refs[n_in + n_out : 2 * n_in + n_out]
-    sems = refs[2 * n_in + n_out]
+    n_tab = 3
+    n_own = n_in - n_tab
+    buffers = refs[n_in + n_out : n_in + n_out + n_own]
+    sems = refs[n_in + n_out + n_own]
+    targets = list(buffers) + list(outs[n_out - n_tab :])
     copies = [
-        pltpu.make_async_copy(sources[i], buffers[i], sems.at[i]) for i in range(n_in)
+        pltpu.make_async_copy(sources[i], targets[i], sems.at[i]) for i in range(n_in)
     ]
     for copy in copies:
         copy.start()
     for copy in copies:
         copy.wait()
-    setup_kernel(local, fields, *buffers, *outs)
+    setup_kernel(local, fields, *targets, *outs[: n_out - n_tab])
 
 
 def per_device(state, velocity, pre_exp, stoich, neighbours, switch, new_owner):
@@ -489,19 +549,38 @@
         ],
         axis=1,
     )
-    fsel = jnp.asarray(to_bf16(np.arange(rows)[:, None] % field_count == np.arange(local_count)[None, :]))
+    fsel_np = np.arange(rows)[:, None] % field_count == np.arange(local_count)[None, :]
     vt = jnp.transpose(velocity, (0, 2, 1))
     row_elem = np.arange(rows) // field_count
-    bcast = jnp.asarray(to_bf16(row_elem[:, None] == np.arange(local_count)[None, :]))
+    bcast_np = row_elem[:, None] == np.arange(local_count)[None, :]
     pick_rows = (np.arange(3)[:, None] + field_count * np.arange(local_count)[None, :]).reshape(-1)
-    sel = jnp.asarray(to_bf16(pick_rows[:, None] == np.arange(rows)[None, :]))
-    lift_t = jnp.asarray(to_bf16(tab["lift"].astype(np.float32).T))
-    d7t = jnp.asarray(tab["d7t"])
-    g7 = jnp.asarray(tab["g7"])
-    d3t = jnp.asarray(tab["d3t"])
-    tm = jnp.asarray(tab["tm"])
-    mds = jnp.asarray(tab["mds"])
-    pjt = jnp.asarray(tab["pjt"])
+    sel_np = pick_rows[:, None] == np.arange(rows)[None, :]
+    n7 = P7**3
+    n3 = P3**3
+    layouts = table_layout(rows, local_count)
+    wide_np = np.zeros((n7 + 6 * n3, 6 * LANE), np.float32)
+    mid_np = np.zeros((3 * n7 + 4 * n3, n7), np.float32)
+    narrow_np = np.zeros((2 * rows + 3 * local_count + 3 * n3, rows), np.float32)
+    pieces = {
+        "g7": tab["g7"][None],
+        "tm": tab["tm"],
+        "mdst": np.transpose(tab["mds"], (0, 2, 1)),
+        "d7t": tab["d7t"],
+        "lift_t": tab["lift"].T[None],
+        "pj": np.transpose(tab["pjt"], (0, 2, 1)),
+        "bcast": bcast_np[None],
+        "sel": sel_np[None],
+        "fsel": fsel_np[None],
+        "d3t": tab["d3t"],
+    }
+    for target, layout in zip((wide_np, mid_np, narrow_np), layouts):
+        for name, (start, count, width) in layout.items():
+            parts = np.asarray(pieces[name], np.float32)
+            for k in range(parts.shape[0]):
+                target[start + k * count : start + (k + 1) * count, :width] = parts[k]
+    wide = jnp.asarray(to_bf16(wide_np))
+    mid = jnp.asarray(to_bf16(mid_np))
+    narrow = jnp.asarray(to_bf16(narrow_np))
 
     send_shape = jax.ShapeDtypeStruct((rows, LANE), bf16)
     u_shape = jax.ShapeDtypeStruct((rows, P7**3), f32)
@@ -532,23 +611,23 @@
         jax.ShapeDtypeStruct((MOVE_CAP * field_count, rows), bf16),
         jax.ShapeDtypeStruct((MOVE_CAP * field_count, rows), bf16),
     ] + [send_shape] * 4
+    setup_out = setup_out + [jax.ShapeDtypeStruct(x.shape, x.dtype) for x in (wide, mid, narrow)]
     u0 = state.reshape(rows, P7**3)
-    setup_in = [u0, vt, packed, lift_t, g7, tm, bcast, fsel]
+    setup_in = [u0, vt, packed, wide, mid, narrow]
     res = pl.pallas_call(
         functools.partial(setup_entry, local_count, field_count, len(setup_in), len(setup_out)),
         out_shape=setup_out,
         in_specs=[pl.BlockSpec(memory_space=pltpu.HBM) for _ in setup_in],
         out_specs=[_vmem() for _ in setup_out],
-        scratch_shapes=[pltpu.VMEM(x.shape, x.dtype) for x in setup_in]
+        scratch_shapes=[pltpu.VMEM(x.shape, x.dtype) for x in setup_in[:3]]
         + [pltpu.SemaphoreType.DMA((len(setup_in),))],
-        compiler_params=pltpu.CompilerParams(vmem_limit_bytes=63 * 1024 * 1024),
+        compiler_params=pltpu.CompilerParams(vmem_limit_bytes=24 * 1024 * 1024),
     )(*setup_in)
     v7, m7, v3, m3, p_local, p_remote, pre, stc, sw = res[:9]
     hinfo, cnt_l, cnt_r, sel_l, sel_r = res[9:14]
-    sends = res[14:]
-    n_from_right = shifted(cnt_l, "curve", -1)
-    n_from_left = shifted(cnt_r, "curve", 1)
-    common = [p_local, p_remote, v7, m7, pre, stc, bcast, sel, d7t, g7]
+    sends = res[14:18]
+    wide, mid, narrow = res[18:21]
+    common = [p_local, p_remote, v7, m7, pre, stc, wide, mid, narrow]
     recv = exchange(sends)
     res = run_stage(
         (False, False, False, True, local_count),
@@ -559,12 +638,12 @@
     recv = exchange(sends)
     res = run_stage(
         (False, True, True, True, local_count),
-        [first, u0] + recv + common + [tm, sw, pjt],
+        [first, u0] + recv + common + [sw],
         [u_shape, c_shape] + [send_shape] * 4,
     )
     after, coarse, sends = res[0], res[1], res[2:]
     recv = exchange(sends)
-    mixed_tail = [v3, m3, d3t, mds, tm, sw]
+    mixed_tail = [v3, m3, sw]
     res = run_stage(
         (True, False, False, True, local_count),
         [after, coarse] + recv + common + mixed_tail,
@@ -572,10 +651,10 @@
     )
     first7, first3, sends = res[0], res[1], res[2:]
     recv = exchange(sends)
-    pay_shape = jax.ShapeDtypeStruct((MOVE_CAP * field_count, P7**3), f32)
+    pay_shape = jax.ShapeDtypeStruct((MOVE_CAP * field_count + 8, P7**3), f32)
     res = run_stage(
         (True, True, False, False, local_count),
-        [first7, first3, after, coarse] + recv + common + mixed_tail + [sel_l, sel_r],
+        [first7, first3, after, coarse] + recv + common + mixed_tail + [sel_l, sel_r, cnt_l, cnt_r],
         [u_shape, c_shape, pay_shape, pay_shape],
     )
     final7, final3, pay_l, pay_r = res
@@ -584,9 +663,9 @@
     held = pl.pallas_call(
         functools.partial(final_kernel, field_count, HOLD7),
         out_shape=jax.ShapeDtypeStruct((HOLD7 * field_count, P7**3), f32),
-        in_specs=[_vmem() for _ in range(6)],
+        in_specs=[_vmem() for _ in range(4)],
         out_specs=_vmem(),
-    )(final7, from_left, from_right, n_from_left, n_from_right, hinfo)
+    )(final7, from_left, from_right, hinfo)
     state7_out = held.reshape(HOLD7, field_count, P7**3)
     state3_out = final3.reshape(local_count, field_count * P3**3)
     return (state7_out, state3_out)

time: 82.7 us -> 74.6 us (0.902)
  starting transfers between devices: 36 us -> 31.6 us
  local copies, waits for them, and re-layouts: 12.9 us -> 9.91 us
    ppermute x20 -> x18, starting transfers between devices: 36 us -> 31.6 us  [shifted(): return lax.ppermute(value, axis, pairs)]
    unnamed x65 -> x23, local copies, waits for them, and re-layouts: 9.88 us -> 7.48 us
    pallas_call x1, Pallas kernels: 4.31 us -> 2.67 us  [per_device(): pl.pallas_call(functools.partial(setup_entry, local_count, field_count, l...]
    pallas_call x4, Pallas kernels: 11.2 us -> 12.2 us  [run_stage(): pl.pallas_call(kernel, out_shape=out_shapes, in_specs=[_vmem() for _ in i...]
    ppermute x20 -> x18, waiting for transfers between devices: 12.7 us -> 12.9 us  [shifted(): return lax.ppermute(value, axis, pairs)]
  transfers between devices with their start and end apart: 20 -> 18, of which waited for: 9 -> 9; matrix products, arithmetic and copies ran while one was open for 1% -> 1% of each run, Pallas kernels for 0% -> 0%
where the time goes in v4:
time: 74.6 us; the launch traced here: 74.2 us
  starting transfers between devices  31.6 us (42%)
  Pallas kernels  17.6 us (24%)
  waiting for transfers between devices  12.9 us (17%)
  local copies, waits for them, and re-layouts  9.91 us (13%)
  other arithmetic  1.33 us (2%)
  between operations  0.83 us (1%)
    ppermute x18, starting transfers between devices, shifted(): return lax.ppermute(value, axis, pairs)  31.6 us
    ppermute x18, waiting for transfers between devices, shifted(): return lax.ppermute(value, axis, pairs)  12.9 us
    pallas_call x4, Pallas kernels, run_stage(): pl.pallas_call(kernel, out_shape=out_shapes, in_specs=[_vmem() for _ in i...  12.2 us
    unnamed x23, local copies, waits for them, and re-layouts  7.48 us
    pallas_call x1, Pallas kernels, per_device(): pl.pallas_call(functools.partial(final_kernel, field_count, HOLD7), out_s...  2.73 us
    pallas_call x1, Pallas kernels, per_device(): pl.pallas_call(functools.partial(setup_entry, local_count, field_count, l...  2.67 us
  transfers between devices with their start and end apart: 18, of which 9 were waited for; matrix products, arithmetic and copies ran while one was open for 1% of the time, Pallas kernels for 0%

profile of v4, /device:TPU:0, one launch (start us, length us, event | category | flops | bytes accessed | tf_op | source)
XLA Modules:
  0.0 74.2 jit_solution(9801091763035273130)
XLA Ops:
  2.0 0.7 copy.26
  2.9 0.7 copy.28
  3.6 0.8 %copy.25 = s32[16,6]{1,0:T(8,128)S(1)} copy(s32[16,6]{0,1:T(8,128)} %param.16) | data formatting | bytes 768 | tf_op args[4]
  4.5 0.9 %copy-done.1 = f32[16,8,512]{2,1,0:T(8,128)S(1)} copy-done((f32[16,8,512]{2,1,0:T(8,128)S(1)}, f32[16,8,512]{2,1,0:T(8,128)}, u32[]{:S(2)}) %copy-start.1) | copy-done | bytes 262168
  5.5 1.5 %copy-done.3 = bf16[1792,512]{1,0:T(8,128)(2,1)S(1)} copy-done((bf16[1792,512]{1,0:T(8,128)(2,1)S(1)}, bf16[1792,512]{1,0:T(8,128)(2,1)}, u32[]{:S(2)}) %copy-start.3) | copy-done | bytes 1835032
  7.0 1.3 %copy-done.4 = bf16[896,768]{1,0:T(8,128)(2,1)S(1)} copy-done((bf16[896,768]{1,0:T(8,128)(2,1)S(1)}, bf16[896,768]{1,0:T(8,128)(2,1)}, u32[]{:S(2)}) %copy-start.4) | copy-done | bytes 1376280
  8.3 0.9 %copy-done.6 = bf16[496,128]{1,0:T(8,128)(2,1)S(1)} copy-done((bf16[496,128]{1,0:T(8,128)(2,1)S(1)}, bf16[496,128]{1,0:T(8,128)(2,1)}, u32[]{:S(2)}) %copy-start.6) | copy-done | bytes 127000
  9.2 0.7 copy-done.8
  9.9 2.7 %shard_map.113 = (bf16[3,128,512]{2,1,0:T(8,128)(2,1)S(1)}, f32[128,768]{1,0:T(8,128)S(1)}, f32[3,128,64]{2,1,0:T(8,128)S(1)}, f32[128,768]{1,0:T(8,128)S(1)}, b...) custom-call(f32[128,512]{1,0:T(8,128)S(1)} %bitcast.9, ...), custom_call_target="tpu_custom_call" | custom-call | tf_op jit(solution)/shard_map/pallas_call | solution.py:617
  13.2 5.0 %collective-permute-start.1 = (bf16[128,128]{1,0:T(8,128)(2,1)S(1)}, bf16[128,128]{1,0:T(8,128)(2,1)S(1)}, u32[]{:S(2)}, u32[]{:S(2)}) collective-permute-start(bf16[128,128]{1,0:T(8,128)(2,1)S(1)} %get-tuple-element.57), channel_id=1, source_target_pairs={{0,15},{1,0},{2,1},{3,2},{4,3},{5,4},{6,5},{7,6},{8,7},{9,8},{10,9... | collective-permute-start | bytes 98312 | tf_op jit(solution)/shard_map/ppermute | solution.py:32
  18.2 1.9 %collective-permute-start.2 = (bf16[128,128]{1,0:T(8,128)(2,1)S(1)}, bf16[128,128]{1,0:T(8,128)(2,1)S(1)}, u32[]{:S(2)}, u32[]{:S(2)}) collective-permute-start(bf16[128,128]{1,0:T(8,128)(2,1)S(1)} %get-tuple-element.58), channel_id=1, source_target_pairs={{0,16},{16,0},{1,17},{17,1},{2,18},{18,2},{3,19},{19,3},{4,20},{20... | collective-permute-start | bytes 98312 | tf_op jit(solution)/shard_map/ppermute | solution.py:32
  20.3 1.9 %collective-permute-done.2.refs_3_ = bf16[128,128]{1,0:T(8,128)(2,1)S(1)} collective-permute-done((bf16[128,128]{1,0:T(8,128)(2,1)S(1)}, bf16[128,128]{1,0:T(8,128)(2,1)S(1)}, u32[]{:S(2)}, u32[]{:S(2)}) %collective-permute-start.2) | collective-permute-done | bytes 32800 | tf_op jit(solution)/shard_map/ppermute | solution.py:32
  22.2 1.9 %collective-permute-done.3.refs_4_ = bf16[128,128]{1,0:T(8,128)(2,1)S(1)} collective-permute-done((bf16[128,128]{1,0:T(8,128)(2,1)S(1)}, bf16[128,128]{1,0:T(8,128)(2,1)S(1)}, u32[]{:S(2)}, u32[]{:S(2)}) %collective-permute-start.3) | collective-permute-done | bytes 32800 | tf_op jit(solution)/shard_map/ppermute | solution.py:32
  24.0 1.9 %shard_map.114 = (f32[128,512]{1,0:T(8,128)S(1)}, bf16[128,128]{1,0:T(8,128)(2,1)S(1)}, bf16[128,128]{1,0:T(8,128)(2,1)S(1)}, bf16[128,128]{1,0:T(8,128)(2,1)S(1)}, bf16[128,128]{1,0:T(8,128)(2,1)S(1)}) custom-call(f32[128,512]{1,0:T(8,128)S(1)} %bitcast.10, bf16[128,128]{1,0:T(8,128)(2,1)S(1)} %collective-permute-done.refs_1_, ...), custom_call_target="tpu_custom_call" | custom-call | tf_op jit(solution)/shard_map/pallas_call | solution.py:373
  26.0 4.4 %collective-permute-start.5 = (bf16[128,128]{1,0:T(8,128)(2,1)S(1)}, bf16[128,128]{1,0:T(8,128)(2,1)S(1)}, u32[]{:S(2)}, u32[]{:S(2)}) collective-permute-start(bf16[128,128]{1,0:T(8,128)(2,1)S(1)} %get-tuple-element.71), channel_id=1, source_target_pairs={{0,15},{1,0},{2,1},{3,2},{4,3},{5,4},{6,5},{7,6},{8,7},{9,8},{10,9... | collective-permute-start | bytes 98312 | tf_op jit(solution)/shard_map/ppermute | solution.py:32
  30.8 1.7 %collective-permute-start.7 = (bf16[128,128]{1,0:T(8,128)(2,1)S(1)}, bf16[128,128]{1,0:T(8,128)(2,1)S(1)}, u32[]{:S(2)}, u32[]{:S(2)}) collective-permute-start(bf16[128,128]{1,0:T(8,128)(2,1)S(1)} %get-tuple-element.73), channel_id=1, source_target_pairs={{0,16},{16,0},{1,17},{17,1},{2,18},{18,2},{3,19},{19,3},{4,20},{20... | collective-permute-start | bytes 98312 | tf_op jit(solution)/shard_map/ppermute | solution.py:32
  32.5 1.9 %collective-permute-done.6.refs_4_ = bf16[128,128]{1,0:T(8,128)(2,1)S(1)} collective-permute-done((bf16[128,128]{1,0:T(8,128)(2,1)S(1)}, bf16[128,128]{1,0:T(8,128)(2,1)S(1)}, u32[]{:S(2)}, u32[]{:S(2)}) %collective-permute-start.6) | collective-permute-done | bytes 32800 | tf_op jit(solution)/shard_map/ppermute | solution.py:32
  34.7 2.8 %shard_map.115 = (f32[128,512]{1,0:T(8,128)S(1)}, f32[128,64]{1,0:T(8,128)S(1)}, bf16[128,128]{1,0:T(8,128)(2,1)S(1)}, bf16[128,128]{1,0:T(8,128)(2,1)S(1)}, bf1...) custom-call(f32[128,512]{1,0:T(8,128)S(1)} %get-tuple-element.69.refs_0_, f32[128,512]{1,0:T(8,128)S(1)} %bitcast.11, ...), custom_call_target="tpu_custom_call" | custom-call | tf_op jit(solution)/shard_map/pallas_call | solution.py:373
  37.6 4.4 %collective-permute-start.9 = (bf16[128,128]{1,0:T(8,128)(2,1)S(1)}, bf16[128,128]{1,0:T(8,128)(2,1)S(1)}, u32[]{:S(2)}, u32[]{:S(2)}) collective-permute-start(bf16[128,128]{1,0:T(8,128)(2,1)S(1)} %get-tuple-element.78), channel_id=1, source_target_pairs={{0,15},{1,0},{2,1},{3,2},{4,3},{5,4},{6,5},{7,6},{8,7},{9,8},{10,9... | collective-permute-start | bytes 98312 | tf_op jit(solution)/shard_map/ppermute | solution.py:32
  42.1 1.7 %collective-permute-start.10 = (bf16[128,128]{1,0:T(8,128)(2,1)S(1)}, bf16[128,128]{1,0:T(8,128)(2,1)S(1)}, u32[]{:S(2)}, u32[]{:S(2)}) collective-permute-start(bf16[128,128]{1,0:T(8,128)(2,1)S(1)} %get-tuple-element.79), channel_id=1, source_target_pairs={{0,16},{16,0},{1,17},{17,1},{2,18},{18,2},{3,19},{19,3},{4,20},{20... | collective-permute-start | bytes 98312 | tf_op jit(solution)/shard_map/ppermute | solution.py:32
  44.1 1.9 %collective-permute-done.10.refs_4_ = bf16[128,128]{1,0:T(8,128)(2,1)S(1)} collective-permute-done((bf16[128,128]{1,0:T(8,128)(2,1)S(1)}, bf16[128,128]{1,0:T(8,128)(2,1)S(1)}, u32[]{:S(2)}, u32[]{:S(2)}) %collective-permute-start.10) | collective-permute-done | bytes 32800 | tf_op jit(solution)/shard_map/ppermute | solution.py:32
  46.0 1.7 %collective-permute-done.11.refs_5_ = bf16[128,128]{1,0:T(8,128)(2,1)S(1)} collective-permute-done((bf16[128,128]{1,0:T(8,128)(2,1)S(1)}, bf16[128,128]{1,0:T(8,128)(2,1)S(1)}, u32[]{:S(2)}, u32[]{:S(2)}) %collective-permute-start.11) | collective-permute-done | bytes 32800 | tf_op jit(solution)/shard_map/ppermute | solution.py:32
  47.7 3.4 %shard_map.116 = (f32[128,512]{1,0:T(8,128)S(1)}, f32[128,64]{1,0:T(8,128)S(1)}, bf16[128,128]{1,0:T(8,128)(2,1)S(1)}, bf16[128,128]{1,0:T(8,128)(2,1)S(1)}, bf1...) custom-call(f32[128,512]{1,0:T(8,128)S(1)} %get-tuple-element.75.refs_0_.refs_2_, ...), custom_call_target="tpu_custom_call" | custom-call | tf_op jit(solution)/shard_map/pallas_call | solution.py:373
  51.1 4.4 %collective-permute-start.13 = (bf16[128,128]{1,0:T(8,128)(2,1)S(1)}, bf16[128,128]{1,0:T(8,128)(2,1)S(1)}, u32[]{:S(2)}, u32[]{:S(2)}) collective-permute-start(bf16[128,128]{1,0:T(8,128)(2,1)S(1)} %get-tuple-element.86), channel_id=1, source_target_pairs={{0,15},{1,0},{2,1},{3,2},{4,3},{5,4},{6,5},{7,6},{8,7},{9,8},{10,9... | collective-permute-start | bytes 98312 | tf_op jit(solution)/shard_map/ppermute | solution.py:32
  55.9 1.7 %collective-permute-start.15 = (bf16[128,128]{1,0:T(8,128)(2,1)S(1)}, bf16[128,128]{1,0:T(8,128)(2,1)S(1)}, u32[]{:S(2)}, u32[]{:S(2)}) collective-permute-start(bf16[128,128]{1,0:T(8,128)(2,1)S(1)} %get-tuple-element.88), channel_id=1, source_target_pairs={{0,16},{16,0},{1,17},{17,1},{2,18},{18,2},{3,19},{19,3},{4,20},{20... | collective-permute-start | bytes 98312 | tf_op jit(solution)/shard_map/ppermute | solution.py:32
  57.6 1.9 %collective-permute-done.14.refs_6_ = bf16[128,128]{1,0:T(8,128)(2,1)S(1)} collective-permute-done((bf16[128,128]{1,0:T(8,128)(2,1)S(1)}, bf16[128,128]{1,0:T(8,128)(2,1)S(1)}, u32[]{:S(2)}, u32[]{:S(2)}) %collective-permute-start.14) | collective-permute-done | bytes 32800 | tf_op jit(solution)/shard_map/ppermute | solution.py:32
  59.8 4.1 %shard_map.117 = (f32[128,512]{1,0:T(8,128)S(1)}, f32[128,64]{1,0:T(8,128)S(1)}, f32[24,512]{1,0:T(8,128)S(1)}, f32[24,512]{1,0:T(8,128)S(1)}) custom-call(f32[128,512]{1,0:T(8,128)S(1)} %get-tuple-element.83.refs_0_, f32[128,64]{1,0:T(8,128)S(1)} %get-tuple-element.84.refs_1_, f32[128,512]{1,0:T(8,128)S(1)} %get-tuple-element.75.refs_0_.refs_2_, ...), custom_call_target="tpu_custom_call" | custom-call | tf_op jit(solution)/shard_map/pallas_call | solution.py:373
  63.9 0.7 copy-done.5
  64.6 4.4 %collective-permute-start.17 = (f32[24,512]{1,0:T(8,128)S(1)}, f32[24,512]{1,0:T(8,128)S(1)}, u32[]{:S(2)}, u32[]{:S(2)}) collective-permute-start(f32[24,512]{1,0:T(8,128)S(1)} %get-tuple-element.95), channel_id=1, source_target_pairs={{0,15},{1,0},{2,1},{3,2},{4,3},{5,4},{6,5},{7,6},{8,7},{9,8},{10,9... | collective-permute-start | bytes 147464 | tf_op jit(solution)/shard_map/ppermute | solution.py:32
  69.0 0.7 reshape.40
  69.7 1.1 %collective-permute-done.16.from_l_ref = f32[24,512]{1,0:T(8,128)S(1)} collective-permute-done((f32[24,512]{1,0:T(8,128)S(1)}, f32[24,512]{1,0:T(8,128)S(1)}, u32[]{:S(2)}, u32[]{:S(2)}) %collective-permute-start.16) | collective-permute-done | bytes 49184 | tf_op jit(solution)/shard_map/ppermute | solution.py:32
  71.4 2.7 %shard_map.118 = f32[96,512]{1,0:T(8,128)} custom-call(f32[128,512]{1,0:T(8,128)} %copy-done.5, f32[24,512]{1,0:T(8,128)} %copy-done.9, f32[24,512]{1,0:T(8,128)} %copy-done.10, f32[128,128]{1,0:T(8,128)} %copy-done.7), custom_call_target="tpu_custom_call" | custom-call | tf_op jit(solution)/shard_map/pallas_call | solution.py:663
  (48 shorter events, 4.9 us)
Async XLA Ops:
  4.5 1.0 %copy-start.1 = (f32[16,8,512]{2,1,0:T(8,128)S(1)}, f32[16,8,512]{2,1,0:T(8,128)}, u32[]{:S(2)}) copy-start(f32[16,8,512]{2,1,0:T(8,128)} %param.12) | copy-start | bytes 786436
  5.5 1.5 %copy-start.3 = (bf16[1792,512]{1,0:T(8,128)(2,1)S(1)}, bf16[1792,512]{1,0:T(8,128)(2,1)}, u32[]{:S(2)}) copy-start(bf16[1792,512]{1,0:T(8,128)(2,1)} %constant.80.clone.refs_4_) | copy-start | bytes 5505028
  7.0 1.3 %copy-start.4 = (bf16[896,768]{1,0:T(8,128)(2,1)S(1)}, bf16[896,768]{1,0:T(8,128)(2,1)}, u32[]{:S(2)}) copy-start(bf16[896,768]{1,0:T(8,128)(2,1)} %constant.79.clone.refs_3_) | copy-start | bytes 4128772
  8.3 0.9 %copy-start.6 = (bf16[496,128]{1,0:T(8,128)(2,1)S(1)}, bf16[496,128]{1,0:T(8,128)(2,1)}, u32[]{:S(2)}) copy-start(bf16[496,128]{1,0:T(8,128)(2,1)} %constant.81.clone.refs_5_) | copy-start | bytes 380932
  9.2 0.7 copy-start.8
  9.9 14.1 %copy-start.2 = (f32[16,8,512]{2,1,0:T(8,128)S(1)}, f32[16,8,512]{2,1,0:T(8,128)}, u32[]{:S(2)}) copy-start(f32[16,8,512]{2,1,0:T(8,128)} %param.12) | copy-start | bytes 786436
  12.6 13.3 %copy-start.7 = (f32[128,128]{1,0:T(8,128)}, f32[128,128]{1,0:T(8,128)S(1)}, u32[]{:S(2)}) copy-start(f32[128,128]{1,0:T(8,128)S(1)} %get-tuple-element.96.hinfo_ref) | copy-start | bytes 196612
  12.6 35.0 %copy-start = (bf16[1792,512]{1,0:T(8,128)(2,1)}, bf16[1792,512]{1,0:T(8,128)(2,1)S(1)}, u32[]{:S(2)}) copy-start(bf16[1792,512]{1,0:T(8,128)(2,1)S(1)} %get-tuple-element.67.refs_12_.refs_13_.refs_15_) | copy-start | bytes 5505028
  12.6 7.6 %collective-permute-start = (bf16[128,128]{1,0:T(8,128)(2,1)S(1)}, bf16[128,128]{1,0:T(8,128)(2,1)S(1)}, u32[]{:S(2)}, u32[]{:S(2)}) collective-permute-start(bf16[128,128]{1,0:T(8,128)(2,1)S(1)} %get-tuple-element.56), channel_id=1, source_target_pairs={{0,1},{1,2},{2,3},{3,4},{4,5},{5,6},{6,7},{7,8},{8,9},{9,10},{10,1... | collective-permute-start | bytes 98312 | tf_op jit(solution)/shard_map/ppermute | solution.py:32
  13.2 7.1 %collective-permute-start.1 = (bf16[128,128]{1,0:T(8,128)(2,1)S(1)}, bf16[128,128]{1,0:T(8,128)(2,1)S(1)}, u32[]{:S(2)}, u32[]{:S(2)}) collective-permute-start(bf16[128,128]{1,0:T(8,128)(2,1)S(1)} %get-tuple-element.57), channel_id=1, source_target_pairs={{0,15},{1,0},{2,1},{3,2},{4,3},{5,4},{6,5},{7,6},{8,7},{9,8},{10,9... | collective-permute-start | bytes 98312 | tf_op jit(solution)/shard_map/ppermute | solution.py:32
  18.2 3.9 %collective-permute-start.2 = (bf16[128,128]{1,0:T(8,128)(2,1)S(1)}, bf16[128,128]{1,0:T(8,128)(2,1)S(1)}, u32[]{:S(2)}, u32[]{:S(2)}) collective-permute-start(bf16[128,128]{1,0:T(8,128)(2,1)S(1)} %get-tuple-element.58), channel_id=1, source_target_pairs={{0,16},{16,0},{1,17},{17,1},{2,18},{18,2},{3,19},{19,3},{4,20},{20... | collective-permute-start | bytes 98312 | tf_op jit(solution)/shard_map/ppermute | solution.py:32
  20.1 3.9 %collective-permute-start.3 = (bf16[128,128]{1,0:T(8,128)(2,1)S(1)}, bf16[128,128]{1,0:T(8,128)(2,1)S(1)}, u32[]{:S(2)}, u32[]{:S(2)}) collective-permute-start(bf16[128,128]{1,0:T(8,128)(2,1)S(1)} %get-tuple-element.59), channel_id=1, source_target_pairs={{0,16},{16,0},{1,17},{17,1},{2,18},{18,2},{3,19},{19,3},{4,20},{20... | collective-permute-start | bytes 98312 | tf_op jit(solution)/shard_map/ppermute | solution.py:32
  26.0 6.5 %collective-permute-start.4 = (bf16[128,128]{1,0:T(8,128)(2,1)S(1)}, bf16[128,128]{1,0:T(8,128)(2,1)S(1)}, u32[]{:S(2)}, u32[]{:S(2)}) collective-permute-start(bf16[128,128]{1,0:T(8,128)(2,1)S(1)} %get-tuple-element.70), channel_id=1, source_target_pairs={{0,1},{1,2},{2,3},{3,4},{4,5},{5,6},{6,7},{7,8},{8,9},{9,10},{10,1... | collective-permute-start | bytes 98312 | tf_op jit(solution)/shard_map/ppermute | solution.py:32
  26.0 6.5 %collective-permute-start.5 = (bf16[128,128]{1,0:T(8,128)(2,1)S(1)}, bf16[128,128]{1,0:T(8,128)(2,1)S(1)}, u32[]{:S(2)}, u32[]{:S(2)}) collective-permute-start(bf16[128,128]{1,0:T(8,128)(2,1)S(1)} %get-tuple-element.71), channel_id=1, source_target_pairs={{0,15},{1,0},{2,1},{3,2},{4,3},{5,4},{6,5},{7,6},{8,7},{9,8},{10,9... | collective-permute-start | bytes 98312 | tf_op jit(solution)/shard_map/ppermute | solution.py:32
  30.5 3.9 %collective-permute-start.6 = (bf16[128,128]{1,0:T(8,128)(2,1)S(1)}, bf16[128,128]{1,0:T(8,128)(2,1)S(1)}, u32[]{:S(2)}, u32[]{:S(2)}) collective-permute-start(bf16[128,128]{1,0:T(8,128)(2,1)S(1)} %get-tuple-element.72), channel_id=1, source_target_pairs={{0,16},{16,0},{1,17},{17,1},{2,18},{18,2},{3,19},{19,3},{4,20},{20... | collective-permute-start | bytes 98312 | tf_op jit(solution)/shard_map/ppermute | solution.py:32
  30.8 3.9 %collective-permute-start.7 = (bf16[128,128]{1,0:T(8,128)(2,1)S(1)}, bf16[128,128]{1,0:T(8,128)(2,1)S(1)}, u32[]{:S(2)}, u32[]{:S(2)}) collective-permute-start(bf16[128,128]{1,0:T(8,128)(2,1)S(1)} %get-tuple-element.73), channel_id=1, source_target_pairs={{0,16},{16,0},{1,17},{17,1},{2,18},{18,2},{3,19},{19,3},{4,20},{20... | collective-permute-start | bytes 98312 | tf_op jit(solution)/shard_map/ppermute | solution.py:32
  37.6 6.5 %collective-permute-start.8 = (bf16[128,128]{1,0:T(8,128)(2,1)S(1)}, bf16[128,128]{1,0:T(8,128)(2,1)S(1)}, u32[]{:S(2)}, u32[]{:S(2)}) collective-permute-start(bf16[128,128]{1,0:T(8,128)(2,1)S(1)} %get-tuple-element.77), channel_id=1, source_target_pairs={{0,1},{1,2},{2,3},{3,4},{4,5},{5,6},{6,7},{7,8},{8,9},{9,10},{10,1... | collective-permute-start | bytes 98312 | tf_op jit(solution)/shard_map/ppermute | solution.py:32
  37.6 6.5 %collective-permute-start.9 = (bf16[128,128]{1,0:T(8,128)(2,1)S(1)}, bf16[128,128]{1,0:T(8,128)(2,1)S(1)}, u32[]{:S(2)}, u32[]{:S(2)}) collective-permute-start(bf16[128,128]{1,0:T(8,128)(2,1)S(1)} %get-tuple-element.78), channel_id=1, source_target_pairs={{0,15},{1,0},{2,1},{3,2},{4,3},{5,4},{6,5},{7,6},{8,7},{9,8},{10,9... | collective-permute-start | bytes 98312 | tf_op jit(solution)/shard_map/ppermute | solution.py:32
  42.1 3.9 %collective-permute-start.10 = (bf16[128,128]{1,0:T(8,128)(2,1)S(1)}, bf16[128,128]{1,0:T(8,128)(2,1)S(1)}, u32[]{:S(2)}, u32[]{:S(2)}) collective-permute-start(bf16[128,128]{1,0:T(8,128)(2,1)S(1)} %get-tuple-element.79), channel_id=1, source_target_pairs={{0,16},{16,0},{1,17},{17,1},{2,18},{18,2},{3,19},{19,3},{4,20},{20... | collective-permute-start | bytes 98312 | tf_op jit(solution)/shard_map/ppermute | solution.py:32
  43.8 3.9 %collective-permute-start.11 = (bf16[128,128]{1,0:T(8,128)(2,1)S(1)}, bf16[128,128]{1,0:T(8,128)(2,1)S(1)}, u32[]{:S(2)}, u32[]{:S(2)}) collective-permute-start(bf16[128,128]{1,0:T(8,128)(2,1)S(1)} %get-tuple-element.80), channel_id=1, source_target_pairs={{0,16},{16,0},{1,17},{17,1},{2,18},{18,2},{3,19},{19,3},{4,20},{20... | collective-permute-start | bytes 98312 | tf_op jit(solution)/shard_map/ppermute | solution.py:32
  51.1 6.5 %collective-permute-start.12 = (bf16[128,128]{1,0:T(8,128)(2,1)S(1)}, bf16[128,128]{1,0:T(8,128)(2,1)S(1)}, u32[]{:S(2)}, u32[]{:S(2)}) collective-permute-start(bf16[128,128]{1,0:T(8,128)(2,1)S(1)} %get-tuple-element.85), channel_id=1, source_target_pairs={{0,1},{1,2},{2,3},{3,4},{4,5},{5,6},{6,7},{7,8},{8,9},{9,10},{10,1... | collective-permute-start | bytes 98312 | tf_op jit(solution)/shard_map/ppermute | solution.py:32
  51.1 6.5 %collective-permute-start.13 = (bf16[128,128]{1,0:T(8,128)(2,1)S(1)}, bf16[128,128]{1,0:T(8,128)(2,1)S(1)}, u32[]{:S(2)}, u32[]{:S(2)}) collective-permute-start(bf16[128,128]{1,0:T(8,128)(2,1)S(1)} %get-tuple-element.86), channel_id=1, source_target_pairs={{0,15},{1,0},{2,1},{3,2},{4,3},{5,4},{6,5},{7,6},{8,7},{9,8},{10,9... | collective-permute-start | bytes 98312 | tf_op jit(solution)/shard_map/ppermute | solution.py:32
  55.6 3.9 %collective-permute-start.14 = (bf16[128,128]{1,0:T(8,128)(2,1)S(1)}, bf16[128,128]{1,0:T(8,128)(2,1)S(1)}, u32[]{:S(2)}, u32[]{:S(2)}) collective-permute-start(bf16[128,128]{1,0:T(8,128)(2,1)S(1)} %get-tuple-element.87), channel_id=1, source_target_pairs={{0,16},{16,0},{1,17},{17,1},{2,18},{18,2},{3,19},{19,3},{4,20},{20... | collective-permute-start | bytes 98312 | tf_op jit(solution)/shard_map/ppermute | solution.py:32
  55.9 3.9 %collective-permute-start.15 = (bf16[128,128]{1,0:T(8,128)(2,1)S(1)}, bf16[128,128]{1,0:T(8,128)(2,1)S(1)}, u32[]{:S(2)}, u32[]{:S(2)}) collective-permute-start(bf16[128,128]{1,0:T(8,128)(2,1)S(1)} %get-tuple-element.88), channel_id=1, source_target_pairs={{0,16},{16,0},{1,17},{17,1},{2,18},{18,2},{3,19},{19,3},{4,20},{20... | collective-permute-start | bytes 98312 | tf_op jit(solution)/shard_map/ppermute | solution.py:32
  63.9 0.7 copy-start.5
  64.6 6.2 %collective-permute-start.16 = (f32[24,512]{1,0:T(8,128)S(1)}, f32[24,512]{1,0:T(8,128)S(1)}, u32[]{:S(2)}, u32[]{:S(2)}) collective-permute-start(f32[24,512]{1,0:T(8,128)S(1)} %get-tuple-element.94), channel_id=1, source_target_pairs={{0,1},{1,2},{2,3},{3,4},{4,5},{5,6},{6,7},{7,8},{8,9},{9,10},{10,1... | collective-permute-start | bytes 147464 | tf_op jit(solution)/shard_map/ppermute | solution.py:32
  64.6 6.2 %collective-permute-start.17 = (f32[24,512]{1,0:T(8,128)S(1)}, f32[24,512]{1,0:T(8,128)S(1)}, u32[]{:S(2)}, u32[]{:S(2)}) collective-permute-start(f32[24,512]{1,0:T(8,128)S(1)} %get-tuple-element.95), channel_id=1, source_target_pairs={{0,15},{1,0},{2,1},{3,2},{4,3},{5,4},{6,5},{7,6},{8,7},{9,8},{10,9... | collective-permute-start | bytes 147464 | tf_op jit(solution)/shard_map/ppermute | solution.py:32
  70.8 0.6 copy-start.9
  70.8 0.6 copy-start.10

commit v5 on v4

--- a/solution.py
+++ b/solution.py
@@ -239,6 +239,23 @@
     return stc * _exact_right(bc, rate)
 
 
+def recv_block(recv, side):
+    ref = recv[side]
+    if side in (4, 5):
+        rows = ref.shape[0] // 2
+        top = 0 if side == 4 else rows
+        return ref[top : top + rows, :]
+    return ref[...]
+
+
+def write_sends(out_refs, send):
+    rows = send.shape[0]
+    out_refs[0][...] = send[:, 0:LANE]
+    out_refs[1][...] = send[:, LANE : 2 * LANE]
+    out_refs[2][0:rows, :] = send[:, 5 * LANE : 6 * LANE]
+    out_refs[2][rows : 2 * rows, :] = send[:, 4 * LANE : 5 * LANE]
+
+
 def stage_kernel(coarse, second, project, sends, local, *refs):
     refs = list(refs)
 
@@ -278,7 +295,7 @@
         cnt_r_ref = take()
     out_u = take()
     out_c = take() if (coarse or project) else None
-    out_send = [take() for _ in SEND_FACES] if sends else None
+    out_send = [take() for _ in range(3)] if sends else None
     if last:
         pay_l_ref = take()
         pay_r_ref = take()
@@ -304,7 +321,7 @@
         near = _dot(pl_ref[side], block)
         if side in SEND_FACES:
             k = SEND_FACES.index(side)
-            near = near + _dot(pr_ref[k], recv[side][...])
+            near = near + _dot(pr_ref[k], recv_block(recv, side))
         near_blocks.append(near)
     near = jnp.concatenate(near_blocks, axis=1)
 
@@ -358,9 +375,7 @@
             send = jnp.where(sw_ref[...] > 0.5, send3, send7)
         else:
             send = send7
-        send = send.astype(bf16)
-        for k, side in enumerate(SEND_FACES):
-            out_send[k][...] = send[:, side * LANE : (side + 1) * LANE]
+        write_sends(out_send, send.astype(bf16))
 
 
 def _vmem():
@@ -460,9 +475,7 @@
         out[...] = _dot_t(eye, jnp.where(hit, 1.0, 0.0).astype(bf16)).astype(bf16)
     pre_out[...] = packed_ref[:, 7:8]
     stc_out[...] = _exact_right(fsel_ref[...], packed_ref[...])[:, 8:9]
-    send = _dot(u_ref[...].astype(bf16), g7_ref[...]).astype(bf16)
-    for k, side in enumerate(SEND_FACES):
-        send_refs[k][...] = send[:, side * LANE : (side + 1) * LANE]
+    write_sends(send_refs, _dot(u_ref[...].astype(bf16), g7_ref[...]).astype(bf16))
 
 
 def final_kernel(fields, hold, home_ref, from_l_ref, from_r_ref, hinfo_ref, out_ref):
@@ -583,17 +596,18 @@
     narrow = jnp.asarray(to_bf16(narrow_np))
 
     send_shape = jax.ShapeDtypeStruct((rows, LANE), bf16)
+    sends_shape = [send_shape, send_shape, jax.ShapeDtypeStruct((2 * rows, LANE), bf16)]
     u_shape = jax.ShapeDtypeStruct((rows, P7**3), f32)
     c_shape = jax.ShapeDtypeStruct((rows, P3**3), f32)
 
     def exchange(sends):
-        out = dict(zip(SEND_FACES, sends))
-        return [
-            shifted(out[1], "curve", 1),
-            shifted(out[0], "curve", -1),
-            shifted(out[5], "slab", 1),
-            shifted(out[4], "slab", -1),
-        ]
+        face0, face1, faces_z = sends
+        from_prev = shifted(faces_z, "slab", 1)
+        if lax.axis_size("slab") == 2:
+            from_next = from_prev
+        else:
+            from_next = shifted(faces_z, "slab", -1)
+        return [shifted(face1, "curve", 1), shifted(face0, "curve", -1), from_prev, from_next]
 
     setup_out = [
         jax.ShapeDtypeStruct((3, rows, P7**3), bf16),
@@ -610,7 +624,7 @@
         jax.ShapeDtypeStruct((8, LANE), f32),
         jax.ShapeDtypeStruct((MOVE_CAP * field_count, rows), bf16),
         jax.ShapeDtypeStruct((MOVE_CAP * field_count, rows), bf16),
-    ] + [send_shape] * 4
+    ] + sends_shape
     setup_out = setup_out + [jax.ShapeDtypeStruct(x.shape, x.dtype) for x in (wide, mid, narrow)]
     u0 = state.reshape(rows, P7**3)
     setup_in = [u0, vt, packed, wide, mid, narrow]
@@ -625,21 +639,21 @@
     )(*setup_in)
     v7, m7, v3, m3, p_local, p_remote, pre, stc, sw = res[:9]
     hinfo, cnt_l, cnt_r, sel_l, sel_r = res[9:14]
-    sends = res[14:18]
-    wide, mid, narrow = res[18:21]
+    sends = res[14:17]
+    wide, mid, narrow = res[17:20]
     common = [p_local, p_remote, v7, m7, pre, stc, wide, mid, narrow]
     recv = exchange(sends)
     res = run_stage(
         (False, False, False, True, local_count),
         [u0] + recv + common,
-        [u_shape] + [send_shape] * 4,
+        [u_shape] + sends_shape,
     )
     first, sends = res[0], res[1:]
     recv = exchange(sends)
     res = run_stage(
         (False, True, True, True, local_count),
         [first, u0] + recv + common + [sw],
-        [u_shape, c_shape] + [send_shape] * 4,
+        [u_shape, c_shape] + sends_shape,
     )
     after, coarse, sends = res[0], res[1], res[2:]
     recv = exchange(sends)
@@ -647,7 +661,7 @@
     res = run_stage(
         (True, False, False, True, local_count),
         [after, coarse] + recv + common + mixed_tail,
-        [u_shape, c_shape] + [send_shape] * 4,
+        [u_shape, c_shape] + sends_shape,
     )
     first7, first3, sends = res[0], res[1], res[2:]
     recv = exchange(sends)

time: 74.6 us -> 65.7 us (0.88)
  waiting for transfers between devices: 12.9 us -> 7.48 us
  starting transfers between devices: 31.6 us -> 27.5 us
    ppermute x18 -> x14, waiting for transfers between devices: 12.9 us -> 7.48 us  [shifted(): return lax.ppermute(value, axis, pairs)]
    ppermute x18 -> x14, starting transfers between devices: 31.6 us -> 27.5 us  [shifted(): return lax.ppermute(value, axis, pairs)]
  transfers between devices with their start and end apart: 18 -> 14, of which waited for: 9 -> 6; matrix products, arithmetic and copies ran while one was open for 1% -> 1% of each run, Pallas kernels for 0% -> 0%
where the time goes in v5:
time: 65.7 us; the launch traced here: 65.3 us
  starting transfers between devices  27.5 us (42%)
  Pallas kernels  17.6 us (27%)
  local copies, waits for them, and re-layouts  10.5 us (16%)
  waiting for transfers between devices  7.48 us (11%)
  other arithmetic  1.33 us (2%)
  between operations  0.81 us (1%)
    ppermute x14, starting transfers between devices, shifted(): return lax.ppermute(value, axis, pairs)  27.5 us
    pallas_call x4, Pallas kernels, run_stage(): pl.pallas_call(kernel, out_shape=out_shapes, in_specs=[_vmem() for _ in i...  12.2 us
    unnamed x23, local copies, waits for them, and re-layouts  8.1 us
    ppermute x14, waiting for transfers between devices, shifted(): return lax.ppermute(value, axis, pairs)  7.48 us
    pallas_call x1, Pallas kernels, per_device(): pl.pallas_call(functools.partial(final_kernel, field_count, HOLD7), out_s...  2.73 us
    pallas_call x1, Pallas kernels, per_device(): pl.pallas_call(functools.partial(setup_entry, local_count, field_count, l...  2.67 us
  transfers between devices with their start and end apart: 14, of which 6 were waited for; matrix products, arithmetic and copies ran while one was open for 1% of the time, Pallas kernels for 0%

profile of v5, /device:TPU:0, one launch (start us, length us, event | category | flops | bytes accessed | tf_op | source)
XLA Modules:
  0.0 65.3 jit_solution(18165238865416990306)
XLA Ops:
  0.7 0.7 %convert_bitcast_fusion.1 = f32[16,1]{0,1:T(1,128)S(1)} fusion(s32[16]{0:T(128)} %param.17), kind=kLoop, calls=%fused_computation.9 | loop fusion | flops 16 | bytes 128 | tf_op jit(solution)/shard_map/broadcast_in_dim | solution.py:553
  1.3 0.7 %convert_bitcast_fusion = f32[16,1]{0,1:T(1,128)S(1)} fusion(s32[16]{0:T(128)} %param.18), kind=kLoop, calls=%fused_computation.8 | loop fusion | flops 16 | bytes 128 | tf_op jit(solution)/shard_map/broadcast_in_dim | solution.py:556
  2.0 0.7 %copy.26 = f32[8,1]{1,0:T(8,128)S(1)} copy(f32[8,1]{0,1:T(1,128)} %bitcast.14) | data formatting | bytes 64 | tf_op jit(solution)/shard_map/broadcast_in_dim | solution.py:555
  2.9 0.7 %copy.28 = f32[16,1]{1,0:T(8,128)S(1)} copy(f32[16,1]{0,1:T(1,128)} %bitcast.15) | data formatting | bytes 128 | tf_op jit(solution)/shard_map/broadcast_in_dim | solution.py:554
  3.6 0.8 %copy.25 = s32[16,6]{1,0:T(8,128)S(1)} copy(s32[16,6]{0,1:T(8,128)} %param.16) | data formatting | bytes 768 | tf_op args[4]
  4.5 0.9 %copy-done.1 = f32[16,8,512]{2,1,0:T(8,128)S(1)} copy-done((f32[16,8,512]{2,1,0:T(8,128)S(1)}, f32[16,8,512]{2,1,0:T(8,128)}, u32[]{:S(2)}) %copy-start.1) | copy-done | bytes 262168
  5.5 1.5 %copy-done.3 = bf16[1792,512]{1,0:T(8,128)(2,1)S(1)} copy-done((bf16[1792,512]{1,0:T(8,128)(2,1)S(1)}, bf16[1792,512]{1,0:T(8,128)(2,1)}, u32[]{:S(2)}) %copy-start.3) | copy-done | bytes 1835032
  7.0 1.3 %copy-done.4 = bf16[896,768]{1,0:T(8,128)(2,1)S(1)} copy-done((bf16[896,768]{1,0:T(8,128)(2,1)S(1)}, bf16[896,768]{1,0:T(8,128)(2,1)}, u32[]{:S(2)}) %copy-start.4) | copy-done | bytes 1376280
  8.3 0.9 %copy-done.6 = bf16[496,128]{1,0:T(8,128)(2,1)S(1)} copy-done((bf16[496,128]{1,0:T(8,128)(2,1)S(1)}, bf16[496,128]{1,0:T(8,128)(2,1)}, u32[]{:S(2)}) %copy-start.6) | copy-done | bytes 127000
  9.2 0.7 %copy-done.8 = bf16[3,64,16]{1,2,0:T(8,128)(2,1)S(1)} copy-done((bf16[3,64,16]{1,2,0:T(8,128)(2,1)S(1)}, bf16[3,64,16]{1,2,0:T(8,128)(2,1)}, u32[]{:S(2)}) %copy-start.8) | copy-done | bytes 6168
  9.9 2.7 %shard_map.113 = (bf16[3,128,512]{2,1,0:T(8,128)(2,1)S(1)}, f32[128,768]{1,0:T(8,128)S(1)}, f32[3,128,64]{2,1,0:T(8,128)S(1)}, f32[128,768]{1,0:T(8,128)S(1)}, b...) custom-call(f32[128,512]{1,0:T(8,128)S(1)} %bitcast.9, ...), custom_call_target="tpu_custom_call" | custom-call | tf_op jit(solution)/shard_map/pallas_call | solution.py:631
  12.6 0.6 copy-done.7
  13.3 3.0 %collective-permute-start.2 = (bf16[256,128]{1,0:T(8,128)(2,1)S(1)}, bf16[256,128]{1,0:T(8,128)(2,1)S(1)}, u32[]{:S(2)}, u32[]{:S(2)}) collective-permute-start(bf16[256,128]{1,0:T(8,128)(2,1)S(1)} %get-tuple-element.54), channel_id=1, source_target_pairs={{0,16},{16,0},{1,17},{17,1},{2,18},{18,2},{3,19},{19,3},{4,20},{20... | collective-permute-start | bytes 196616 | tf_op jit(solution)/shard_map/ppermute | solution.py:32
  16.2 4.4 %collective-permute-start.1 = (bf16[128,128]{1,0:T(8,128)(2,1)S(1)}, bf16[128,128]{1,0:T(8,128)(2,1)S(1)}, u32[]{:S(2)}, u32[]{:S(2)}) collective-permute-start(bf16[128,128]{1,0:T(8,128)(2,1)S(1)} %get-tuple-element.53), channel_id=1, source_target_pairs={{0,15},{1,0},{2,1},{3,2},{4,3},{5,4},{6,5},{7,6},{8,7},{9,8},{10,9... | collective-permute-start | bytes 98312 | tf_op jit(solution)/shard_map/ppermute | solution.py:32
  20.7 1.6 %collective-permute-done.refs_1_ = bf16[128,128]{1,0:T(8,128)(2,1)S(1)} collective-permute-done((bf16[128,128]{1,0:T(8,128)(2,1)S(1)}, bf16[128,128]{1,0:T(8,128)(2,1)S(1)}, u32[]{:S(2)}, u32[]{:S(2)}) %collective-permute-start) | collective-permute-done | bytes 32800 | tf_op jit(solution)/shard_map/ppermute | solution.py:32
  22.3 1.9 %shard_map.114 = (f32[128,512]{1,0:T(8,128)S(1)}, bf16[128,128]{1,0:T(8,128)(2,1)S(1)}, bf16[128,128]{1,0:T(8,128)(2,1)S(1)}, bf16[256,128]{1,0:T(8,128)(2,1)S(1)}) custom-call(f32[128,512]{1,0:T(8,128)S(1)} %bitcast.10, bf16[128,128]{1,0:T(8,128)(2,1)S(1)} %collective-permute-done.refs_1_, bf16[128,128]{1,0:T(8,128)(2,1)S(1)} %collective-permute-done.1.refs_2_, ...), custom_call_target="tpu_custom_call" | custom-call | tf_op jit(solution)/shard_map/pallas_call | solution.py:388
  24.4 4.5 %collective-permute-start.4 = (bf16[128,128]{1,0:T(8,128)(2,1)S(1)}, bf16[128,128]{1,0:T(8,128)(2,1)S(1)}, u32[]{:S(2)}, u32[]{:S(2)}) collective-permute-start(bf16[128,128]{1,0:T(8,128)(2,1)S(1)} %get-tuple-element.66), channel_id=1, source_target_pairs={{0,15},{1,0},{2,1},{3,2},{4,3},{5,4},{6,5},{7,6},{8,7},{9,8},{10,9... | collective-permute-start | bytes 98312 | tf_op jit(solution)/shard_map/ppermute | solution.py:32
  28.8 1.5 %collective-permute-done.3.refs_2_ = bf16[128,128]{1,0:T(8,128)(2,1)S(1)} collective-permute-done((bf16[128,128]{1,0:T(8,128)(2,1)S(1)}, bf16[128,128]{1,0:T(8,128)(2,1)S(1)}, u32[]{:S(2)}, u32[]{:S(2)}) %collective-permute-start.3) | collective-permute-done | bytes 32800 | tf_op jit(solution)/shard_map/ppermute | solution.py:32
  30.4 2.8 %shard_map.115 = (f32[128,512]{1,0:T(8,128)S(1)}, f32[128,64]{1,0:T(8,128)S(1)}, bf16[128,128]{1,0:T(8,128)(2,1)S(1)}, bf16[128,128]{1,0:T(8,128)(2,1)S(1)}, bf16[256,128]{1,0:T(8,128)(2,1)S(1)}) custom-call(f32[128,512]{1,0:T(8,128)S(1)} %get-tuple-element.64.refs_0_, f32[128,512]{1,0:T(8,128)S(1)} %bitcast.11, ...), custom_call_target="tpu_custom_call" | custom-call | tf_op jit(solution)/shard_map/pallas_call | solution.py:388
  33.3 2.0 %collective-permute-start.8 = (bf16[256,128]{1,0:T(8,128)(2,1)S(1)}, bf16[256,128]{1,0:T(8,128)(2,1)S(1)}, u32[]{:S(2)}, u32[]{:S(2)}) collective-permute-start(bf16[256,128]{1,0:T(8,128)(2,1)S(1)} %get-tuple-element.73), channel_id=1, source_target_pairs={{0,16},{16,0},{1,17},{17,1},{2,18},{18,2},{3,19},{19,3},{4,20},{20... | collective-permute-start | bytes 196616 | tf_op jit(solution)/shard_map/ppermute | solution.py:32
  35.3 4.4 %collective-permute-start.7 = (bf16[128,128]{1,0:T(8,128)(2,1)S(1)}, bf16[128,128]{1,0:T(8,128)(2,1)S(1)}, u32[]{:S(2)}, u32[]{:S(2)}) collective-permute-start(bf16[128,128]{1,0:T(8,128)(2,1)S(1)} %get-tuple-element.72), channel_id=1, source_target_pairs={{0,15},{1,0},{2,1},{3,2},{4,3},{5,4},{6,5},{7,6},{8,7},{9,8},{10,9... | collective-permute-start | bytes 98312 | tf_op jit(solution)/shard_map/ppermute | solution.py:32
  39.7 1.6 %collective-permute-done.6.refs_2_ = bf16[128,128]{1,0:T(8,128)(2,1)S(1)} collective-permute-done((bf16[128,128]{1,0:T(8,128)(2,1)S(1)}, bf16[128,128]{1,0:T(8,128)(2,1)S(1)}, u32[]{:S(2)}, u32[]{:S(2)}) %collective-permute-start.6) | collective-permute-done | bytes 32800 | tf_op jit(solution)/shard_map/ppermute | solution.py:32
  41.3 3.4 %shard_map.116 = (f32[128,512]{1,0:T(8,128)S(1)}, f32[128,64]{1,0:T(8,128)S(1)}, bf16[128,128]{1,0:T(8,128)(2,1)S(1)}, bf16[128,128]{1,0:T(8,128)(2,1)S(1)}, bf16[256,128]{1,0:T(8,128)(2,1)S(1)}) custom-call(f32[128,512]{1,0:T(8,128)S(1)} %get-tuple-element.69.refs_0_.refs_2_, f32[128,64]{1,0:T(8,128)S(1)} %get-tuple-element.70.refs_1_.refs_3_, ...), custom_call_target="tpu_custom_call" | custom-call | tf_op jit(solution)/shard_map/pallas_call | solution.py:388
  44.9 4.4 %collective-permute-start.10 = (bf16[128,128]{1,0:T(8,128)(2,1)S(1)}, bf16[128,128]{1,0:T(8,128)(2,1)S(1)}, u32[]{:S(2)}, u32[]{:S(2)}) collective-permute-start(bf16[128,128]{1,0:T(8,128)(2,1)S(1)} %get-tuple-element.79), channel_id=1, source_target_pairs={{0,15},{1,0},{2,1},{3,2},{4,3},{5,4},{6,5},{7,6},{8,7},{9,8},{10,9... | collective-permute-start | bytes 98312 | tf_op jit(solution)/shard_map/ppermute | solution.py:32
  49.3 1.6 %collective-permute-done.9.refs_4_ = bf16[128,128]{1,0:T(8,128)(2,1)S(1)} collective-permute-done((bf16[128,128]{1,0:T(8,128)(2,1)S(1)}, bf16[128,128]{1,0:T(8,128)(2,1)S(1)}, u32[]{:S(2)}, u32[]{:S(2)}) %collective-permute-start.9) | collective-permute-done | bytes 32800 | tf_op jit(solution)/shard_map/ppermute | solution.py:32
  50.9 4.1 %shard_map.117 = (f32[128,512]{1,0:T(8,128)S(1)}, f32[128,64]{1,0:T(8,128)S(1)}, f32[24,512]{1,0:T(8,128)S(1)}, f32[24,512]{1,0:T(8,128)S(1)}) custom-call(f32[128,512]{1,0:T(8,128)S(1)} %get-tuple-element.76.refs_0_, f32[128,64]{1,0:T(8,128)S(1)} %get-tuple-element.77.refs_1_, f32[128,512]{1,0:T(8,128)S(1)} %get-tuple-element.69.refs_0_.refs_2_, ...), custom_call_target="tpu_custom_call" | custom-call | tf_op jit(solution)/shard_map/pallas_call | solution.py:388
  55.0 0.7 %copy-done.5 = f32[128,512]{1,0:T(8,128)} copy-done((f32[128,512]{1,0:T(8,128)}, f32[128,512]{1,0:T(8,128)S(1)}, u32[]{:S(2)}) %copy-start.5) | copy-done | bytes 262168
  55.7 4.4 %collective-permute-start.13 = (f32[24,512]{1,0:T(8,128)S(1)}, f32[24,512]{1,0:T(8,128)S(1)}, u32[]{:S(2)}, u32[]{:S(2)}) collective-permute-start(f32[24,512]{1,0:T(8,128)S(1)} %get-tuple-element.87), channel_id=1, source_target_pairs={{0,15},{1,0},{2,1},{3,2},{4,3},{5,4},{6,5},{7,6},{8,7},{9,8},{10,9... | collective-permute-start | bytes 147464 | tf_op jit(solution)/shard_map/ppermute | solution.py:32
  60.2 0.7 %reshape.40 = f32[16,512]{1,0:T(8,128)} reshape(f32[128,64]{1,0:T(8,128)S(1)} %get-tuple-element.89) | data formatting | bytes 65536 | tf_op jit(solution)/shard_map/reshape | solution.py:684
  60.9 1.1 %collective-permute-done.12.from_l_ref = f32[24,512]{1,0:T(8,128)S(1)} collective-permute-done((f32[24,512]{1,0:T(8,128)S(1)}, f32[24,512]{1,0:T(8,128)S(1)}, u32[]{:S(2)}, u32[]{:S(2)}) %collective-permute-start.12) | collective-permute-done | bytes 49184 | tf_op jit(solution)/shard_map/ppermute | solution.py:32
  61.9 0.6 copy-done.9
  62.6 2.7 %shard_map.118 = f32[96,512]{1,0:T(8,128)} custom-call(f32[128,512]{1,0:T(8,128)} %copy-done.5, f32[24,512]{1,0:T(8,128)} %copy-done.9, f32[24,512]{1,0:T(8,128)} %copy-done.10, f32[128,128]{1,0:T(8,128)} %copy-done.7), custom_call_target="tpu_custom_call" | custom-call | tf_op jit(solution)/shard_map/pallas_call | solution.py:677
  (40 shorter events, 0.7 us)
Async XLA Ops:
  4.5 1.0 %copy-start.1 = (f32[16,8,512]{2,1,0:T(8,128)S(1)}, f32[16,8,512]{2,1,0:T(8,128)}, u32[]{:S(2)}) copy-start(f32[16,8,512]{2,1,0:T(8,128)} %param.12) | copy-start | bytes 786436
  5.5 1.5 %copy-start.3 = (bf16[1792,512]{1,0:T(8,128)(2,1)S(1)}, bf16[1792,512]{1,0:T(8,128)(2,1)}, u32[]{:S(2)}) copy-start(bf16[1792,512]{1,0:T(8,128)(2,1)} %constant.80.clone.refs_4_) | copy-start | bytes 5505028
  7.0 1.3 %copy-start.4 = (bf16[896,768]{1,0:T(8,128)(2,1)S(1)}, bf16[896,768]{1,0:T(8,128)(2,1)}, u32[]{:S(2)}) copy-start(bf16[896,768]{1,0:T(8,128)(2,1)} %constant.79.clone.refs_3_) | copy-start | bytes 4128772
  8.3 0.9 %copy-start.6 = (bf16[496,128]{1,0:T(8,128)(2,1)S(1)}, bf16[496,128]{1,0:T(8,128)(2,1)}, u32[]{:S(2)}) copy-start(bf16[496,128]{1,0:T(8,128)(2,1)} %constant.81.clone.refs_5_) | copy-start | bytes 380932
  9.2 0.7 %copy-start.8 = (bf16[3,64,16]{1,2,0:T(8,128)(2,1)S(1)}, bf16[3,64,16]{1,2,0:T(8,128)(2,1)}, u32[]{:S(2)}) copy-start(bf16[3,64,16]{1,2,0:T(8,128)(2,1)} %param.13) | copy-start | bytes 18436
  9.9 12.3 %copy-start.2 = (f32[16,8,512]{2,1,0:T(8,128)S(1)}, f32[16,8,512]{2,1,0:T(8,128)}, u32[]{:S(2)}) copy-start(f32[16,8,512]{2,1,0:T(8,128)} %param.12) | copy-start | bytes 786436
  12.6 0.6 copy-start.7
  13.3 28.1 %copy-start = (bf16[1792,512]{1,0:T(8,128)(2,1)}, bf16[1792,512]{1,0:T(8,128)(2,1)S(1)}, u32[]{:S(2)}) copy-start(bf16[1792,512]{1,0:T(8,128)(2,1)S(1)} %get-tuple-element.62.refs_12_.refs_13_.refs_15_) | copy-start | bytes 5505028
  13.3 9.0 %collective-permute-start.2 = (bf16[256,128]{1,0:T(8,128)(2,1)S(1)}, bf16[256,128]{1,0:T(8,128)(2,1)S(1)}, u32[]{:S(2)}, u32[]{:S(2)}) collective-permute-start(bf16[256,128]{1,0:T(8,128)(2,1)S(1)} %get-tuple-element.54), channel_id=1, source_target_pairs={{0,16},{16,0},{1,17},{17,1},{2,18},{18,2},{3,19},{19,3},{4,20},{20... | collective-permute-start | bytes 196616 | tf_op jit(solution)/shard_map/ppermute | solution.py:32
  16.2 6.0 %collective-permute-start = (bf16[128,128]{1,0:T(8,128)(2,1)S(1)}, bf16[128,128]{1,0:T(8,128)(2,1)S(1)}, u32[]{:S(2)}, u32[]{:S(2)}) collective-permute-start(bf16[128,128]{1,0:T(8,128)(2,1)S(1)} %get-tuple-element.52), channel_id=1, source_target_pairs={{0,1},{1,2},{2,3},{3,4},{4,5},{5,6},{6,7},{7,8},{8,9},{9,10},{10,1... | collective-permute-start | bytes 98312 | tf_op jit(solution)/shard_map/ppermute | solution.py:32
  16.2 6.0 %collective-permute-start.1 = (bf16[128,128]{1,0:T(8,128)(2,1)S(1)}, bf16[128,128]{1,0:T(8,128)(2,1)S(1)}, u32[]{:S(2)}, u32[]{:S(2)}) collective-permute-start(bf16[128,128]{1,0:T(8,128)(2,1)S(1)} %get-tuple-element.53), channel_id=1, source_target_pairs={{0,15},{1,0},{2,1},{3,2},{4,3},{5,4},{6,5},{7,6},{8,7},{9,8},{10,9... | collective-permute-start | bytes 98312 | tf_op jit(solution)/shard_map/ppermute | solution.py:32
  24.2 6.2 %collective-permute-start.5 = (bf16[256,128]{1,0:T(8,128)(2,1)S(1)}, bf16[256,128]{1,0:T(8,128)(2,1)S(1)}, u32[]{:S(2)}, u32[]{:S(2)}) collective-permute-start(bf16[256,128]{1,0:T(8,128)(2,1)S(1)} %get-tuple-element.67), channel_id=1, source_target_pairs={{0,16},{16,0},{1,17},{17,1},{2,18},{18,2},{3,19},{19,3},{4,20},{20... | collective-permute-start | bytes 196616 | tf_op jit(solution)/shard_map/ppermute | solution.py:32
  24.3 6.1 %collective-permute-start.3 = (bf16[128,128]{1,0:T(8,128)(2,1)S(1)}, bf16[128,128]{1,0:T(8,128)(2,1)S(1)}, u32[]{:S(2)}, u32[]{:S(2)}) collective-permute-start(bf16[128,128]{1,0:T(8,128)(2,1)S(1)} %get-tuple-element.65), channel_id=1, source_target_pairs={{0,1},{1,2},{2,3},{3,4},{4,5},{5,6},{6,7},{7,8},{8,9},{9,10},{10,1... | collective-permute-start | bytes 98312 | tf_op jit(solution)/shard_map/ppermute | solution.py:32
  24.4 6.1 %collective-permute-start.4 = (bf16[128,128]{1,0:T(8,128)(2,1)S(1)}, bf16[128,128]{1,0:T(8,128)(2,1)S(1)}, u32[]{:S(2)}, u32[]{:S(2)}) collective-permute-start(bf16[128,128]{1,0:T(8,128)(2,1)S(1)} %get-tuple-element.66), channel_id=1, source_target_pairs={{0,15},{1,0},{2,1},{3,2},{4,3},{5,4},{6,5},{7,6},{8,7},{9,8},{10,9... | collective-permute-start | bytes 98312 | tf_op jit(solution)/shard_map/ppermute | solution.py:32
  33.3 8.0 %collective-permute-start.8 = (bf16[256,128]{1,0:T(8,128)(2,1)S(1)}, bf16[256,128]{1,0:T(8,128)(2,1)S(1)}, u32[]{:S(2)}, u32[]{:S(2)}) collective-permute-start(bf16[256,128]{1,0:T(8,128)(2,1)S(1)} %get-tuple-element.73), channel_id=1, source_target_pairs={{0,16},{16,0},{1,17},{17,1},{2,18},{18,2},{3,19},{19,3},{4,20},{20... | collective-permute-start | bytes 196616 | tf_op jit(solution)/shard_map/ppermute | solution.py:32
  35.3 6.0 %collective-permute-start.6 = (bf16[128,128]{1,0:T(8,128)(2,1)S(1)}, bf16[128,128]{1,0:T(8,128)(2,1)S(1)}, u32[]{:S(2)}, u32[]{:S(2)}) collective-permute-start(bf16[128,128]{1,0:T(8,128)(2,1)S(1)} %get-tuple-element.71), channel_id=1, source_target_pairs={{0,1},{1,2},{2,3},{3,4},{4,5},{5,6},{6,7},{7,8},{8,9},{9,10},{10,1... | collective-permute-start | bytes 98312 | tf_op jit(solution)/shard_map/ppermute | solution.py:32
  35.3 6.0 %collective-permute-start.7 = (bf16[128,128]{1,0:T(8,128)(2,1)S(1)}, bf16[128,128]{1,0:T(8,128)(2,1)S(1)}, u32[]{:S(2)}, u32[]{:S(2)}) collective-permute-start(bf16[128,128]{1,0:T(8,128)(2,1)S(1)} %get-tuple-element.72), channel_id=1, source_target_pairs={{0,15},{1,0},{2,1},{3,2},{4,3},{5,4},{6,5},{7,6},{8,7},{9,8},{10,9... | collective-permute-start | bytes 98312 | tf_op jit(solution)/shard_map/ppermute | solution.py:32
  44.7 6.2 %collective-permute-start.11 = (bf16[256,128]{1,0:T(8,128)(2,1)S(1)}, bf16[256,128]{1,0:T(8,128)(2,1)S(1)}, u32[]{:S(2)}, u32[]{:S(2)}) collective-permute-start(bf16[256,128]{1,0:T(8,128)(2,1)S(1)} %get-tuple-element.80), channel_id=1, source_target_pairs={{0,16},{16,0},{1,17},{17,1},{2,18},{18,2},{3,19},{19,3},{4,20},{20... | collective-permute-start | bytes 196616 | tf_op jit(solution)/shard_map/ppermute | solution.py:32
  44.9 6.0 %collective-permute-start.9 = (bf16[128,128]{1,0:T(8,128)(2,1)S(1)}, bf16[128,128]{1,0:T(8,128)(2,1)S(1)}, u32[]{:S(2)}, u32[]{:S(2)}) collective-permute-start(bf16[128,128]{1,0:T(8,128)(2,1)S(1)} %get-tuple-element.78), channel_id=1, source_target_pairs={{0,1},{1,2},{2,3},{3,4},{4,5},{5,6},{6,7},{7,8},{8,9},{9,10},{10,1... | collective-permute-start | bytes 98312 | tf_op jit(solution)/shard_map/ppermute | solution.py:32
  44.9 6.0 %collective-permute-start.10 = (bf16[128,128]{1,0:T(8,128)(2,1)S(1)}, bf16[128,128]{1,0:T(8,128)(2,1)S(1)}, u32[]{:S(2)}, u32[]{:S(2)}) collective-permute-start(bf16[128,128]{1,0:T(8,128)(2,1)S(1)} %get-tuple-element.79), channel_id=1, source_target_pairs={{0,15},{1,0},{2,1},{3,2},{4,3},{5,4},{6,5},{7,6},{8,7},{9,8},{10,9... | collective-permute-start | bytes 98312 | tf_op jit(solution)/shard_map/ppermute | solution.py:32
  55.0 0.7 %copy-start.5 = (f32[128,512]{1,0:T(8,128)}, f32[128,512]{1,0:T(8,128)S(1)}, u32[]{:S(2)}) copy-start(f32[128,512]{1,0:T(8,128)S(1)} %get-tuple-element.85.home_ref) | copy-start | bytes 786436
  55.7 6.2 %collective-permute-start.12 = (f32[24,512]{1,0:T(8,128)S(1)}, f32[24,512]{1,0:T(8,128)S(1)}, u32[]{:S(2)}, u32[]{:S(2)}) collective-permute-start(f32[24,512]{1,0:T(8,128)S(1)} %get-tuple-element.86), channel_id=1, source_target_pairs={{0,1},{1,2},{2,3},{3,4},{4,5},{5,6},{6,7},{7,8},{8,9},{9,10},{10,1... | collective-permute-start | bytes 147464 | tf_op jit(solution)/shard_map/ppermute | solution.py:32
  55.7 6.2 %collective-permute-start.13 = (f32[24,512]{1,0:T(8,128)S(1)}, f32[24,512]{1,0:T(8,128)S(1)}, u32[]{:S(2)}, u32[]{:S(2)}) collective-permute-start(f32[24,512]{1,0:T(8,128)S(1)} %get-tuple-element.87), channel_id=1, source_target_pairs={{0,15},{1,0},{2,1},{3,2},{4,3},{5,4},{6,5},{7,6},{8,7},{9,8},{10,9... | collective-permute-start | bytes 147464 | tf_op jit(solution)/shard_map/ppermute | solution.py:32
  61.9 0.6 copy-start.9
  61.9 0.6 copy-start.10

commit v6 on v5

--- a/solution.py
+++ b/solution.py
@@ -293,6 +293,8 @@
         sel_r_ref = take()
         cnt_l_ref = take()
         cnt_r_ref = take()
+    res7_ref = take()
+    res3_ref = take() if coarse else None
     out_u = take()
     out_c = take() if (coarse or project) else None
     out_send = [take() for _ in range(3)] if sends else None
@@ -325,22 +327,12 @@
         near_blocks.append(near)
     near = jnp.concatenate(near_blocks, axis=1)
 
-    divergence = None
-    for d in range(3):
-        flux = (v7_ref[d].astype(f32) * u).astype(bf16)
-        term = _dot(flux, d7_ref[d])
-        divergence = term if divergence is None else divergence + term
-    result = _rate_source(u, pre, stc, bcast, sel, local) - divergence
+    result = res7_ref[...]
     jump = (P7 * (P7 - 1) / 2.0) * (m7_ref[...] * (trace7 - near))
     rate7 = result + _exact_left_t(jump, g7_ref[...])
 
     if coarse:
-        div3 = None
-        for d in range(3):
-            flux3 = (v3_ref[d] * c).astype(bf16)
-            term = _dot(flux3, d3_ref[d])
-            div3 = term if div3 is None else div3 + term
-        result3 = _rate_source(c, pre, stc, bcast, sel, local) - div3
+        result3 = res3_ref[...]
         jump3 = m3_ref[...] * (trace3 - near)
         rate3 = result3 + (P3 * (P3 - 1) / 2.0) * _full_t(jump3, mds_ref)
 
@@ -380,6 +372,46 @@
 
 def _vmem():
     return pl.BlockSpec(memory_space=pltpu.VMEM)
+
+
+def bulk_kernel(coarse, local, *refs):
+    refs = list(refs)
+    u_ref = refs.pop(0)
+    c_ref = refs.pop(0) if coarse else None
+    v7_ref, pre_ref, stc_ref = refs.pop(0), refs.pop(0), refs.pop(0)
+    views = table_views(refs.pop(0), refs.pop(0), refs.pop(0), local)
+    v3_ref = refs.pop(0) if coarse else None
+    out7 = refs.pop(0)
+    out3 = refs.pop(0) if coarse else None
+    pre = pre_ref[...]
+    stc = stc_ref[...]
+    bcast = views["bcast"][...]
+    sel = views["sel"][...]
+    u = u_ref[...]
+    divergence = None
+    for d in range(3):
+        flux = (v7_ref[d].astype(f32) * u).astype(bf16)
+        term = _dot(flux, views["d7t"][d])
+        divergence = term if divergence is None else divergence + term
+    out7[...] = _rate_source(u, pre, stc, bcast, sel, local) - divergence
+    if coarse:
+        c = c_ref[...]
+        div3 = None
+        for d in range(3):
+            flux3 = (v3_ref[d] * c).astype(bf16)
+            term = _dot(flux3, views["d3t"][d])
+            div3 = term if div3 is None else div3 + term
+        out3[...] = _rate_source(c, pre, stc, bcast, sel, local) - div3
+
+
+def run_bulk(coarse, local, inputs, out_shapes):
+    return pl.pallas_call(
+        functools.partial(bulk_kernel, coarse, local),
+        out_shape=out_shapes,
+        in_specs=[_vmem() for _ in inputs],
+        out_specs=[_vmem() for _ in out_shapes],
+        compiler_params=pltpu.CompilerParams(vmem_limit_bytes=24 * 1024 * 1024),
+    )(*inputs)
 
 
 def run_stage(flags, inputs, out_shapes):
@@ -643,32 +675,38 @@
     wide, mid, narrow = res[17:20]
     common = [p_local, p_remote, v7, m7, pre, stc, wide, mid, narrow]
     recv = exchange(sends)
+    bulk_tabs = [v7, pre, stc, wide, mid, narrow]
+    (bulk7,) = run_bulk(False, local_count, [u0] + bulk_tabs, [u_shape])
     res = run_stage(
         (False, False, False, True, local_count),
-        [u0] + recv + common,
+        [u0] + recv + common + [bulk7],
         [u_shape] + sends_shape,
     )
     first, sends = res[0], res[1:]
     recv = exchange(sends)
+    (bulk7,) = run_bulk(False, local_count, [first] + bulk_tabs, [u_shape])
     res = run_stage(
         (False, True, True, True, local_count),
-        [first, u0] + recv + common + [sw],
+        [first, u0] + recv + common + [sw, bulk7],
         [u_shape, c_shape] + sends_shape,
     )
     after, coarse, sends = res[0], res[1], res[2:]
     recv = exchange(sends)
     mixed_tail = [v3, m3, sw]
+    bulk7, bulk3 = run_bulk(True, local_count, [after, coarse] + bulk_tabs + [v3], [u_shape, c_shape])
     res = run_stage(
         (True, False, False, True, local_count),
-        [after, coarse] + recv + common + mixed_tail,
+        [after, coarse] + recv + common + mixed_tail + [bulk7, bulk3],
         [u_shape, c_shape] + sends_shape,
     )
     first7, first3, sends = res[0], res[1], res[2:]
     recv = exchange(sends)
     pay_shape = jax.ShapeDtypeStruct((MOVE_CAP * field_count + 8, P7**3), f32)
+    bulk7, bulk3 = run_bulk(True, local_count, [first7, first3] + bulk_tabs + [v3], [u_shape, c_shape])
     res = run_stage(
         (True, True, False, False, local_count),
-        [first7, first3, after, coarse] + recv + common + mixed_tail + [sel_l, sel_r, cnt_l, cnt_r],
+        [first7, first3, after, coarse] + recv + common + mixed_tail
+        + [sel_l, sel_r, cnt_l, cnt_r, bulk7, bulk3],
         [u_shape, c_shape, pay_shape, pay_shape],
     )
     final7, final3, pay_l, pay_r = res

time: 65.7 us -> 65.2 us (level)
  waiting for transfers between devices: 7.48 us -> 4.16 us
  Pallas kernels: 17.6 us -> 20.4 us
    ppermute x14, waiting for transfers between devices: 7.48 us -> 4.16 us  [shifted(): return lax.ppermute(value, axis, pairs)]
    pallas_call x0 -> x4, Pallas kernels: none -> 3.28 us  [run_bulk(): pl.pallas_call(functools.partial(bulk_kernel, coarse, local), out_shape=o...]
    unnamed x23 -> x25, local copies, waits for them, and re-layouts: 8.1 us -> 8.09 us
  transfers between devices with their start and end apart: 14 -> 14, of which waited for: 6 -> 6; matrix products, arithmetic and copies ran while one was open for 1% -> 1% of each run, Pallas kernels for 0% -> 5%
where the time goes in v6:
time: 65.2 us; the launch traced here: 64.8 us
  starting transfers between devices  27.5 us (42%)
  Pallas kernels  20.4 us (31%)
  local copies, waits for them, and re-layouts  10.5 us (16%)
  waiting for transfers between devices  4.16 us (6%)
  other arithmetic  1.33 us (2%)
  between operations  0.84 us (1%)
    ppermute x14, starting transfers between devices, shifted(): return lax.ppermute(value, axis, pairs)  27.5 us
    pallas_call x4, Pallas kernels, run_stage(): pl.pallas_call(kernel, out_shape=out_shapes, in_specs=[_vmem() for _ in i...  11.7 us
    unnamed x25, local copies, waits for them, and re-layouts  8.09 us
    ppermute x14, waiting for transfers between devices, shifted(): return lax.ppermute(value, axis, pairs)  4.16 us
    pallas_call x4, Pallas kernels, run_bulk(): pl.pallas_call(functools.partial(bulk_kernel, coarse, local), out_shape=o...  3.28 us
    pallas_call x1, Pallas kernels, per_device(): pl.pallas_call(functools.partial(final_kernel, field_count, HOLD7), out_s...  2.73 us
    pallas_call x1, Pallas kernels, per_device(): pl.pallas_call(functools.partial(setup_entry, local_count, field_count, l...  2.67 us
  transfers between devices with their start and end apart: 14, of which 6 were waited for; matrix products, arithmetic and copies ran while one was open for 1% of the time, Pallas kernels for 5%

profile of v6, /device:TPU:0, one launch (start us, length us, event | category | flops | bytes accessed | tf_op | source)
XLA Modules:
  0.0 64.8 jit_solution(5681113077333791495)
XLA Ops:
  0.7 0.7 %convert_bitcast_fusion.1 = f32[16,1]{0,1:T(1,128)S(1)} fusion(s32[16]{0:T(128)} %param.17), kind=kLoop, calls=%fused_computation.9 | loop fusion | flops 16 | bytes 128 | tf_op jit(solution)/shard_map/broadcast_in_dim | solution.py:585
  2.0 0.7 %copy.26 = f32[8,1]{1,0:T(8,128)S(1)} copy(f32[8,1]{0,1:T(1,128)} %bitcast.15) | data formatting | bytes 64 | tf_op jit(solution)/shard_map/broadcast_in_dim | solution.py:587
  2.9 0.7 %copy.28 = f32[16,1]{1,0:T(8,128)S(1)} copy(f32[16,1]{0,1:T(1,128)} %bitcast.16) | data formatting | bytes 128 | tf_op jit(solution)/shard_map/broadcast_in_dim | solution.py:586
  3.6 0.8 %copy.25 = s32[16,6]{1,0:T(8,128)S(1)} copy(s32[16,6]{0,1:T(8,128)} %param.16) | data formatting | bytes 768 | tf_op args[4]
  4.5 0.9 %copy-done.2 = f32[16,8,512]{2,1,0:T(8,128)S(1)} copy-done((f32[16,8,512]{2,1,0:T(8,128)S(1)}, f32[16,8,512]{2,1,0:T(8,128)}, u32[]{:S(2)}) %copy-start.2) | copy-done | bytes 262168
  5.5 1.5 %copy-done.4 = bf16[1792,512]{1,0:T(8,128)(2,1)S(1)} copy-done((bf16[1792,512]{1,0:T(8,128)(2,1)S(1)}, bf16[1792,512]{1,0:T(8,128)(2,1)}, u32[]{:S(2)}) %copy-start.4) | copy-done | bytes 1835032
  7.0 1.3 %copy-done.5 = bf16[896,768]{1,0:T(8,128)(2,1)S(1)} copy-done((bf16[896,768]{1,0:T(8,128)(2,1)S(1)}, bf16[896,768]{1,0:T(8,128)(2,1)}, u32[]{:S(2)}) %copy-start.5) | copy-done | bytes 1376280
  8.3 0.9 %copy-done.7 = bf16[496,128]{1,0:T(8,128)(2,1)S(1)} copy-done((bf16[496,128]{1,0:T(8,128)(2,1)S(1)}, bf16[496,128]{1,0:T(8,128)(2,1)}, u32[]{:S(2)}) %copy-start.7) | copy-done | bytes 127000
  9.2 0.7 %copy-done.9 = bf16[3,64,16]{1,2,0:T(8,128)(2,1)S(1)} copy-done((bf16[3,64,16]{1,2,0:T(8,128)(2,1)S(1)}, bf16[3,64,16]{1,2,0:T(8,128)(2,1)}, u32[]{:S(2)}) %copy-start.9) | copy-done | bytes 6168
  9.9 2.7 %shard_map.113 = (bf16[3,128,512]{2,1,0:T(8,128)(2,1)S(1)}, f32[128,768]{1,0:T(8,128)S(1)}, f32[3,128,64]{2,1,0:T(8,128)S(1)}, f32[128,768]{1,0:T(8,128)S(1)}, b...) custom-call(f32[128,512]{1,0:T(8,128)S(1)} %bitcast.9, ...), custom_call_target="tpu_custom_call" | custom-call | tf_op jit(solution)/shard_map/pallas_call | solution.py:663
  13.2 3.0 %collective-permute-start.2 = (bf16[256,128]{1,0:T(8,128)(2,1)S(1)}, bf16[256,128]{1,0:T(8,128)(2,1)S(1)}, u32[]{:S(2)}, u32[]{:S(2)}) collective-permute-start(bf16[256,128]{1,0:T(8,128)(2,1)S(1)} %get-tuple-element.58), channel_id=1, source_target_pairs={{0,16},{16,0},{1,17},{17,1},{2,18},{18,2},{3,19},{19,3},{4,20},{20... | collective-permute-start | bytes 196616 | tf_op jit(solution)/shard_map/ppermute | solution.py:32
  16.2 4.4 %collective-permute-start.1 = (bf16[128,128]{1,0:T(8,128)(2,1)S(1)}, bf16[128,128]{1,0:T(8,128)(2,1)S(1)}, u32[]{:S(2)}, u32[]{:S(2)}) collective-permute-start(bf16[128,128]{1,0:T(8,128)(2,1)S(1)} %get-tuple-element.57), channel_id=1, source_target_pairs={{0,15},{1,0},{2,1},{3,2},{4,3},{5,4},{6,5},{7,6},{8,7},{9,8},{10,9... | collective-permute-start | bytes 98312 | tf_op jit(solution)/shard_map/ppermute | solution.py:32
  20.7 0.7 %shard_map.114.refs_14_ = f32[128,512]{1,0:T(8,128)S(1)} custom-call(f32[128,512]{1,0:T(8,128)S(1)} %bitcast.10, bf16[3,128,512]{2,1,0:T(8,128)(2,1)S(1)} %get-tuple-element.61.refs_1_.refs_7_.refs_8_.refs_2_.refs_10_, f32[16,1]{1,0:T(8,128)S(1)} %get-tuple-element.63.refs_2_.refs_9_.refs_10_.refs_3_.refs_12_, ...), custom_call_target="tpu_custom_call" | custom-call | tf_op jit(solution)/shard_map/pallas_call | solution.py:408
  21.4 0.9 %collective-permute-done.refs_1_ = bf16[128,128]{1,0:T(8,128)(2,1)S(1)} collective-permute-done((bf16[128,128]{1,0:T(8,128)(2,1)S(1)}, bf16[128,128]{1,0:T(8,128)(2,1)S(1)}, u32[]{:S(2)}, u32[]{:S(2)}) %collective-permute-start) | collective-permute-done | bytes 32800 | tf_op jit(solution)/shard_map/ppermute | solution.py:32
  22.3 1.5 %shard_map.115 = (f32[128,512]{1,0:T(8,128)S(1)}, bf16[128,128]{1,0:T(8,128)(2,1)S(1)}, bf16[128,128]{1,0:T(8,128)(2,1)S(1)}, bf16[256,128]{1,0:T(8,128)(2,1)S(1)}) custom-call(f32[128,512]{1,0:T(8,128)S(1)} %bitcast.11, bf16[128,128]{1,0:T(8,128)(2,1)S(1)} %collective-permute-done.refs_1_, bf16[128,128]{1,0:T(8,128)(2,1)S(1)} %collective-permute-done.1.refs_2_, ...), custom_call_target="tpu_custom_call" | custom-call | tf_op jit(solution)/shard_map/pallas_call | solution.py:420
  23.9 4.5 %collective-permute-start.4 = (bf16[128,128]{1,0:T(8,128)(2,1)S(1)}, bf16[128,128]{1,0:T(8,128)(2,1)S(1)}, u32[]{:S(2)}, u32[]{:S(2)}) collective-permute-start(bf16[128,128]{1,0:T(8,128)(2,1)S(1)} %get-tuple-element.70), channel_id=1, source_target_pairs={{0,15},{1,0},{2,1},{3,2},{4,3},{5,4},{6,5},{7,6},{8,7},{9,8},{10,9... | collective-permute-start | bytes 98312 | tf_op jit(solution)/shard_map/ppermute | solution.py:32
  28.4 0.7 %shard_map.116.refs_16_ = f32[128,512]{1,0:T(8,128)S(1)} custom-call(f32[128,512]{1,0:T(8,128)S(1)} %get-tuple-element.68.refs_0_, bf16[3,128,512]{2,1,0:T(8,128)(2,1)S(1)} %get-tuple-element.61.refs_1_.refs_7_.refs_8_.refs_2_.refs_10_, f32[16,1]{1,0:T(8,128)S(1)} %get-tuple-element.63.refs_2_.refs_9_.refs_10_.refs_3_.refs_12_, ...), custom_call_target="tpu_custom_call" | custom-call | tf_op jit(solution)/shard_map/pallas_call | solution.py:408
  29.1 0.8 %collective-permute-done.3.refs_2_ = bf16[128,128]{1,0:T(8,128)(2,1)S(1)} collective-permute-done((bf16[128,128]{1,0:T(8,128)(2,1)S(1)}, bf16[128,128]{1,0:T(8,128)(2,1)S(1)}, u32[]{:S(2)}, u32[]{:S(2)}) %collective-permute-start.3) | collective-permute-done | bytes 32800 | tf_op jit(solution)/shard_map/ppermute | solution.py:32
  30.0 2.3 %shard_map.117 = (f32[128,512]{1,0:T(8,128)S(1)}, f32[128,64]{1,0:T(8,128)S(1)}, bf16[128,128]{1,0:T(8,128)(2,1)S(1)}, bf16[128,128]{1,0:T(8,128)(2,1)S(1)}, bf16[256,128]{1,0:T(8,128)(2,1)S(1)}) custom-call(f32[128,512]{1,0:T(8,128)S(1)} %get-tuple-element.68.refs_0_, f32[128,512]{1,0:T(8,128)S(1)} %bitcast.12, ...), custom_call_target="tpu_custom_call" | custom-call | tf_op jit(solution)/shard_map/pallas_call | solution.py:420
  32.2 2.0 %collective-permute-start.8 = (bf16[256,128]{1,0:T(8,128)(2,1)S(1)}, bf16[256,128]{1,0:T(8,128)(2,1)S(1)}, u32[]{:S(2)}, u32[]{:S(2)}) collective-permute-start(bf16[256,128]{1,0:T(8,128)(2,1)S(1)} %get-tuple-element.77), channel_id=1, source_target_pairs={{0,16},{16,0},{1,17},{17,1},{2,18},{18,2},{3,19},{19,3},{4,20},{20... | collective-permute-start | bytes 196616 | tf_op jit(solution)/shard_map/ppermute | solution.py:32
  34.2 4.4 %collective-permute-start.7 = (bf16[128,128]{1,0:T(8,128)(2,1)S(1)}, bf16[128,128]{1,0:T(8,128)(2,1)S(1)}, u32[]{:S(2)}, u32[]{:S(2)}) collective-permute-start(bf16[128,128]{1,0:T(8,128)(2,1)S(1)} %get-tuple-element.76), channel_id=1, source_target_pairs={{0,15},{1,0},{2,1},{3,2},{4,3},{5,4},{6,5},{7,6},{8,7},{9,8},{10,9... | collective-permute-start | bytes 98312 | tf_op jit(solution)/shard_map/ppermute | solution.py:32
  38.6 0.9 %shard_map.118 = (f32[128,512]{1,0:T(8,128)S(1)}, f32[128,64]{1,0:T(8,128)S(1)}) custom-call(f32[128,512]{1,0:T(8,128)S(1)} %get-tuple-element.73.refs_0_.refs_2_, f32[128,64]{1,0:T(8,128)S(1)} %get-tuple-element.74.refs_1_.refs_3_, bf16[3,128,512]{2,1,0:T(8,128)(2,1)S(1)} %get-tuple-element.61.refs_1_.refs_7_.refs_8_.refs_2_.refs_10_, ...), custom_call_target="tpu_custom_call" | custom-call | tf_op jit(solution)/shard_map/pallas_call | solution.py:408
  39.6 0.7 %collective-permute-done.6.refs_2_ = bf16[128,128]{1,0:T(8,128)(2,1)S(1)} collective-permute-done((bf16[128,128]{1,0:T(8,128)(2,1)S(1)}, bf16[128,128]{1,0:T(8,128)(2,1)S(1)}, u32[]{:S(2)}, u32[]{:S(2)}) %collective-permute-start.6) | collective-permute-done | bytes 32800 | tf_op jit(solution)/shard_map/ppermute | solution.py:32
  40.2 4.3 %shard_map.119 = (f32[128,512]{1,0:T(8,128)S(1)}, f32[128,64]{1,0:T(8,128)S(1)}, bf16[128,128]{1,0:T(8,128)(2,1)S(1)}, bf16[128,128]{1,0:T(8,128)(2,1)S(1)}, bf16[256,128]{1,0:T(8,128)(2,1)S(1)}) custom-call(f32[128,512]{1,0:T(8,128)S(1)} %get-tuple-element.73.refs_0_.refs_2_, f32[128,64]{1,0:T(8,128)S(1)} %get-tuple-element.74.refs_1_.refs_3_, ...), custom_call_target="tpu_custom_call" | custom-call | tf_op jit(solution)/shard_map/pallas_call | solution.py:420
  44.8 4.4 %collective-permute-start.10 = (bf16[128,128]{1,0:T(8,128)(2,1)S(1)}, bf16[128,128]{1,0:T(8,128)(2,1)S(1)}, u32[]{:S(2)}, u32[]{:S(2)}) collective-permute-start(bf16[128,128]{1,0:T(8,128)(2,1)S(1)} %get-tuple-element.85), channel_id=1, source_target_pairs={{0,15},{1,0},{2,1},{3,2},{4,3},{5,4},{6,5},{7,6},{8,7},{9,8},{10,9... | collective-permute-start | bytes 98312 | tf_op jit(solution)/shard_map/ppermute | solution.py:32
  49.2 0.9 %shard_map.120 = (f32[128,512]{1,0:T(8,128)S(1)}, f32[128,64]{1,0:T(8,128)S(1)}) custom-call(f32[128,512]{1,0:T(8,128)S(1)} %get-tuple-element.82.refs_0_, f32[128,64]{1,0:T(8,128)S(1)} %get-tuple-element.83.refs_1_, bf16[3,128,512]{2,1,0:T(8,128)(2,1)S(1)} %get-tuple-element.61.refs_1_.refs_7_.refs_8_.refs_2_.refs_10_, ...), custom_call_target="tpu_custom_call" | custom-call | tf_op jit(solution)/shard_map/pallas_call | solution.py:408
  50.8 3.7 %shard_map.121 = (f32[128,512]{1,0:T(8,128)S(1)}, f32[128,64]{1,0:T(8,128)S(1)}, f32[24,512]{1,0:T(8,128)S(1)}, f32[24,512]{1,0:T(8,128)S(1)}) custom-call(f32[128,512]{1,0:T(8,128)S(1)} %get-tuple-element.82.refs_0_, f32[128,64]{1,0:T(8,128)S(1)} %get-tuple-element.83.refs_1_, f32[128,512]{1,0:T(8,128)S(1)} %get-tuple-element.73.refs_0_.refs_2_, ...), custom_call_target="tpu_custom_call" | custom-call | tf_op jit(solution)/shard_map/pallas_call | solution.py:420
  54.5 0.7 %copy-done.6 = f32[128,512]{1,0:T(8,128)} copy-done((f32[128,512]{1,0:T(8,128)}, f32[128,512]{1,0:T(8,128)S(1)}, u32[]{:S(2)}) %copy-start.6) | copy-done | bytes 262168
  55.2 4.4 %collective-permute-start.13 = (f32[24,512]{1,0:T(8,128)S(1)}, f32[24,512]{1,0:T(8,128)S(1)}, u32[]{:S(2)}, u32[]{:S(2)}) collective-permute-start(f32[24,512]{1,0:T(8,128)S(1)} %get-tuple-element.95), channel_id=1, source_target_pairs={{0,15},{1,0},{2,1},{3,2},{4,3},{5,4},{6,5},{7,6},{8,7},{9,8},{10,9... | collective-permute-start | bytes 147464 | tf_op jit(solution)/shard_map/ppermute | solution.py:32
  59.6 0.7 %reshape.40 = f32[16,512]{1,0:T(8,128)} reshape(f32[128,64]{1,0:T(8,128)S(1)} %get-tuple-element.97) | data formatting | bytes 65536 | tf_op jit(solution)/shard_map/reshape | solution.py:722
  60.3 1.1 %collective-permute-done.12.from_l_ref = f32[24,512]{1,0:T(8,128)S(1)} collective-permute-done((f32[24,512]{1,0:T(8,128)S(1)}, f32[24,512]{1,0:T(8,128)S(1)}, u32[]{:S(2)}, u32[]{:S(2)}) %collective-permute-start.12) | collective-permute-done | bytes 49184 | tf_op jit(solution)/shard_map/ppermute | solution.py:32
  62.0 2.7 %shard_map.122 = f32[96,512]{1,0:T(8,128)} custom-call(f32[128,512]{1,0:T(8,128)} %copy-done.6, f32[24,512]{1,0:T(8,128)} %copy-done.10, f32[24,512]{1,0:T(8,128)} %copy-done.11, f32[128,128]{1,0:T(8,128)} %copy-done.8), custom_call_target="tpu_custom_call" | custom-call | tf_op jit(solution)/shard_map/pallas_call | solution.py:715
  (46 shorter events, 3.3 us)
Async XLA Ops:
  4.5 1.0 %copy-start.2 = (f32[16,8,512]{2,1,0:T(8,128)S(1)}, f32[16,8,512]{2,1,0:T(8,128)}, u32[]{:S(2)}) copy-start(f32[16,8,512]{2,1,0:T(8,128)} %param.12) | copy-start | bytes 786436
  5.5 1.5 %copy-start.4 = (bf16[1792,512]{1,0:T(8,128)(2,1)S(1)}, bf16[1792,512]{1,0:T(8,128)(2,1)}, u32[]{:S(2)}) copy-start(bf16[1792,512]{1,0:T(8,128)(2,1)} %constant.80.clone.refs_4_) | copy-start | bytes 5505028
  7.0 1.3 %copy-start.5 = (bf16[896,768]{1,0:T(8,128)(2,1)S(1)}, bf16[896,768]{1,0:T(8,128)(2,1)}, u32[]{:S(2)}) copy-start(bf16[896,768]{1,0:T(8,128)(2,1)} %constant.79.clone.refs_3_) | copy-start | bytes 4128772
  8.3 0.9 %copy-start.7 = (bf16[496,128]{1,0:T(8,128)(2,1)S(1)}, bf16[496,128]{1,0:T(8,128)(2,1)}, u32[]{:S(2)}) copy-start(bf16[496,128]{1,0:T(8,128)(2,1)} %constant.81.clone.refs_5_) | copy-start | bytes 380932
  9.2 0.7 %copy-start.9 = (bf16[3,64,16]{1,2,0:T(8,128)(2,1)S(1)}, bf16[3,64,16]{1,2,0:T(8,128)(2,1)}, u32[]{:S(2)}) copy-start(bf16[3,64,16]{1,2,0:T(8,128)(2,1)} %param.13) | copy-start | bytes 18436
  12.6 0.6 copy-start.8
  13.2 25.4 %copy-start = (bf16[1792,512]{1,0:T(8,128)(2,1)}, bf16[1792,512]{1,0:T(8,128)(2,1)S(1)}, u32[]{:S(2)}) copy-start(bf16[1792,512]{1,0:T(8,128)(2,1)S(1)} %get-tuple-element.66.refs_5_.refs_12_.refs_13_.refs_6_.refs_15_) | copy-start | bytes 5505028
  13.2 9.0 %collective-permute-start.2 = (bf16[256,128]{1,0:T(8,128)(2,1)S(1)}, bf16[256,128]{1,0:T(8,128)(2,1)S(1)}, u32[]{:S(2)}, u32[]{:S(2)}) collective-permute-start(bf16[256,128]{1,0:T(8,128)(2,1)S(1)} %get-tuple-element.58), channel_id=1, source_target_pairs={{0,16},{16,0},{1,17},{17,1},{2,18},{18,2},{3,19},{19,3},{4,20},{20... | collective-permute-start | bytes 196616 | tf_op jit(solution)/shard_map/ppermute | solution.py:32
  16.2 6.0 %collective-permute-start = (bf16[128,128]{1,0:T(8,128)(2,1)S(1)}, bf16[128,128]{1,0:T(8,128)(2,1)S(1)}, u32[]{:S(2)}, u32[]{:S(2)}) collective-permute-start(bf16[128,128]{1,0:T(8,128)(2,1)S(1)} %get-tuple-element.56), channel_id=1, source_target_pairs={{0,1},{1,2},{2,3},{3,4},{4,5},{5,6},{6,7},{7,8},{8,9},{9,10},{10,1... | collective-permute-start | bytes 98312 | tf_op jit(solution)/shard_map/ppermute | solution.py:32
  16.2 6.0 %collective-permute-start.1 = (bf16[128,128]{1,0:T(8,128)(2,1)S(1)}, bf16[128,128]{1,0:T(8,128)(2,1)S(1)}, u32[]{:S(2)}, u32[]{:S(2)}) collective-permute-start(bf16[128,128]{1,0:T(8,128)(2,1)S(1)} %get-tuple-element.57), channel_id=1, source_target_pairs={{0,15},{1,0},{2,1},{3,2},{4,3},{5,4},{6,5},{7,6},{8,7},{9,8},{10,9... | collective-permute-start | bytes 98312 | tf_op jit(solution)/shard_map/ppermute | solution.py:32
  20.7 1.6 %copy-start.3 = (f32[16,8,512]{2,1,0:T(8,128)S(1)}, f32[16,8,512]{2,1,0:T(8,128)}, u32[]{:S(2)}) copy-start(f32[16,8,512]{2,1,0:T(8,128)} %param.12) | copy-start | bytes 786436
  23.7 6.2 %collective-permute-start.5 = (bf16[256,128]{1,0:T(8,128)(2,1)S(1)}, bf16[256,128]{1,0:T(8,128)(2,1)S(1)}, u32[]{:S(2)}, u32[]{:S(2)}) collective-permute-start(bf16[256,128]{1,0:T(8,128)(2,1)S(1)} %get-tuple-element.71), channel_id=1, source_target_pairs={{0,16},{16,0},{1,17},{17,1},{2,18},{18,2},{3,19},{19,3},{4,20},{20... | collective-permute-start | bytes 196616 | tf_op jit(solution)/shard_map/ppermute | solution.py:32
  23.8 6.1 %collective-permute-start.3 = (bf16[128,128]{1,0:T(8,128)(2,1)S(1)}, bf16[128,128]{1,0:T(8,128)(2,1)S(1)}, u32[]{:S(2)}, u32[]{:S(2)}) collective-permute-start(bf16[128,128]{1,0:T(8,128)(2,1)S(1)} %get-tuple-element.69), channel_id=1, source_target_pairs={{0,1},{1,2},{2,3},{3,4},{4,5},{5,6},{6,7},{7,8},{8,9},{9,10},{10,1... | collective-permute-start | bytes 98312 | tf_op jit(solution)/shard_map/ppermute | solution.py:32
  23.9 6.1 %collective-permute-start.4 = (bf16[128,128]{1,0:T(8,128)(2,1)S(1)}, bf16[128,128]{1,0:T(8,128)(2,1)S(1)}, u32[]{:S(2)}, u32[]{:S(2)}) collective-permute-start(bf16[128,128]{1,0:T(8,128)(2,1)S(1)} %get-tuple-element.70), channel_id=1, source_target_pairs={{0,15},{1,0},{2,1},{3,2},{4,3},{5,4},{6,5},{7,6},{8,7},{9,8},{10,9... | collective-permute-start | bytes 98312 | tf_op jit(solution)/shard_map/ppermute | solution.py:32
  32.2 8.0 %collective-permute-start.8 = (bf16[256,128]{1,0:T(8,128)(2,1)S(1)}, bf16[256,128]{1,0:T(8,128)(2,1)S(1)}, u32[]{:S(2)}, u32[]{:S(2)}) collective-permute-start(bf16[256,128]{1,0:T(8,128)(2,1)S(1)} %get-tuple-element.77), channel_id=1, source_target_pairs={{0,16},{16,0},{1,17},{17,1},{2,18},{18,2},{3,19},{19,3},{4,20},{20... | collective-permute-start | bytes 196616 | tf_op jit(solution)/shard_map/ppermute | solution.py:32
  34.2 6.0 %collective-permute-start.6 = (bf16[128,128]{1,0:T(8,128)(2,1)S(1)}, bf16[128,128]{1,0:T(8,128)(2,1)S(1)}, u32[]{:S(2)}, u32[]{:S(2)}) collective-permute-start(bf16[128,128]{1,0:T(8,128)(2,1)S(1)} %get-tuple-element.75), channel_id=1, source_target_pairs={{0,1},{1,2},{2,3},{3,4},{4,5},{5,6},{6,7},{7,8},{8,9},{9,10},{10,1... | collective-permute-start | bytes 98312 | tf_op jit(solution)/shard_map/ppermute | solution.py:32
  34.2 6.0 %collective-permute-start.7 = (bf16[128,128]{1,0:T(8,128)(2,1)S(1)}, bf16[128,128]{1,0:T(8,128)(2,1)S(1)}, u32[]{:S(2)}, u32[]{:S(2)}) collective-permute-start(bf16[128,128]{1,0:T(8,128)(2,1)S(1)} %get-tuple-element.76), channel_id=1, source_target_pairs={{0,15},{1,0},{2,1},{3,2},{4,3},{5,4},{6,5},{7,6},{8,7},{9,8},{10,9... | collective-permute-start | bytes 98312 | tf_op jit(solution)/shard_map/ppermute | solution.py:32
  40.2 9.0 %copy-start.1 = (bf16[1792,512]{1,0:T(8,128)(2,1)S(1)}, bf16[1792,512]{1,0:T(8,128)(2,1)}, u32[]{:S(2)}) copy-start(bf16[1792,512]{1,0:T(8,128)(2,1)} %copy-done) | copy-start | bytes 5505028
  44.6 6.2 %collective-permute-start.11 = (bf16[256,128]{1,0:T(8,128)(2,1)S(1)}, bf16[256,128]{1,0:T(8,128)(2,1)S(1)}, u32[]{:S(2)}, u32[]{:S(2)}) collective-permute-start(bf16[256,128]{1,0:T(8,128)(2,1)S(1)} %get-tuple-element.86), channel_id=1, source_target_pairs={{0,16},{16,0},{1,17},{17,1},{2,18},{18,2},{3,19},{19,3},{4,20},{20... | collective-permute-start | bytes 196616 | tf_op jit(solution)/shard_map/ppermute | solution.py:32
  44.8 6.0 %collective-permute-start.9 = (bf16[128,128]{1,0:T(8,128)(2,1)S(1)}, bf16[128,128]{1,0:T(8,128)(2,1)S(1)}, u32[]{:S(2)}, u32[]{:S(2)}) collective-permute-start(bf16[128,128]{1,0:T(8,128)(2,1)S(1)} %get-tuple-element.84), channel_id=1, source_target_pairs={{0,1},{1,2},{2,3},{3,4},{4,5},{5,6},{6,7},{7,8},{8,9},{9,10},{10,1... | collective-permute-start | bytes 98312 | tf_op jit(solution)/shard_map/ppermute | solution.py:32
  44.8 6.0 %collective-permute-start.10 = (bf16[128,128]{1,0:T(8,128)(2,1)S(1)}, bf16[128,128]{1,0:T(8,128)(2,1)S(1)}, u32[]{:S(2)}, u32[]{:S(2)}) collective-permute-start(bf16[128,128]{1,0:T(8,128)(2,1)S(1)} %get-tuple-element.85), channel_id=1, source_target_pairs={{0,15},{1,0},{2,1},{3,2},{4,3},{5,4},{6,5},{7,6},{8,7},{9,8},{10,9... | collective-permute-start | bytes 98312 | tf_op jit(solution)/shard_map/ppermute | solution.py:32
  54.5 0.7 %copy-start.6 = (f32[128,512]{1,0:T(8,128)}, f32[128,512]{1,0:T(8,128)S(1)}, u32[]{:S(2)}) copy-start(f32[128,512]{1,0:T(8,128)S(1)} %get-tuple-element.93.home_ref) | copy-start | bytes 786436
  55.2 6.2 %collective-permute-start.12 = (f32[24,512]{1,0:T(8,128)S(1)}, f32[24,512]{1,0:T(8,128)S(1)}, u32[]{:S(2)}, u32[]{:S(2)}) collective-permute-start(f32[24,512]{1,0:T(8,128)S(1)} %get-tuple-element.94), channel_id=1, source_target_pairs={{0,1},{1,2},{2,3},{3,4},{4,5},{5,6},{6,7},{7,8},{8,9},{9,10},{10,1... | collective-permute-start | bytes 147464 | tf_op jit(solution)/shard_map/ppermute | solution.py:32
  55.2 6.2 %collective-permute-start.13 = (f32[24,512]{1,0:T(8,128)S(1)}, f32[24,512]{1,0:T(8,128)S(1)}, u32[]{:S(2)}, u32[]{:S(2)}) collective-permute-start(f32[24,512]{1,0:T(8,128)S(1)} %get-tuple-element.95), channel_id=1, source_target_pairs={{0,15},{1,0},{2,1},{3,2},{4,3},{5,4},{6,5},{7,6},{8,7},{9,8},{10,9... | collective-permute-start | bytes 147464 | tf_op jit(solution)/shard_map/ppermute | solution.py:32
  61.4 0.6 copy-start.10
  61.4 0.6 copy-start.11

commit v7 on v6

--- a/solution.py
+++ b/solution.py
@@ -455,7 +455,13 @@
     m7_out[...] = _dot(bcast, m7.astype(bf16))
     m3 = jnp.minimum(sign * by_block(mvg), 0.0)
     m3_out[...] = _exact_right(bcast, m3)
-    rep = _dot(bcast, packed_ref[...].astype(bf16))
+    eye16 = jnp.where(
+        lax.broadcasted_iota(jnp.int32, (local, LANE), 0)
+        == lax.broadcasted_iota(jnp.int32, (local, LANE), 1), 1.0, 0.0
+    ).astype(bf16)
+    p_hi, p_mid, p_lo = _split(packed_ref[...])
+    packed = (_dot_t(eye16, p_hi) + _dot_t(eye16, p_mid)) + _dot_t(eye16, p_lo)
+    rep = _dot(bcast, packed.astype(bf16))
     row_f = (lax.broadcasted_iota(jnp.int32, (rows, 1), 0) % fields).astype(f32)
     cols = lax.broadcasted_iota(jnp.int32, (rows, rows), 1).astype(f32)
     for side in range(6):
@@ -467,10 +473,15 @@
         if side in SEND_FACES:
             pr_out[SEND_FACES.index(side)] = jnp.where(hit & far, 1.0, 0.0).astype(bf16)
     sw_out[...] = rep[:, 6:7]
-    packed = packed_ref[...]
+    curve_count = lax.axis_size("curve")
+    curve_pos = lax.axis_index("curve")
+    left_f = ((curve_pos + curve_count - 1) % curve_count).astype(f32)
+    right_f = ((curve_pos + 1) % curve_count).astype(f32)
+    first_f = jnp.where(curve_pos == 0, 1.0, 0.0)
+    last_f = jnp.where(curve_pos == curve_count - 1, 1.0, 0.0)
     stay_sw = packed[:, 6:7] < 0.5
-    go_left = (packed[:, 9:10] == packed[:, 10:11]) & stay_sw
-    go_right = (packed[:, 9:10] == packed[:, 11:12]) & stay_sw
+    go_left = (packed[:, 9:10] == left_f) & stay_sw
+    go_right = (packed[:, 9:10] == right_f) & stay_sw
     stays = stay_sw & ~go_left & ~go_right
     lane16 = lax.broadcasted_iota(jnp.int32, (local, LANE), 1)
     marks = jnp.where(
@@ -485,8 +496,8 @@
     for k in range(3):
         info = jnp.where(lane16 == 3 + k, before[:, k : k + 1], info)
     info = jnp.where(lane16 == 6, totals[:, 2:3], info)
-    info = jnp.where(lane16 == 7, packed[:, 12:13], info)
-    info = jnp.where(lane16 == 8, packed[:, 13:14], info)
+    info = jnp.where(lane16 == 7, first_f, info)
+    info = jnp.where(lane16 == 8, last_f, info)
     hinfo = _dot(bcast, info.astype(bf16))
     hinfo_out[...] = hinfo
     cnt_l_out[...] = jnp.broadcast_to(totals[0:1, 0:1], cnt_l_out.shape)
@@ -505,8 +516,8 @@
             & (cc < MOVE_CAP * fields)
         )
         out[...] = _dot_t(eye, jnp.where(hit, 1.0, 0.0).astype(bf16)).astype(bf16)
-    pre_out[...] = packed_ref[:, 7:8]
-    stc_out[...] = _exact_right(fsel_ref[...], packed_ref[...])[:, 8:9]
+    pre_out[...] = packed[:, 7:8]
+    stc_out[...] = _exact_right(fsel_ref[...], packed)[:, 8:9]
     write_sends(send_refs, _dot(u_ref[...].astype(bf16), g7_ref[...]).astype(bf16))
 
 
@@ -575,25 +586,16 @@
     near_local = neighbours - near_device * local_count
     remote = near_device != device_id
     codes = (near_local + local_count * remote.astype(jnp.int32)).astype(f32)
-    sto_col = jnp.zeros((local_count,), f32).at[:field_count].set(stoich)
     left_pos = (curve_pos + curve_count - 1) % curve_count
     right_pos = (curve_pos + 1) % curve_count
-    ones = jnp.ones((local_count, 1), f32)
-    packed = jnp.concatenate(
+    sto_col = jnp.pad(stoich, (0, local_count - field_count))
+    packed_t = jnp.concatenate(
         [
-            codes,
-            switch.astype(f32)[:, None],
-            pre_exp[:, None],
-            sto_col[:, None],
-            new_owner.astype(f32)[:, None],
-            ones * left_pos.astype(f32),
-            ones * right_pos.astype(f32),
-            ones * (curve_pos == 0).astype(f32),
-            ones * (curve_pos == curve_count - 1).astype(f32),
-            jnp.zeros((local_count, LANE - 14), f32),
-        ],
-        axis=1,
-    )
+            jnp.transpose(codes),
+            jnp.stack([switch.astype(f32), pre_exp, sto_col, new_owner.astype(f32)]),
+        ]
+    )
+    packed = jnp.pad(packed_t, ((0, local_count - 10), (0, LANE - local_count)))
     fsel_np = np.arange(rows)[:, None] % field_count == np.arange(local_count)[None, :]
     vt = jnp.transpose(velocity, (0, 2, 1))
     row_elem = np.arange(rows) // field_count

time: 65.2 us -> 64.2 us (0.985)
  local copies, waits for them, and re-layouts: 10.5 us -> 9.39 us
    broadcast_in_dim x5 -> x0, local copies, waits for them, and re-layouts: 1.63 us -> none  [the longest x1 0.73 us: per_device(): pre_exp[:, None]]
    broadcast_in_dim x2 -> x0, other arithmetic: 1.32 us -> none  [the longest x1 0.66 us: per_device(): switch.astype(f32)[:, None]]
    unnamed x25 -> x24, local copies, waits for them, and re-layouts: 8.09 us -> 7.34 us
    transpose x0 -> x1, other arithmetic: none -> 0.7 us  [per_device(): jnp.transpose(codes)]
    another operation x0 -> x1, other arithmetic: none -> 0.67 us  [per_device(): jnp.stack([switch.astype(f32), pre_exp, sto_col, new_owner.astype(f32)])]
    another operation x0 -> x1, local copies, waits for them, and re-layouts: none -> 0.66 us  [per_device(): jnp.stack([switch.astype(f32), pre_exp, sto_col, new_owner.astype(f32)])]
where the time goes in v7:
time: 64.2 us; the launch traced here: 63.9 us
  starting transfers between devices  27.5 us (43%)
  Pallas kernels  20.7 us (32%)
  local copies, waits for them, and re-layouts  9.39 us (15%)
  waiting for transfers between devices  4.16 us (6%)
  other arithmetic  1.37 us (2%)
  between operations  0.76 us (1%)
    ppermute x14, starting transfers between devices, shifted(): return lax.ppermute(value, axis, pairs)  27.5 us
    pallas_call x4, Pallas kernels, run_stage(): pl.pallas_call(kernel, out_shape=out_shapes, in_specs=[_vmem() for _ in i...  11.7 us
    unnamed x24, local copies, waits for them, and re-layouts  7.34 us
    ppermute x14, waiting for transfers between devices, shifted(): return lax.ppermute(value, axis, pairs)  4.16 us
    pallas_call x4, Pallas kernels, run_bulk(): pl.pallas_call(functools.partial(bulk_kernel, coarse, local), out_shape=o...  3.28 us
    pallas_call x1, Pallas kernels, per_device(): pl.pallas_call(functools.partial(setup_entry, local_count, field_count, l...  2.92 us
    pallas_call x1, Pallas kernels, per_device(): pl.pallas_call(functools.partial(final_kernel, field_count, HOLD7), out_s...  2.74 us
  transfers between devices with their start and end apart: 14, of which 6 were waited for; matrix products, arithmetic and copies ran while one was open for 1% of the time, Pallas kernels for 5%

profile of v7, /device:TPU:0, one launch (start us, length us, event | category | flops | bytes accessed | tf_op | source)
XLA Modules:
  0.0 63.9 jit_solution(2348372198609111631)
XLA Ops:
  0.6 0.7 %pad_bitcast_fusion = f32[1,16]{1,0:T(1,128)S(1)} fusion(f32[8]{0:T(128)} %param.13), kind=kLoop, calls=%fused_computation.9 | loop fusion | bytes 96 | tf_op jit(solution)/shard_map/stack | solution.py:595
  1.3 0.7 %convert_bitcast_fusion.1 = (f32[1,16]{1,0:T(1,128)S(1)}, f32[1,16]{1,0:T(1,128)S(1)}) fusion(s32[16]{0:T(128)} %param.16, s32[16]{0:T(128)} %param.15), kind=kLoop, calls=%fused_computation.8 | loop fusion | flops 32 | bytes 256 | tf_op jit(solution)/shard_map/stack | solution.py:595
  2.0 0.7 %convert_bitcast_fusion = f32[6,16]{1,0:T(8,128)S(1)} fusion(s32[16,6]{0,1:T(8,128)} %param.14, s32[]{:T(128)S(6)} %add.11), kind=kLoop, calls=%fused_computation.5 | loop fusion | flops 2016 | bytes 772 | tf_op jit(solution)/shard_map/transpose | solution.py:594
  2.7 0.7 %concatenate.3 = f32[10,16]{1,0:T(8,128)S(1)} concatenate(f32[6,16]{1,0:T(8,128)S(1)} %convert_bitcast_fusion, f32[1,16]{1,0:T(1,128)S(1)} %get-tuple-element.87, f32[1,16]{1,0:T(1,128)} %bitcast.18, f32[1,16]{1,0:T(1,128)S(1)} %pad_bitcast_fusion, f32[1,16]{1,0:T(1,128)S(1)} %get-tuple-element.86), dimensions={0} | concatenate | bytes 1280 | tf_op jit(solution)/shard_map/concatenate | solution.py:592
  3.4 0.9 %copy-done.2 = f32[16,8,512]{2,1,0:T(8,128)S(1)} copy-done((f32[16,8,512]{2,1,0:T(8,128)S(1)}, f32[16,8,512]{2,1,0:T(8,128)}, u32[]{:S(2)}) %copy-start.2) | copy-done | bytes 262168
  4.3 1.5 %copy-done.4 = bf16[1792,512]{1,0:T(8,128)(2,1)S(1)} copy-done((bf16[1792,512]{1,0:T(8,128)(2,1)S(1)}, bf16[1792,512]{1,0:T(8,128)(2,1)}, u32[]{:S(2)}) %copy-start.4) | copy-done | bytes 1835032
  5.8 1.3 %copy-done.5 = bf16[896,768]{1,0:T(8,128)(2,1)S(1)} copy-done((bf16[896,768]{1,0:T(8,128)(2,1)S(1)}, bf16[896,768]{1,0:T(8,128)(2,1)}, u32[]{:S(2)}) %copy-start.5) | copy-done | bytes 1376280
  7.2 0.9 %copy-done.7 = bf16[496,128]{1,0:T(8,128)(2,1)S(1)} copy-done((bf16[496,128]{1,0:T(8,128)(2,1)S(1)}, bf16[496,128]{1,0:T(8,128)(2,1)}, u32[]{:S(2)}) %copy-start.7) | copy-done | bytes 127000
  8.1 0.7 %copy-done.9 = bf16[3,64,16]{1,2,0:T(8,128)(2,1)S(1)} copy-done((bf16[3,64,16]{1,2,0:T(8,128)(2,1)S(1)}, bf16[3,64,16]{1,2,0:T(8,128)(2,1)}, u32[]{:S(2)}) %copy-start.9) | copy-done | bytes 6168
  8.8 2.9 %shard_map.113 = (bf16[3,128,512]{2,1,0:T(8,128)(2,1)S(1)}, f32[128,768]{1,0:T(8,128)S(1)}, f32[3,128,64]{2,1,0:T(8,128)S(1)}, f32[128,768]{1,0:T(8,128)S(1)}, b...) custom-call(f32[128,512]{1,0:T(8,128)S(1)} %bitcast.12, ...), custom_call_target="tpu_custom_call" | custom-call | tf_op jit(solution)/shard_map/pallas_call | solution.py:665
  12.3 3.0 %collective-permute-start.2 = (bf16[256,128]{1,0:T(8,128)(2,1)S(1)}, bf16[256,128]{1,0:T(8,128)(2,1)S(1)}, u32[]{:S(2)}, u32[]{:S(2)}) collective-permute-start(bf16[256,128]{1,0:T(8,128)(2,1)S(1)} %get-tuple-element.46), channel_id=1, source_target_pairs={{0,16},{16,0},{1,17},{17,1},{2,18},{18,2},{3,19},{19,3},{4,20},{20... | collective-permute-start | bytes 196616 | tf_op jit(solution)/shard_map/ppermute | solution.py:32
  15.3 4.4 %collective-permute-start.1 = (bf16[128,128]{1,0:T(8,128)(2,1)S(1)}, bf16[128,128]{1,0:T(8,128)(2,1)S(1)}, u32[]{:S(2)}, u32[]{:S(2)}) collective-permute-start(bf16[128,128]{1,0:T(8,128)(2,1)S(1)} %get-tuple-element.45), channel_id=1, source_target_pairs={{0,15},{1,0},{2,1},{3,2},{4,3},{5,4},{6,5},{7,6},{8,7},{9,8},{10,9... | collective-permute-start | bytes 98312 | tf_op jit(solution)/shard_map/ppermute | solution.py:32
  19.7 0.7 %shard_map.114.refs_14_ = f32[128,512]{1,0:T(8,128)S(1)} custom-call(f32[128,512]{1,0:T(8,128)S(1)} %bitcast.13, bf16[3,128,512]{2,1,0:T(8,128)(2,1)S(1)} %get-tuple-element.49.refs_1_.refs_7_.refs_8_.refs_2_.refs_10_, f32[16,1]{1,0:T(8,128)S(1)} %get-tuple-element.51.refs_2_.refs_9_.refs_10_.refs_3_.refs_12_, ...), custom_call_target="tpu_custom_call" | custom-call | tf_op jit(solution)/shard_map/pallas_call | solution.py:408
  20.5 0.9 %collective-permute-done.refs_1_ = bf16[128,128]{1,0:T(8,128)(2,1)S(1)} collective-permute-done((bf16[128,128]{1,0:T(8,128)(2,1)S(1)}, bf16[128,128]{1,0:T(8,128)(2,1)S(1)}, u32[]{:S(2)}, u32[]{:S(2)}) %collective-permute-start) | collective-permute-done | bytes 32800 | tf_op jit(solution)/shard_map/ppermute | solution.py:32
  21.3 1.5 %shard_map.115 = (f32[128,512]{1,0:T(8,128)S(1)}, bf16[128,128]{1,0:T(8,128)(2,1)S(1)}, bf16[128,128]{1,0:T(8,128)(2,1)S(1)}, bf16[256,128]{1,0:T(8,128)(2,1)S(1)}) custom-call(f32[128,512]{1,0:T(8,128)S(1)} %bitcast.14, bf16[128,128]{1,0:T(8,128)(2,1)S(1)} %collective-permute-done.refs_1_, bf16[128,128]{1,0:T(8,128)(2,1)S(1)} %collective-permute-done.1.refs_2_, ...), custom_call_target="tpu_custom_call" | custom-call | tf_op jit(solution)/shard_map/pallas_call | solution.py:420
  23.0 4.5 %collective-permute-start.4 = (bf16[128,128]{1,0:T(8,128)(2,1)S(1)}, bf16[128,128]{1,0:T(8,128)(2,1)S(1)}, u32[]{:S(2)}, u32[]{:S(2)}) collective-permute-start(bf16[128,128]{1,0:T(8,128)(2,1)S(1)} %get-tuple-element.58), channel_id=1, source_target_pairs={{0,15},{1,0},{2,1},{3,2},{4,3},{5,4},{6,5},{7,6},{8,7},{9,8},{10,9... | collective-permute-start | bytes 98312 | tf_op jit(solution)/shard_map/ppermute | solution.py:32
  27.4 0.7 %shard_map.116.refs_16_ = f32[128,512]{1,0:T(8,128)S(1)} custom-call(f32[128,512]{1,0:T(8,128)S(1)} %get-tuple-element.56.refs_0_, bf16[3,128,512]{2,1,0:T(8,128)(2,1)S(1)} %get-tuple-element.49.refs_1_.refs_7_.refs_8_.refs_2_.refs_10_, f32[16,1]{1,0:T(8,128)S(1)} %get-tuple-element.51.refs_2_.refs_9_.refs_10_.refs_3_.refs_12_, ...), custom_call_target="tpu_custom_call" | custom-call | tf_op jit(solution)/shard_map/pallas_call | solution.py:408
  28.2 0.8 %collective-permute-done.3.refs_2_ = bf16[128,128]{1,0:T(8,128)(2,1)S(1)} collective-permute-done((bf16[128,128]{1,0:T(8,128)(2,1)S(1)}, bf16[128,128]{1,0:T(8,128)(2,1)S(1)}, u32[]{:S(2)}, u32[]{:S(2)}) %collective-permute-start.3) | collective-permute-done | bytes 32800 | tf_op jit(solution)/shard_map/ppermute | solution.py:32
  29.0 2.3 %shard_map.117 = (f32[128,512]{1,0:T(8,128)S(1)}, f32[128,64]{1,0:T(8,128)S(1)}, bf16[128,128]{1,0:T(8,128)(2,1)S(1)}, bf16[128,128]{1,0:T(8,128)(2,1)S(1)}, bf16[256,128]{1,0:T(8,128)(2,1)S(1)}) custom-call(f32[128,512]{1,0:T(8,128)S(1)} %get-tuple-element.56.refs_0_, f32[128,512]{1,0:T(8,128)S(1)} %bitcast.15, ...), custom_call_target="tpu_custom_call" | custom-call | tf_op jit(solution)/shard_map/pallas_call | solution.py:420
  31.3 2.0 %collective-permute-start.8 = (bf16[256,128]{1,0:T(8,128)(2,1)S(1)}, bf16[256,128]{1,0:T(8,128)(2,1)S(1)}, u32[]{:S(2)}, u32[]{:S(2)}) collective-permute-start(bf16[256,128]{1,0:T(8,128)(2,1)S(1)} %get-tuple-element.65), channel_id=1, source_target_pairs={{0,16},{16,0},{1,17},{17,1},{2,18},{18,2},{3,19},{19,3},{4,20},{20... | collective-permute-start | bytes 196616 | tf_op jit(solution)/shard_map/ppermute | solution.py:32
  33.3 4.4 %collective-permute-start.7 = (bf16[128,128]{1,0:T(8,128)(2,1)S(1)}, bf16[128,128]{1,0:T(8,128)(2,1)S(1)}, u32[]{:S(2)}, u32[]{:S(2)}) collective-permute-start(bf16[128,128]{1,0:T(8,128)(2,1)S(1)} %get-tuple-element.64), channel_id=1, source_target_pairs={{0,15},{1,0},{2,1},{3,2},{4,3},{5,4},{6,5},{7,6},{8,7},{9,8},{10,9... | collective-permute-start | bytes 98312 | tf_op jit(solution)/shard_map/ppermute | solution.py:32
  37.7 0.9 %shard_map.118 = (f32[128,512]{1,0:T(8,128)S(1)}, f32[128,64]{1,0:T(8,128)S(1)}) custom-call(f32[128,512]{1,0:T(8,128)S(1)} %get-tuple-element.61.refs_0_.refs_2_, f32[128,64]{1,0:T(8,128)S(1)} %get-tuple-element.62.refs_1_.refs_3_, bf16[3,128,512]{2,1,0:T(8,128)(2,1)S(1)} %get-tuple-element.49.refs_1_.refs_7_.refs_8_.refs_2_.refs_10_, ...), custom_call_target="tpu_custom_call" | custom-call | tf_op jit(solution)/shard_map/pallas_call | solution.py:408
  38.7 0.7 %collective-permute-done.6.refs_2_ = bf16[128,128]{1,0:T(8,128)(2,1)S(1)} collective-permute-done((bf16[128,128]{1,0:T(8,128)(2,1)S(1)}, bf16[128,128]{1,0:T(8,128)(2,1)S(1)}, u32[]{:S(2)}, u32[]{:S(2)}) %collective-permute-start.6) | collective-permute-done | bytes 32800 | tf_op jit(solution)/shard_map/ppermute | solution.py:32
  39.3 4.3 %shard_map.119 = (f32[128,512]{1,0:T(8,128)S(1)}, f32[128,64]{1,0:T(8,128)S(1)}, bf16[128,128]{1,0:T(8,128)(2,1)S(1)}, bf16[128,128]{1,0:T(8,128)(2,1)S(1)}, bf16[256,128]{1,0:T(8,128)(2,1)S(1)}) custom-call(f32[128,512]{1,0:T(8,128)S(1)} %get-tuple-element.61.refs_0_.refs_2_, f32[128,64]{1,0:T(8,128)S(1)} %get-tuple-element.62.refs_1_.refs_3_, ...), custom_call_target="tpu_custom_call" | custom-call | tf_op jit(solution)/shard_map/pallas_call | solution.py:420
  43.9 4.4 %collective-permute-start.10 = (bf16[128,128]{1,0:T(8,128)(2,1)S(1)}, bf16[128,128]{1,0:T(8,128)(2,1)S(1)}, u32[]{:S(2)}, u32[]{:S(2)}) collective-permute-start(bf16[128,128]{1,0:T(8,128)(2,1)S(1)} %get-tuple-element.73), channel_id=1, source_target_pairs={{0,15},{1,0},{2,1},{3,2},{4,3},{5,4},{6,5},{7,6},{8,7},{9,8},{10,9... | collective-permute-start | bytes 98312 | tf_op jit(solution)/shard_map/ppermute | solution.py:32
  48.3 0.9 %shard_map.120 = (f32[128,512]{1,0:T(8,128)S(1)}, f32[128,64]{1,0:T(8,128)S(1)}) custom-call(f32[128,512]{1,0:T(8,128)S(1)} %get-tuple-element.70.refs_0_, f32[128,64]{1,0:T(8,128)S(1)} %get-tuple-element.71.refs_1_, bf16[3,128,512]{2,1,0:T(8,128)(2,1)S(1)} %get-tuple-element.49.refs_1_.refs_7_.refs_8_.refs_2_.refs_10_, ...), custom_call_target="tpu_custom_call" | custom-call | tf_op jit(solution)/shard_map/pallas_call | solution.py:408
  49.9 3.7 %shard_map.121 = (f32[128,512]{1,0:T(8,128)S(1)}, f32[128,64]{1,0:T(8,128)S(1)}, f32[24,512]{1,0:T(8,128)S(1)}, f32[24,512]{1,0:T(8,128)S(1)}) custom-call(f32[128,512]{1,0:T(8,128)S(1)} %get-tuple-element.70.refs_0_, f32[128,64]{1,0:T(8,128)S(1)} %get-tuple-element.71.refs_1_, f32[128,512]{1,0:T(8,128)S(1)} %get-tuple-element.61.refs_0_.refs_2_, ...), custom_call_target="tpu_custom_call" | custom-call | tf_op jit(solution)/shard_map/pallas_call | solution.py:420
  53.6 0.7 %copy-done.6 = f32[128,512]{1,0:T(8,128)} copy-done((f32[128,512]{1,0:T(8,128)}, f32[128,512]{1,0:T(8,128)S(1)}, u32[]{:S(2)}) %copy-start.6) | copy-done | bytes 262168
  54.3 4.4 %collective-permute-start.13 = (f32[24,512]{1,0:T(8,128)S(1)}, f32[24,512]{1,0:T(8,128)S(1)}, u32[]{:S(2)}, u32[]{:S(2)}) collective-permute-start(f32[24,512]{1,0:T(8,128)S(1)} %get-tuple-element.83), channel_id=1, source_target_pairs={{0,15},{1,0},{2,1},{3,2},{4,3},{5,4},{6,5},{7,6},{8,7},{9,8},{10,9... | collective-permute-start | bytes 147464 | tf_op jit(solution)/shard_map/ppermute | solution.py:32
  58.7 0.7 %reshape.15 = f32[16,512]{1,0:T(8,128)} reshape(f32[128,64]{1,0:T(8,128)S(1)} %get-tuple-element.85) | data formatting | bytes 65536 | tf_op jit(solution)/shard_map/reshape | solution.py:724
  59.4 1.1 %collective-permute-done.12.from_l_ref = f32[24,512]{1,0:T(8,128)S(1)} collective-permute-done((f32[24,512]{1,0:T(8,128)S(1)}, f32[24,512]{1,0:T(8,128)S(1)}, u32[]{:S(2)}, u32[]{:S(2)}) %collective-permute-start.12) | collective-permute-done | bytes 49184 | tf_op jit(solution)/shard_map/ppermute | solution.py:32
  61.1 2.7 %shard_map.122 = f32[96,512]{1,0:T(8,128)} custom-call(f32[128,512]{1,0:T(8,128)} %copy-done.6, f32[24,512]{1,0:T(8,128)} %copy-done.10, f32[24,512]{1,0:T(8,128)} %copy-done.11, f32[128,128]{1,0:T(8,128)} %copy-done.8), custom_call_target="tpu_custom_call" | custom-call | tf_op jit(solution)/shard_map/pallas_call | solution.py:717
  (36 shorter events, 2.3 us)
Async XLA Ops:
  3.4 0.9 %copy-start.2 = (f32[16,8,512]{2,1,0:T(8,128)S(1)}, f32[16,8,512]{2,1,0:T(8,128)}, u32[]{:S(2)}) copy-start(f32[16,8,512]{2,1,0:T(8,128)} %param.10) | copy-start | bytes 786436
  4.3 1.5 %copy-start.4 = (bf16[1792,512]{1,0:T(8,128)(2,1)S(1)}, bf16[1792,512]{1,0:T(8,128)(2,1)}, u32[]{:S(2)}) copy-start(bf16[1792,512]{1,0:T(8,128)(2,1)} %constant.38.clone.refs_4_) | copy-start | bytes 5505028
  5.8 1.3 %copy-start.5 = (bf16[896,768]{1,0:T(8,128)(2,1)S(1)}, bf16[896,768]{1,0:T(8,128)(2,1)}, u32[]{:S(2)}) copy-start(bf16[896,768]{1,0:T(8,128)(2,1)} %constant.37.clone.refs_3_) | copy-start | bytes 4128772
  7.2 0.9 %copy-start.7 = (bf16[496,128]{1,0:T(8,128)(2,1)S(1)}, bf16[496,128]{1,0:T(8,128)(2,1)}, u32[]{:S(2)}) copy-start(bf16[496,128]{1,0:T(8,128)(2,1)} %constant.39.clone.refs_5_) | copy-start | bytes 380932
  8.1 0.7 %copy-start.9 = (bf16[3,64,16]{1,2,0:T(8,128)(2,1)S(1)}, bf16[3,64,16]{1,2,0:T(8,128)(2,1)}, u32[]{:S(2)}) copy-start(bf16[3,64,16]{1,2,0:T(8,128)(2,1)} %param.11) | copy-start | bytes 18436
  11.7 0.6 copy-start.8
  12.3 25.4 %copy-start = (bf16[1792,512]{1,0:T(8,128)(2,1)}, bf16[1792,512]{1,0:T(8,128)(2,1)S(1)}, u32[]{:S(2)}) copy-start(bf16[1792,512]{1,0:T(8,128)(2,1)S(1)} %get-tuple-element.54.refs_5_.refs_12_.refs_13_.refs_6_.refs_15_) | copy-start | bytes 5505028
  12.3 9.0 %collective-permute-start.2 = (bf16[256,128]{1,0:T(8,128)(2,1)S(1)}, bf16[256,128]{1,0:T(8,128)(2,1)S(1)}, u32[]{:S(2)}, u32[]{:S(2)}) collective-permute-start(bf16[256,128]{1,0:T(8,128)(2,1)S(1)} %get-tuple-element.46), channel_id=1, source_target_pairs={{0,16},{16,0},{1,17},{17,1},{2,18},{18,2},{3,19},{19,3},{4,20},{20... | collective-permute-start | bytes 196616 | tf_op jit(solution)/shard_map/ppermute | solution.py:32
  15.3 6.0 %collective-permute-start = (bf16[128,128]{1,0:T(8,128)(2,1)S(1)}, bf16[128,128]{1,0:T(8,128)(2,1)S(1)}, u32[]{:S(2)}, u32[]{:S(2)}) collective-permute-start(bf16[128,128]{1,0:T(8,128)(2,1)S(1)} %get-tuple-element.44), channel_id=1, source_target_pairs={{0,1},{1,2},{2,3},{3,4},{4,5},{5,6},{6,7},{7,8},{8,9},{9,10},{10,1... | collective-permute-start | bytes 98312 | tf_op jit(solution)/shard_map/ppermute | solution.py:32
  15.3 6.0 %collective-permute-start.1 = (bf16[128,128]{1,0:T(8,128)(2,1)S(1)}, bf16[128,128]{1,0:T(8,128)(2,1)S(1)}, u32[]{:S(2)}, u32[]{:S(2)}) collective-permute-start(bf16[128,128]{1,0:T(8,128)(2,1)S(1)} %get-tuple-element.45), channel_id=1, source_target_pairs={{0,15},{1,0},{2,1},{3,2},{4,3},{5,4},{6,5},{7,6},{8,7},{9,8},{10,9... | collective-permute-start | bytes 98312 | tf_op jit(solution)/shard_map/ppermute | solution.py:32
  19.7 1.6 %copy-start.3 = (f32[16,8,512]{2,1,0:T(8,128)S(1)}, f32[16,8,512]{2,1,0:T(8,128)}, u32[]{:S(2)}) copy-start(f32[16,8,512]{2,1,0:T(8,128)} %param.10) | copy-start | bytes 786436
  22.8 6.2 %collective-permute-start.5 = (bf16[256,128]{1,0:T(8,128)(2,1)S(1)}, bf16[256,128]{1,0:T(8,128)(2,1)S(1)}, u32[]{:S(2)}, u32[]{:S(2)}) collective-permute-start(bf16[256,128]{1,0:T(8,128)(2,1)S(1)} %get-tuple-element.59), channel_id=1, source_target_pairs={{0,16},{16,0},{1,17},{17,1},{2,18},{18,2},{3,19},{19,3},{4,20},{20... | collective-permute-start | bytes 196616 | tf_op jit(solution)/shard_map/ppermute | solution.py:32
  22.9 6.1 %collective-permute-start.3 = (bf16[128,128]{1,0:T(8,128)(2,1)S(1)}, bf16[128,128]{1,0:T(8,128)(2,1)S(1)}, u32[]{:S(2)}, u32[]{:S(2)}) collective-permute-start(bf16[128,128]{1,0:T(8,128)(2,1)S(1)} %get-tuple-element.57), channel_id=1, source_target_pairs={{0,1},{1,2},{2,3},{3,4},{4,5},{5,6},{6,7},{7,8},{8,9},{9,10},{10,1... | collective-permute-start | bytes 98312 | tf_op jit(solution)/shard_map/ppermute | solution.py:32
  23.0 6.1 %collective-permute-start.4 = (bf16[128,128]{1,0:T(8,128)(2,1)S(1)}, bf16[128,128]{1,0:T(8,128)(2,1)S(1)}, u32[]{:S(2)}, u32[]{:S(2)}) collective-permute-start(bf16[128,128]{1,0:T(8,128)(2,1)S(1)} %get-tuple-element.58), channel_id=1, source_target_pairs={{0,15},{1,0},{2,1},{3,2},{4,3},{5,4},{6,5},{7,6},{8,7},{9,8},{10,9... | collective-permute-start | bytes 98312 | tf_op jit(solution)/shard_map/ppermute | solution.py:32
  31.3 8.0 %collective-permute-start.8 = (bf16[256,128]{1,0:T(8,128)(2,1)S(1)}, bf16[256,128]{1,0:T(8,128)(2,1)S(1)}, u32[]{:S(2)}, u32[]{:S(2)}) collective-permute-start(bf16[256,128]{1,0:T(8,128)(2,1)S(1)} %get-tuple-element.65), channel_id=1, source_target_pairs={{0,16},{16,0},{1,17},{17,1},{2,18},{18,2},{3,19},{19,3},{4,20},{20... | collective-permute-start | bytes 196616 | tf_op jit(solution)/shard_map/ppermute | solution.py:32
  33.3 6.0 %collective-permute-start.6 = (bf16[128,128]{1,0:T(8,128)(2,1)S(1)}, bf16[128,128]{1,0:T(8,128)(2,1)S(1)}, u32[]{:S(2)}, u32[]{:S(2)}) collective-permute-start(bf16[128,128]{1,0:T(8,128)(2,1)S(1)} %get-tuple-element.63), channel_id=1, source_target_pairs={{0,1},{1,2},{2,3},{3,4},{4,5},{5,6},{6,7},{7,8},{8,9},{9,10},{10,1... | collective-permute-start | bytes 98312 | tf_op jit(solution)/shard_map/ppermute | solution.py:32
  33.3 6.0 %collective-permute-start.7 = (bf16[128,128]{1,0:T(8,128)(2,1)S(1)}, bf16[128,128]{1,0:T(8,128)(2,1)S(1)}, u32[]{:S(2)}, u32[]{:S(2)}) collective-permute-start(bf16[128,128]{1,0:T(8,128)(2,1)S(1)} %get-tuple-element.64), channel_id=1, source_target_pairs={{0,15},{1,0},{2,1},{3,2},{4,3},{5,4},{6,5},{7,6},{8,7},{9,8},{10,9... | collective-permute-start | bytes 98312 | tf_op jit(solution)/shard_map/ppermute | solution.py:32
  39.3 9.0 %copy-start.1 = (bf16[1792,512]{1,0:T(8,128)(2,1)S(1)}, bf16[1792,512]{1,0:T(8,128)(2,1)}, u32[]{:S(2)}) copy-start(bf16[1792,512]{1,0:T(8,128)(2,1)} %copy-done) | copy-start | bytes 5505028
  43.7 6.2 %collective-permute-start.11 = (bf16[256,128]{1,0:T(8,128)(2,1)S(1)}, bf16[256,128]{1,0:T(8,128)(2,1)S(1)}, u32[]{:S(2)}, u32[]{:S(2)}) collective-permute-start(bf16[256,128]{1,0:T(8,128)(2,1)S(1)} %get-tuple-element.74), channel_id=1, source_target_pairs={{0,16},{16,0},{1,17},{17,1},{2,18},{18,2},{3,19},{19,3},{4,20},{20... | collective-permute-start | bytes 196616 | tf_op jit(solution)/shard_map/ppermute | solution.py:32
  43.9 6.0 %collective-permute-start.9 = (bf16[128,128]{1,0:T(8,128)(2,1)S(1)}, bf16[128,128]{1,0:T(8,128)(2,1)S(1)}, u32[]{:S(2)}, u32[]{:S(2)}) collective-permute-start(bf16[128,128]{1,0:T(8,128)(2,1)S(1)} %get-tuple-element.72), channel_id=1, source_target_pairs={{0,1},{1,2},{2,3},{3,4},{4,5},{5,6},{6,7},{7,8},{8,9},{9,10},{10,1... | collective-permute-start | bytes 98312 | tf_op jit(solution)/shard_map/ppermute | solution.py:32
  43.9 6.0 %collective-permute-start.10 = (bf16[128,128]{1,0:T(8,128)(2,1)S(1)}, bf16[128,128]{1,0:T(8,128)(2,1)S(1)}, u32[]{:S(2)}, u32[]{:S(2)}) collective-permute-start(bf16[128,128]{1,0:T(8,128)(2,1)S(1)} %get-tuple-element.73), channel_id=1, source_target_pairs={{0,15},{1,0},{2,1},{3,2},{4,3},{5,4},{6,5},{7,6},{8,7},{9,8},{10,9... | collective-permute-start | bytes 98312 | tf_op jit(solution)/shard_map/ppermute | solution.py:32
  53.6 0.7 %copy-start.6 = (f32[128,512]{1,0:T(8,128)}, f32[128,512]{1,0:T(8,128)S(1)}, u32[]{:S(2)}) copy-start(f32[128,512]{1,0:T(8,128)S(1)} %get-tuple-element.81.home_ref) | copy-start | bytes 786436
  54.3 6.2 %collective-permute-start.12 = (f32[24,512]{1,0:T(8,128)S(1)}, f32[24,512]{1,0:T(8,128)S(1)}, u32[]{:S(2)}, u32[]{:S(2)}) collective-permute-start(f32[24,512]{1,0:T(8,128)S(1)} %get-tuple-element.82), channel_id=1, source_target_pairs={{0,1},{1,2},{2,3},{3,4},{4,5},{5,6},{6,7},{7,8},{8,9},{9,10},{10,1... | collective-permute-start | bytes 147464 | tf_op jit(solution)/shard_map/ppermute | solution.py:32
  54.3 6.2 %collective-permute-start.13 = (f32[24,512]{1,0:T(8,128)S(1)}, f32[24,512]{1,0:T(8,128)S(1)}, u32[]{:S(2)}, u32[]{:S(2)}) collective-permute-start(f32[24,512]{1,0:T(8,128)S(1)} %get-tuple-element.83), channel_id=1, source_target_pairs={{0,15},{1,0},{2,1},{3,2},{4,3},{5,4},{6,5},{7,6},{8,7},{9,8},{10,9... | collective-permute-start | bytes 147464 | tf_op jit(solution)/shard_map/ppermute | solution.py:32
  60.5 0.6 copy-start.10
  60.5 0.6 copy-start.11

commit v8 on v7

--- a/solution.py
+++ b/solution.py
@@ -200,7 +200,12 @@
     n7 = P7**3
     n3 = P3**3
     wide = {"g7": (0, n7, 6 * LANE), "tm": (n7, n3, 6 * LANE), "mdst": (n7 + 3 * n3, n3, 6 * LANE)}
-    mid = {"d7t": (0, n7, n7), "lift_t": (3 * n7, n3, n7), "pj": (3 * n7 + n3, n3, n7)}
+    mid = {
+        "dx": (0, n7, n7),
+        "lift_t": (n7, n3, n7),
+        "pj": (n7 + n3, n3, n7),
+        "byz": (n7 + 4 * n3, LANE, LANE),
+    }
     narrow = {
         "bcast": (0, rows, local),
         "sel": (rows, 3 * local, rows),
@@ -276,7 +281,6 @@
     views = table_views(take(), take(), take(), local)
     bc_tab = views["bcast"]
     sel_tab = views["sel"]
-    d7_ref = views["d7t"]
     g7_ref = views["g7"]
     d3_ref = views["d3t"]
     mds_ref = views["mdst"]
@@ -388,11 +392,15 @@
     bcast = views["bcast"][...]
     sel = views["sel"][...]
     u = u_ref[...]
-    divergence = None
-    for d in range(3):
-        flux = (v7_ref[d].astype(f32) * u).astype(bf16)
-        term = _dot(flux, views["d7t"][d])
-        divergence = term if divergence is None else divergence + term
+    fluxes = [(v7_ref[d].astype(f32) * u).astype(bf16) for d in range(3)]
+    divergence = _dot(fluxes[0], views["dx"][0])
+    by = views["byz"][0]
+    bz = views["byz"][1]
+    chunks = []
+    for k in range(u.shape[1] // LANE):
+        part = slice(k * LANE, (k + 1) * LANE)
+        chunks.append(_dot(fluxes[1][:, part], by) + _dot(fluxes[2][:, part], bz))
+    divergence = divergence + jnp.concatenate(chunks, axis=1)
     out7[...] = _rate_source(u, pre, stc, bcast, sel, local) - divergence
     if coarse:
         c = c_ref[...]
@@ -606,13 +614,19 @@
     n3 = P3**3
     layouts = table_layout(rows, local_count)
     wide_np = np.zeros((n7 + 6 * n3, 6 * LANE), np.float32)
-    mid_np = np.zeros((3 * n7 + 4 * n3, n7), np.float32)
+    mid_np = np.zeros((n7 + 4 * n3 + 2 * LANE, n7), np.float32)
+    for d in (1, 2):
+        block = tab["d7t"][d][:LANE, :LANE].astype(np.float32)
+        assert np.array_equal(
+            tab["d7t"][d].astype(np.float32), np.kron(np.eye(n7 // LANE), block)
+        )
     narrow_np = np.zeros((2 * rows + 3 * local_count + 3 * n3, rows), np.float32)
     pieces = {
         "g7": tab["g7"][None],
         "tm": tab["tm"],
         "mdst": np.transpose(tab["mds"], (0, 2, 1)),
-        "d7t": tab["d7t"],
+        "dx": tab["d7t"][0:1],
+        "byz": np.stack([tab["d7t"][1][:LANE, :LANE], tab["d7t"][2][:LANE, :LANE]]),
         "lift_t": tab["lift"].T[None],
         "pj": np.transpose(tab["pjt"], (0, 2, 1)),
         "bcast": bcast_np[None],

time: 64.2 us -> 60.8 us (0.947)
  Pallas kernels: 20.7 us -> 17.2 us
    pallas_call x4, Pallas kernels: 11.7 us -> 8.61 us  [run_stage(): pl.pallas_call(kernel, out_shape=out_shapes, in_specs=[_vmem() for _ in i...]
    unnamed x24 -> x20, local copies, waits for them, and re-layouts: 7.34 us -> 7.05 us
where the time goes in v8:
time: 60.8 us; the launch traced here: 60.4 us
  starting transfers between devices  27.5 us (45%)
  Pallas kernels  17.2 us (28%)
  local copies, waits for them, and re-layouts  9.11 us (15%)
  waiting for transfers between devices  4.42 us (7%)
  other arithmetic  1.37 us (2%)
  between operations  0.76 us (1%)
    ppermute x14, starting transfers between devices, shifted(): return lax.ppermute(value, axis, pairs)  27.5 us
    pallas_call x4, Pallas kernels, run_stage(): pl.pallas_call(kernel, out_shape=out_shapes, in_specs=[_vmem() for _ in i...  8.61 us
    unnamed x20, local copies, waits for them, and re-layouts  7.05 us
    ppermute x14, waiting for transfers between devices, shifted(): return lax.ppermute(value, axis, pairs)  4.42 us
    pallas_call x4, Pallas kernels, run_bulk(): pl.pallas_call(functools.partial(bulk_kernel, coarse, local), out_shape=o...  3.02 us
    pallas_call x1, Pallas kernels, per_device(): pl.pallas_call(functools.partial(setup_entry, local_count, field_count, l...  2.87 us
    pallas_call x1, Pallas kernels, per_device(): pl.pallas_call(functools.partial(final_kernel, field_count, HOLD7), out_s...  2.73 us
  transfers between devices with their start and end apart: 14, of which 6 were waited for; matrix products, arithmetic and copies ran while one was open for 1% of the time, Pallas kernels for 5%

profile of v8, /device:TPU:0, one launch (start us, length us, event | category | flops | bytes accessed | tf_op | source)
XLA Modules:
  0.0 60.4 jit_solution(12987983868940291712)
XLA Ops:
  0.6 0.7 %pad_bitcast_fusion = f32[1,16]{1,0:T(1,128)S(1)} fusion(f32[8]{0:T(128)} %param.13), kind=kLoop, calls=%fused_computation.9 | loop fusion | bytes 96 | tf_op jit(solution)/shard_map/stack | solution.py:603
  1.3 0.7 %convert_bitcast_fusion.1 = (f32[1,16]{1,0:T(1,128)S(1)}, f32[1,16]{1,0:T(1,128)S(1)}) fusion(s32[16]{0:T(128)} %param.16, s32[16]{0:T(128)} %param.15), kind=kLoop, calls=%fused_computation.8 | loop fusion | flops 32 | bytes 256 | tf_op jit(solution)/shard_map/stack | solution.py:603
  2.0 0.7 %convert_bitcast_fusion = f32[6,16]{1,0:T(8,128)S(1)} fusion(s32[16,6]{0,1:T(8,128)} %param.14, s32[]{:T(128)S(6)} %add.11), kind=kLoop, calls=%fused_computation.5 | loop fusion | flops 2016 | bytes 772 | tf_op jit(solution)/shard_map/transpose | solution.py:602
  2.7 0.7 %concatenate.3 = f32[10,16]{1,0:T(8,128)S(1)} concatenate(f32[6,16]{1,0:T(8,128)S(1)} %convert_bitcast_fusion, f32[1,16]{1,0:T(1,128)S(1)} %get-tuple-element.87, f32[1,16]{1,0:T(1,128)} %bitcast.18, f32[1,16]{1,0:T(1,128)S(1)} %pad_bitcast_fusion, f32[1,16]{1,0:T(1,128)S(1)} %get-tuple-element.86), dimensions={0} | concatenate | bytes 1280 | tf_op jit(solution)/shard_map/concatenate | solution.py:600
  3.4 0.9 %copy-done = f32[16,8,512]{2,1,0:T(8,128)S(1)} copy-done((f32[16,8,512]{2,1,0:T(8,128)S(1)}, f32[16,8,512]{2,1,0:T(8,128)}, u32[]{:S(2)}) %copy-start) | copy-done | bytes 262168
  4.3 1.3 %copy-done.2 = bf16[896,768]{1,0:T(8,128)(2,1)S(1)} copy-done((bf16[896,768]{1,0:T(8,128)(2,1)S(1)}, bf16[896,768]{1,0:T(8,128)(2,1)}, u32[]{:S(2)}) %copy-start.2) | copy-done | bytes 1376280
  5.7 1.2 %copy-done.3 = bf16[1024,512]{1,0:T(8,128)(2,1)S(1)} copy-done((bf16[1024,512]{1,0:T(8,128)(2,1)S(1)}, bf16[1024,512]{1,0:T(8,128)(2,1)}, u32[]{:S(2)}) %copy-start.3) | copy-done | bytes 1048600
  6.9 0.9 %copy-done.5 = bf16[496,128]{1,0:T(8,128)(2,1)S(1)} copy-done((bf16[496,128]{1,0:T(8,128)(2,1)S(1)}, bf16[496,128]{1,0:T(8,128)(2,1)}, u32[]{:S(2)}) %copy-start.5) | copy-done | bytes 127000
  7.8 0.7 %copy-done.7 = bf16[3,64,16]{1,2,0:T(8,128)(2,1)S(1)} copy-done((bf16[3,64,16]{1,2,0:T(8,128)(2,1)S(1)}, bf16[3,64,16]{1,2,0:T(8,128)(2,1)}, u32[]{:S(2)}) %copy-start.7) | copy-done | bytes 6168
  8.5 2.9 %shard_map.113 = (bf16[3,128,512]{2,1,0:T(8,128)(2,1)S(1)}, f32[128,768]{1,0:T(8,128)S(1)}, f32[3,128,64]{2,1,0:T(8,128)S(1)}, f32[128,768]{1,0:T(8,128)S(1)}, b...) custom-call(f32[128,512]{1,0:T(8,128)S(1)} %bitcast.12, ...), custom_call_target="tpu_custom_call" | custom-call | tf_op jit(solution)/shard_map/pallas_call | solution.py:679
  12.0 3.0 %collective-permute-start.2 = (bf16[256,128]{1,0:T(8,128)(2,1)S(1)}, bf16[256,128]{1,0:T(8,128)(2,1)S(1)}, u32[]{:S(2)}, u32[]{:S(2)}) collective-permute-start(bf16[256,128]{1,0:T(8,128)(2,1)S(1)} %get-tuple-element.46), channel_id=1, source_target_pairs={{0,16},{16,0},{1,17},{17,1},{2,18},{18,2},{3,19},{19,3},{4,20},{20... | collective-permute-start | bytes 196616 | tf_op jit(solution)/shard_map/ppermute | solution.py:32
  15.0 4.4 %collective-permute-start.1 = (bf16[128,128]{1,0:T(8,128)(2,1)S(1)}, bf16[128,128]{1,0:T(8,128)(2,1)S(1)}, u32[]{:S(2)}, u32[]{:S(2)}) collective-permute-start(bf16[128,128]{1,0:T(8,128)(2,1)S(1)} %get-tuple-element.45), channel_id=1, source_target_pairs={{0,15},{1,0},{2,1},{3,2},{4,3},{5,4},{6,5},{7,6},{8,7},{9,8},{10,9... | collective-permute-start | bytes 98312 | tf_op jit(solution)/shard_map/ppermute | solution.py:32
  19.4 0.6 %shard_map.114.refs_14_ = f32[128,512]{1,0:T(8,128)S(1)} custom-call(f32[128,512]{1,0:T(8,128)S(1)} %bitcast.13, bf16[3,128,512]{2,1,0:T(8,128)(2,1)S(1)} %get-tuple-element.49.refs_1_.refs_7_.refs_8_.refs_2_.refs_10_, f32[16,1]{1,0:T(8,128)S(1)} %get-tuple-element.51.refs_2_.refs_9_.refs_10_.refs_3_.refs_12_, ...), custom_call_target="tpu_custom_call" | custom-call | tf_op jit(solution)/shard_map/pallas_call | solution.py:416
  20.1 0.9 %collective-permute-done.refs_1_ = bf16[128,128]{1,0:T(8,128)(2,1)S(1)} collective-permute-done((bf16[128,128]{1,0:T(8,128)(2,1)S(1)}, bf16[128,128]{1,0:T(8,128)(2,1)S(1)}, u32[]{:S(2)}, u32[]{:S(2)}) %collective-permute-start) | collective-permute-done | bytes 32800 | tf_op jit(solution)/shard_map/ppermute | solution.py:32
  21.0 1.5 %shard_map.115 = (f32[128,512]{1,0:T(8,128)S(1)}, bf16[128,128]{1,0:T(8,128)(2,1)S(1)}, bf16[128,128]{1,0:T(8,128)(2,1)S(1)}, bf16[256,128]{1,0:T(8,128)(2,1)S(1)}) custom-call(f32[128,512]{1,0:T(8,128)S(1)} %bitcast.14, bf16[128,128]{1,0:T(8,128)(2,1)S(1)} %collective-permute-done.refs_1_, bf16[128,128]{1,0:T(8,128)(2,1)S(1)} %collective-permute-done.1.refs_2_, ...), custom_call_target="tpu_custom_call" | custom-call | tf_op jit(solution)/shard_map/pallas_call | solution.py:428
  22.6 4.5 %collective-permute-start.4 = (bf16[128,128]{1,0:T(8,128)(2,1)S(1)}, bf16[128,128]{1,0:T(8,128)(2,1)S(1)}, u32[]{:S(2)}, u32[]{:S(2)}) collective-permute-start(bf16[128,128]{1,0:T(8,128)(2,1)S(1)} %get-tuple-element.58), channel_id=1, source_target_pairs={{0,15},{1,0},{2,1},{3,2},{4,3},{5,4},{6,5},{7,6},{8,7},{9,8},{10,9... | collective-permute-start | bytes 98312 | tf_op jit(solution)/shard_map/ppermute | solution.py:32
  27.8 0.9 %collective-permute-done.3.refs_2_ = bf16[128,128]{1,0:T(8,128)(2,1)S(1)} collective-permute-done((bf16[128,128]{1,0:T(8,128)(2,1)S(1)}, bf16[128,128]{1,0:T(8,128)(2,1)S(1)}, u32[]{:S(2)}, u32[]{:S(2)}) %collective-permute-start.3) | collective-permute-done | bytes 32800 | tf_op jit(solution)/shard_map/ppermute | solution.py:32
  28.7 2.3 %shard_map.117 = (f32[128,512]{1,0:T(8,128)S(1)}, f32[128,64]{1,0:T(8,128)S(1)}, bf16[128,128]{1,0:T(8,128)(2,1)S(1)}, bf16[128,128]{1,0:T(8,128)(2,1)S(1)}, bf16[256,128]{1,0:T(8,128)(2,1)S(1)}) custom-call(f32[128,512]{1,0:T(8,128)S(1)} %get-tuple-element.56.refs_0_, f32[128,512]{1,0:T(8,128)S(1)} %bitcast.15, ...), custom_call_target="tpu_custom_call" | custom-call | tf_op jit(solution)/shard_map/pallas_call | solution.py:428
  31.0 2.0 %collective-permute-start.8 = (bf16[256,128]{1,0:T(8,128)(2,1)S(1)}, bf16[256,128]{1,0:T(8,128)(2,1)S(1)}, u32[]{:S(2)}, u32[]{:S(2)}) collective-permute-start(bf16[256,128]{1,0:T(8,128)(2,1)S(1)} %get-tuple-element.65), channel_id=1, source_target_pairs={{0,16},{16,0},{1,17},{17,1},{2,18},{18,2},{3,19},{19,3},{4,20},{20... | collective-permute-start | bytes 196616 | tf_op jit(solution)/shard_map/ppermute | solution.py:32
  33.0 4.4 %collective-permute-start.7 = (bf16[128,128]{1,0:T(8,128)(2,1)S(1)}, bf16[128,128]{1,0:T(8,128)(2,1)S(1)}, u32[]{:S(2)}, u32[]{:S(2)}) collective-permute-start(bf16[128,128]{1,0:T(8,128)(2,1)S(1)} %get-tuple-element.64), channel_id=1, source_target_pairs={{0,15},{1,0},{2,1},{3,2},{4,3},{5,4},{6,5},{7,6},{8,7},{9,8},{10,9... | collective-permute-start | bytes 98312 | tf_op jit(solution)/shard_map/ppermute | solution.py:32
  37.4 0.9 %shard_map.118 = (f32[128,512]{1,0:T(8,128)S(1)}, f32[128,64]{1,0:T(8,128)S(1)}) custom-call(f32[128,512]{1,0:T(8,128)S(1)} %get-tuple-element.61.refs_0_.refs_2_, f32[128,64]{1,0:T(8,128)S(1)} %get-tuple-element.62.refs_1_.refs_3_, bf16[3,128,512]{2,1,0:T(8,128)(2,1)S(1)} %get-tuple-element.49.refs_1_.refs_7_.refs_8_.refs_2_.refs_10_, ...), custom_call_target="tpu_custom_call" | custom-call | tf_op jit(solution)/shard_map/pallas_call | solution.py:416
  38.3 0.7 %collective-permute-done.6.refs_2_ = bf16[128,128]{1,0:T(8,128)(2,1)S(1)} collective-permute-done((bf16[128,128]{1,0:T(8,128)(2,1)S(1)}, bf16[128,128]{1,0:T(8,128)(2,1)S(1)}, u32[]{:S(2)}, u32[]{:S(2)}) %collective-permute-start.6) | collective-permute-done | bytes 32800 | tf_op jit(solution)/shard_map/ppermute | solution.py:32
  39.0 2.7 %shard_map.119 = (f32[128,512]{1,0:T(8,128)S(1)}, f32[128,64]{1,0:T(8,128)S(1)}, bf16[128,128]{1,0:T(8,128)(2,1)S(1)}, bf16[128,128]{1,0:T(8,128)(2,1)S(1)}, bf16[256,128]{1,0:T(8,128)(2,1)S(1)}) custom-call(f32[128,512]{1,0:T(8,128)S(1)} %get-tuple-element.61.refs_0_.refs_2_, f32[128,64]{1,0:T(8,128)S(1)} %get-tuple-element.62.refs_1_.refs_3_, ...), custom_call_target="tpu_custom_call" | custom-call | tf_op jit(solution)/shard_map/pallas_call | solution.py:428
  41.9 4.4 %collective-permute-start.10 = (bf16[128,128]{1,0:T(8,128)(2,1)S(1)}, bf16[128,128]{1,0:T(8,128)(2,1)S(1)}, u32[]{:S(2)}, u32[]{:S(2)}) collective-permute-start(bf16[128,128]{1,0:T(8,128)(2,1)S(1)} %get-tuple-element.73), channel_id=1, source_target_pairs={{0,15},{1,0},{2,1},{3,2},{4,3},{5,4},{6,5},{7,6},{8,7},{9,8},{10,9... | collective-permute-start | bytes 98312 | tf_op jit(solution)/shard_map/ppermute | solution.py:32
  46.3 0.9 %shard_map.120 = (f32[128,512]{1,0:T(8,128)S(1)}, f32[128,64]{1,0:T(8,128)S(1)}) custom-call(f32[128,512]{1,0:T(8,128)S(1)} %get-tuple-element.70.refs_0_, f32[128,64]{1,0:T(8,128)S(1)} %get-tuple-element.71.refs_1_, bf16[3,128,512]{2,1,0:T(8,128)(2,1)S(1)} %get-tuple-element.49.refs_1_.refs_7_.refs_8_.refs_2_.refs_10_, ...), custom_call_target="tpu_custom_call" | custom-call | tf_op jit(solution)/shard_map/pallas_call | solution.py:416
  47.2 0.7 %collective-permute-done.9.refs_4_ = bf16[128,128]{1,0:T(8,128)(2,1)S(1)} collective-permute-done((bf16[128,128]{1,0:T(8,128)(2,1)S(1)}, bf16[128,128]{1,0:T(8,128)(2,1)S(1)}, u32[]{:S(2)}, u32[]{:S(2)}) %collective-permute-start.9) | collective-permute-done | bytes 32800 | tf_op jit(solution)/shard_map/ppermute | solution.py:32
  47.9 2.2 %shard_map.121 = (f32[128,512]{1,0:T(8,128)S(1)}, f32[128,64]{1,0:T(8,128)S(1)}, f32[24,512]{1,0:T(8,128)S(1)}, f32[24,512]{1,0:T(8,128)S(1)}) custom-call(f32[128,512]{1,0:T(8,128)S(1)} %get-tuple-element.70.refs_0_, f32[128,64]{1,0:T(8,128)S(1)} %get-tuple-element.71.refs_1_, f32[128,512]{1,0:T(8,128)S(1)} %get-tuple-element.61.refs_0_.refs_2_, ...), custom_call_target="tpu_custom_call" | custom-call | tf_op jit(solution)/shard_map/pallas_call | solution.py:428
  50.1 0.7 %copy-done.4 = f32[128,512]{1,0:T(8,128)} copy-done((f32[128,512]{1,0:T(8,128)}, f32[128,512]{1,0:T(8,128)S(1)}, u32[]{:S(2)}) %copy-start.4) | copy-done | bytes 262168
  50.8 4.4 %collective-permute-start.13 = (f32[24,512]{1,0:T(8,128)S(1)}, f32[24,512]{1,0:T(8,128)S(1)}, u32[]{:S(2)}, u32[]{:S(2)}) collective-permute-start(f32[24,512]{1,0:T(8,128)S(1)} %get-tuple-element.83), channel_id=1, source_target_pairs={{0,15},{1,0},{2,1},{3,2},{4,3},{5,4},{6,5},{7,6},{8,7},{9,8},{10,9... | collective-permute-start | bytes 147464 | tf_op jit(solution)/shard_map/ppermute | solution.py:32
  55.3 0.7 %reshape.15 = f32[16,512]{1,0:T(8,128)} reshape(f32[128,64]{1,0:T(8,128)S(1)} %get-tuple-element.85) | data formatting | bytes 65536 | tf_op jit(solution)/shard_map/reshape | solution.py:738
  56.0 1.1 %collective-permute-done.12.from_l_ref = f32[24,512]{1,0:T(8,128)S(1)} collective-permute-done((f32[24,512]{1,0:T(8,128)S(1)}, f32[24,512]{1,0:T(8,128)S(1)}, u32[]{:S(2)}, u32[]{:S(2)}) %collective-permute-start.12) | collective-permute-done | bytes 49184 | tf_op jit(solution)/shard_map/ppermute | solution.py:32
  57.7 2.7 %shard_map.122 = f32[96,512]{1,0:T(8,128)} custom-call(f32[128,512]{1,0:T(8,128)} %copy-done.4, f32[24,512]{1,0:T(8,128)} %copy-done.8, f32[24,512]{1,0:T(8,128)} %copy-done.9, f32[128,128]{1,0:T(8,128)} %copy-done.6), custom_call_target="tpu_custom_call" | custom-call | tf_op jit(solution)/shard_map/pallas_call | solution.py:731
  (32 shorter events, 2.3 us)
Async XLA Ops:
  3.4 0.9 %copy-start = (f32[16,8,512]{2,1,0:T(8,128)S(1)}, f32[16,8,512]{2,1,0:T(8,128)}, u32[]{:S(2)}) copy-start(f32[16,8,512]{2,1,0:T(8,128)} %param.10) | copy-start | bytes 786436
  4.3 1.3 %copy-start.2 = (bf16[896,768]{1,0:T(8,128)(2,1)S(1)}, bf16[896,768]{1,0:T(8,128)(2,1)}, u32[]{:S(2)}) copy-start(bf16[896,768]{1,0:T(8,128)(2,1)} %constant.37.clone.refs_3_) | copy-start | bytes 4128772
  5.7 1.2 %copy-start.3 = (bf16[1024,512]{1,0:T(8,128)(2,1)S(1)}, bf16[1024,512]{1,0:T(8,128)(2,1)}, u32[]{:S(2)}) copy-start(bf16[1024,512]{1,0:T(8,128)(2,1)} %constant.38.clone.refs_4_) | copy-start | bytes 3145732
  6.9 0.9 %copy-start.5 = (bf16[496,128]{1,0:T(8,128)(2,1)S(1)}, bf16[496,128]{1,0:T(8,128)(2,1)}, u32[]{:S(2)}) copy-start(bf16[496,128]{1,0:T(8,128)(2,1)} %constant.39.clone.refs_5_) | copy-start | bytes 380932
  7.8 0.7 %copy-start.7 = (bf16[3,64,16]{1,2,0:T(8,128)(2,1)S(1)}, bf16[3,64,16]{1,2,0:T(8,128)(2,1)}, u32[]{:S(2)}) copy-start(bf16[3,64,16]{1,2,0:T(8,128)(2,1)} %param.11) | copy-start | bytes 18436
  11.4 0.6 %copy-start.6 = (f32[128,128]{1,0:T(8,128)}, f32[128,128]{1,0:T(8,128)S(1)}, u32[]{:S(2)}) copy-start(f32[128,128]{1,0:T(8,128)S(1)} %get-tuple-element.84.hinfo_ref) | copy-start | bytes 196612
  12.0 9.0 %collective-permute-start.2 = (bf16[256,128]{1,0:T(8,128)(2,1)S(1)}, bf16[256,128]{1,0:T(8,128)(2,1)S(1)}, u32[]{:S(2)}, u32[]{:S(2)}) collective-permute-start(bf16[256,128]{1,0:T(8,128)(2,1)S(1)} %get-tuple-element.46), channel_id=1, source_target_pairs={{0,16},{16,0},{1,17},{17,1},{2,18},{18,2},{3,19},{19,3},{4,20},{20... | collective-permute-start | bytes 196616 | tf_op jit(solution)/shard_map/ppermute | solution.py:32
  15.0 6.0 %collective-permute-start = (bf16[128,128]{1,0:T(8,128)(2,1)S(1)}, bf16[128,128]{1,0:T(8,128)(2,1)S(1)}, u32[]{:S(2)}, u32[]{:S(2)}) collective-permute-start(bf16[128,128]{1,0:T(8,128)(2,1)S(1)} %get-tuple-element.44), channel_id=1, source_target_pairs={{0,1},{1,2},{2,3},{3,4},{4,5},{5,6},{6,7},{7,8},{8,9},{9,10},{10,1... | collective-permute-start | bytes 98312 | tf_op jit(solution)/shard_map/ppermute | solution.py:32
  15.0 6.0 %collective-permute-start.1 = (bf16[128,128]{1,0:T(8,128)(2,1)S(1)}, bf16[128,128]{1,0:T(8,128)(2,1)S(1)}, u32[]{:S(2)}, u32[]{:S(2)}) collective-permute-start(bf16[128,128]{1,0:T(8,128)(2,1)S(1)} %get-tuple-element.45), channel_id=1, source_target_pairs={{0,15},{1,0},{2,1},{3,2},{4,3},{5,4},{6,5},{7,6},{8,7},{9,8},{10,9... | collective-permute-start | bytes 98312 | tf_op jit(solution)/shard_map/ppermute | solution.py:32
  19.4 1.6 %copy-start.1 = (f32[16,8,512]{2,1,0:T(8,128)S(1)}, f32[16,8,512]{2,1,0:T(8,128)}, u32[]{:S(2)}) copy-start(f32[16,8,512]{2,1,0:T(8,128)} %param.10) | copy-start | bytes 786436
  22.5 6.2 %collective-permute-start.5 = (bf16[256,128]{1,0:T(8,128)(2,1)S(1)}, bf16[256,128]{1,0:T(8,128)(2,1)S(1)}, u32[]{:S(2)}, u32[]{:S(2)}) collective-permute-start(bf16[256,128]{1,0:T(8,128)(2,1)S(1)} %get-tuple-element.59), channel_id=1, source_target_pairs={{0,16},{16,0},{1,17},{17,1},{2,18},{18,2},{3,19},{19,3},{4,20},{20... | collective-permute-start | bytes 196616 | tf_op jit(solution)/shard_map/ppermute | solution.py:32
  22.6 6.1 %collective-permute-start.3 = (bf16[128,128]{1,0:T(8,128)(2,1)S(1)}, bf16[128,128]{1,0:T(8,128)(2,1)S(1)}, u32[]{:S(2)}, u32[]{:S(2)}) collective-permute-start(bf16[128,128]{1,0:T(8,128)(2,1)S(1)} %get-tuple-element.57), channel_id=1, source_target_pairs={{0,1},{1,2},{2,3},{3,4},{4,5},{5,6},{6,7},{7,8},{8,9},{9,10},{10,1... | collective-permute-start | bytes 98312 | tf_op jit(solution)/shard_map/ppermute | solution.py:32
  22.6 6.1 %collective-permute-start.4 = (bf16[128,128]{1,0:T(8,128)(2,1)S(1)}, bf16[128,128]{1,0:T(8,128)(2,1)S(1)}, u32[]{:S(2)}, u32[]{:S(2)}) collective-permute-start(bf16[128,128]{1,0:T(8,128)(2,1)S(1)} %get-tuple-element.58), channel_id=1, source_target_pairs={{0,15},{1,0},{2,1},{3,2},{4,3},{5,4},{6,5},{7,6},{8,7},{9,8},{10,9... | collective-permute-start | bytes 98312 | tf_op jit(solution)/shard_map/ppermute | solution.py:32
  31.0 8.0 %collective-permute-start.8 = (bf16[256,128]{1,0:T(8,128)(2,1)S(1)}, bf16[256,128]{1,0:T(8,128)(2,1)S(1)}, u32[]{:S(2)}, u32[]{:S(2)}) collective-permute-start(bf16[256,128]{1,0:T(8,128)(2,1)S(1)} %get-tuple-element.65), channel_id=1, source_target_pairs={{0,16},{16,0},{1,17},{17,1},{2,18},{18,2},{3,19},{19,3},{4,20},{20... | collective-permute-start | bytes 196616 | tf_op jit(solution)/shard_map/ppermute | solution.py:32
  33.0 6.0 %collective-permute-start.6 = (bf16[128,128]{1,0:T(8,128)(2,1)S(1)}, bf16[128,128]{1,0:T(8,128)(2,1)S(1)}, u32[]{:S(2)}, u32[]{:S(2)}) collective-permute-start(bf16[128,128]{1,0:T(8,128)(2,1)S(1)} %get-tuple-element.63), channel_id=1, source_target_pairs={{0,1},{1,2},{2,3},{3,4},{4,5},{5,6},{6,7},{7,8},{8,9},{9,10},{10,1... | collective-permute-start | bytes 98312 | tf_op jit(solution)/shard_map/ppermute | solution.py:32
  33.0 6.0 %collective-permute-start.7 = (bf16[128,128]{1,0:T(8,128)(2,1)S(1)}, bf16[128,128]{1,0:T(8,128)(2,1)S(1)}, u32[]{:S(2)}, u32[]{:S(2)}) collective-permute-start(bf16[128,128]{1,0:T(8,128)(2,1)S(1)} %get-tuple-element.64), channel_id=1, source_target_pairs={{0,15},{1,0},{2,1},{3,2},{4,3},{5,4},{6,5},{7,6},{8,7},{9,8},{10,9... | collective-permute-start | bytes 98312 | tf_op jit(solution)/shard_map/ppermute | solution.py:32
  41.7 6.2 %collective-permute-start.11 = (bf16[256,128]{1,0:T(8,128)(2,1)S(1)}, bf16[256,128]{1,0:T(8,128)(2,1)S(1)}, u32[]{:S(2)}, u32[]{:S(2)}) collective-permute-start(bf16[256,128]{1,0:T(8,128)(2,1)S(1)} %get-tuple-element.74), channel_id=1, source_target_pairs={{0,16},{16,0},{1,17},{17,1},{2,18},{18,2},{3,19},{19,3},{4,20},{20... | collective-permute-start | bytes 196616 | tf_op jit(solution)/shard_map/ppermute | solution.py:32
  41.9 6.0 %collective-permute-start.9 = (bf16[128,128]{1,0:T(8,128)(2,1)S(1)}, bf16[128,128]{1,0:T(8,128)(2,1)S(1)}, u32[]{:S(2)}, u32[]{:S(2)}) collective-permute-start(bf16[128,128]{1,0:T(8,128)(2,1)S(1)} %get-tuple-element.72), channel_id=1, source_target_pairs={{0,1},{1,2},{2,3},{3,4},{4,5},{5,6},{6,7},{7,8},{8,9},{9,10},{10,1... | collective-permute-start | bytes 98312 | tf_op jit(solution)/shard_map/ppermute | solution.py:32
  41.9 6.0 %collective-permute-start.10 = (bf16[128,128]{1,0:T(8,128)(2,1)S(1)}, bf16[128,128]{1,0:T(8,128)(2,1)S(1)}, u32[]{:S(2)}, u32[]{:S(2)}) collective-permute-start(bf16[128,128]{1,0:T(8,128)(2,1)S(1)} %get-tuple-element.73), channel_id=1, source_target_pairs={{0,15},{1,0},{2,1},{3,2},{4,3},{5,4},{6,5},{7,6},{8,7},{9,8},{10,9... | collective-permute-start | bytes 98312 | tf_op jit(solution)/shard_map/ppermute | solution.py:32
  50.1 0.7 %copy-start.4 = (f32[128,512]{1,0:T(8,128)}, f32[128,512]{1,0:T(8,128)S(1)}, u32[]{:S(2)}) copy-start(f32[128,512]{1,0:T(8,128)S(1)} %get-tuple-element.81.home_ref) | copy-start | bytes 786436
  50.8 6.2 %collective-permute-start.12 = (f32[24,512]{1,0:T(8,128)S(1)}, f32[24,512]{1,0:T(8,128)S(1)}, u32[]{:S(2)}, u32[]{:S(2)}) collective-permute-start(f32[24,512]{1,0:T(8,128)S(1)} %get-tuple-element.82), channel_id=1, source_target_pairs={{0,1},{1,2},{2,3},{3,4},{4,5},{5,6},{6,7},{7,8},{8,9},{9,10},{10,1... | collective-permute-start | bytes 147464 | tf_op jit(solution)/shard_map/ppermute | solution.py:32
  50.8 6.2 %collective-permute-start.13 = (f32[24,512]{1,0:T(8,128)S(1)}, f32[24,512]{1,0:T(8,128)S(1)}, u32[]{:S(2)}, u32[]{:S(2)}) collective-permute-start(f32[24,512]{1,0:T(8,128)S(1)} %get-tuple-element.83), channel_id=1, source_target_pairs={{0,15},{1,0},{2,1},{3,2},{4,3},{5,4},{6,5},{7,6},{8,7},{9,8},{10,9... | collective-permute-start | bytes 147464 | tf_op jit(solution)/shard_map/ppermute | solution.py:32
  57.0 0.6 %copy-start.8 = (f32[24,512]{1,0:T(8,128)}, f32[24,512]{1,0:T(8,128)S(1)}, u32[]{:S(2)}) copy-start(f32[24,512]{1,0:T(8,128)S(1)} %collective-permute-done.12.from_l_ref) | copy-start | bytes 147460
  57.1 0.6 %copy-start.9 = (f32[24,512]{1,0:T(8,128)}, f32[24,512]{1,0:T(8,128)S(1)}, u32[]{:S(2)}) copy-start(f32[24,512]{1,0:T(8,128)S(1)} %collective-permute-done.13.from_r_ref) | copy-start | bytes 147460

commit v9 on v8

--- a/solution.py
+++ b/solution.py
@@ -183,46 +183,50 @@
 
 
 class View:
-    def __init__(self, ref, start, rows, width):
+    def __init__(self, ref, start, rows, width, lane0):
         self.ref = ref
         self.start = start
         self.rows = rows
         self.width = width
+        self.lane0 = lane0
 
     def __getitem__(self, k):
         if k is Ellipsis:
             k = 0
         top = self.start + k * self.rows
-        return self.ref[top : top + self.rows, 0 : self.width]
+        return self.ref[top : top + self.rows, self.lane0 : self.lane0 + self.width]
 
 
 def table_layout(rows, local):
     n7 = P7**3
     n3 = P3**3
-    wide = {"g7": (0, n7, 6 * LANE), "tm": (n7, n3, 6 * LANE), "mdst": (n7 + 3 * n3, n3, 6 * LANE)}
-    mid = {
-        "dx": (0, n7, n7),
-        "lift_t": (n7, n3, n7),
-        "pj": (n7 + n3, n3, n7),
-        "byz": (n7 + 4 * n3, LANE, LANE),
+    wide = 6 * LANE
+    base = n7 + 6 * n3
+    side = 4 * LANE
+    return {
+        "g7": (0, n7, wide, 0),
+        "tm": (n7, n3, wide, 0),
+        "mdst": (n7 + 3 * n3, n3, wide, 0),
+        "dx": (base, n7, n7, 0),
+        "lift_t": (base + n7, n3, n7, 0),
+        "pj": (base + n7 + n3, n3, n7, 0),
+        "byz": (base, LANE, LANE, 5 * LANE),
+        "bcast": (base, rows, local, side),
+        "sel": (base + rows, 3 * local, rows, side),
+        "fsel": (base + rows + 3 * local, rows, local, side),
+        "d3t": (base + 2 * rows + 3 * local, n3, n3, side),
     }
-    narrow = {
-        "bcast": (0, rows, local),
-        "sel": (rows, 3 * local, rows),
-        "fsel": (rows + 3 * local, rows, local),
-        "d3t": (2 * rows + 3 * local, n3, n3),
+
+
+def table_rows():
+    return P7**3 + 6 * P3**3 + P7**3 + 4 * P3**3
+
+
+def table_views(tab_ref, rows, local):
+    return {
+        name: View(tab_ref, start, count, width, lane0)
+        for name, (start, count, width, lane0) in table_layout(rows, local).items()
     }
-    return wide, mid, narrow
-
-
-def table_views(wide_ref, mid_ref, narrow_ref, local):
-    rows = narrow_ref.shape[1]
-    layouts = table_layout(rows, local)
-    views = {}
-    for ref, layout in zip((wide_ref, mid_ref, narrow_ref), layouts):
-        for name, (start, count, width) in layout.items():
-            views[name] = View(ref, start, count, width)
-    return views
 
 
 def _full(x, parts_ref):
@@ -278,7 +282,7 @@
     m7_ref = take()
     pre_ref = take()
     stc_ref = take()
-    views = table_views(take(), take(), take(), local)
+    views = table_views(take(), u_ref.shape[0], local)
     bc_tab = views["bcast"]
     sel_tab = views["sel"]
     g7_ref = views["g7"]
@@ -383,7 +387,7 @@
     u_ref = refs.pop(0)
     c_ref = refs.pop(0) if coarse else None
     v7_ref, pre_ref, stc_ref = refs.pop(0), refs.pop(0), refs.pop(0)
-    views = table_views(refs.pop(0), refs.pop(0), refs.pop(0), local)
+    views = table_views(refs.pop(0), u_ref.shape[0], local)
     v3_ref = refs.pop(0) if coarse else None
     out7 = refs.pop(0)
     out3 = refs.pop(0) if coarse else None
@@ -434,11 +438,11 @@
     )(*inputs)
 
 
-def setup_kernel(local, fields, u_ref, vt_ref, packed_ref, wide_ref, mid_ref, narrow_ref, v7_out, m7_out, v3_out, m3_out, pl_out, pr_out,
+def setup_kernel(local, fields, u_ref, vt_ref, packed_ref, tab_ref, v7_out, m7_out, v3_out, m3_out, pl_out, pr_out,
                  pre_out, stc_out, sw_out, hinfo_out, cnt_l_out, cnt_r_out, sel_l_out,
                  sel_r_out, *send_refs):
     rows = local * fields
-    views = table_views(wide_ref, mid_ref, narrow_ref, local)
+    views = table_views(tab_ref, rows, local)
     lift_ref = views["lift_t"]
     g7_ref = views["g7"]
     tm_ref = views["tm"]
@@ -564,7 +568,7 @@
 def setup_entry(local, fields, n_in, n_out, *refs):
     sources = refs[:n_in]
     outs = refs[n_in : n_in + n_out]
-    n_tab = 3
+    n_tab = 1
     n_own = n_in - n_tab
     buffers = refs[n_in + n_out : n_in + n_out + n_own]
     sems = refs[n_in + n_out + n_own]
@@ -612,15 +616,13 @@
     sel_np = pick_rows[:, None] == np.arange(rows)[None, :]
     n7 = P7**3
     n3 = P3**3
-    layouts = table_layout(rows, local_count)
-    wide_np = np.zeros((n7 + 6 * n3, 6 * LANE), np.float32)
-    mid_np = np.zeros((n7 + 4 * n3 + 2 * LANE, n7), np.float32)
+    layout = table_layout(rows, local_count)
+    table_np = np.zeros((table_rows(), 6 * LANE), np.float32)
     for d in (1, 2):
         block = tab["d7t"][d][:LANE, :LANE].astype(np.float32)
         assert np.array_equal(
             tab["d7t"][d].astype(np.float32), np.kron(np.eye(n7 // LANE), block)
         )
-    narrow_np = np.zeros((2 * rows + 3 * local_count + 3 * n3, rows), np.float32)
     pieces = {
         "g7": tab["g7"][None],
         "tm": tab["tm"],
@@ -634,14 +636,15 @@
         "fsel": fsel_np[None],
         "d3t": tab["d3t"],
     }
-    for target, layout in zip((wide_np, mid_np, narrow_np), layouts):
-        for name, (start, count, width) in layout.items():
-            parts = np.asarray(pieces[name], np.float32)
-            for k in range(parts.shape[0]):
-                target[start + k * count : start + (k + 1) * count, :width] = parts[k]
-    wide = jnp.asarray(to_bf16(wide_np))
-    mid = jnp.asarray(to_bf16(mid_np))
-    narrow = jnp.asarray(to_bf16(narrow_np))
+    filled = np.zeros(table_np.shape, bool)
+    for name, (start, count, width, lane0) in layout.items():
+        parts = np.asarray(pieces[name], np.float32)
+        for k in range(parts.shape[0]):
+            window = (slice(start + k * count, start + (k + 1) * count), slice(lane0, lane0 + width))
+            assert not filled[window].any()
+            filled[window] = True
+            table_np[window] = parts[k]
+    table = jnp.asarray(to_bf16(table_np))
 
     send_shape = jax.ShapeDtypeStruct((rows, LANE), bf16)
     sends_shape = [send_shape, send_shape, jax.ShapeDtypeStruct((2 * rows, LANE), bf16)]
@@ -673,9 +676,9 @@
         jax.ShapeDtypeStruct((MOVE_CAP * field_count, rows), bf16),
         jax.ShapeDtypeStruct((MOVE_CAP * field_count, rows), bf16),
     ] + sends_shape
-    setup_out = setup_out + [jax.ShapeDtypeStruct(x.shape, x.dtype) for x in (wide, mid, narrow)]
+    setup_out = setup_out + [jax.ShapeDtypeStruct(table.shape, table.dtype)]
     u0 = state.reshape(rows, P7**3)
-    setup_in = [u0, vt, packed, wide, mid, narrow]
+    setup_in = [u0, vt, packed, table]
     res = pl.pallas_call(
         functools.partial(setup_entry, local_count, field_count, len(setup_in), len(setup_out)),
         out_shape=setup_out,
@@ -688,10 +691,10 @@
     v7, m7, v3, m3, p_local, p_remote, pre, stc, sw = res[:9]
     hinfo, cnt_l, cnt_r, sel_l, sel_r = res[9:14]
     sends = res[14:17]
-    wide, mid, narrow = res[17:20]
-    common = [p_local, p_remote, v7, m7, pre, stc, wide, mid, narrow]
+    table = res[17]
+    common = [p_local, p_remote, v7, m7, pre, stc, table]
     recv = exchange(sends)
-    bulk_tabs = [v7, pre, stc, wide, mid, narrow]
+    bulk_tabs = [v7, pre, stc, table]
     (bulk7,) = run_bulk(False, local_count, [u0] + bulk_tabs, [u_shape])
     res = run_stage(
         (False, False, False, True, local_count),

time: 60.8 us -> 59 us (0.970)
  local copies, waits for them, and re-layouts: 9.11 us -> 7.36 us
    unnamed x20 -> x16, local copies, waits for them, and re-layouts: 7.05 us -> 5.31 us
where the time goes in v9:
time: 59 us; the launch traced here: 58.7 us
  starting transfers between devices  27.5 us (47%)
  Pallas kernels  17.3 us (29%)
  local copies, waits for them, and re-layouts  7.36 us (12%)
  waiting for transfers between devices  4.35 us (7%)
  other arithmetic  1.37 us (2%)
  between operations  0.75 us (1%)
    ppermute x14, starting transfers between devices, shifted(): return lax.ppermute(value, axis, pairs)  27.5 us
    pallas_call x4, Pallas kernels, run_stage(): pl.pallas_call(kernel, out_shape=out_shapes, in_specs=[_vmem() for _ in i...  8.6 us
    unnamed x16, local copies, waits for them, and re-layouts  5.31 us
    ppermute x14, waiting for transfers between devices, shifted(): return lax.ppermute(value, axis, pairs)  4.35 us
    pallas_call x4, Pallas kernels, run_bulk(): pl.pallas_call(functools.partial(bulk_kernel, coarse, local), out_shape=o...  3.1 us
    pallas_call x1, Pallas kernels, per_device(): pl.pallas_call(functools.partial(setup_entry, local_count, field_count, l...  2.86 us
    pallas_call x1, Pallas kernels, per_device(): pl.pallas_call(functools.partial(final_kernel, field_count, HOLD7), out_s...  2.73 us
  transfers between devices with their start and end apart: 14, of which 6 were waited for; matrix products, arithmetic and copies ran while one was open for 1% of the time, Pallas kernels for 5%

profile of v9, /device:TPU:0, one launch (start us, length us, event | category | flops | bytes accessed | tf_op | source)
XLA Modules:
  0.0 58.7 jit_solution(14067307201581751625)
XLA Ops:
  0.6 0.7 %pad_bitcast_fusion = f32[1,16]{1,0:T(1,128)S(1)} fusion(f32[8]{0:T(128)} %param.11), kind=kLoop, calls=%fused_computation.9 | loop fusion | bytes 96 | tf_op jit(solution)/shard_map/stack | solution.py:607
  1.3 0.7 %convert_bitcast_fusion.1 = (f32[1,16]{1,0:T(1,128)S(1)}, f32[1,16]{1,0:T(1,128)S(1)}) fusion(s32[16]{0:T(128)} %param.14, s32[16]{0:T(128)} %param.13), kind=kLoop, calls=%fused_computation.8 | loop fusion | flops 32 | bytes 256 | tf_op jit(solution)/shard_map/stack | solution.py:607
  2.0 0.7 %convert_bitcast_fusion = f32[6,16]{1,0:T(8,128)S(1)} fusion(s32[16,6]{0,1:T(8,128)} %param.12, s32[]{:T(128)S(6)} %add.11), kind=kLoop, calls=%fused_computation.5 | loop fusion | flops 2016 | bytes 772 | tf_op jit(solution)/shard_map/transpose | solution.py:606
  2.7 0.7 %concatenate.3 = f32[10,16]{1,0:T(8,128)S(1)} concatenate(f32[6,16]{1,0:T(8,128)S(1)} %convert_bitcast_fusion, f32[1,16]{1,0:T(1,128)S(1)} %get-tuple-element.83, f32[1,16]{1,0:T(1,128)} %bitcast.18, f32[1,16]{1,0:T(1,128)S(1)} %pad_bitcast_fusion, f32[1,16]{1,0:T(1,128)S(1)} %get-tuple-element.82), dimensions={0} | concatenate | bytes 1280 | tf_op jit(solution)/shard_map/concatenate | solution.py:604
  3.4 0.9 %copy-done = f32[16,8,512]{2,1,0:T(8,128)S(1)} copy-done((f32[16,8,512]{2,1,0:T(8,128)S(1)}, f32[16,8,512]{2,1,0:T(8,128)}, u32[]{:S(2)}) %copy-start) | copy-done | bytes 262168
  4.3 1.7 %copy-done.2 = bf16[1664,768]{1,0:T(8,128)(2,1)S(1)} copy-done((bf16[1664,768]{1,0:T(8,128)(2,1)S(1)}, bf16[1664,768]{1,0:T(8,128)(2,1)}, u32[]{:S(2)}) %copy-start.2) | copy-done | bytes 2555928
  6.0 0.7 %copy-done.5 = bf16[3,64,16]{1,2,0:T(8,128)(2,1)S(1)} copy-done((bf16[3,64,16]{1,2,0:T(8,128)(2,1)S(1)}, bf16[3,64,16]{1,2,0:T(8,128)(2,1)}, u32[]{:S(2)}) %copy-start.5) | copy-done | bytes 6168
  6.8 2.9 %shard_map.95 = (bf16[3,128,512]{2,1,0:T(8,128)(2,1)S(1)}, f32[128,768]{1,0:T(8,128)S(1)}, f32[3,128,64]{2,1,0:T(8,128)S(1)}, f32[128,768]{1,0:T(8,128)S(1)}, bf...) custom-call(f32[128,512]{1,0:T(8,128)S(1)} %bitcast.12, ...), custom_call_target="tpu_custom_call" | custom-call | tf_op jit(solution)/shard_map/pallas_call | solution.py:682
  10.2 3.0 %collective-permute-start.2 = (bf16[256,128]{1,0:T(8,128)(2,1)S(1)}, bf16[256,128]{1,0:T(8,128)(2,1)S(1)}, u32[]{:S(2)}, u32[]{:S(2)}) collective-permute-start(bf16[256,128]{1,0:T(8,128)(2,1)S(1)} %get-tuple-element.44), channel_id=1, source_target_pairs={{0,16},{16,0},{1,17},{17,1},{2,18},{18,2},{3,19},{19,3},{4,20},{20... | collective-permute-start | bytes 196616 | tf_op jit(solution)/shard_map/ppermute | solution.py:32
  13.2 4.4 %collective-permute-start.1 = (bf16[128,128]{1,0:T(8,128)(2,1)S(1)}, bf16[128,128]{1,0:T(8,128)(2,1)S(1)}, u32[]{:S(2)}, u32[]{:S(2)}) collective-permute-start(bf16[128,128]{1,0:T(8,128)(2,1)S(1)} %get-tuple-element.43), channel_id=1, source_target_pairs={{0,15},{1,0},{2,1},{3,2},{4,3},{5,4},{6,5},{7,6},{8,7},{9,8},{10,9... | collective-permute-start | bytes 98312 | tf_op jit(solution)/shard_map/ppermute | solution.py:32
  17.6 0.7 %shard_map.96.refs_12_ = f32[128,512]{1,0:T(8,128)S(1)} custom-call(f32[128,512]{1,0:T(8,128)S(1)} %bitcast.13, bf16[3,128,512]{2,1,0:T(8,128)(2,1)S(1)} %get-tuple-element.47.refs_1_.refs_7_.refs_8_.refs_2_.refs_10_, f32[16,1]{1,0:T(8,128)S(1)} %get-tuple-element.49.refs_2_.refs_9_.refs_10_.refs_3_.refs_12_, ...), custom_call_target="tpu_custom_call" | custom-call | tf_op jit(solution)/shard_map/pallas_call | solution.py:420
  18.3 0.9 %collective-permute-done.refs_1_ = bf16[128,128]{1,0:T(8,128)(2,1)S(1)} collective-permute-done((bf16[128,128]{1,0:T(8,128)(2,1)S(1)}, bf16[128,128]{1,0:T(8,128)(2,1)S(1)}, u32[]{:S(2)}, u32[]{:S(2)}) %collective-permute-start) | collective-permute-done | bytes 32800 | tf_op jit(solution)/shard_map/ppermute | solution.py:32
  19.3 1.4 %shard_map.97 = (f32[128,512]{1,0:T(8,128)S(1)}, bf16[128,128]{1,0:T(8,128)(2,1)S(1)}, bf16[128,128]{1,0:T(8,128)(2,1)S(1)}, bf16[256,128]{1,0:T(8,128)(2,1)S(1)}) custom-call(f32[128,512]{1,0:T(8,128)S(1)} %bitcast.14, bf16[128,128]{1,0:T(8,128)(2,1)S(1)} %collective-permute-done.refs_1_, bf16[128,128]{1,0:T(8,128)(2,1)S(1)} %collective-permute-done.1.refs_2_, ...), custom_call_target="tpu_custom_call" | custom-call | tf_op jit(solution)/shard_map/pallas_call | solution.py:432
  20.9 4.5 %collective-permute-start.4 = (bf16[128,128]{1,0:T(8,128)(2,1)S(1)}, bf16[128,128]{1,0:T(8,128)(2,1)S(1)}, u32[]{:S(2)}, u32[]{:S(2)}) collective-permute-start(bf16[128,128]{1,0:T(8,128)(2,1)S(1)} %get-tuple-element.54), channel_id=1, source_target_pairs={{0,15},{1,0},{2,1},{3,2},{4,3},{5,4},{6,5},{7,6},{8,7},{9,8},{10,9... | collective-permute-start | bytes 98312 | tf_op jit(solution)/shard_map/ppermute | solution.py:32
  25.3 0.7 %shard_map.98.refs_14_ = f32[128,512]{1,0:T(8,128)S(1)} custom-call(f32[128,512]{1,0:T(8,128)S(1)} %get-tuple-element.52.refs_0_, bf16[3,128,512]{2,1,0:T(8,128)(2,1)S(1)} %get-tuple-element.47.refs_1_.refs_7_.refs_8_.refs_2_.refs_10_, f32[16,1]{1,0:T(8,128)S(1)} %get-tuple-element.49.refs_2_.refs_9_.refs_10_.refs_3_.refs_12_, ...), custom_call_target="tpu_custom_call" | custom-call | tf_op jit(solution)/shard_map/pallas_call | solution.py:420
  26.0 0.9 %collective-permute-done.3.refs_2_ = bf16[128,128]{1,0:T(8,128)(2,1)S(1)} collective-permute-done((bf16[128,128]{1,0:T(8,128)(2,1)S(1)}, bf16[128,128]{1,0:T(8,128)(2,1)S(1)}, u32[]{:S(2)}, u32[]{:S(2)}) %collective-permute-start.3) | collective-permute-done | bytes 32800 | tf_op jit(solution)/shard_map/ppermute | solution.py:32
  26.9 2.3 %shard_map.99 = (f32[128,512]{1,0:T(8,128)S(1)}, f32[128,64]{1,0:T(8,128)S(1)}, bf16[128,128]{1,0:T(8,128)(2,1)S(1)}, bf16[128,128]{1,0:T(8,128)(2,1)S(1)}, bf16[256,128]{1,0:T(8,128)(2,1)S(1)}) custom-call(f32[128,512]{1,0:T(8,128)S(1)} %get-tuple-element.52.refs_0_, f32[128,512]{1,0:T(8,128)S(1)} %bitcast.15, ...), custom_call_target="tpu_custom_call" | custom-call | tf_op jit(solution)/shard_map/pallas_call | solution.py:432
  29.2 2.0 %collective-permute-start.8 = (bf16[256,128]{1,0:T(8,128)(2,1)S(1)}, bf16[256,128]{1,0:T(8,128)(2,1)S(1)}, u32[]{:S(2)}, u32[]{:S(2)}) collective-permute-start(bf16[256,128]{1,0:T(8,128)(2,1)S(1)} %get-tuple-element.61), channel_id=1, source_target_pairs={{0,16},{16,0},{1,17},{17,1},{2,18},{18,2},{3,19},{19,3},{4,20},{20... | collective-permute-start | bytes 196616 | tf_op jit(solution)/shard_map/ppermute | solution.py:32
  31.2 4.4 %collective-permute-start.7 = (bf16[128,128]{1,0:T(8,128)(2,1)S(1)}, bf16[128,128]{1,0:T(8,128)(2,1)S(1)}, u32[]{:S(2)}, u32[]{:S(2)}) collective-permute-start(bf16[128,128]{1,0:T(8,128)(2,1)S(1)} %get-tuple-element.60), channel_id=1, source_target_pairs={{0,15},{1,0},{2,1},{3,2},{4,3},{5,4},{6,5},{7,6},{8,7},{9,8},{10,9... | collective-permute-start | bytes 98312 | tf_op jit(solution)/shard_map/ppermute | solution.py:32
  35.6 0.9 %shard_map.100 = (f32[128,512]{1,0:T(8,128)S(1)}, f32[128,64]{1,0:T(8,128)S(1)}) custom-call(f32[128,512]{1,0:T(8,128)S(1)} %get-tuple-element.57.refs_0_.refs_2_, f32[128,64]{1,0:T(8,128)S(1)} %get-tuple-element.58.refs_1_.refs_3_, bf16[3,128,512]{2,1,0:T(8,128)(2,1)S(1)} %get-tuple-element.47.refs_1_.refs_7_.refs_8_.refs_2_.refs_10_, ...), custom_call_target="tpu_custom_call" | custom-call | tf_op jit(solution)/shard_map/pallas_call | solution.py:420
  36.5 0.7 %collective-permute-done.6.refs_2_ = bf16[128,128]{1,0:T(8,128)(2,1)S(1)} collective-permute-done((bf16[128,128]{1,0:T(8,128)(2,1)S(1)}, bf16[128,128]{1,0:T(8,128)(2,1)S(1)}, u32[]{:S(2)}, u32[]{:S(2)}) %collective-permute-start.6) | collective-permute-done | bytes 32800 | tf_op jit(solution)/shard_map/ppermute | solution.py:32
  37.2 2.7 %shard_map.101 = (f32[128,512]{1,0:T(8,128)S(1)}, f32[128,64]{1,0:T(8,128)S(1)}, bf16[128,128]{1,0:T(8,128)(2,1)S(1)}, bf16[128,128]{1,0:T(8,128)(2,1)S(1)}, bf16[256,128]{1,0:T(8,128)(2,1)S(1)}) custom-call(f32[128,512]{1,0:T(8,128)S(1)} %get-tuple-element.57.refs_0_.refs_2_, f32[128,64]{1,0:T(8,128)S(1)} %get-tuple-element.58.refs_1_.refs_3_, ...), custom_call_target="tpu_custom_call" | custom-call | tf_op jit(solution)/shard_map/pallas_call | solution.py:432
  40.1 4.4 %collective-permute-start.10 = (bf16[128,128]{1,0:T(8,128)(2,1)S(1)}, bf16[128,128]{1,0:T(8,128)(2,1)S(1)}, u32[]{:S(2)}, u32[]{:S(2)}) collective-permute-start(bf16[128,128]{1,0:T(8,128)(2,1)S(1)} %get-tuple-element.69), channel_id=1, source_target_pairs={{0,15},{1,0},{2,1},{3,2},{4,3},{5,4},{6,5},{7,6},{8,7},{9,8},{10,9... | collective-permute-start | bytes 98312 | tf_op jit(solution)/shard_map/ppermute | solution.py:32
  44.6 0.9 %shard_map.102 = (f32[128,512]{1,0:T(8,128)S(1)}, f32[128,64]{1,0:T(8,128)S(1)}) custom-call(f32[128,512]{1,0:T(8,128)S(1)} %get-tuple-element.66.refs_0_, f32[128,64]{1,0:T(8,128)S(1)} %get-tuple-element.67.refs_1_, bf16[3,128,512]{2,1,0:T(8,128)(2,1)S(1)} %get-tuple-element.47.refs_1_.refs_7_.refs_8_.refs_2_.refs_10_, ...), custom_call_target="tpu_custom_call" | custom-call | tf_op jit(solution)/shard_map/pallas_call | solution.py:420
  45.5 0.7 %collective-permute-done.9.refs_4_ = bf16[128,128]{1,0:T(8,128)(2,1)S(1)} collective-permute-done((bf16[128,128]{1,0:T(8,128)(2,1)S(1)}, bf16[128,128]{1,0:T(8,128)(2,1)S(1)}, u32[]{:S(2)}, u32[]{:S(2)}) %collective-permute-start.9) | collective-permute-done | bytes 32800 | tf_op jit(solution)/shard_map/ppermute | solution.py:32
  46.2 2.2 %shard_map.103 = (f32[128,512]{1,0:T(8,128)S(1)}, f32[128,64]{1,0:T(8,128)S(1)}, f32[24,512]{1,0:T(8,128)S(1)}, f32[24,512]{1,0:T(8,128)S(1)}) custom-call(f32[128,512]{1,0:T(8,128)S(1)} %get-tuple-element.66.refs_0_, f32[128,64]{1,0:T(8,128)S(1)} %get-tuple-element.67.refs_1_, f32[128,512]{1,0:T(8,128)S(1)} %get-tuple-element.57.refs_0_.refs_2_, ...), custom_call_target="tpu_custom_call" | custom-call | tf_op jit(solution)/shard_map/pallas_call | solution.py:432
  48.4 0.7 %copy-done.3 = f32[128,512]{1,0:T(8,128)} copy-done((f32[128,512]{1,0:T(8,128)}, f32[128,512]{1,0:T(8,128)S(1)}, u32[]{:S(2)}) %copy-start.3) | copy-done | bytes 262168
  49.1 4.4 %collective-permute-start.13 = (f32[24,512]{1,0:T(8,128)S(1)}, f32[24,512]{1,0:T(8,128)S(1)}, u32[]{:S(2)}, u32[]{:S(2)}) collective-permute-start(f32[24,512]{1,0:T(8,128)S(1)} %get-tuple-element.79), channel_id=1, source_target_pairs={{0,15},{1,0},{2,1},{3,2},{4,3},{5,4},{6,5},{7,6},{8,7},{9,8},{10,9... | collective-permute-start | bytes 147464 | tf_op jit(solution)/shard_map/ppermute | solution.py:32
  53.5 0.7 %reshape.15 = f32[16,512]{1,0:T(8,128)} reshape(f32[128,64]{1,0:T(8,128)S(1)} %get-tuple-element.81) | data formatting | bytes 65536 | tf_op jit(solution)/shard_map/reshape | solution.py:741
  54.2 1.1 %collective-permute-done.12.from_l_ref = f32[24,512]{1,0:T(8,128)S(1)} collective-permute-done((f32[24,512]{1,0:T(8,128)S(1)}, f32[24,512]{1,0:T(8,128)S(1)}, u32[]{:S(2)}, u32[]{:S(2)}) %collective-permute-start.12) | collective-permute-done | bytes 49184 | tf_op jit(solution)/shard_map/ppermute | solution.py:32
  55.3 0.6 %copy-done.6 = f32[24,512]{1,0:T(8,128)} copy-done((f32[24,512]{1,0:T(8,128)}, f32[24,512]{1,0:T(8,128)S(1)}, u32[]{:S(2)}) %copy-start.6) | copy-done | bytes 49176
  55.9 2.7 %shard_map.104 = f32[96,512]{1,0:T(8,128)} custom-call(f32[128,512]{1,0:T(8,128)} %copy-done.3, f32[24,512]{1,0:T(8,128)} %copy-done.6, f32[24,512]{1,0:T(8,128)} %copy-done.7, f32[128,128]{1,0:T(8,128)} %copy-done.4), custom_call_target="tpu_custom_call" | custom-call | tf_op jit(solution)/shard_map/pallas_call | solution.py:734
  (28 shorter events, 1.1 us)
Async XLA Ops:
  3.4 0.9 %copy-start = (f32[16,8,512]{2,1,0:T(8,128)S(1)}, f32[16,8,512]{2,1,0:T(8,128)}, u32[]{:S(2)}) copy-start(f32[16,8,512]{2,1,0:T(8,128)} %param.8) | copy-start | bytes 786436
  4.3 1.7 %copy-start.2 = (bf16[1664,768]{1,0:T(8,128)(2,1)S(1)}, bf16[1664,768]{1,0:T(8,128)(2,1)}, u32[]{:S(2)}) copy-start(bf16[1664,768]{1,0:T(8,128)(2,1)} %constant.33.clone.refs_3_) | copy-start | bytes 7667716
  6.0 0.7 %copy-start.5 = (bf16[3,64,16]{1,2,0:T(8,128)(2,1)S(1)}, bf16[3,64,16]{1,2,0:T(8,128)(2,1)}, u32[]{:S(2)}) copy-start(bf16[3,64,16]{1,2,0:T(8,128)(2,1)} %param.9) | copy-start | bytes 18436
  6.8 12.5 %copy-start.1 = (f32[16,8,512]{2,1,0:T(8,128)S(1)}, f32[16,8,512]{2,1,0:T(8,128)}, u32[]{:S(2)}) copy-start(f32[16,8,512]{2,1,0:T(8,128)} %param.8) | copy-start | bytes 786436
  9.6 0.6 %copy-start.4 = (f32[128,128]{1,0:T(8,128)}, f32[128,128]{1,0:T(8,128)S(1)}, u32[]{:S(2)}) copy-start(f32[128,128]{1,0:T(8,128)S(1)} %get-tuple-element.80.hinfo_ref) | copy-start | bytes 196612
  10.2 9.0 %collective-permute-start.2 = (bf16[256,128]{1,0:T(8,128)(2,1)S(1)}, bf16[256,128]{1,0:T(8,128)(2,1)S(1)}, u32[]{:S(2)}, u32[]{:S(2)}) collective-permute-start(bf16[256,128]{1,0:T(8,128)(2,1)S(1)} %get-tuple-element.44), channel_id=1, source_target_pairs={{0,16},{16,0},{1,17},{17,1},{2,18},{18,2},{3,19},{19,3},{4,20},{20... | collective-permute-start | bytes 196616 | tf_op jit(solution)/shard_map/ppermute | solution.py:32
  13.2 6.0 %collective-permute-start = (bf16[128,128]{1,0:T(8,128)(2,1)S(1)}, bf16[128,128]{1,0:T(8,128)(2,1)S(1)}, u32[]{:S(2)}, u32[]{:S(2)}) collective-permute-start(bf16[128,128]{1,0:T(8,128)(2,1)S(1)} %get-tuple-element.42), channel_id=1, source_target_pairs={{0,1},{1,2},{2,3},{3,4},{4,5},{5,6},{6,7},{7,8},{8,9},{9,10},{10,1... | collective-permute-start | bytes 98312 | tf_op jit(solution)/shard_map/ppermute | solution.py:32
  13.2 6.0 %collective-permute-start.1 = (bf16[128,128]{1,0:T(8,128)(2,1)S(1)}, bf16[128,128]{1,0:T(8,128)(2,1)S(1)}, u32[]{:S(2)}, u32[]{:S(2)}) collective-permute-start(bf16[128,128]{1,0:T(8,128)(2,1)S(1)} %get-tuple-element.43), channel_id=1, source_target_pairs={{0,15},{1,0},{2,1},{3,2},{4,3},{5,4},{6,5},{7,6},{8,7},{9,8},{10,9... | collective-permute-start | bytes 98312 | tf_op jit(solution)/shard_map/ppermute | solution.py:32
  20.7 6.2 %collective-permute-start.5 = (bf16[256,128]{1,0:T(8,128)(2,1)S(1)}, bf16[256,128]{1,0:T(8,128)(2,1)S(1)}, u32[]{:S(2)}, u32[]{:S(2)}) collective-permute-start(bf16[256,128]{1,0:T(8,128)(2,1)S(1)} %get-tuple-element.55), channel_id=1, source_target_pairs={{0,16},{16,0},{1,17},{17,1},{2,18},{18,2},{3,19},{19,3},{4,20},{20... | collective-permute-start | bytes 196616 | tf_op jit(solution)/shard_map/ppermute | solution.py:32
  20.8 6.1 %collective-permute-start.3 = (bf16[128,128]{1,0:T(8,128)(2,1)S(1)}, bf16[128,128]{1,0:T(8,128)(2,1)S(1)}, u32[]{:S(2)}, u32[]{:S(2)}) collective-permute-start(bf16[128,128]{1,0:T(8,128)(2,1)S(1)} %get-tuple-element.53), channel_id=1, source_target_pairs={{0,1},{1,2},{2,3},{3,4},{4,5},{5,6},{6,7},{7,8},{8,9},{9,10},{10,1... | collective-permute-start | bytes 98312 | tf_op jit(solution)/shard_map/ppermute | solution.py:32
  20.9 6.1 %collective-permute-start.4 = (bf16[128,128]{1,0:T(8,128)(2,1)S(1)}, bf16[128,128]{1,0:T(8,128)(2,1)S(1)}, u32[]{:S(2)}, u32[]{:S(2)}) collective-permute-start(bf16[128,128]{1,0:T(8,128)(2,1)S(1)} %get-tuple-element.54), channel_id=1, source_target_pairs={{0,15},{1,0},{2,1},{3,2},{4,3},{5,4},{6,5},{7,6},{8,7},{9,8},{10,9... | collective-permute-start | bytes 98312 | tf_op jit(solution)/shard_map/ppermute | solution.py:32
  29.2 8.0 %collective-permute-start.8 = (bf16[256,128]{1,0:T(8,128)(2,1)S(1)}, bf16[256,128]{1,0:T(8,128)(2,1)S(1)}, u32[]{:S(2)}, u32[]{:S(2)}) collective-permute-start(bf16[256,128]{1,0:T(8,128)(2,1)S(1)} %get-tuple-element.61), channel_id=1, source_target_pairs={{0,16},{16,0},{1,17},{17,1},{2,18},{18,2},{3,19},{19,3},{4,20},{20... | collective-permute-start | bytes 196616 | tf_op jit(solution)/shard_map/ppermute | solution.py:32
  31.2 6.0 %collective-permute-start.6 = (bf16[128,128]{1,0:T(8,128)(2,1)S(1)}, bf16[128,128]{1,0:T(8,128)(2,1)S(1)}, u32[]{:S(2)}, u32[]{:S(2)}) collective-permute-start(bf16[128,128]{1,0:T(8,128)(2,1)S(1)} %get-tuple-element.59), channel_id=1, source_target_pairs={{0,1},{1,2},{2,3},{3,4},{4,5},{5,6},{6,7},{7,8},{8,9},{9,10},{10,1... | collective-permute-start | bytes 98312 | tf_op jit(solution)/shard_map/ppermute | solution.py:32
  31.2 6.0 %collective-permute-start.7 = (bf16[128,128]{1,0:T(8,128)(2,1)S(1)}, bf16[128,128]{1,0:T(8,128)(2,1)S(1)}, u32[]{:S(2)}, u32[]{:S(2)}) collective-permute-start(bf16[128,128]{1,0:T(8,128)(2,1)S(1)} %get-tuple-element.60), channel_id=1, source_target_pairs={{0,15},{1,0},{2,1},{3,2},{4,3},{5,4},{6,5},{7,6},{8,7},{9,8},{10,9... | collective-permute-start | bytes 98312 | tf_op jit(solution)/shard_map/ppermute | solution.py:32
  40.0 6.2 %collective-permute-start.11 = (bf16[256,128]{1,0:T(8,128)(2,1)S(1)}, bf16[256,128]{1,0:T(8,128)(2,1)S(1)}, u32[]{:S(2)}, u32[]{:S(2)}) collective-permute-start(bf16[256,128]{1,0:T(8,128)(2,1)S(1)} %get-tuple-element.70), channel_id=1, source_target_pairs={{0,16},{16,0},{1,17},{17,1},{2,18},{18,2},{3,19},{19,3},{4,20},{20... | collective-permute-start | bytes 196616 | tf_op jit(solution)/shard_map/ppermute | solution.py:32
  40.1 6.0 %collective-permute-start.9 = (bf16[128,128]{1,0:T(8,128)(2,1)S(1)}, bf16[128,128]{1,0:T(8,128)(2,1)S(1)}, u32[]{:S(2)}, u32[]{:S(2)}) collective-permute-start(bf16[128,128]{1,0:T(8,128)(2,1)S(1)} %get-tuple-element.68), channel_id=1, source_target_pairs={{0,1},{1,2},{2,3},{3,4},{4,5},{5,6},{6,7},{7,8},{8,9},{9,10},{10,1... | collective-permute-start | bytes 98312 | tf_op jit(solution)/shard_map/ppermute | solution.py:32
  40.1 6.0 %collective-permute-start.10 = (bf16[128,128]{1,0:T(8,128)(2,1)S(1)}, bf16[128,128]{1,0:T(8,128)(2,1)S(1)}, u32[]{:S(2)}, u32[]{:S(2)}) collective-permute-start(bf16[128,128]{1,0:T(8,128)(2,1)S(1)} %get-tuple-element.69), channel_id=1, source_target_pairs={{0,15},{1,0},{2,1},{3,2},{4,3},{5,4},{6,5},{7,6},{8,7},{9,8},{10,9... | collective-permute-start | bytes 98312 | tf_op jit(solution)/shard_map/ppermute | solution.py:32
  48.4 0.7 %copy-start.3 = (f32[128,512]{1,0:T(8,128)}, f32[128,512]{1,0:T(8,128)S(1)}, u32[]{:S(2)}) copy-start(f32[128,512]{1,0:T(8,128)S(1)} %get-tuple-element.77.home_ref) | copy-start | bytes 786436
  49.1 6.2 %collective-permute-start.12 = (f32[24,512]{1,0:T(8,128)S(1)}, f32[24,512]{1,0:T(8,128)S(1)}, u32[]{:S(2)}, u32[]{:S(2)}) collective-permute-start(f32[24,512]{1,0:T(8,128)S(1)} %get-tuple-element.78), channel_id=1, source_target_pairs={{0,1},{1,2},{2,3},{3,4},{4,5},{5,6},{6,7},{7,8},{8,9},{9,10},{10,1... | collective-permute-start | bytes 147464 | tf_op jit(solution)/shard_map/ppermute | solution.py:32
  49.1 6.2 %collective-permute-start.13 = (f32[24,512]{1,0:T(8,128)S(1)}, f32[24,512]{1,0:T(8,128)S(1)}, u32[]{:S(2)}, u32[]{:S(2)}) collective-permute-start(f32[24,512]{1,0:T(8,128)S(1)} %get-tuple-element.79), channel_id=1, source_target_pairs={{0,15},{1,0},{2,1},{3,2},{4,3},{5,4},{6,5},{7,6},{8,7},{9,8},{10,9... | collective-permute-start | bytes 147464 | tf_op jit(solution)/shard_map/ppermute | solution.py:32
  55.3 0.6 %copy-start.6 = (f32[24,512]{1,0:T(8,128)}, f32[24,512]{1,0:T(8,128)S(1)}, u32[]{:S(2)}) copy-start(f32[24,512]{1,0:T(8,128)S(1)} %collective-permute-done.12.from_l_ref) | copy-start | bytes 147460
  55.3 0.6 %copy-start.7 = (f32[24,512]{1,0:T(8,128)}, f32[24,512]{1,0:T(8,128)S(1)}, u32[]{:S(2)}) copy-start(f32[24,512]{1,0:T(8,128)S(1)} %collective-permute-done.13.from_r_ref) | copy-start | bytes 147460

commit v10 on v9

--- a/solution.py
+++ b/solution.py
@@ -565,6 +565,20 @@
     out_ref[...] = total
 
 
+def final_entry(fields, hold, *refs):
+    count = 4
+    sources = refs[:count]
+    out_ref = refs[count]
+    buffers = refs[count + 1 : 2 * count + 1]
+    sems = refs[2 * count + 1]
+    copies = [pltpu.make_async_copy(sources[i], buffers[i], sems.at[i]) for i in range(count)]
+    for copy in copies:
+        copy.start()
+    for copy in copies:
+        copy.wait()
+    final_kernel(fields, hold, *buffers, out_ref)
+
+
 def setup_entry(local, fields, n_in, n_out, *refs):
     sources = refs[:n_in]
     outs = refs[n_in : n_in + n_out]
@@ -731,12 +745,15 @@
     final7, final3, pay_l, pay_r = res
     from_right = shifted(pay_l, "curve", -1)
     from_left = shifted(pay_r, "curve", 1)
+    final_in = [final7, from_left, from_right, hinfo]
     held = pl.pallas_call(
-        functools.partial(final_kernel, field_count, HOLD7),
+        functools.partial(final_entry, field_count, HOLD7),
         out_shape=jax.ShapeDtypeStruct((HOLD7 * field_count, P7**3), f32),
-        in_specs=[_vmem() for _ in range(4)],
+        in_specs=[pl.BlockSpec(memory_space=pl.ANY) for _ in final_in],
         out_specs=_vmem(),
-    )(final7, from_left, from_right, hinfo)
+        scratch_shapes=[pltpu.VMEM(x.shape, x.dtype) for x in final_in]
+        + [pltpu.SemaphoreType.DMA((len(final_in),))],
+    )(*final_in)
     state7_out = held.reshape(HOLD7, field_count, P7**3)
     state3_out = final3.reshape(local_count, field_count * P3**3)
     return (state7_out, state3_out)

time: 59 us -> 59 us (level)
  no operation moved by 1% of the time
where the time goes in v10:
time: 59 us; the launch traced here: 58.7 us
  starting transfers between devices  27.5 us (47%)
  Pallas kernels  17.3 us (29%)
  local copies, waits for them, and re-layouts  7.36 us (12%)
  waiting for transfers between devices  4.35 us (7%)
  other arithmetic  1.37 us (2%)
  between operations  0.75 us (1%)
    ppermute x14, starting transfers between devices, shifted(): return lax.ppermute(value, axis, pairs)  27.5 us
    pallas_call x4, Pallas kernels, run_stage(): pl.pallas_call(kernel, out_shape=out_shapes, in_specs=[_vmem() for _ in i...  8.6 us
    unnamed x16, local copies, waits for them, and re-layouts  5.31 us
    ppermute x14, waiting for transfers between devices, shifted(): return lax.ppermute(value, axis, pairs)  4.35 us
    pallas_call x4, Pallas kernels, run_bulk(): pl.pallas_call(functools.partial(bulk_kernel, coarse, local), out_shape=o...  3.1 us
    pallas_call x1, Pallas kernels, per_device(): pl.pallas_call(functools.partial(setup_entry, local_count, field_count, l...  2.86 us
    pallas_call x1, Pallas kernels, per_device(): pl.pallas_call(functools.partial(final_entry, field_count, HOLD7), out_sh...  2.75 us
  transfers between devices with their start and end apart: 14, of which 6 were waited for; matrix products, arithmetic and copies ran while one was open for 1% of the time, Pallas kernels for 5%

profile of v10, /device:TPU:0, one launch (start us, length us, event | category | flops | bytes accessed | tf_op | source)
XLA Modules:
  0.0 58.7 jit_solution(6356521094443405690)
XLA Ops:
  0.6 0.7 %pad_bitcast_fusion = f32[1,16]{1,0:T(1,128)S(1)} fusion(f32[8]{0:T(128)} %param.11), kind=kLoop, calls=%fused_computation.9 | loop fusion | bytes 96 | tf_op jit(solution)/shard_map/stack | solution.py:621
  1.3 0.7 %convert_bitcast_fusion.1 = (f32[1,16]{1,0:T(1,128)S(1)}, f32[1,16]{1,0:T(1,128)S(1)}) fusion(s32[16]{0:T(128)} %param.14, s32[16]{0:T(128)} %param.13), kind=kLoop, calls=%fused_computation.8 | loop fusion | flops 32 | bytes 256 | tf_op jit(solution)/shard_map/stack | solution.py:621
  2.0 0.7 %convert_bitcast_fusion = f32[6,16]{1,0:T(8,128)S(1)} fusion(s32[16,6]{0,1:T(8,128)} %param.12, s32[]{:T(128)S(6)} %add.11), kind=kLoop, calls=%fused_computation.5 | loop fusion | flops 2016 | bytes 772 | tf_op jit(solution)/shard_map/transpose | solution.py:620
  2.7 0.7 %concatenate.3 = f32[10,16]{1,0:T(8,128)S(1)} concatenate(f32[6,16]{1,0:T(8,128)S(1)} %convert_bitcast_fusion, f32[1,16]{1,0:T(1,128)S(1)} %get-tuple-element.83, f32[1,16]{1,0:T(1,128)} %bitcast.18, f32[1,16]{1,0:T(1,128)S(1)} %pad_bitcast_fusion, f32[1,16]{1,0:T(1,128)S(1)} %get-tuple-element.82), dimensions={0} | concatenate | bytes 1280 | tf_op jit(solution)/shard_map/concatenate | solution.py:618
  3.4 0.9 %copy-done = f32[16,8,512]{2,1,0:T(8,128)S(1)} copy-done((f32[16,8,512]{2,1,0:T(8,128)S(1)}, f32[16,8,512]{2,1,0:T(8,128)}, u32[]{:S(2)}) %copy-start) | copy-done | bytes 262168
  4.3 1.7 %copy-done.2 = bf16[1664,768]{1,0:T(8,128)(2,1)S(1)} copy-done((bf16[1664,768]{1,0:T(8,128)(2,1)S(1)}, bf16[1664,768]{1,0:T(8,128)(2,1)}, u32[]{:S(2)}) %copy-start.2) | copy-done | bytes 2555928
  6.0 0.7 %copy-done.5 = bf16[3,64,16]{1,2,0:T(8,128)(2,1)S(1)} copy-done((bf16[3,64,16]{1,2,0:T(8,128)(2,1)S(1)}, bf16[3,64,16]{1,2,0:T(8,128)(2,1)}, u32[]{:S(2)}) %copy-start.5) | copy-done | bytes 6168
  6.8 2.9 %shard_map.95 = (bf16[3,128,512]{2,1,0:T(8,128)(2,1)S(1)}, f32[128,768]{1,0:T(8,128)S(1)}, f32[3,128,64]{2,1,0:T(8,128)S(1)}, f32[128,768]{1,0:T(8,128)S(1)}, bf...) custom-call(f32[128,512]{1,0:T(8,128)S(1)} %bitcast.12, ...), custom_call_target="tpu_custom_call" | custom-call | tf_op jit(solution)/shard_map/pallas_call | solution.py:696
  10.2 3.0 %collective-permute-start.2 = (bf16[256,128]{1,0:T(8,128)(2,1)S(1)}, bf16[256,128]{1,0:T(8,128)(2,1)S(1)}, u32[]{:S(2)}, u32[]{:S(2)}) collective-permute-start(bf16[256,128]{1,0:T(8,128)(2,1)S(1)} %get-tuple-element.44), channel_id=1, source_target_pairs={{0,16},{16,0},{1,17},{17,1},{2,18},{18,2},{3,19},{19,3},{4,20},{20... | collective-permute-start | bytes 196616 | tf_op jit(solution)/shard_map/ppermute | solution.py:32
  13.2 4.4 %collective-permute-start.1 = (bf16[128,128]{1,0:T(8,128)(2,1)S(1)}, bf16[128,128]{1,0:T(8,128)(2,1)S(1)}, u32[]{:S(2)}, u32[]{:S(2)}) collective-permute-start(bf16[128,128]{1,0:T(8,128)(2,1)S(1)} %get-tuple-element.43), channel_id=1, source_target_pairs={{0,15},{1,0},{2,1},{3,2},{4,3},{5,4},{6,5},{7,6},{8,7},{9,8},{10,9... | collective-permute-start | bytes 98312 | tf_op jit(solution)/shard_map/ppermute | solution.py:32
  17.6 0.7 %shard_map.96.refs_12_ = f32[128,512]{1,0:T(8,128)S(1)} custom-call(f32[128,512]{1,0:T(8,128)S(1)} %bitcast.13, bf16[3,128,512]{2,1,0:T(8,128)(2,1)S(1)} %get-tuple-element.47.refs_1_.refs_7_.refs_8_.refs_2_.refs_10_, f32[16,1]{1,0:T(8,128)S(1)} %get-tuple-element.49.refs_2_.refs_9_.refs_10_.refs_3_.refs_12_, ...), custom_call_target="tpu_custom_call" | custom-call | tf_op jit(solution)/shard_map/pallas_call | solution.py:420
  18.3 0.9 %collective-permute-done.refs_1_ = bf16[128,128]{1,0:T(8,128)(2,1)S(1)} collective-permute-done((bf16[128,128]{1,0:T(8,128)(2,1)S(1)}, bf16[128,128]{1,0:T(8,128)(2,1)S(1)}, u32[]{:S(2)}, u32[]{:S(2)}) %collective-permute-start) | collective-permute-done | bytes 32800 | tf_op jit(solution)/shard_map/ppermute | solution.py:32
  19.3 1.4 %shard_map.97 = (f32[128,512]{1,0:T(8,128)S(1)}, bf16[128,128]{1,0:T(8,128)(2,1)S(1)}, bf16[128,128]{1,0:T(8,128)(2,1)S(1)}, bf16[256,128]{1,0:T(8,128)(2,1)S(1)}) custom-call(f32[128,512]{1,0:T(8,128)S(1)} %bitcast.14, bf16[128,128]{1,0:T(8,128)(2,1)S(1)} %collective-permute-done.refs_1_, bf16[128,128]{1,0:T(8,128)(2,1)S(1)} %collective-permute-done.1.refs_2_, ...), custom_call_target="tpu_custom_call" | custom-call | tf_op jit(solution)/shard_map/pallas_call | solution.py:432
  20.9 4.5 %collective-permute-start.4 = (bf16[128,128]{1,0:T(8,128)(2,1)S(1)}, bf16[128,128]{1,0:T(8,128)(2,1)S(1)}, u32[]{:S(2)}, u32[]{:S(2)}) collective-permute-start(bf16[128,128]{1,0:T(8,128)(2,1)S(1)} %get-tuple-element.54), channel_id=1, source_target_pairs={{0,15},{1,0},{2,1},{3,2},{4,3},{5,4},{6,5},{7,6},{8,7},{9,8},{10,9... | collective-permute-start | bytes 98312 | tf_op jit(solution)/shard_map/ppermute | solution.py:32
  25.3 0.7 %shard_map.98.refs_14_ = f32[128,512]{1,0:T(8,128)S(1)} custom-call(f32[128,512]{1,0:T(8,128)S(1)} %get-tuple-element.52.refs_0_, bf16[3,128,512]{2,1,0:T(8,128)(2,1)S(1)} %get-tuple-element.47.refs_1_.refs_7_.refs_8_.refs_2_.refs_10_, f32[16,1]{1,0:T(8,128)S(1)} %get-tuple-element.49.refs_2_.refs_9_.refs_10_.refs_3_.refs_12_, ...), custom_call_target="tpu_custom_call" | custom-call | tf_op jit(solution)/shard_map/pallas_call | solution.py:420
  26.0 0.9 %collective-permute-done.3.refs_2_ = bf16[128,128]{1,0:T(8,128)(2,1)S(1)} collective-permute-done((bf16[128,128]{1,0:T(8,128)(2,1)S(1)}, bf16[128,128]{1,0:T(8,128)(2,1)S(1)}, u32[]{:S(2)}, u32[]{:S(2)}) %collective-permute-start.3) | collective-permute-done | bytes 32800 | tf_op jit(solution)/shard_map/ppermute | solution.py:32
  26.9 2.3 %shard_map.99 = (f32[128,512]{1,0:T(8,128)S(1)}, f32[128,64]{1,0:T(8,128)S(1)}, bf16[128,128]{1,0:T(8,128)(2,1)S(1)}, bf16[128,128]{1,0:T(8,128)(2,1)S(1)}, bf16[256,128]{1,0:T(8,128)(2,1)S(1)}) custom-call(f32[128,512]{1,0:T(8,128)S(1)} %get-tuple-element.52.refs_0_, f32[128,512]{1,0:T(8,128)S(1)} %bitcast.15, ...), custom_call_target="tpu_custom_call" | custom-call | tf_op jit(solution)/shard_map/pallas_call | solution.py:432
  29.2 2.0 %collective-permute-start.8 = (bf16[256,128]{1,0:T(8,128)(2,1)S(1)}, bf16[256,128]{1,0:T(8,128)(2,1)S(1)}, u32[]{:S(2)}, u32[]{:S(2)}) collective-permute-start(bf16[256,128]{1,0:T(8,128)(2,1)S(1)} %get-tuple-element.61), channel_id=1, source_target_pairs={{0,16},{16,0},{1,17},{17,1},{2,18},{18,2},{3,19},{19,3},{4,20},{20... | collective-permute-start | bytes 196616 | tf_op jit(solution)/shard_map/ppermute | solution.py:32
  31.2 4.4 %collective-permute-start.7 = (bf16[128,128]{1,0:T(8,128)(2,1)S(1)}, bf16[128,128]{1,0:T(8,128)(2,1)S(1)}, u32[]{:S(2)}, u32[]{:S(2)}) collective-permute-start(bf16[128,128]{1,0:T(8,128)(2,1)S(1)} %get-tuple-element.60), channel_id=1, source_target_pairs={{0,15},{1,0},{2,1},{3,2},{4,3},{5,4},{6,5},{7,6},{8,7},{9,8},{10,9... | collective-permute-start | bytes 98312 | tf_op jit(solution)/shard_map/ppermute | solution.py:32
  35.6 0.9 %shard_map.100 = (f32[128,512]{1,0:T(8,128)S(1)}, f32[128,64]{1,0:T(8,128)S(1)}) custom-call(f32[128,512]{1,0:T(8,128)S(1)} %get-tuple-element.57.refs_0_.refs_2_, f32[128,64]{1,0:T(8,128)S(1)} %get-tuple-element.58.refs_1_.refs_3_, bf16[3,128,512]{2,1,0:T(8,128)(2,1)S(1)} %get-tuple-element.47.refs_1_.refs_7_.refs_8_.refs_2_.refs_10_, ...), custom_call_target="tpu_custom_call" | custom-call | tf_op jit(solution)/shard_map/pallas_call | solution.py:420
  36.5 0.7 %collective-permute-done.6.refs_2_ = bf16[128,128]{1,0:T(8,128)(2,1)S(1)} collective-permute-done((bf16[128,128]{1,0:T(8,128)(2,1)S(1)}, bf16[128,128]{1,0:T(8,128)(2,1)S(1)}, u32[]{:S(2)}, u32[]{:S(2)}) %collective-permute-start.6) | collective-permute-done | bytes 32800 | tf_op jit(solution)/shard_map/ppermute | solution.py:32
  37.2 2.7 %shard_map.101 = (f32[128,512]{1,0:T(8,128)S(1)}, f32[128,64]{1,0:T(8,128)S(1)}, bf16[128,128]{1,0:T(8,128)(2,1)S(1)}, bf16[128,128]{1,0:T(8,128)(2,1)S(1)}, bf16[256,128]{1,0:T(8,128)(2,1)S(1)}) custom-call(f32[128,512]{1,0:T(8,128)S(1)} %get-tuple-element.57.refs_0_.refs_2_, f32[128,64]{1,0:T(8,128)S(1)} %get-tuple-element.58.refs_1_.refs_3_, ...), custom_call_target="tpu_custom_call" | custom-call | tf_op jit(solution)/shard_map/pallas_call | solution.py:432
  40.1 4.4 %collective-permute-start.10 = (bf16[128,128]{1,0:T(8,128)(2,1)S(1)}, bf16[128,128]{1,0:T(8,128)(2,1)S(1)}, u32[]{:S(2)}, u32[]{:S(2)}) collective-permute-start(bf16[128,128]{1,0:T(8,128)(2,1)S(1)} %get-tuple-element.69), channel_id=1, source_target_pairs={{0,15},{1,0},{2,1},{3,2},{4,3},{5,4},{6,5},{7,6},{8,7},{9,8},{10,9... | collective-permute-start | bytes 98312 | tf_op jit(solution)/shard_map/ppermute | solution.py:32
  44.6 0.9 %shard_map.102 = (f32[128,512]{1,0:T(8,128)S(1)}, f32[128,64]{1,0:T(8,128)S(1)}) custom-call(f32[128,512]{1,0:T(8,128)S(1)} %get-tuple-element.66.refs_0_, f32[128,64]{1,0:T(8,128)S(1)} %get-tuple-element.67.refs_1_, bf16[3,128,512]{2,1,0:T(8,128)(2,1)S(1)} %get-tuple-element.47.refs_1_.refs_7_.refs_8_.refs_2_.refs_10_, ...), custom_call_target="tpu_custom_call" | custom-call | tf_op jit(solution)/shard_map/pallas_call | solution.py:420
  45.5 0.7 %collective-permute-done.9.refs_4_ = bf16[128,128]{1,0:T(8,128)(2,1)S(1)} collective-permute-done((bf16[128,128]{1,0:T(8,128)(2,1)S(1)}, bf16[128,128]{1,0:T(8,128)(2,1)S(1)}, u32[]{:S(2)}, u32[]{:S(2)}) %collective-permute-start.9) | collective-permute-done | bytes 32800 | tf_op jit(solution)/shard_map/ppermute | solution.py:32
  46.2 2.2 %shard_map.103 = (f32[128,512]{1,0:T(8,128)S(1)}, f32[128,64]{1,0:T(8,128)S(1)}, f32[24,512]{1,0:T(8,128)S(1)}, f32[24,512]{1,0:T(8,128)S(1)}) custom-call(f32[128,512]{1,0:T(8,128)S(1)} %get-tuple-element.66.refs_0_, f32[128,64]{1,0:T(8,128)S(1)} %get-tuple-element.67.refs_1_, f32[128,512]{1,0:T(8,128)S(1)} %get-tuple-element.57.refs_0_.refs_2_, ...), custom_call_target="tpu_custom_call" | custom-call | tf_op jit(solution)/shard_map/pallas_call | solution.py:432
  48.4 0.7 %copy-done.3 = f32[128,512]{1,0:T(8,128)} copy-done((f32[128,512]{1,0:T(8,128)}, f32[128,512]{1,0:T(8,128)S(1)}, u32[]{:S(2)}) %copy-start.3) | copy-done | bytes 262168
  49.1 4.4 %collective-permute-start.13 = (f32[24,512]{1,0:T(8,128)S(1)}, f32[24,512]{1,0:T(8,128)S(1)}, u32[]{:S(2)}, u32[]{:S(2)}) collective-permute-start(f32[24,512]{1,0:T(8,128)S(1)} %get-tuple-element.79), channel_id=1, source_target_pairs={{0,15},{1,0},{2,1},{3,2},{4,3},{5,4},{6,5},{7,6},{8,7},{9,8},{10,9... | collective-permute-start | bytes 147464 | tf_op jit(solution)/shard_map/ppermute | solution.py:32
  53.5 0.7 %reshape.15 = f32[16,512]{1,0:T(8,128)} reshape(f32[128,64]{1,0:T(8,128)S(1)} %get-tuple-element.81) | data formatting | bytes 65536 | tf_op jit(solution)/shard_map/reshape | solution.py:758
  54.2 1.1 %collective-permute-done.12.refs_1_ = f32[24,512]{1,0:T(8,128)S(1)} collective-permute-done((f32[24,512]{1,0:T(8,128)S(1)}, f32[24,512]{1,0:T(8,128)S(1)}, u32[]{:S(2)}, u32[]{:S(2)}) %collective-permute-start.12) | collective-permute-done | bytes 49184 | tf_op jit(solution)/shard_map/ppermute | solution.py:32
  55.3 0.6 %copy-done.6 = f32[24,512]{1,0:T(8,128)} copy-done((f32[24,512]{1,0:T(8,128)}, f32[24,512]{1,0:T(8,128)S(1)}, u32[]{:S(2)}) %copy-start.6) | copy-done | bytes 49176
  55.9 2.7 %shard_map.104 = f32[96,512]{1,0:T(8,128)} custom-call(f32[128,512]{1,0:T(8,128)} %copy-done.3, f32[24,512]{1,0:T(8,128)} %copy-done.6, f32[24,512]{1,0:T(8,128)} %copy-done.7, f32[128,128]{1,0:T(8,128)} %copy-done.4), custom_call_target="tpu_custom_call" | custom-call | tf_op jit(solution)/shard_map/pallas_call | solution.py:749
  (28 shorter events, 1.1 us)
Async XLA Ops:
  3.4 0.9 %copy-start = (f32[16,8,512]{2,1,0:T(8,128)S(1)}, f32[16,8,512]{2,1,0:T(8,128)}, u32[]{:S(2)}) copy-start(f32[16,8,512]{2,1,0:T(8,128)} %param.8) | copy-start | bytes 786436
  4.3 1.7 %copy-start.2 = (bf16[1664,768]{1,0:T(8,128)(2,1)S(1)}, bf16[1664,768]{1,0:T(8,128)(2,1)}, u32[]{:S(2)}) copy-start(bf16[1664,768]{1,0:T(8,128)(2,1)} %constant.33.clone.refs_3_) | copy-start | bytes 7667716
  6.0 0.7 %copy-start.5 = (bf16[3,64,16]{1,2,0:T(8,128)(2,1)S(1)}, bf16[3,64,16]{1,2,0:T(8,128)(2,1)}, u32[]{:S(2)}) copy-start(bf16[3,64,16]{1,2,0:T(8,128)(2,1)} %param.9) | copy-start | bytes 18436
  6.8 12.5 %copy-start.1 = (f32[16,8,512]{2,1,0:T(8,128)S(1)}, f32[16,8,512]{2,1,0:T(8,128)}, u32[]{:S(2)}) copy-start(f32[16,8,512]{2,1,0:T(8,128)} %param.8) | copy-start | bytes 786436
  9.6 0.6 %copy-start.4 = (f32[128,128]{1,0:T(8,128)}, f32[128,128]{1,0:T(8,128)S(1)}, u32[]{:S(2)}) copy-start(f32[128,128]{1,0:T(8,128)S(1)} %get-tuple-element.80.refs_3_) | copy-start | bytes 196612
  10.2 9.0 %collective-permute-start.2 = (bf16[256,128]{1,0:T(8,128)(2,1)S(1)}, bf16[256,128]{1,0:T(8,128)(2,1)S(1)}, u32[]{:S(2)}, u32[]{:S(2)}) collective-permute-start(bf16[256,128]{1,0:T(8,128)(2,1)S(1)} %get-tuple-element.44), channel_id=1, source_target_pairs={{0,16},{16,0},{1,17},{17,1},{2,18},{18,2},{3,19},{19,3},{4,20},{20... | collective-permute-start | bytes 196616 | tf_op jit(solution)/shard_map/ppermute | solution.py:32
  13.2 6.0 %collective-permute-start = (bf16[128,128]{1,0:T(8,128)(2,1)S(1)}, bf16[128,128]{1,0:T(8,128)(2,1)S(1)}, u32[]{:S(2)}, u32[]{:S(2)}) collective-permute-start(bf16[128,128]{1,0:T(8,128)(2,1)S(1)} %get-tuple-element.42), channel_id=1, source_target_pairs={{0,1},{1,2},{2,3},{3,4},{4,5},{5,6},{6,7},{7,8},{8,9},{9,10},{10,1... | collective-permute-start | bytes 98312 | tf_op jit(solution)/shard_map/ppermute | solution.py:32
  13.2 6.0 %collective-permute-start.1 = (bf16[128,128]{1,0:T(8,128)(2,1)S(1)}, bf16[128,128]{1,0:T(8,128)(2,1)S(1)}, u32[]{:S(2)}, u32[]{:S(2)}) collective-permute-start(bf16[128,128]{1,0:T(8,128)(2,1)S(1)} %get-tuple-element.43), channel_id=1, source_target_pairs={{0,15},{1,0},{2,1},{3,2},{4,3},{5,4},{6,5},{7,6},{8,7},{9,8},{10,9... | collective-permute-start | bytes 98312 | tf_op jit(solution)/shard_map/ppermute | solution.py:32
  20.7 6.2 %collective-permute-start.5 = (bf16[256,128]{1,0:T(8,128)(2,1)S(1)}, bf16[256,128]{1,0:T(8,128)(2,1)S(1)}, u32[]{:S(2)}, u32[]{:S(2)}) collective-permute-start(bf16[256,128]{1,0:T(8,128)(2,1)S(1)} %get-tuple-element.55), channel_id=1, source_target_pairs={{0,16},{16,0},{1,17},{17,1},{2,18},{18,2},{3,19},{19,3},{4,20},{20... | collective-permute-start | bytes 196616 | tf_op jit(solution)/shard_map/ppermute | solution.py:32
  20.8 6.1 %collective-permute-start.3 = (bf16[128,128]{1,0:T(8,128)(2,1)S(1)}, bf16[128,128]{1,0:T(8,128)(2,1)S(1)}, u32[]{:S(2)}, u32[]{:S(2)}) collective-permute-start(bf16[128,128]{1,0:T(8,128)(2,1)S(1)} %get-tuple-element.53), channel_id=1, source_target_pairs={{0,1},{1,2},{2,3},{3,4},{4,5},{5,6},{6,7},{7,8},{8,9},{9,10},{10,1... | collective-permute-start | bytes 98312 | tf_op jit(solution)/shard_map/ppermute | solution.py:32
  20.9 6.1 %collective-permute-start.4 = (bf16[128,128]{1,0:T(8,128)(2,1)S(1)}, bf16[128,128]{1,0:T(8,128)(2,1)S(1)}, u32[]{:S(2)}, u32[]{:S(2)}) collective-permute-start(bf16[128,128]{1,0:T(8,128)(2,1)S(1)} %get-tuple-element.54), channel_id=1, source_target_pairs={{0,15},{1,0},{2,1},{3,2},{4,3},{5,4},{6,5},{7,6},{8,7},{9,8},{10,9... | collective-permute-start | bytes 98312 | tf_op jit(solution)/shard_map/ppermute | solution.py:32
  29.2 8.0 %collective-permute-start.8 = (bf16[256,128]{1,0:T(8,128)(2,1)S(1)}, bf16[256,128]{1,0:T(8,128)(2,1)S(1)}, u32[]{:S(2)}, u32[]{:S(2)}) collective-permute-start(bf16[256,128]{1,0:T(8,128)(2,1)S(1)} %get-tuple-element.61), channel_id=1, source_target_pairs={{0,16},{16,0},{1,17},{17,1},{2,18},{18,2},{3,19},{19,3},{4,20},{20... | collective-permute-start | bytes 196616 | tf_op jit(solution)/shard_map/ppermute | solution.py:32
  31.2 6.0 %collective-permute-start.6 = (bf16[128,128]{1,0:T(8,128)(2,1)S(1)}, bf16[128,128]{1,0:T(8,128)(2,1)S(1)}, u32[]{:S(2)}, u32[]{:S(2)}) collective-permute-start(bf16[128,128]{1,0:T(8,128)(2,1)S(1)} %get-tuple-element.59), channel_id=1, source_target_pairs={{0,1},{1,2},{2,3},{3,4},{4,5},{5,6},{6,7},{7,8},{8,9},{9,10},{10,1... | collective-permute-start | bytes 98312 | tf_op jit(solution)/shard_map/ppermute | solution.py:32
  31.2 6.0 %collective-permute-start.7 = (bf16[128,128]{1,0:T(8,128)(2,1)S(1)}, bf16[128,128]{1,0:T(8,128)(2,1)S(1)}, u32[]{:S(2)}, u32[]{:S(2)}) collective-permute-start(bf16[128,128]{1,0:T(8,128)(2,1)S(1)} %get-tuple-element.60), channel_id=1, source_target_pairs={{0,15},{1,0},{2,1},{3,2},{4,3},{5,4},{6,5},{7,6},{8,7},{9,8},{10,9... | collective-permute-start | bytes 98312 | tf_op jit(solution)/shard_map/ppermute | solution.py:32
  40.0 6.2 %collective-permute-start.11 = (bf16[256,128]{1,0:T(8,128)(2,1)S(1)}, bf16[256,128]{1,0:T(8,128)(2,1)S(1)}, u32[]{:S(2)}, u32[]{:S(2)}) collective-permute-start(bf16[256,128]{1,0:T(8,128)(2,1)S(1)} %get-tuple-element.70), channel_id=1, source_target_pairs={{0,16},{16,0},{1,17},{17,1},{2,18},{18,2},{3,19},{19,3},{4,20},{20... | collective-permute-start | bytes 196616 | tf_op jit(solution)/shard_map/ppermute | solution.py:32
  40.1 6.0 %collective-permute-start.9 = (bf16[128,128]{1,0:T(8,128)(2,1)S(1)}, bf16[128,128]{1,0:T(8,128)(2,1)S(1)}, u32[]{:S(2)}, u32[]{:S(2)}) collective-permute-start(bf16[128,128]{1,0:T(8,128)(2,1)S(1)} %get-tuple-element.68), channel_id=1, source_target_pairs={{0,1},{1,2},{2,3},{3,4},{4,5},{5,6},{6,7},{7,8},{8,9},{9,10},{10,1... | collective-permute-start | bytes 98312 | tf_op jit(solution)/shard_map/ppermute | solution.py:32
  40.1 6.0 %collective-permute-start.10 = (bf16[128,128]{1,0:T(8,128)(2,1)S(1)}, bf16[128,128]{1,0:T(8,128)(2,1)S(1)}, u32[]{:S(2)}, u32[]{:S(2)}) collective-permute-start(bf16[128,128]{1,0:T(8,128)(2,1)S(1)} %get-tuple-element.69), channel_id=1, source_target_pairs={{0,15},{1,0},{2,1},{3,2},{4,3},{5,4},{6,5},{7,6},{8,7},{9,8},{10,9... | collective-permute-start | bytes 98312 | tf_op jit(solution)/shard_map/ppermute | solution.py:32
  48.4 0.7 %copy-start.3 = (f32[128,512]{1,0:T(8,128)}, f32[128,512]{1,0:T(8,128)S(1)}, u32[]{:S(2)}) copy-start(f32[128,512]{1,0:T(8,128)S(1)} %get-tuple-element.77.refs_0_) | copy-start | bytes 786436
  49.1 6.2 %collective-permute-start.12 = (f32[24,512]{1,0:T(8,128)S(1)}, f32[24,512]{1,0:T(8,128)S(1)}, u32[]{:S(2)}, u32[]{:S(2)}) collective-permute-start(f32[24,512]{1,0:T(8,128)S(1)} %get-tuple-element.78), channel_id=1, source_target_pairs={{0,1},{1,2},{2,3},{3,4},{4,5},{5,6},{6,7},{7,8},{8,9},{9,10},{10,1... | collective-permute-start | bytes 147464 | tf_op jit(solution)/shard_map/ppermute | solution.py:32
  49.1 6.2 %collective-permute-start.13 = (f32[24,512]{1,0:T(8,128)S(1)}, f32[24,512]{1,0:T(8,128)S(1)}, u32[]{:S(2)}, u32[]{:S(2)}) collective-permute-start(f32[24,512]{1,0:T(8,128)S(1)} %get-tuple-element.79), channel_id=1, source_target_pairs={{0,15},{1,0},{2,1},{3,2},{4,3},{5,4},{6,5},{7,6},{8,7},{9,8},{10,9... | collective-permute-start | bytes 147464 | tf_op jit(solution)/shard_map/ppermute | solution.py:32
  55.3 0.6 %copy-start.6 = (f32[24,512]{1,0:T(8,128)}, f32[24,512]{1,0:T(8,128)S(1)}, u32[]{:S(2)}) copy-start(f32[24,512]{1,0:T(8,128)S(1)} %collective-permute-done.12.refs_1_) | copy-start | bytes 147460
  55.3 0.6 %copy-start.7 = (f32[24,512]{1,0:T(8,128)}, f32[24,512]{1,0:T(8,128)S(1)}, u32[]{:S(2)}) copy-start(f32[24,512]{1,0:T(8,128)S(1)} %collective-permute-done.13.refs_2_) | copy-start | bytes 147460

commit v11 on v10

--- a/solution.py
+++ b/solution.py
@@ -570,13 +570,17 @@
     sources = refs[:count]
     out_ref = refs[count]
     buffers = refs[count + 1 : 2 * count + 1]
-    sems = refs[2 * count + 1]
+    staged = refs[2 * count + 1]
+    sems = refs[2 * count + 2]
     copies = [pltpu.make_async_copy(sources[i], buffers[i], sems.at[i]) for i in range(count)]
     for copy in copies:
         copy.start()
     for copy in copies:
         copy.wait()
-    final_kernel(fields, hold, *buffers, out_ref)
+    final_kernel(fields, hold, *buffers, staged)
+    out_copy = pltpu.make_async_copy(staged, out_ref, sems.at[count])
+    out_copy.start()
+    out_copy.wait()
 
 
 def setup_entry(local, fields, n_in, n_out, *refs):
@@ -750,9 +754,10 @@
         functools.partial(final_entry, field_count, HOLD7),
         out_shape=jax.ShapeDtypeStruct((HOLD7 * field_count, P7**3), f32),
         in_specs=[pl.BlockSpec(memory_space=pl.ANY) for _ in final_in],
-        out_specs=_vmem(),
+        out_specs=pl.BlockSpec(memory_space=pl.ANY),
         scratch_shapes=[pltpu.VMEM(x.shape, x.dtype) for x in final_in]
-        + [pltpu.SemaphoreType.DMA((len(final_in),))],
+        + [pltpu.VMEM((HOLD7 * field_count, P7**3), f32)]
+        + [pltpu.SemaphoreType.DMA((len(final_in) + 1,))],
     )(*final_in)
     state7_out = held.reshape(HOLD7, field_count, P7**3)
     state3_out = final3.reshape(local_count, field_count * P3**3)

time: 59 us -> 59 us (level)
  no operation moved by 1% of the time
where the time goes in v11:
time: 59 us; the launch traced here: 58.7 us
  starting transfers between devices  27.5 us (47%)
  Pallas kernels  17.3 us (29%)
  local copies, waits for them, and re-layouts  7.36 us (12%)
  waiting for transfers between devices  4.35 us (7%)
  other arithmetic  1.37 us (2%)
  between operations  0.75 us (1%)
    ppermute x14, starting transfers between devices, shifted(): return lax.ppermute(value, axis, pairs)  27.5 us
    pallas_call x4, Pallas kernels, run_stage(): pl.pallas_call(kernel, out_shape=out_shapes, in_specs=[_vmem() for _ in i...  8.6 us
    unnamed x16, local copies, waits for them, and re-layouts  5.31 us
    ppermute x14, waiting for transfers between devices, shifted(): return lax.ppermute(value, axis, pairs)  4.35 us
    pallas_call x4, Pallas kernels, run_bulk(): pl.pallas_call(functools.partial(bulk_kernel, coarse, local), out_shape=o...  3.1 us
    pallas_call x1, Pallas kernels, per_device(): pl.pallas_call(functools.partial(setup_entry, local_count, field_count, l...  2.86 us
    pallas_call x1, Pallas kernels, per_device(): pl.pallas_call(functools.partial(final_entry, field_count, HOLD7), out_sh...  2.76 us
  transfers between devices with their start and end apart: 14, of which 6 were waited for; matrix products, arithmetic and copies ran while one was open for 1% of the time, Pallas kernels for 5%

profile of v11, /device:TPU:0, one launch (start us, length us, event | category | flops | bytes accessed | tf_op | source)
XLA Modules:
  0.0 58.7 jit_solution(15332326749606200679)
XLA Ops:
  0.6 0.7 %pad_bitcast_fusion = f32[1,16]{1,0:T(1,128)S(1)} fusion(f32[8]{0:T(128)} %param.11), kind=kLoop, calls=%fused_computation.9 | loop fusion | bytes 96 | tf_op jit(solution)/shard_map/stack | solution.py:625
  1.3 0.7 %convert_bitcast_fusion.1 = (f32[1,16]{1,0:T(1,128)S(1)}, f32[1,16]{1,0:T(1,128)S(1)}) fusion(s32[16]{0:T(128)} %param.14, s32[16]{0:T(128)} %param.13), kind=kLoop, calls=%fused_computation.8 | loop fusion | flops 32 | bytes 256 | tf_op jit(solution)/shard_map/stack | solution.py:625
  2.0 0.7 %convert_bitcast_fusion = f32[6,16]{1,0:T(8,128)S(1)} fusion(s32[16,6]{0,1:T(8,128)} %param.12, s32[]{:T(128)S(6)} %add.11), kind=kLoop, calls=%fused_computation.5 | loop fusion | flops 2016 | bytes 772 | tf_op jit(solution)/shard_map/transpose | solution.py:624
  2.7 0.7 %concatenate.3 = f32[10,16]{1,0:T(8,128)S(1)} concatenate(f32[6,16]{1,0:T(8,128)S(1)} %convert_bitcast_fusion, f32[1,16]{1,0:T(1,128)S(1)} %get-tuple-element.83, f32[1,16]{1,0:T(1,128)} %bitcast.18, f32[1,16]{1,0:T(1,128)S(1)} %pad_bitcast_fusion, f32[1,16]{1,0:T(1,128)S(1)} %get-tuple-element.82), dimensions={0} | concatenate | bytes 1280 | tf_op jit(solution)/shard_map/concatenate | solution.py:622
  3.4 0.9 %copy-done = f32[16,8,512]{2,1,0:T(8,128)S(1)} copy-done((f32[16,8,512]{2,1,0:T(8,128)S(1)}, f32[16,8,512]{2,1,0:T(8,128)}, u32[]{:S(2)}) %copy-start) | copy-done | bytes 262168
  4.3 1.7 %copy-done.2 = bf16[1664,768]{1,0:T(8,128)(2,1)S(1)} copy-done((bf16[1664,768]{1,0:T(8,128)(2,1)S(1)}, bf16[1664,768]{1,0:T(8,128)(2,1)}, u32[]{:S(2)}) %copy-start.2) | copy-done | bytes 2555928
  6.0 0.7 %copy-done.5 = bf16[3,64,16]{1,2,0:T(8,128)(2,1)S(1)} copy-done((bf16[3,64,16]{1,2,0:T(8,128)(2,1)S(1)}, bf16[3,64,16]{1,2,0:T(8,128)(2,1)}, u32[]{:S(2)}) %copy-start.5) | copy-done | bytes 6168
  6.8 2.9 %shard_map.95 = (bf16[3,128,512]{2,1,0:T(8,128)(2,1)S(1)}, f32[128,768]{1,0:T(8,128)S(1)}, f32[3,128,64]{2,1,0:T(8,128)S(1)}, f32[128,768]{1,0:T(8,128)S(1)}, bf...) custom-call(f32[128,512]{1,0:T(8,128)S(1)} %bitcast.12, ...), custom_call_target="tpu_custom_call" | custom-call | tf_op jit(solution)/shard_map/pallas_call | solution.py:700
  10.2 3.0 %collective-permute-start.2 = (bf16[256,128]{1,0:T(8,128)(2,1)S(1)}, bf16[256,128]{1,0:T(8,128)(2,1)S(1)}, u32[]{:S(2)}, u32[]{:S(2)}) collective-permute-start(bf16[256,128]{1,0:T(8,128)(2,1)S(1)} %get-tuple-element.44), channel_id=1, source_target_pairs={{0,16},{16,0},{1,17},{17,1},{2,18},{18,2},{3,19},{19,3},{4,20},{20... | collective-permute-start | bytes 196616 | tf_op jit(solution)/shard_map/ppermute | solution.py:32
  13.2 4.4 %collective-permute-start.1 = (bf16[128,128]{1,0:T(8,128)(2,1)S(1)}, bf16[128,128]{1,0:T(8,128)(2,1)S(1)}, u32[]{:S(2)}, u32[]{:S(2)}) collective-permute-start(bf16[128,128]{1,0:T(8,128)(2,1)S(1)} %get-tuple-element.43), channel_id=1, source_target_pairs={{0,15},{1,0},{2,1},{3,2},{4,3},{5,4},{6,5},{7,6},{8,7},{9,8},{10,9... | collective-permute-start | bytes 98312 | tf_op jit(solution)/shard_map/ppermute | solution.py:32
  17.6 0.7 %shard_map.96.refs_12_ = f32[128,512]{1,0:T(8,128)S(1)} custom-call(f32[128,512]{1,0:T(8,128)S(1)} %bitcast.13, bf16[3,128,512]{2,1,0:T(8,128)(2,1)S(1)} %get-tuple-element.47.refs_1_.refs_7_.refs_8_.refs_2_.refs_10_, f32[16,1]{1,0:T(8,128)S(1)} %get-tuple-element.49.refs_2_.refs_9_.refs_10_.refs_3_.refs_12_, ...), custom_call_target="tpu_custom_call" | custom-call | tf_op jit(solution)/shard_map/pallas_call | solution.py:420
  18.3 0.9 %collective-permute-done.refs_1_ = bf16[128,128]{1,0:T(8,128)(2,1)S(1)} collective-permute-done((bf16[128,128]{1,0:T(8,128)(2,1)S(1)}, bf16[128,128]{1,0:T(8,128)(2,1)S(1)}, u32[]{:S(2)}, u32[]{:S(2)}) %collective-permute-start) | collective-permute-done | bytes 32800 | tf_op jit(solution)/shard_map/ppermute | solution.py:32
  19.3 1.4 %shard_map.97 = (f32[128,512]{1,0:T(8,128)S(1)}, bf16[128,128]{1,0:T(8,128)(2,1)S(1)}, bf16[128,128]{1,0:T(8,128)(2,1)S(1)}, bf16[256,128]{1,0:T(8,128)(2,1)S(1)}) custom-call(f32[128,512]{1,0:T(8,128)S(1)} %bitcast.14, bf16[128,128]{1,0:T(8,128)(2,1)S(1)} %collective-permute-done.refs_1_, bf16[128,128]{1,0:T(8,128)(2,1)S(1)} %collective-permute-done.1.refs_2_, ...), custom_call_target="tpu_custom_call" | custom-call | tf_op jit(solution)/shard_map/pallas_call | solution.py:432
  20.9 4.5 %collective-permute-start.4 = (bf16[128,128]{1,0:T(8,128)(2,1)S(1)}, bf16[128,128]{1,0:T(8,128)(2,1)S(1)}, u32[]{:S(2)}, u32[]{:S(2)}) collective-permute-start(bf16[128,128]{1,0:T(8,128)(2,1)S(1)} %get-tuple-element.54), channel_id=1, source_target_pairs={{0,15},{1,0},{2,1},{3,2},{4,3},{5,4},{6,5},{7,6},{8,7},{9,8},{10,9... | collective-permute-start | bytes 98312 | tf_op jit(solution)/shard_map/ppermute | solution.py:32
  25.3 0.7 %shard_map.98.refs_14_ = f32[128,512]{1,0:T(8,128)S(1)} custom-call(f32[128,512]{1,0:T(8,128)S(1)} %get-tuple-element.52.refs_0_, bf16[3,128,512]{2,1,0:T(8,128)(2,1)S(1)} %get-tuple-element.47.refs_1_.refs_7_.refs_8_.refs_2_.refs_10_, f32[16,1]{1,0:T(8,128)S(1)} %get-tuple-element.49.refs_2_.refs_9_.refs_10_.refs_3_.refs_12_, ...), custom_call_target="tpu_custom_call" | custom-call | tf_op jit(solution)/shard_map/pallas_call | solution.py:420
  26.0 0.9 %collective-permute-done.3.refs_2_ = bf16[128,128]{1,0:T(8,128)(2,1)S(1)} collective-permute-done((bf16[128,128]{1,0:T(8,128)(2,1)S(1)}, bf16[128,128]{1,0:T(8,128)(2,1)S(1)}, u32[]{:S(2)}, u32[]{:S(2)}) %collective-permute-start.3) | collective-permute-done | bytes 32800 | tf_op jit(solution)/shard_map/ppermute | solution.py:32
  26.9 2.3 %shard_map.99 = (f32[128,512]{1,0:T(8,128)S(1)}, f32[128,64]{1,0:T(8,128)S(1)}, bf16[128,128]{1,0:T(8,128)(2,1)S(1)}, bf16[128,128]{1,0:T(8,128)(2,1)S(1)}, bf16[256,128]{1,0:T(8,128)(2,1)S(1)}) custom-call(f32[128,512]{1,0:T(8,128)S(1)} %get-tuple-element.52.refs_0_, f32[128,512]{1,0:T(8,128)S(1)} %bitcast.15, ...), custom_call_target="tpu_custom_call" | custom-call | tf_op jit(solution)/shard_map/pallas_call | solution.py:432
  29.2 2.0 %collective-permute-start.8 = (bf16[256,128]{1,0:T(8,128)(2,1)S(1)}, bf16[256,128]{1,0:T(8,128)(2,1)S(1)}, u32[]{:S(2)}, u32[]{:S(2)}) collective-permute-start(bf16[256,128]{1,0:T(8,128)(2,1)S(1)} %get-tuple-element.61), channel_id=1, source_target_pairs={{0,16},{16,0},{1,17},{17,1},{2,18},{18,2},{3,19},{19,3},{4,20},{20... | collective-permute-start | bytes 196616 | tf_op jit(solution)/shard_map/ppermute | solution.py:32
  31.2 4.4 %collective-permute-start.7 = (bf16[128,128]{1,0:T(8,128)(2,1)S(1)}, bf16[128,128]{1,0:T(8,128)(2,1)S(1)}, u32[]{:S(2)}, u32[]{:S(2)}) collective-permute-start(bf16[128,128]{1,0:T(8,128)(2,1)S(1)} %get-tuple-element.60), channel_id=1, source_target_pairs={{0,15},{1,0},{2,1},{3,2},{4,3},{5,4},{6,5},{7,6},{8,7},{9,8},{10,9... | collective-permute-start | bytes 98312 | tf_op jit(solution)/shard_map/ppermute | solution.py:32
  35.6 0.9 %shard_map.100 = (f32[128,512]{1,0:T(8,128)S(1)}, f32[128,64]{1,0:T(8,128)S(1)}) custom-call(f32[128,512]{1,0:T(8,128)S(1)} %get-tuple-element.57.refs_0_.refs_2_, f32[128,64]{1,0:T(8,128)S(1)} %get-tuple-element.58.refs_1_.refs_3_, bf16[3,128,512]{2,1,0:T(8,128)(2,1)S(1)} %get-tuple-element.47.refs_1_.refs_7_.refs_8_.refs_2_.refs_10_, ...), custom_call_target="tpu_custom_call" | custom-call | tf_op jit(solution)/shard_map/pallas_call | solution.py:420
  36.5 0.7 %collective-permute-done.6.refs_2_ = bf16[128,128]{1,0:T(8,128)(2,1)S(1)} collective-permute-done((bf16[128,128]{1,0:T(8,128)(2,1)S(1)}, bf16[128,128]{1,0:T(8,128)(2,1)S(1)}, u32[]{:S(2)}, u32[]{:S(2)}) %collective-permute-start.6) | collective-permute-done | bytes 32800 | tf_op jit(solution)/shard_map/ppermute | solution.py:32
  37.2 2.7 %shard_map.101 = (f32[128,512]{1,0:T(8,128)S(1)}, f32[128,64]{1,0:T(8,128)S(1)}, bf16[128,128]{1,0:T(8,128)(2,1)S(1)}, bf16[128,128]{1,0:T(8,128)(2,1)S(1)}, bf16[256,128]{1,0:T(8,128)(2,1)S(1)}) custom-call(f32[128,512]{1,0:T(8,128)S(1)} %get-tuple-element.57.refs_0_.refs_2_, f32[128,64]{1,0:T(8,128)S(1)} %get-tuple-element.58.refs_1_.refs_3_, ...), custom_call_target="tpu_custom_call" | custom-call | tf_op jit(solution)/shard_map/pallas_call | solution.py:432
  40.1 4.4 %collective-permute-start.10 = (bf16[128,128]{1,0:T(8,128)(2,1)S(1)}, bf16[128,128]{1,0:T(8,128)(2,1)S(1)}, u32[]{:S(2)}, u32[]{:S(2)}) collective-permute-start(bf16[128,128]{1,0:T(8,128)(2,1)S(1)} %get-tuple-element.69), channel_id=1, source_target_pairs={{0,15},{1,0},{2,1},{3,2},{4,3},{5,4},{6,5},{7,6},{8,7},{9,8},{10,9... | collective-permute-start | bytes 98312 | tf_op jit(solution)/shard_map/ppermute | solution.py:32
  44.6 0.9 %shard_map.102 = (f32[128,512]{1,0:T(8,128)S(1)}, f32[128,64]{1,0:T(8,128)S(1)}) custom-call(f32[128,512]{1,0:T(8,128)S(1)} %get-tuple-element.66.refs_0_, f32[128,64]{1,0:T(8,128)S(1)} %get-tuple-element.67.refs_1_, bf16[3,128,512]{2,1,0:T(8,128)(2,1)S(1)} %get-tuple-element.47.refs_1_.refs_7_.refs_8_.refs_2_.refs_10_, ...), custom_call_target="tpu_custom_call" | custom-call | tf_op jit(solution)/shard_map/pallas_call | solution.py:420
  45.5 0.7 %collective-permute-done.9.refs_4_ = bf16[128,128]{1,0:T(8,128)(2,1)S(1)} collective-permute-done((bf16[128,128]{1,0:T(8,128)(2,1)S(1)}, bf16[128,128]{1,0:T(8,128)(2,1)S(1)}, u32[]{:S(2)}, u32[]{:S(2)}) %collective-permute-start.9) | collective-permute-done | bytes 32800 | tf_op jit(solution)/shard_map/ppermute | solution.py:32
  46.2 2.2 %shard_map.103 = (f32[128,512]{1,0:T(8,128)S(1)}, f32[128,64]{1,0:T(8,128)S(1)}, f32[24,512]{1,0:T(8,128)S(1)}, f32[24,512]{1,0:T(8,128)S(1)}) custom-call(f32[128,512]{1,0:T(8,128)S(1)} %get-tuple-element.66.refs_0_, f32[128,64]{1,0:T(8,128)S(1)} %get-tuple-element.67.refs_1_, f32[128,512]{1,0:T(8,128)S(1)} %get-tuple-element.57.refs_0_.refs_2_, ...), custom_call_target="tpu_custom_call" | custom-call | tf_op jit(solution)/shard_map/pallas_call | solution.py:432
  48.4 0.7 %copy-done.3 = f32[128,512]{1,0:T(8,128)} copy-done((f32[128,512]{1,0:T(8,128)}, f32[128,512]{1,0:T(8,128)S(1)}, u32[]{:S(2)}) %copy-start.3) | copy-done | bytes 262168
  49.1 4.4 %collective-permute-start.13 = (f32[24,512]{1,0:T(8,128)S(1)}, f32[24,512]{1,0:T(8,128)S(1)}, u32[]{:S(2)}, u32[]{:S(2)}) collective-permute-start(f32[24,512]{1,0:T(8,128)S(1)} %get-tuple-element.79), channel_id=1, source_target_pairs={{0,15},{1,0},{2,1},{3,2},{4,3},{5,4},{6,5},{7,6},{8,7},{9,8},{10,9... | collective-permute-start | bytes 147464 | tf_op jit(solution)/shard_map/ppermute | solution.py:32
  53.5 0.7 %reshape.15 = f32[16,512]{1,0:T(8,128)} reshape(f32[128,64]{1,0:T(8,128)S(1)} %get-tuple-element.81) | data formatting | bytes 65536 | tf_op jit(solution)/shard_map/reshape | solution.py:763
  54.2 1.1 %collective-permute-done.12.refs_1_ = f32[24,512]{1,0:T(8,128)S(1)} collective-permute-done((f32[24,512]{1,0:T(8,128)S(1)}, f32[24,512]{1,0:T(8,128)S(1)}, u32[]{:S(2)}, u32[]{:S(2)}) %collective-permute-start.12) | collective-permute-done | bytes 49184 | tf_op jit(solution)/shard_map/ppermute | solution.py:32
  55.3 0.6 %copy-done.6 = f32[24,512]{1,0:T(8,128)} copy-done((f32[24,512]{1,0:T(8,128)}, f32[24,512]{1,0:T(8,128)S(1)}, u32[]{:S(2)}) %copy-start.6) | copy-done | bytes 49176
  55.9 2.8 %shard_map.104 = f32[96,512]{1,0:T(8,128)} custom-call(f32[128,512]{1,0:T(8,128)} %copy-done.3, f32[24,512]{1,0:T(8,128)} %copy-done.6, f32[24,512]{1,0:T(8,128)} %copy-done.7, f32[128,128]{1,0:T(8,128)} %copy-done.4), custom_call_target="tpu_custom_call" | custom-call | tf_op jit(solution)/shard_map/pallas_call | solution.py:753
  (28 shorter events, 1.1 us)
Async XLA Ops:
  3.4 0.9 %copy-start = (f32[16,8,512]{2,1,0:T(8,128)S(1)}, f32[16,8,512]{2,1,0:T(8,128)}, u32[]{:S(2)}) copy-start(f32[16,8,512]{2,1,0:T(8,128)} %param.8) | copy-start | bytes 786436
  4.3 1.7 %copy-start.2 = (bf16[1664,768]{1,0:T(8,128)(2,1)S(1)}, bf16[1664,768]{1,0:T(8,128)(2,1)}, u32[]{:S(2)}) copy-start(bf16[1664,768]{1,0:T(8,128)(2,1)} %constant.33.clone.refs_3_) | copy-start | bytes 7667716
  6.0 0.7 %copy-start.5 = (bf16[3,64,16]{1,2,0:T(8,128)(2,1)S(1)}, bf16[3,64,16]{1,2,0:T(8,128)(2,1)}, u32[]{:S(2)}) copy-start(bf16[3,64,16]{1,2,0:T(8,128)(2,1)} %param.9) | copy-start | bytes 18436
  6.8 12.5 %copy-start.1 = (f32[16,8,512]{2,1,0:T(8,128)S(1)}, f32[16,8,512]{2,1,0:T(8,128)}, u32[]{:S(2)}) copy-start(f32[16,8,512]{2,1,0:T(8,128)} %param.8) | copy-start | bytes 786436
  9.6 0.6 %copy-start.4 = (f32[128,128]{1,0:T(8,128)}, f32[128,128]{1,0:T(8,128)S(1)}, u32[]{:S(2)}) copy-start(f32[128,128]{1,0:T(8,128)S(1)} %get-tuple-element.80.refs_3_) | copy-start | bytes 196612
  10.2 9.0 %collective-permute-start.2 = (bf16[256,128]{1,0:T(8,128)(2,1)S(1)}, bf16[256,128]{1,0:T(8,128)(2,1)S(1)}, u32[]{:S(2)}, u32[]{:S(2)}) collective-permute-start(bf16[256,128]{1,0:T(8,128)(2,1)S(1)} %get-tuple-element.44), channel_id=1, source_target_pairs={{0,16},{16,0},{1,17},{17,1},{2,18},{18,2},{3,19},{19,3},{4,20},{20... | collective-permute-start | bytes 196616 | tf_op jit(solution)/shard_map/ppermute | solution.py:32
  13.2 6.0 %collective-permute-start = (bf16[128,128]{1,0:T(8,128)(2,1)S(1)}, bf16[128,128]{1,0:T(8,128)(2,1)S(1)}, u32[]{:S(2)}, u32[]{:S(2)}) collective-permute-start(bf16[128,128]{1,0:T(8,128)(2,1)S(1)} %get-tuple-element.42), channel_id=1, source_target_pairs={{0,1},{1,2},{2,3},{3,4},{4,5},{5,6},{6,7},{7,8},{8,9},{9,10},{10,1... | collective-permute-start | bytes 98312 | tf_op jit(solution)/shard_map/ppermute | solution.py:32
  13.2 6.0 %collective-permute-start.1 = (bf16[128,128]{1,0:T(8,128)(2,1)S(1)}, bf16[128,128]{1,0:T(8,128)(2,1)S(1)}, u32[]{:S(2)}, u32[]{:S(2)}) collective-permute-start(bf16[128,128]{1,0:T(8,128)(2,1)S(1)} %get-tuple-element.43), channel_id=1, source_target_pairs={{0,15},{1,0},{2,1},{3,2},{4,3},{5,4},{6,5},{7,6},{8,7},{9,8},{10,9... | collective-permute-start | bytes 98312 | tf_op jit(solution)/shard_map/ppermute | solution.py:32
  20.7 6.2 %collective-permute-start.5 = (bf16[256,128]{1,0:T(8,128)(2,1)S(1)}, bf16[256,128]{1,0:T(8,128)(2,1)S(1)}, u32[]{:S(2)}, u32[]{:S(2)}) collective-permute-start(bf16[256,128]{1,0:T(8,128)(2,1)S(1)} %get-tuple-element.55), channel_id=1, source_target_pairs={{0,16},{16,0},{1,17},{17,1},{2,18},{18,2},{3,19},{19,3},{4,20},{20... | collective-permute-start | bytes 196616 | tf_op jit(solution)/shard_map/ppermute | solution.py:32
  20.8 6.1 %collective-permute-start.3 = (bf16[128,128]{1,0:T(8,128)(2,1)S(1)}, bf16[128,128]{1,0:T(8,128)(2,1)S(1)}, u32[]{:S(2)}, u32[]{:S(2)}) collective-permute-start(bf16[128,128]{1,0:T(8,128)(2,1)S(1)} %get-tuple-element.53), channel_id=1, source_target_pairs={{0,1},{1,2},{2,3},{3,4},{4,5},{5,6},{6,7},{7,8},{8,9},{9,10},{10,1... | collective-permute-start | bytes 98312 | tf_op jit(solution)/shard_map/ppermute | solution.py:32
  20.9 6.1 %collective-permute-start.4 = (bf16[128,128]{1,0:T(8,128)(2,1)S(1)}, bf16[128,128]{1,0:T(8,128)(2,1)S(1)}, u32[]{:S(2)}, u32[]{:S(2)}) collective-permute-start(bf16[128,128]{1,0:T(8,128)(2,1)S(1)} %get-tuple-element.54), channel_id=1, source_target_pairs={{0,15},{1,0},{2,1},{3,2},{4,3},{5,4},{6,5},{7,6},{8,7},{9,8},{10,9... | collective-permute-start | bytes 98312 | tf_op jit(solution)/shard_map/ppermute | solution.py:32
  29.2 8.0 %collective-permute-start.8 = (bf16[256,128]{1,0:T(8,128)(2,1)S(1)}, bf16[256,128]{1,0:T(8,128)(2,1)S(1)}, u32[]{:S(2)}, u32[]{:S(2)}) collective-permute-start(bf16[256,128]{1,0:T(8,128)(2,1)S(1)} %get-tuple-element.61), channel_id=1, source_target_pairs={{0,16},{16,0},{1,17},{17,1},{2,18},{18,2},{3,19},{19,3},{4,20},{20... | collective-permute-start | bytes 196616 | tf_op jit(solution)/shard_map/ppermute | solution.py:32
  31.2 6.0 %collective-permute-start.6 = (bf16[128,128]{1,0:T(8,128)(2,1)S(1)}, bf16[128,128]{1,0:T(8,128)(2,1)S(1)}, u32[]{:S(2)}, u32[]{:S(2)}) collective-permute-start(bf16[128,128]{1,0:T(8,128)(2,1)S(1)} %get-tuple-element.59), channel_id=1, source_target_pairs={{0,1},{1,2},{2,3},{3,4},{4,5},{5,6},{6,7},{7,8},{8,9},{9,10},{10,1... | collective-permute-start | bytes 98312 | tf_op jit(solution)/shard_map/ppermute | solution.py:32
  31.2 6.0 %collective-permute-start.7 = (bf16[128,128]{1,0:T(8,128)(2,1)S(1)}, bf16[128,128]{1,0:T(8,128)(2,1)S(1)}, u32[]{:S(2)}, u32[]{:S(2)}) collective-permute-start(bf16[128,128]{1,0:T(8,128)(2,1)S(1)} %get-tuple-element.60), channel_id=1, source_target_pairs={{0,15},{1,0},{2,1},{3,2},{4,3},{5,4},{6,5},{7,6},{8,7},{9,8},{10,9... | collective-permute-start | bytes 98312 | tf_op jit(solution)/shard_map/ppermute | solution.py:32
  40.0 6.2 %collective-permute-start.11 = (bf16[256,128]{1,0:T(8,128)(2,1)S(1)}, bf16[256,128]{1,0:T(8,128)(2,1)S(1)}, u32[]{:S(2)}, u32[]{:S(2)}) collective-permute-start(bf16[256,128]{1,0:T(8,128)(2,1)S(1)} %get-tuple-element.70), channel_id=1, source_target_pairs={{0,16},{16,0},{1,17},{17,1},{2,18},{18,2},{3,19},{19,3},{4,20},{20... | collective-permute-start | bytes 196616 | tf_op jit(solution)/shard_map/ppermute | solution.py:32
  40.1 6.0 %collective-permute-start.9 = (bf16[128,128]{1,0:T(8,128)(2,1)S(1)}, bf16[128,128]{1,0:T(8,128)(2,1)S(1)}, u32[]{:S(2)}, u32[]{:S(2)}) collective-permute-start(bf16[128,128]{1,0:T(8,128)(2,1)S(1)} %get-tuple-element.68), channel_id=1, source_target_pairs={{0,1},{1,2},{2,3},{3,4},{4,5},{5,6},{6,7},{7,8},{8,9},{9,10},{10,1... | collective-permute-start | bytes 98312 | tf_op jit(solution)/shard_map/ppermute | solution.py:32
  40.1 6.0 %collective-permute-start.10 = (bf16[128,128]{1,0:T(8,128)(2,1)S(1)}, bf16[128,128]{1,0:T(8,128)(2,1)S(1)}, u32[]{:S(2)}, u32[]{:S(2)}) collective-permute-start(bf16[128,128]{1,0:T(8,128)(2,1)S(1)} %get-tuple-element.69), channel_id=1, source_target_pairs={{0,15},{1,0},{2,1},{3,2},{4,3},{5,4},{6,5},{7,6},{8,7},{9,8},{10,9... | collective-permute-start | bytes 98312 | tf_op jit(solution)/shard_map/ppermute | solution.py:32
  48.4 0.7 %copy-start.3 = (f32[128,512]{1,0:T(8,128)}, f32[128,512]{1,0:T(8,128)S(1)}, u32[]{:S(2)}) copy-start(f32[128,512]{1,0:T(8,128)S(1)} %get-tuple-element.77.refs_0_) | copy-start | bytes 786436
  49.1 6.2 %collective-permute-start.12 = (f32[24,512]{1,0:T(8,128)S(1)}, f32[24,512]{1,0:T(8,128)S(1)}, u32[]{:S(2)}, u32[]{:S(2)}) collective-permute-start(f32[24,512]{1,0:T(8,128)S(1)} %get-tuple-element.78), channel_id=1, source_target_pairs={{0,1},{1,2},{2,3},{3,4},{4,5},{5,6},{6,7},{7,8},{8,9},{9,10},{10,1... | collective-permute-start | bytes 147464 | tf_op jit(solution)/shard_map/ppermute | solution.py:32
  49.1 6.2 %collective-permute-start.13 = (f32[24,512]{1,0:T(8,128)S(1)}, f32[24,512]{1,0:T(8,128)S(1)}, u32[]{:S(2)}, u32[]{:S(2)}) collective-permute-start(f32[24,512]{1,0:T(8,128)S(1)} %get-tuple-element.79), channel_id=1, source_target_pairs={{0,15},{1,0},{2,1},{3,2},{4,3},{5,4},{6,5},{7,6},{8,7},{9,8},{10,9... | collective-permute-start | bytes 147464 | tf_op jit(solution)/shard_map/ppermute | solution.py:32
  55.3 0.6 %copy-start.6 = (f32[24,512]{1,0:T(8,128)}, f32[24,512]{1,0:T(8,128)S(1)}, u32[]{:S(2)}) copy-start(f32[24,512]{1,0:T(8,128)S(1)} %collective-permute-done.12.refs_1_) | copy-start | bytes 147460
  55.3 0.6 %copy-start.7 = (f32[24,512]{1,0:T(8,128)}, f32[24,512]{1,0:T(8,128)S(1)}, u32[]{:S(2)}) copy-start(f32[24,512]{1,0:T(8,128)S(1)} %collective-permute-done.13.refs_2_) | copy-start | bytes 147460

commit v12 on v9

--- a/solution.py
+++ b/solution.py
@@ -438,9 +438,8 @@
     )(*inputs)
 
 
-def setup_kernel(local, fields, u_ref, vt_ref, packed_ref, tab_ref, v7_out, m7_out, v3_out, m3_out, pl_out, pr_out,
-                 pre_out, stc_out, sw_out, hinfo_out, cnt_l_out, cnt_r_out, sel_l_out,
-                 sel_r_out, *send_refs):
+def setup_kernel(local, fields, u_ref, vt_ref, packed_ref, tab_ref, v7_out, m7_out, pl_out, pr_out,
+                 pre_out, stc_out, sw_out, *send_refs):
     rows = local * fields
     views = table_views(tab_ref, rows, local)
     lift_ref = views["lift_t"]
@@ -456,17 +455,13 @@
         vt = vt_ref[d]
         fv = _dot(vt, lift_ref[...]).astype(bf16)
         v7_out[d] = _dot(bcast, fv).astype(bf16)
-        v3_out[d] = _dot(bcast, vt)
         fvg.append(_dot(fv, g7_ref[...]))
-        mvg.append((_dot(vt, tm_ref[0]) + _dot(vt, tm_ref[1])) + _dot(vt, tm_ref[2]))
 
     def by_block(parts):
         return jnp.where(lanes < 2, parts[0], jnp.where(lanes < 4, parts[1], parts[2]))
 
     m7 = jnp.minimum(sign * by_block(fvg), 0.0)
     m7_out[...] = _dot(bcast, m7.astype(bf16))
-    m3 = jnp.minimum(sign * by_block(mvg), 0.0)
-    m3_out[...] = _exact_right(bcast, m3)
     eye16 = jnp.where(
         lax.broadcasted_iota(jnp.int32, (local, LANE), 0)
         == lax.broadcasted_iota(jnp.int32, (local, LANE), 1), 1.0, 0.0
@@ -485,6 +480,32 @@
         if side in SEND_FACES:
             pr_out[SEND_FACES.index(side)] = jnp.where(hit & far, 1.0, 0.0).astype(bf16)
     sw_out[...] = rep[:, 6:7]
+    pre_out[...] = packed[:, 7:8]
+    stc_out[...] = _exact_right(fsel_ref[...], packed)[:, 8:9]
+    write_sends(send_refs, _dot(u_ref[...].astype(bf16), g7_ref[...]).astype(bf16))
+
+
+def late_kernel(local, fields, vt_ref, packed_ref, tab_ref, v3_out, m3_out, hinfo_out,
+                cnt_l_out, cnt_r_out, sel_l_out, sel_r_out):
+    rows = local * fields
+    views = table_views(tab_ref, rows, local)
+    tm_ref = views["tm"]
+    bcast = views["bcast"][...]
+    lanes = lax.broadcasted_iota(jnp.int32, (local, 6 * LANE), 1) // LANE
+    sign = jnp.where(lanes % 2 == 0, -1.0, 1.0)
+    mvg = []
+    for d in range(3):
+        vt = vt_ref[d]
+        v3_out[d] = _dot(bcast, vt)
+        mvg.append((_dot(vt, tm_ref[0]) + _dot(vt, tm_ref[1])) + _dot(vt, tm_ref[2]))
+    by_block = jnp.where(lanes < 2, mvg[0], jnp.where(lanes < 4, mvg[1], mvg[2]))
+    m3_out[...] = _exact_right(bcast, jnp.minimum(sign * by_block, 0.0))
+    eye16 = jnp.where(
+        lax.broadcasted_iota(jnp.int32, (local, LANE), 0)
+        == lax.broadcasted_iota(jnp.int32, (local, LANE), 1), 1.0, 0.0
+    ).astype(bf16)
+    p_hi, p_mid, p_lo = _split(packed_ref[...])
+    packed = (_dot_t(eye16, p_hi) + _dot_t(eye16, p_mid)) + _dot_t(eye16, p_lo)
     curve_count = lax.axis_size("curve")
     curve_pos = lax.axis_index("curve")
     left_f = ((curve_pos + curve_count - 1) % curve_count).astype(f32)
@@ -528,9 +549,6 @@
             & (cc < MOVE_CAP * fields)
         )
         out[...] = _dot_t(eye, jnp.where(hit, 1.0, 0.0).astype(bf16)).astype(bf16)
-    pre_out[...] = packed[:, 7:8]
-    stc_out[...] = _exact_right(fsel_ref[...], packed)[:, 8:9]
-    write_sends(send_refs, _dot(u_ref[...].astype(bf16), g7_ref[...]).astype(bf16))
 
 
 def final_kernel(fields, hold, home_ref, from_l_ref, from_r_ref, hinfo_ref, out_ref):
@@ -663,19 +681,21 @@
     setup_out = [
         jax.ShapeDtypeStruct((3, rows, P7**3), bf16),
         jax.ShapeDtypeStruct((rows, 6 * LANE), f32),
-        jax.ShapeDtypeStruct((3, rows, P3**3), f32),
-        jax.ShapeDtypeStruct((rows, 6 * LANE), f32),
         jax.ShapeDtypeStruct((6, rows, rows), bf16),
         jax.ShapeDtypeStruct((len(SEND_FACES), rows, rows), bf16),
         jax.ShapeDtypeStruct((local_count, 1), f32),
         jax.ShapeDtypeStruct((rows, 1), f32),
         jax.ShapeDtypeStruct((rows, 1), f32),
+    ] + sends_shape
+    late_out = [
+        jax.ShapeDtypeStruct((3, rows, P3**3), f32),
+        jax.ShapeDtypeStruct((rows, 6 * LANE), f32),
         jax.ShapeDtypeStruct((rows, LANE), f32),
         jax.ShapeDtypeStruct((8, LANE), f32),
         jax.ShapeDtypeStruct((8, LANE), f32),
         jax.ShapeDtypeStruct((MOVE_CAP * field_count, rows), bf16),
         jax.ShapeDtypeStruct((MOVE_CAP * field_count, rows), bf16),
-    ] + sends_shape
+    ]
     setup_out = setup_out + [jax.ShapeDtypeStruct(table.shape, table.dtype)]
     u0 = state.reshape(rows, P7**3)
     setup_in = [u0, vt, packed, table]
@@ -688,10 +708,16 @@
         + [pltpu.SemaphoreType.DMA((len(setup_in),))],
         compiler_params=pltpu.CompilerParams(vmem_limit_bytes=24 * 1024 * 1024),
     )(*setup_in)
-    v7, m7, v3, m3, p_local, p_remote, pre, stc, sw = res[:9]
-    hinfo, cnt_l, cnt_r, sel_l, sel_r = res[9:14]
-    sends = res[14:17]
-    table = res[17]
+    v7, m7, p_local, p_remote, pre, stc, sw = res[:7]
+    sends = res[7:10]
+    table = res[10]
+    v3, m3, hinfo, cnt_l, cnt_r, sel_l, sel_r = pl.pallas_call(
+        functools.partial(late_kernel, local_count, field_count),
+        out_shape=late_out,
+        in_specs=[_vmem() for _ in range(3)],
+        out_specs=[_vmem() for _ in late_out],
+        compiler_params=pltpu.CompilerParams(vmem_limit_bytes=24 * 1024 * 1024),
+    )(vt, packed, table)
     common = [p_local, p_remote, v7, m7, pre, stc, table]
     recv = exchange(sends)
     bulk_tabs = [v7, pre, stc, table]

time: 59 us -> 58.3 us (0.988)
  waiting for transfers between devices: 4.35 us -> 3.65 us
  local copies, waits for them, and re-layouts: 7.36 us -> 6.76 us
    pallas_call x0 -> x1, Pallas kernels: none -> 1.27 us  [per_device(): pl.pallas_call(functools.partial(late_kernel, local_count, field_count),...]
    pallas_call x1, Pallas kernels: 2.86 us -> 2.12 us  [per_device(): pl.pallas_call(functools.partial(setup_entry, local_count, field_count, l...]
    ppermute x14, waiting for transfers between devices: 4.35 us -> 3.65 us  [shifted(): return lax.ppermute(value, axis, pairs)]
    unnamed x16 -> x18, local copies, waits for them, and re-layouts: 5.31 us -> 4.71 us
  transfers between devices with their start and end apart: 14 -> 14, of which waited for: 6 -> 5; matrix products, arithmetic and copies ran while one was open for 1% -> 1% of each run, Pallas kernels for 5% -> 8%
where the time goes in v12:
time: 58.3 us; the launch traced here: 58 us
  starting transfers between devices  27.6 us (47%)
  Pallas kernels  17.8 us (31%)
  local copies, waits for them, and re-layouts  6.76 us (12%)
  waiting for transfers between devices  3.65 us (6%)
  other arithmetic  1.37 us (2%)
  between operations  0.78 us (1%)
    ppermute x14, starting transfers between devices, shifted(): return lax.ppermute(value, axis, pairs)  27.6 us
    pallas_call x4, Pallas kernels, run_stage(): pl.pallas_call(kernel, out_shape=out_shapes, in_specs=[_vmem() for _ in i...  8.62 us
    unnamed x18, local copies, waits for them, and re-layouts  4.71 us
    ppermute x14, waiting for transfers between devices, shifted(): return lax.ppermute(value, axis, pairs)  3.65 us
    pallas_call x4, Pallas kernels, run_bulk(): pl.pallas_call(functools.partial(bulk_kernel, coarse, local), out_shape=o...  3.1 us
    pallas_call x1, Pallas kernels, per_device(): pl.pallas_call(functools.partial(final_kernel, field_count, HOLD7), out_s...  2.74 us
    pallas_call x1, Pallas kernels, per_device(): pl.pallas_call(functools.partial(setup_entry, local_count, field_count, l...  2.12 us
    pallas_call x1, Pallas kernels, per_device(): pl.pallas_call(functools.partial(late_kernel, local_count, field_count),...  1.27 us
  transfers between devices with their start and end apart: 14, of which 5 were waited for; matrix products, arithmetic and copies ran while one was open for 1% of the time, Pallas kernels for 8%

profile of v12, /device:TPU:0, one launch (start us, length us, event | category | flops | bytes accessed | tf_op | source)
XLA Modules:
  0.0 58.0 jit_solution(2344533339956931120)
XLA Ops:
  0.6 0.7 %pad_bitcast_fusion = f32[1,16]{1,0:T(1,128)S(1)} fusion(f32[8]{0:T(128)} %param.11), kind=kLoop, calls=%fused_computation.9 | loop fusion | bytes 96 | tf_op jit(solution)/shard_map/stack | solution.py:625
  1.3 0.7 %convert_bitcast_fusion.1 = (f32[1,16]{1,0:T(1,128)S(1)}, f32[1,16]{1,0:T(1,128)S(1)}) fusion(s32[16]{0:T(128)} %param.14, s32[16]{0:T(128)} %param.13), kind=kLoop, calls=%fused_computation.8 | loop fusion | flops 32 | bytes 256 | tf_op jit(solution)/shard_map/stack | solution.py:625
  2.0 0.7 %convert_bitcast_fusion = f32[6,16]{1,0:T(8,128)S(1)} fusion(s32[16,6]{0,1:T(8,128)} %param.12, s32[]{:T(128)S(6)} %add.11), kind=kLoop, calls=%fused_computation.5 | loop fusion | flops 2016 | bytes 772 | tf_op jit(solution)/shard_map/transpose | solution.py:624
  2.7 0.7 %concatenate.3 = f32[10,16]{1,0:T(8,128)S(1)} concatenate(f32[6,16]{1,0:T(8,128)S(1)} %convert_bitcast_fusion, f32[1,16]{1,0:T(1,128)S(1)} %get-tuple-element.83, f32[1,16]{1,0:T(1,128)} %bitcast.19, f32[1,16]{1,0:T(1,128)S(1)} %pad_bitcast_fusion, f32[1,16]{1,0:T(1,128)S(1)} %get-tuple-element.82), dimensions={0} | concatenate | bytes 1280 | tf_op jit(solution)/shard_map/concatenate | solution.py:622
  3.4 0.9 %copy-done = f32[16,8,512]{2,1,0:T(8,128)S(1)} copy-done((f32[16,8,512]{2,1,0:T(8,128)S(1)}, f32[16,8,512]{2,1,0:T(8,128)}, u32[]{:S(2)}) %copy-start) | copy-done | bytes 262168
  4.3 1.7 %copy-done.2 = bf16[1664,768]{1,0:T(8,128)(2,1)S(1)} copy-done((bf16[1664,768]{1,0:T(8,128)(2,1)S(1)}, bf16[1664,768]{1,0:T(8,128)(2,1)}, u32[]{:S(2)}) %copy-start.2) | copy-done | bytes 2555928
  6.0 0.7 %copy-done.5 = bf16[3,64,16]{1,2,0:T(8,128)(2,1)S(1)} copy-done((bf16[3,64,16]{1,2,0:T(8,128)(2,1)S(1)}, bf16[3,64,16]{1,2,0:T(8,128)(2,1)}, u32[]{:S(2)}) %copy-start.5) | copy-done | bytes 6168
  6.8 2.1 %shard_map.95 = (bf16[3,128,512]{2,1,0:T(8,128)(2,1)S(1)}, f32[128,768]{1,0:T(8,128)S(1)}, bf16[6,128,128]{2,1,0:T(8,128)(2,1)S(1)}, bf16[4,128,128]{2,1,0:T(8,1...) custom-call(f32[128,512]{1,0:T(8,128)S(1)} %bitcast.12, ...), custom_call_target="tpu_custom_call" | custom-call | tf_op jit(solution)/shard_map/pallas_call | solution.py:702
  8.9 3.0 %collective-permute-start.2 = (bf16[256,128]{1,0:T(8,128)(2,1)S(1)}, bf16[256,128]{1,0:T(8,128)(2,1)S(1)}, u32[]{:S(2)}, u32[]{:S(2)}) collective-permute-start(bf16[256,128]{1,0:T(8,128)(2,1)S(1)} %get-tuple-element.44), channel_id=1, source_target_pairs={{0,16},{16,0},{1,17},{17,1},{2,18},{18,2},{3,19},{19,3},{4,20},{20... | collective-permute-start | bytes 196616 | tf_op jit(solution)/shard_map/ppermute | solution.py:32
  11.9 4.4 %collective-permute-start.1 = (bf16[128,128]{1,0:T(8,128)(2,1)S(1)}, bf16[128,128]{1,0:T(8,128)(2,1)S(1)}, u32[]{:S(2)}, u32[]{:S(2)}) collective-permute-start(bf16[128,128]{1,0:T(8,128)(2,1)S(1)} %get-tuple-element.43), channel_id=1, source_target_pairs={{0,15},{1,0},{2,1},{3,2},{4,3},{5,4},{6,5},{7,6},{8,7},{9,8},{10,9... | collective-permute-start | bytes 98312 | tf_op jit(solution)/shard_map/ppermute | solution.py:32
  16.4 0.7 %shard_map.96.refs_12_ = f32[128,512]{1,0:T(8,128)S(1)} custom-call(f32[128,512]{1,0:T(8,128)S(1)} %bitcast.13, bf16[3,128,512]{2,1,0:T(8,128)(2,1)S(1)} %get-tuple-element.47.refs_1_.refs_7_.refs_8_.refs_2_.refs_10_, f32[16,1]{1,0:T(8,128)S(1)} %get-tuple-element.49.refs_2_.refs_9_.refs_10_.refs_3_.refs_12_, ...), custom_call_target="tpu_custom_call" | custom-call | tf_op jit(solution)/shard_map/pallas_call | solution.py:420
  17.0 0.9 %collective-permute-done.refs_1_ = bf16[128,128]{1,0:T(8,128)(2,1)S(1)} collective-permute-done((bf16[128,128]{1,0:T(8,128)(2,1)S(1)}, bf16[128,128]{1,0:T(8,128)(2,1)S(1)}, u32[]{:S(2)}, u32[]{:S(2)}) %collective-permute-start) | collective-permute-done | bytes 32800 | tf_op jit(solution)/shard_map/ppermute | solution.py:32
  18.0 1.5 %shard_map.97 = (f32[128,512]{1,0:T(8,128)S(1)}, bf16[128,128]{1,0:T(8,128)(2,1)S(1)}, bf16[128,128]{1,0:T(8,128)(2,1)S(1)}, bf16[256,128]{1,0:T(8,128)(2,1)S(1)}) custom-call(f32[128,512]{1,0:T(8,128)S(1)} %bitcast.14, bf16[128,128]{1,0:T(8,128)(2,1)S(1)} %collective-permute-done.refs_1_, bf16[128,128]{1,0:T(8,128)(2,1)S(1)} %collective-permute-done.1.refs_2_, ...), custom_call_target="tpu_custom_call" | custom-call | tf_op jit(solution)/shard_map/pallas_call | solution.py:432
  19.6 4.5 %collective-permute-start.4 = (bf16[128,128]{1,0:T(8,128)(2,1)S(1)}, bf16[128,128]{1,0:T(8,128)(2,1)S(1)}, u32[]{:S(2)}, u32[]{:S(2)}) collective-permute-start(bf16[128,128]{1,0:T(8,128)(2,1)S(1)} %get-tuple-element.54), channel_id=1, source_target_pairs={{0,15},{1,0},{2,1},{3,2},{4,3},{5,4},{6,5},{7,6},{8,7},{9,8},{10,9... | collective-permute-start | bytes 98312 | tf_op jit(solution)/shard_map/ppermute | solution.py:32
  24.1 0.7 %shard_map.98.refs_14_ = f32[128,512]{1,0:T(8,128)S(1)} custom-call(f32[128,512]{1,0:T(8,128)S(1)} %get-tuple-element.52.refs_0_, bf16[3,128,512]{2,1,0:T(8,128)(2,1)S(1)} %get-tuple-element.47.refs_1_.refs_7_.refs_8_.refs_2_.refs_10_, f32[16,1]{1,0:T(8,128)S(1)} %get-tuple-element.49.refs_2_.refs_9_.refs_10_.refs_3_.refs_12_, ...), custom_call_target="tpu_custom_call" | custom-call | tf_op jit(solution)/shard_map/pallas_call | solution.py:420
  24.7 0.9 %collective-permute-done.3.refs_2_ = bf16[128,128]{1,0:T(8,128)(2,1)S(1)} collective-permute-done((bf16[128,128]{1,0:T(8,128)(2,1)S(1)}, bf16[128,128]{1,0:T(8,128)(2,1)S(1)}, u32[]{:S(2)}, u32[]{:S(2)}) %collective-permute-start.3) | collective-permute-done | bytes 32800 | tf_op jit(solution)/shard_map/ppermute | solution.py:32
  25.7 2.3 %shard_map.99 = (f32[128,512]{1,0:T(8,128)S(1)}, f32[128,64]{1,0:T(8,128)S(1)}, bf16[128,128]{1,0:T(8,128)(2,1)S(1)}, bf16[128,128]{1,0:T(8,128)(2,1)S(1)}, bf16[256,128]{1,0:T(8,128)(2,1)S(1)}) custom-call(f32[128,512]{1,0:T(8,128)S(1)} %get-tuple-element.52.refs_0_, f32[128,512]{1,0:T(8,128)S(1)} %bitcast.15, ...), custom_call_target="tpu_custom_call" | custom-call | tf_op jit(solution)/shard_map/pallas_call | solution.py:432
  28.0 2.0 %collective-permute-start.8 = (bf16[256,128]{1,0:T(8,128)(2,1)S(1)}, bf16[256,128]{1,0:T(8,128)(2,1)S(1)}, u32[]{:S(2)}, u32[]{:S(2)}) collective-permute-start(bf16[256,128]{1,0:T(8,128)(2,1)S(1)} %get-tuple-element.61), channel_id=1, source_target_pairs={{0,16},{16,0},{1,17},{17,1},{2,18},{18,2},{3,19},{19,3},{4,20},{20... | collective-permute-start | bytes 196616 | tf_op jit(solution)/shard_map/ppermute | solution.py:32
  29.9 4.4 %collective-permute-start.7 = (bf16[128,128]{1,0:T(8,128)(2,1)S(1)}, bf16[128,128]{1,0:T(8,128)(2,1)S(1)}, u32[]{:S(2)}, u32[]{:S(2)}) collective-permute-start(bf16[128,128]{1,0:T(8,128)(2,1)S(1)} %get-tuple-element.60), channel_id=1, source_target_pairs={{0,15},{1,0},{2,1},{3,2},{4,3},{5,4},{6,5},{7,6},{8,7},{9,8},{10,9... | collective-permute-start | bytes 98312 | tf_op jit(solution)/shard_map/ppermute | solution.py:32
  34.4 1.3 %shard_map.100 = (f32[3,128,64]{2,1,0:T(8,128)S(1)}, f32[128,768]{1,0:T(8,128)S(1)}, f32[128,128]{1,0:T(8,128)S(1)}, f32[8,128]{1,0:T(8,128)S(1)}, f32[8,128]{1,...) custom-call(bf16[3,16,64]{2,1,0:T(8,128)(2,1)S(1)} %bitcast.17, ...), custom_call_target="tpu_custom_call" | custom-call | tf_op jit(solution)/shard_map/pallas_call | solution.py:714
  35.6 0.9 %shard_map.101 = (f32[128,512]{1,0:T(8,128)S(1)}, f32[128,64]{1,0:T(8,128)S(1)}) custom-call(f32[128,512]{1,0:T(8,128)S(1)} %get-tuple-element.57.refs_0_.refs_2_, f32[128,64]{1,0:T(8,128)S(1)} %get-tuple-element.58.refs_1_.refs_3_, bf16[3,128,512]{2,1,0:T(8,128)(2,1)S(1)} %get-tuple-element.47.refs_1_.refs_7_.refs_8_.refs_2_.refs_10_, ...), custom_call_target="tpu_custom_call" | custom-call | tf_op jit(solution)/shard_map/pallas_call | solution.py:420
  36.6 2.7 %shard_map.102 = (f32[128,512]{1,0:T(8,128)S(1)}, f32[128,64]{1,0:T(8,128)S(1)}, bf16[128,128]{1,0:T(8,128)(2,1)S(1)}, bf16[128,128]{1,0:T(8,128)(2,1)S(1)}, bf16[256,128]{1,0:T(8,128)(2,1)S(1)}) custom-call(f32[128,512]{1,0:T(8,128)S(1)} %get-tuple-element.57.refs_0_.refs_2_, f32[128,64]{1,0:T(8,128)S(1)} %get-tuple-element.58.refs_1_.refs_3_, ...), custom_call_target="tpu_custom_call" | custom-call | tf_op jit(solution)/shard_map/pallas_call | solution.py:432
  39.5 4.4 %collective-permute-start.10 = (bf16[128,128]{1,0:T(8,128)(2,1)S(1)}, bf16[128,128]{1,0:T(8,128)(2,1)S(1)}, u32[]{:S(2)}, u32[]{:S(2)}) collective-permute-start(bf16[128,128]{1,0:T(8,128)(2,1)S(1)} %get-tuple-element.69), channel_id=1, source_target_pairs={{0,15},{1,0},{2,1},{3,2},{4,3},{5,4},{6,5},{7,6},{8,7},{9,8},{10,9... | collective-permute-start | bytes 98312 | tf_op jit(solution)/shard_map/ppermute | solution.py:32
  43.9 0.9 %shard_map.103 = (f32[128,512]{1,0:T(8,128)S(1)}, f32[128,64]{1,0:T(8,128)S(1)}) custom-call(f32[128,512]{1,0:T(8,128)S(1)} %get-tuple-element.66.refs_0_, f32[128,64]{1,0:T(8,128)S(1)} %get-tuple-element.67.refs_1_, bf16[3,128,512]{2,1,0:T(8,128)(2,1)S(1)} %get-tuple-element.47.refs_1_.refs_7_.refs_8_.refs_2_.refs_10_, ...), custom_call_target="tpu_custom_call" | custom-call | tf_op jit(solution)/shard_map/pallas_call | solution.py:420
  44.8 0.7 %collective-permute-done.9.refs_4_ = bf16[128,128]{1,0:T(8,128)(2,1)S(1)} collective-permute-done((bf16[128,128]{1,0:T(8,128)(2,1)S(1)}, bf16[128,128]{1,0:T(8,128)(2,1)S(1)}, u32[]{:S(2)}, u32[]{:S(2)}) %collective-permute-start.9) | collective-permute-done | bytes 32800 | tf_op jit(solution)/shard_map/ppermute | solution.py:32
  45.5 2.2 %shard_map.104 = (f32[128,512]{1,0:T(8,128)S(1)}, f32[128,64]{1,0:T(8,128)S(1)}, f32[24,512]{1,0:T(8,128)S(1)}, f32[24,512]{1,0:T(8,128)S(1)}) custom-call(f32[128,512]{1,0:T(8,128)S(1)} %get-tuple-element.66.refs_0_, f32[128,64]{1,0:T(8,128)S(1)} %get-tuple-element.67.refs_1_, f32[128,512]{1,0:T(8,128)S(1)} %get-tuple-element.57.refs_0_.refs_2_, ...), custom_call_target="tpu_custom_call" | custom-call | tf_op jit(solution)/shard_map/pallas_call | solution.py:432
  47.7 0.7 %copy-done.3 = f32[128,512]{1,0:T(8,128)} copy-done((f32[128,512]{1,0:T(8,128)}, f32[128,512]{1,0:T(8,128)S(1)}, u32[]{:S(2)}) %copy-start.3) | copy-done | bytes 262168
  48.4 4.4 %collective-permute-start.13 = (f32[24,512]{1,0:T(8,128)S(1)}, f32[24,512]{1,0:T(8,128)S(1)}, u32[]{:S(2)}, u32[]{:S(2)}) collective-permute-start(f32[24,512]{1,0:T(8,128)S(1)} %get-tuple-element.79), channel_id=1, source_target_pairs={{0,15},{1,0},{2,1},{3,2},{4,3},{5,4},{6,5},{7,6},{8,7},{9,8},{10,9... | collective-permute-start | bytes 147464 | tf_op jit(solution)/shard_map/ppermute | solution.py:32
  52.9 0.7 %reshape.15 = f32[16,512]{1,0:T(8,128)} reshape(f32[128,64]{1,0:T(8,128)S(1)} %get-tuple-element.81) | data formatting | bytes 65536 | tf_op jit(solution)/shard_map/reshape | solution.py:767
  53.6 1.1 %collective-permute-done.12.from_l_ref = f32[24,512]{1,0:T(8,128)S(1)} collective-permute-done((f32[24,512]{1,0:T(8,128)S(1)}, f32[24,512]{1,0:T(8,128)S(1)}, u32[]{:S(2)}, u32[]{:S(2)}) %collective-permute-start.12) | collective-permute-done | bytes 49184 | tf_op jit(solution)/shard_map/ppermute | solution.py:32
  54.6 0.6 %copy-done.7 = f32[24,512]{1,0:T(8,128)} copy-done((f32[24,512]{1,0:T(8,128)}, f32[24,512]{1,0:T(8,128)S(1)}, u32[]{:S(2)}) %copy-start.7) | copy-done | bytes 49176
  55.3 2.7 %shard_map.105 = f32[96,512]{1,0:T(8,128)} custom-call(f32[128,512]{1,0:T(8,128)} %copy-done.3, f32[24,512]{1,0:T(8,128)} %copy-done.7, f32[24,512]{1,0:T(8,128)} %copy-done.8, f32[128,128]{1,0:T(8,128)} %copy-done.4), custom_call_target="tpu_custom_call" | custom-call | tf_op jit(solution)/shard_map/pallas_call | solution.py:760
  (31 shorter events, 0.5 us)
Async XLA Ops:
  3.4 0.9 %copy-start = (f32[16,8,512]{2,1,0:T(8,128)S(1)}, f32[16,8,512]{2,1,0:T(8,128)}, u32[]{:S(2)}) copy-start(f32[16,8,512]{2,1,0:T(8,128)} %param.8) | copy-start | bytes 786436
  4.3 1.7 %copy-start.2 = (bf16[1664,768]{1,0:T(8,128)(2,1)S(1)}, bf16[1664,768]{1,0:T(8,128)(2,1)}, u32[]{:S(2)}) copy-start(bf16[1664,768]{1,0:T(8,128)(2,1)} %constant.33.clone.refs_3_) | copy-start | bytes 7667716
  6.0 0.7 %copy-start.5 = (bf16[3,64,16]{1,2,0:T(8,128)(2,1)S(1)}, bf16[3,64,16]{1,2,0:T(8,128)(2,1)}, u32[]{:S(2)}) copy-start(bf16[3,64,16]{1,2,0:T(8,128)(2,1)} %param.9) | copy-start | bytes 18436
  6.8 11.2 %copy-start.1 = (f32[16,8,512]{2,1,0:T(8,128)S(1)}, f32[16,8,512]{2,1,0:T(8,128)}, u32[]{:S(2)}) copy-start(f32[16,8,512]{2,1,0:T(8,128)} %param.8) | copy-start | bytes 786436
  8.9 9.1 %collective-permute-start.2 = (bf16[256,128]{1,0:T(8,128)(2,1)S(1)}, bf16[256,128]{1,0:T(8,128)(2,1)S(1)}, u32[]{:S(2)}, u32[]{:S(2)}) collective-permute-start(bf16[256,128]{1,0:T(8,128)(2,1)S(1)} %get-tuple-element.44), channel_id=1, source_target_pairs={{0,16},{16,0},{1,17},{17,1},{2,18},{18,2},{3,19},{19,3},{4,20},{20... | collective-permute-start | bytes 196616 | tf_op jit(solution)/shard_map/ppermute | solution.py:32
  11.9 6.0 %collective-permute-start = (bf16[128,128]{1,0:T(8,128)(2,1)S(1)}, bf16[128,128]{1,0:T(8,128)(2,1)S(1)}, u32[]{:S(2)}, u32[]{:S(2)}) collective-permute-start(bf16[128,128]{1,0:T(8,128)(2,1)S(1)} %get-tuple-element.42), channel_id=1, source_target_pairs={{0,1},{1,2},{2,3},{3,4},{4,5},{5,6},{6,7},{7,8},{8,9},{9,10},{10,1... | collective-permute-start | bytes 98312 | tf_op jit(solution)/shard_map/ppermute | solution.py:32
  11.9 6.0 %collective-permute-start.1 = (bf16[128,128]{1,0:T(8,128)(2,1)S(1)}, bf16[128,128]{1,0:T(8,128)(2,1)S(1)}, u32[]{:S(2)}, u32[]{:S(2)}) collective-permute-start(bf16[128,128]{1,0:T(8,128)(2,1)S(1)} %get-tuple-element.43), channel_id=1, source_target_pairs={{0,15},{1,0},{2,1},{3,2},{4,3},{5,4},{6,5},{7,6},{8,7},{9,8},{10,9... | collective-permute-start | bytes 98312 | tf_op jit(solution)/shard_map/ppermute | solution.py:32
  19.4 6.2 %collective-permute-start.5 = (bf16[256,128]{1,0:T(8,128)(2,1)S(1)}, bf16[256,128]{1,0:T(8,128)(2,1)S(1)}, u32[]{:S(2)}, u32[]{:S(2)}) collective-permute-start(bf16[256,128]{1,0:T(8,128)(2,1)S(1)} %get-tuple-element.55), channel_id=1, source_target_pairs={{0,16},{16,0},{1,17},{17,1},{2,18},{18,2},{3,19},{19,3},{4,20},{20... | collective-permute-start | bytes 196616 | tf_op jit(solution)/shard_map/ppermute | solution.py:32
  19.6 6.0 %collective-permute-start.3 = (bf16[128,128]{1,0:T(8,128)(2,1)S(1)}, bf16[128,128]{1,0:T(8,128)(2,1)S(1)}, u32[]{:S(2)}, u32[]{:S(2)}) collective-permute-start(bf16[128,128]{1,0:T(8,128)(2,1)S(1)} %get-tuple-element.53), channel_id=1, source_target_pairs={{0,1},{1,2},{2,3},{3,4},{4,5},{5,6},{6,7},{7,8},{8,9},{9,10},{10,1... | collective-permute-start | bytes 98312 | tf_op jit(solution)/shard_map/ppermute | solution.py:32
  19.6 6.1 %collective-permute-start.4 = (bf16[128,128]{1,0:T(8,128)(2,1)S(1)}, bf16[128,128]{1,0:T(8,128)(2,1)S(1)}, u32[]{:S(2)}, u32[]{:S(2)}) collective-permute-start(bf16[128,128]{1,0:T(8,128)(2,1)S(1)} %get-tuple-element.54), channel_id=1, source_target_pairs={{0,15},{1,0},{2,1},{3,2},{4,3},{5,4},{6,5},{7,6},{8,7},{9,8},{10,9... | collective-permute-start | bytes 98312 | tf_op jit(solution)/shard_map/ppermute | solution.py:32
  24.7 9.6 %copy-start.6 = (bf16[3,64,16]{1,2,0:T(8,128)(2,1)S(1)}, bf16[3,64,16]{1,2,0:T(8,128)(2,1)}, u32[]{:S(2)}) copy-start(bf16[3,64,16]{1,2,0:T(8,128)(2,1)} %param.9) | copy-start | bytes 18436
  28.0 8.6 %collective-permute-start.8 = (bf16[256,128]{1,0:T(8,128)(2,1)S(1)}, bf16[256,128]{1,0:T(8,128)(2,1)S(1)}, u32[]{:S(2)}, u32[]{:S(2)}) collective-permute-start(bf16[256,128]{1,0:T(8,128)(2,1)S(1)} %get-tuple-element.61), channel_id=1, source_target_pairs={{0,16},{16,0},{1,17},{17,1},{2,18},{18,2},{3,19},{19,3},{4,20},{20... | collective-permute-start | bytes 196616 | tf_op jit(solution)/shard_map/ppermute | solution.py:32
  29.9 6.6 %collective-permute-start.6 = (bf16[128,128]{1,0:T(8,128)(2,1)S(1)}, bf16[128,128]{1,0:T(8,128)(2,1)S(1)}, u32[]{:S(2)}, u32[]{:S(2)}) collective-permute-start(bf16[128,128]{1,0:T(8,128)(2,1)S(1)} %get-tuple-element.59), channel_id=1, source_target_pairs={{0,1},{1,2},{2,3},{3,4},{4,5},{5,6},{6,7},{7,8},{8,9},{9,10},{10,1... | collective-permute-start | bytes 98312 | tf_op jit(solution)/shard_map/ppermute | solution.py:32
  29.9 6.6 %collective-permute-start.7 = (bf16[128,128]{1,0:T(8,128)(2,1)S(1)}, bf16[128,128]{1,0:T(8,128)(2,1)S(1)}, u32[]{:S(2)}, u32[]{:S(2)}) collective-permute-start(bf16[128,128]{1,0:T(8,128)(2,1)S(1)} %get-tuple-element.60), channel_id=1, source_target_pairs={{0,15},{1,0},{2,1},{3,2},{4,3},{5,4},{6,5},{7,6},{8,7},{9,8},{10,9... | collective-permute-start | bytes 98312 | tf_op jit(solution)/shard_map/ppermute | solution.py:32
  35.6 0.9 %copy-start.4 = (f32[128,128]{1,0:T(8,128)}, f32[128,128]{1,0:T(8,128)S(1)}, u32[]{:S(2)}) copy-start(f32[128,128]{1,0:T(8,128)S(1)} %get-tuple-element.80.hinfo_ref) | copy-start | bytes 196612
  39.3 6.3 %collective-permute-start.11 = (bf16[256,128]{1,0:T(8,128)(2,1)S(1)}, bf16[256,128]{1,0:T(8,128)(2,1)S(1)}, u32[]{:S(2)}, u32[]{:S(2)}) collective-permute-start(bf16[256,128]{1,0:T(8,128)(2,1)S(1)} %get-tuple-element.70), channel_id=1, source_target_pairs={{0,16},{16,0},{1,17},{17,1},{2,18},{18,2},{3,19},{19,3},{4,20},{20... | collective-permute-start | bytes 196616 | tf_op jit(solution)/shard_map/ppermute | solution.py:32
  39.5 6.0 %collective-permute-start.9 = (bf16[128,128]{1,0:T(8,128)(2,1)S(1)}, bf16[128,128]{1,0:T(8,128)(2,1)S(1)}, u32[]{:S(2)}, u32[]{:S(2)}) collective-permute-start(bf16[128,128]{1,0:T(8,128)(2,1)S(1)} %get-tuple-element.68), channel_id=1, source_target_pairs={{0,1},{1,2},{2,3},{3,4},{4,5},{5,6},{6,7},{7,8},{8,9},{9,10},{10,1... | collective-permute-start | bytes 98312 | tf_op jit(solution)/shard_map/ppermute | solution.py:32
  39.5 6.0 %collective-permute-start.10 = (bf16[128,128]{1,0:T(8,128)(2,1)S(1)}, bf16[128,128]{1,0:T(8,128)(2,1)S(1)}, u32[]{:S(2)}, u32[]{:S(2)}) collective-permute-start(bf16[128,128]{1,0:T(8,128)(2,1)S(1)} %get-tuple-element.69), channel_id=1, source_target_pairs={{0,15},{1,0},{2,1},{3,2},{4,3},{5,4},{6,5},{7,6},{8,7},{9,8},{10,9... | collective-permute-start | bytes 98312 | tf_op jit(solution)/shard_map/ppermute | solution.py:32
  47.7 0.7 %copy-start.3 = (f32[128,512]{1,0:T(8,128)}, f32[128,512]{1,0:T(8,128)S(1)}, u32[]{:S(2)}) copy-start(f32[128,512]{1,0:T(8,128)S(1)} %get-tuple-element.77.home_ref) | copy-start | bytes 786436
  48.4 6.2 %collective-permute-start.12 = (f32[24,512]{1,0:T(8,128)S(1)}, f32[24,512]{1,0:T(8,128)S(1)}, u32[]{:S(2)}, u32[]{:S(2)}) collective-permute-start(f32[24,512]{1,0:T(8,128)S(1)} %get-tuple-element.78), channel_id=1, source_target_pairs={{0,1},{1,2},{2,3},{3,4},{4,5},{5,6},{6,7},{7,8},{8,9},{9,10},{10,1... | collective-permute-start | bytes 147464 | tf_op jit(solution)/shard_map/ppermute | solution.py:32
  48.4 6.2 %collective-permute-start.13 = (f32[24,512]{1,0:T(8,128)S(1)}, f32[24,512]{1,0:T(8,128)S(1)}, u32[]{:S(2)}, u32[]{:S(2)}) collective-permute-start(f32[24,512]{1,0:T(8,128)S(1)} %get-tuple-element.79), channel_id=1, source_target_pairs={{0,15},{1,0},{2,1},{3,2},{4,3},{5,4},{6,5},{7,6},{8,7},{9,8},{10,9... | collective-permute-start | bytes 147464 | tf_op jit(solution)/shard_map/ppermute | solution.py:32
  54.6 0.6 %copy-start.7 = (f32[24,512]{1,0:T(8,128)}, f32[24,512]{1,0:T(8,128)S(1)}, u32[]{:S(2)}) copy-start(f32[24,512]{1,0:T(8,128)S(1)} %collective-permute-done.12.from_l_ref) | copy-start | bytes 147460
  54.6 0.6 %copy-start.8 = (f32[24,512]{1,0:T(8,128)}, f32[24,512]{1,0:T(8,128)S(1)}, u32[]{:S(2)}) copy-start(f32[24,512]{1,0:T(8,128)S(1)} %collective-permute-done.13.from_r_ref) | copy-start | bytes 147460

commit v13 on v12

--- a/solution.py
+++ b/solution.py
@@ -438,8 +438,8 @@
     )(*inputs)
 
 
-def setup_kernel(local, fields, u_ref, vt_ref, packed_ref, tab_ref, v7_out, m7_out, pl_out, pr_out,
-                 pre_out, stc_out, sw_out, *send_refs):
+def setup_kernel(local, fields, u_ref, vt_ref, packed_ref, tab_ref, v7_out, m7_out,
+                 pre_out, stc_out, *send_refs):
     rows = local * fields
     views = table_views(tab_ref, rows, local)
     lift_ref = views["lift_t"]
@@ -468,6 +468,19 @@
     ).astype(bf16)
     p_hi, p_mid, p_lo = _split(packed_ref[...])
     packed = (_dot_t(eye16, p_hi) + _dot_t(eye16, p_mid)) + _dot_t(eye16, p_lo)
+    pre_out[...] = packed[:, 7:8]
+    stc_out[...] = _exact_right(fsel_ref[...], packed)[:, 8:9]
+    write_sends(send_refs, _dot(u_ref[...].astype(bf16), g7_ref[...]).astype(bf16))
+
+
+def near_kernel(local, fields, packed_ref, tab_ref, pl_out, pr_out, sw_out):
+    rows = local * fields
+    bcast = table_views(tab_ref, rows, local)["bcast"][...]
+    eye16 = jnp.where(
+        lax.broadcasted_iota(jnp.int32, (local, LANE), 0)
+        == lax.broadcasted_iota(jnp.int32, (local, LANE), 1), 1.0, 0.0
+    ).astype(bf16)
+    packed = _dot_t(eye16, packed_ref[...].astype(bf16))
     rep = _dot(bcast, packed.astype(bf16))
     row_f = (lax.broadcasted_iota(jnp.int32, (rows, 1), 0) % fields).astype(f32)
     cols = lax.broadcasted_iota(jnp.int32, (rows, rows), 1).astype(f32)
@@ -480,9 +493,6 @@
         if side in SEND_FACES:
             pr_out[SEND_FACES.index(side)] = jnp.where(hit & far, 1.0, 0.0).astype(bf16)
     sw_out[...] = rep[:, 6:7]
-    pre_out[...] = packed[:, 7:8]
-    stc_out[...] = _exact_right(fsel_ref[...], packed)[:, 8:9]
-    write_sends(send_refs, _dot(u_ref[...].astype(bf16), g7_ref[...]).astype(bf16))
 
 
 def late_kernel(local, fields, vt_ref, packed_ref, tab_ref, v3_out, m3_out, hinfo_out,
@@ -681,12 +691,14 @@
     setup_out = [
         jax.ShapeDtypeStruct((3, rows, P7**3), bf16),
         jax.ShapeDtypeStruct((rows, 6 * LANE), f32),
+        jax.ShapeDtypeStruct((local_count, 1), f32),
+        jax.ShapeDtypeStruct((rows, 1), f32),
+    ] + sends_shape
+    near_out = [
         jax.ShapeDtypeStruct((6, rows, rows), bf16),
         jax.ShapeDtypeStruct((len(SEND_FACES), rows, rows), bf16),
-        jax.ShapeDtypeStruct((local_count, 1), f32),
         jax.ShapeDtypeStruct((rows, 1), f32),
-        jax.ShapeDtypeStruct((rows, 1), f32),
-    ] + sends_shape
+    ]
     late_out = [
         jax.ShapeDtypeStruct((3, rows, P3**3), f32),
         jax.ShapeDtypeStruct((rows, 6 * LANE), f32),
@@ -708,9 +720,16 @@
         + [pltpu.SemaphoreType.DMA((len(setup_in),))],
         compiler_params=pltpu.CompilerParams(vmem_limit_bytes=24 * 1024 * 1024),
     )(*setup_in)
-    v7, m7, p_local, p_remote, pre, stc, sw = res[:7]
-    sends = res[7:10]
-    table = res[10]
+    v7, m7, pre, stc = res[:4]
+    sends = res[4:7]
+    table = res[7]
+    p_local, p_remote, sw = pl.pallas_call(
+        functools.partial(near_kernel, local_count, field_count),
+        out_shape=near_out,
+        in_specs=[_vmem() for _ in range(2)],
+        out_specs=[_vmem() for _ in near_out],
+        compiler_params=pltpu.CompilerParams(vmem_limit_bytes=24 * 1024 * 1024),
+    )(packed, table)
     v3, m3, hinfo, cnt_l, cnt_r, sel_l, sel_r = pl.pallas_call(
         functools.partial(late_kernel, local_count, field_count),
         out_shape=late_out,

time: 58.3 us -> 57.9 us (level)
  waiting for transfers between devices: 3.65 us -> 3.03 us
    pallas_call x0 -> x1, Pallas kernels: none -> 0.63 us  [per_device(): pl.pallas_call(functools.partial(near_kernel, local_count, field_count),...]
    ppermute x14, waiting for transfers between devices: 3.65 us -> 3.03 us  [shifted(): return lax.ppermute(value, axis, pairs)]
  transfers between devices with their start and end apart: 14 -> 14, of which waited for: 5 -> 5; matrix products, arithmetic and copies ran while one was open for 1% -> 1% of each run, Pallas kernels for 8% -> 9%
where the time goes in v13:
time: 57.9 us; the launch traced here: 57.6 us
  starting transfers between devices  27.6 us (48%)
  Pallas kernels  18.1 us (31%)
  local copies, waits for them, and re-layouts  6.76 us (12%)
  waiting for transfers between devices  3.03 us (5%)
  other arithmetic  1.37 us (2%)
  between operations  0.79 us (1%)
    ppermute x14, starting transfers between devices, shifted(): return lax.ppermute(value, axis, pairs)  27.6 us
    pallas_call x4, Pallas kernels, run_stage(): pl.pallas_call(kernel, out_shape=out_shapes, in_specs=[_vmem() for _ in i...  8.61 us
    unnamed x18, local copies, waits for them, and re-layouts  4.7 us
    pallas_call x4, Pallas kernels, run_bulk(): pl.pallas_call(functools.partial(bulk_kernel, coarse, local), out_shape=o...  3.07 us
    ppermute x14, waiting for transfers between devices, shifted(): return lax.ppermute(value, axis, pairs)  3.03 us
    pallas_call x1, Pallas kernels, per_device(): pl.pallas_call(functools.partial(final_kernel, field_count, HOLD7), out_s...  2.74 us
    pallas_call x1, Pallas kernels, per_device(): pl.pallas_call(functools.partial(setup_entry, local_count, field_count, l...  1.77 us
    pallas_call x1, Pallas kernels, per_device(): pl.pallas_call(functools.partial(late_kernel, local_count, field_count),...  1.27 us
  transfers between devices with their start and end apart: 14, of which 5 were waited for; matrix products, arithmetic and copies ran while one was open for 1% of the time, Pallas kernels for 9%

profile of v13, /device:TPU:0, one launch (start us, length us, event | category | flops | bytes accessed | tf_op | source)
XLA Modules:
  0.0 57.6 jit_solution(4937799327419549414)
XLA Ops:
  0.6 0.7 %pad_bitcast_fusion = f32[1,16]{1,0:T(1,128)S(1)} fusion(f32[8]{0:T(128)} %param.11), kind=kLoop, calls=%fused_computation.9 | loop fusion | bytes 96 | tf_op jit(solution)/shard_map/stack | solution.py:635
  1.3 0.7 %convert_bitcast_fusion.1 = (f32[1,16]{1,0:T(1,128)S(1)}, f32[1,16]{1,0:T(1,128)S(1)}) fusion(s32[16]{0:T(128)} %param.14, s32[16]{0:T(128)} %param.13), kind=kLoop, calls=%fused_computation.8 | loop fusion | flops 32 | bytes 256 | tf_op jit(solution)/shard_map/stack | solution.py:635
  2.0 0.7 %convert_bitcast_fusion = f32[6,16]{1,0:T(8,128)S(1)} fusion(s32[16,6]{0,1:T(8,128)} %param.12, s32[]{:T(128)S(6)} %add.11), kind=kLoop, calls=%fused_computation.5 | loop fusion | flops 2016 | bytes 772 | tf_op jit(solution)/shard_map/transpose | solution.py:634
  2.7 0.7 %concatenate.3 = f32[10,16]{1,0:T(8,128)S(1)} concatenate(f32[6,16]{1,0:T(8,128)S(1)} %convert_bitcast_fusion, f32[1,16]{1,0:T(1,128)S(1)} %get-tuple-element.83, f32[1,16]{1,0:T(1,128)} %bitcast.19, f32[1,16]{1,0:T(1,128)S(1)} %pad_bitcast_fusion, f32[1,16]{1,0:T(1,128)S(1)} %get-tuple-element.82), dimensions={0} | concatenate | bytes 1280 | tf_op jit(solution)/shard_map/concatenate | solution.py:632
  3.4 0.9 %copy-done = f32[16,8,512]{2,1,0:T(8,128)S(1)} copy-done((f32[16,8,512]{2,1,0:T(8,128)S(1)}, f32[16,8,512]{2,1,0:T(8,128)}, u32[]{:S(2)}) %copy-start) | copy-done | bytes 262168
  4.3 1.7 %copy-done.2 = bf16[1664,768]{1,0:T(8,128)(2,1)S(1)} copy-done((bf16[1664,768]{1,0:T(8,128)(2,1)S(1)}, bf16[1664,768]{1,0:T(8,128)(2,1)}, u32[]{:S(2)}) %copy-start.2) | copy-done | bytes 2555928
  6.0 0.7 %copy-done.5 = bf16[3,64,16]{1,2,0:T(8,128)(2,1)S(1)} copy-done((bf16[3,64,16]{1,2,0:T(8,128)(2,1)S(1)}, bf16[3,64,16]{1,2,0:T(8,128)(2,1)}, u32[]{:S(2)}) %copy-start.5) | copy-done | bytes 6168
  6.8 1.8 %shard_map.95 = (bf16[3,128,512]{2,1,0:T(8,128)(2,1)S(1)}, f32[128,768]{1,0:T(8,128)S(1)}, f32[16,1]{1,0:T(8,128)S(1)}, f32[128,1]{1,0:T(8,128)S(1)}, bf16[128,1...) custom-call(f32[128,512]{1,0:T(8,128)S(1)} %bitcast.12, ...), custom_call_target="tpu_custom_call" | custom-call | tf_op jit(solution)/shard_map/pallas_call | solution.py:714
  8.5 3.0 %collective-permute-start.2 = (bf16[256,128]{1,0:T(8,128)(2,1)S(1)}, bf16[256,128]{1,0:T(8,128)(2,1)S(1)}, u32[]{:S(2)}, u32[]{:S(2)}) collective-permute-start(bf16[256,128]{1,0:T(8,128)(2,1)S(1)} %get-tuple-element.44), channel_id=1, source_target_pairs={{0,16},{16,0},{1,17},{17,1},{2,18},{18,2},{3,19},{19,3},{4,20},{20... | collective-permute-start | bytes 196616 | tf_op jit(solution)/shard_map/ppermute | solution.py:32
  11.6 4.4 %collective-permute-start.1 = (bf16[128,128]{1,0:T(8,128)(2,1)S(1)}, bf16[128,128]{1,0:T(8,128)(2,1)S(1)}, u32[]{:S(2)}, u32[]{:S(2)}) collective-permute-start(bf16[128,128]{1,0:T(8,128)(2,1)S(1)} %get-tuple-element.43), channel_id=1, source_target_pairs={{0,15},{1,0},{2,1},{3,2},{4,3},{5,4},{6,5},{7,6},{8,7},{9,8},{10,9... | collective-permute-start | bytes 98312 | tf_op jit(solution)/shard_map/ppermute | solution.py:32
  16.0 0.6 %shard_map.96 = (bf16[6,128,128]{2,1,0:T(8,128)(2,1)S(1)}, bf16[4,128,128]{2,1,0:T(8,128)(2,1)S(1)}, f32[128,1]{1,0:T(8,128)S(1)}) custom-call(f32[16,128]{1,0:T(8,128)S(1)} %pad.9.refs_2_.packed_ref, bf16[1664,768]{1,0:T(8,128)(2,1)S(1)} %get-tuple-element.45.tab_ref.refs_4_.refs_11_.refs_12_.refs_5_.refs_14_), custom_call_target="tpu_custom_call" | custom-call | tf_op jit(solution)/shard_map/pallas_call | solution.py:726
  16.6 0.7 %shard_map.97.refs_12_ = f32[128,512]{1,0:T(8,128)S(1)} custom-call(f32[128,512]{1,0:T(8,128)S(1)} %bitcast.13, bf16[3,128,512]{2,1,0:T(8,128)(2,1)S(1)} %get-tuple-element.48.refs_1_.refs_7_.refs_8_.refs_2_.refs_10_, f32[16,1]{1,0:T(8,128)S(1)} %get-tuple-element.50.refs_2_.refs_9_.refs_10_.refs_3_.refs_12_, ...), custom_call_target="tpu_custom_call" | custom-call | tf_op jit(solution)/shard_map/pallas_call | solution.py:420
  17.6 1.5 %shard_map.98 = (f32[128,512]{1,0:T(8,128)S(1)}, bf16[128,128]{1,0:T(8,128)(2,1)S(1)}, bf16[128,128]{1,0:T(8,128)(2,1)S(1)}, bf16[256,128]{1,0:T(8,128)(2,1)S(1)}) custom-call(f32[128,512]{1,0:T(8,128)S(1)} %bitcast.14, bf16[128,128]{1,0:T(8,128)(2,1)S(1)} %collective-permute-done.refs_1_, bf16[128,128]{1,0:T(8,128)(2,1)S(1)} %collective-permute-done.1.refs_2_, ...), custom_call_target="tpu_custom_call" | custom-call | tf_op jit(solution)/shard_map/pallas_call | solution.py:432
  19.2 4.5 %collective-permute-start.4 = (bf16[128,128]{1,0:T(8,128)(2,1)S(1)}, bf16[128,128]{1,0:T(8,128)(2,1)S(1)}, u32[]{:S(2)}, u32[]{:S(2)}) collective-permute-start(bf16[128,128]{1,0:T(8,128)(2,1)S(1)} %get-tuple-element.54), channel_id=1, source_target_pairs={{0,15},{1,0},{2,1},{3,2},{4,3},{5,4},{6,5},{7,6},{8,7},{9,8},{10,9... | collective-permute-start | bytes 98312 | tf_op jit(solution)/shard_map/ppermute | solution.py:32
  23.7 0.6 %shard_map.99.refs_14_ = f32[128,512]{1,0:T(8,128)S(1)} custom-call(f32[128,512]{1,0:T(8,128)S(1)} %get-tuple-element.52.refs_0_, bf16[3,128,512]{2,1,0:T(8,128)(2,1)S(1)} %get-tuple-element.48.refs_1_.refs_7_.refs_8_.refs_2_.refs_10_, f32[16,1]{1,0:T(8,128)S(1)} %get-tuple-element.50.refs_2_.refs_9_.refs_10_.refs_3_.refs_12_, ...), custom_call_target="tpu_custom_call" | custom-call | tf_op jit(solution)/shard_map/pallas_call | solution.py:420
  24.4 0.9 %collective-permute-done.3.refs_2_ = bf16[128,128]{1,0:T(8,128)(2,1)S(1)} collective-permute-done((bf16[128,128]{1,0:T(8,128)(2,1)S(1)}, bf16[128,128]{1,0:T(8,128)(2,1)S(1)}, u32[]{:S(2)}, u32[]{:S(2)}) %collective-permute-start.3) | collective-permute-done | bytes 32800 | tf_op jit(solution)/shard_map/ppermute | solution.py:32
  25.3 2.3 %shard_map.100 = (f32[128,512]{1,0:T(8,128)S(1)}, f32[128,64]{1,0:T(8,128)S(1)}, bf16[128,128]{1,0:T(8,128)(2,1)S(1)}, bf16[128,128]{1,0:T(8,128)(2,1)S(1)}, bf16[256,128]{1,0:T(8,128)(2,1)S(1)}) custom-call(f32[128,512]{1,0:T(8,128)S(1)} %get-tuple-element.52.refs_0_, f32[128,512]{1,0:T(8,128)S(1)} %bitcast.15, ...), custom_call_target="tpu_custom_call" | custom-call | tf_op jit(solution)/shard_map/pallas_call | solution.py:432
  27.6 2.0 %collective-permute-start.8 = (bf16[256,128]{1,0:T(8,128)(2,1)S(1)}, bf16[256,128]{1,0:T(8,128)(2,1)S(1)}, u32[]{:S(2)}, u32[]{:S(2)}) collective-permute-start(bf16[256,128]{1,0:T(8,128)(2,1)S(1)} %get-tuple-element.61), channel_id=1, source_target_pairs={{0,16},{16,0},{1,17},{17,1},{2,18},{18,2},{3,19},{19,3},{4,20},{20... | collective-permute-start | bytes 196616 | tf_op jit(solution)/shard_map/ppermute | solution.py:32
  29.5 4.4 %collective-permute-start.7 = (bf16[128,128]{1,0:T(8,128)(2,1)S(1)}, bf16[128,128]{1,0:T(8,128)(2,1)S(1)}, u32[]{:S(2)}, u32[]{:S(2)}) collective-permute-start(bf16[128,128]{1,0:T(8,128)(2,1)S(1)} %get-tuple-element.60), channel_id=1, source_target_pairs={{0,15},{1,0},{2,1},{3,2},{4,3},{5,4},{6,5},{7,6},{8,7},{9,8},{10,9... | collective-permute-start | bytes 98312 | tf_op jit(solution)/shard_map/ppermute | solution.py:32
  34.0 1.3 %shard_map.101 = (f32[3,128,64]{2,1,0:T(8,128)S(1)}, f32[128,768]{1,0:T(8,128)S(1)}, f32[128,128]{1,0:T(8,128)S(1)}, f32[8,128]{1,0:T(8,128)S(1)}, f32[8,128]{1,...) custom-call(bf16[3,16,64]{2,1,0:T(8,128)(2,1)S(1)} %bitcast.17, ...), custom_call_target="tpu_custom_call" | custom-call | tf_op jit(solution)/shard_map/pallas_call | solution.py:733
  35.3 0.9 %shard_map.102 = (f32[128,512]{1,0:T(8,128)S(1)}, f32[128,64]{1,0:T(8,128)S(1)}) custom-call(f32[128,512]{1,0:T(8,128)S(1)} %get-tuple-element.57.refs_0_.refs_2_, f32[128,64]{1,0:T(8,128)S(1)} %get-tuple-element.58.refs_1_.refs_3_, bf16[3,128,512]{2,1,0:T(8,128)(2,1)S(1)} %get-tuple-element.48.refs_1_.refs_7_.refs_8_.refs_2_.refs_10_, ...), custom_call_target="tpu_custom_call" | custom-call | tf_op jit(solution)/shard_map/pallas_call | solution.py:420
  36.2 2.7 %shard_map.103 = (f32[128,512]{1,0:T(8,128)S(1)}, f32[128,64]{1,0:T(8,128)S(1)}, bf16[128,128]{1,0:T(8,128)(2,1)S(1)}, bf16[128,128]{1,0:T(8,128)(2,1)S(1)}, bf16[256,128]{1,0:T(8,128)(2,1)S(1)}) custom-call(f32[128,512]{1,0:T(8,128)S(1)} %get-tuple-element.57.refs_0_.refs_2_, f32[128,64]{1,0:T(8,128)S(1)} %get-tuple-element.58.refs_1_.refs_3_, ...), custom_call_target="tpu_custom_call" | custom-call | tf_op jit(solution)/shard_map/pallas_call | solution.py:432
  39.1 4.4 %collective-permute-start.10 = (bf16[128,128]{1,0:T(8,128)(2,1)S(1)}, bf16[128,128]{1,0:T(8,128)(2,1)S(1)}, u32[]{:S(2)}, u32[]{:S(2)}) collective-permute-start(bf16[128,128]{1,0:T(8,128)(2,1)S(1)} %get-tuple-element.69), channel_id=1, source_target_pairs={{0,15},{1,0},{2,1},{3,2},{4,3},{5,4},{6,5},{7,6},{8,7},{9,8},{10,9... | collective-permute-start | bytes 98312 | tf_op jit(solution)/shard_map/ppermute | solution.py:32
  43.6 0.9 %shard_map.104 = (f32[128,512]{1,0:T(8,128)S(1)}, f32[128,64]{1,0:T(8,128)S(1)}) custom-call(f32[128,512]{1,0:T(8,128)S(1)} %get-tuple-element.66.refs_0_, f32[128,64]{1,0:T(8,128)S(1)} %get-tuple-element.67.refs_1_, bf16[3,128,512]{2,1,0:T(8,128)(2,1)S(1)} %get-tuple-element.48.refs_1_.refs_7_.refs_8_.refs_2_.refs_10_, ...), custom_call_target="tpu_custom_call" | custom-call | tf_op jit(solution)/shard_map/pallas_call | solution.py:420
  44.4 0.7 %collective-permute-done.9.refs_4_ = bf16[128,128]{1,0:T(8,128)(2,1)S(1)} collective-permute-done((bf16[128,128]{1,0:T(8,128)(2,1)S(1)}, bf16[128,128]{1,0:T(8,128)(2,1)S(1)}, u32[]{:S(2)}, u32[]{:S(2)}) %collective-permute-start.9) | collective-permute-done | bytes 32800 | tf_op jit(solution)/shard_map/ppermute | solution.py:32
  45.2 2.2 %shard_map.105 = (f32[128,512]{1,0:T(8,128)S(1)}, f32[128,64]{1,0:T(8,128)S(1)}, f32[24,512]{1,0:T(8,128)S(1)}, f32[24,512]{1,0:T(8,128)S(1)}) custom-call(f32[128,512]{1,0:T(8,128)S(1)} %get-tuple-element.66.refs_0_, f32[128,64]{1,0:T(8,128)S(1)} %get-tuple-element.67.refs_1_, f32[128,512]{1,0:T(8,128)S(1)} %get-tuple-element.57.refs_0_.refs_2_, ...), custom_call_target="tpu_custom_call" | custom-call | tf_op jit(solution)/shard_map/pallas_call | solution.py:432
  47.3 0.7 %copy-done.3 = f32[128,512]{1,0:T(8,128)} copy-done((f32[128,512]{1,0:T(8,128)}, f32[128,512]{1,0:T(8,128)S(1)}, u32[]{:S(2)}) %copy-start.3) | copy-done | bytes 262168
  48.0 4.4 %collective-permute-start.13 = (f32[24,512]{1,0:T(8,128)S(1)}, f32[24,512]{1,0:T(8,128)S(1)}, u32[]{:S(2)}, u32[]{:S(2)}) collective-permute-start(f32[24,512]{1,0:T(8,128)S(1)} %get-tuple-element.79), channel_id=1, source_target_pairs={{0,15},{1,0},{2,1},{3,2},{4,3},{5,4},{6,5},{7,6},{8,7},{9,8},{10,9... | collective-permute-start | bytes 147464 | tf_op jit(solution)/shard_map/ppermute | solution.py:32
  52.5 0.7 %reshape.15 = f32[16,512]{1,0:T(8,128)} reshape(f32[128,64]{1,0:T(8,128)S(1)} %get-tuple-element.81) | data formatting | bytes 65536 | tf_op jit(solution)/shard_map/reshape | solution.py:786
  53.2 1.1 %collective-permute-done.12.from_l_ref = f32[24,512]{1,0:T(8,128)S(1)} collective-permute-done((f32[24,512]{1,0:T(8,128)S(1)}, f32[24,512]{1,0:T(8,128)S(1)}, u32[]{:S(2)}, u32[]{:S(2)}) %collective-permute-start.12) | collective-permute-done | bytes 49184 | tf_op jit(solution)/shard_map/ppermute | solution.py:32
  54.3 0.6 %copy-done.7 = f32[24,512]{1,0:T(8,128)} copy-done((f32[24,512]{1,0:T(8,128)}, f32[24,512]{1,0:T(8,128)S(1)}, u32[]{:S(2)}) %copy-start.7) | copy-done | bytes 49176
  54.9 2.7 %shard_map.106 = f32[96,512]{1,0:T(8,128)} custom-call(f32[128,512]{1,0:T(8,128)} %copy-done.3, f32[24,512]{1,0:T(8,128)} %copy-done.7, f32[24,512]{1,0:T(8,128)} %copy-done.8, f32[128,128]{1,0:T(8,128)} %copy-done.4), custom_call_target="tpu_custom_call" | custom-call | tf_op jit(solution)/shard_map/pallas_call | solution.py:779
  (32 shorter events, 0.8 us)
Async XLA Ops:
  3.4 0.9 %copy-start = (f32[16,8,512]{2,1,0:T(8,128)S(1)}, f32[16,8,512]{2,1,0:T(8,128)}, u32[]{:S(2)}) copy-start(f32[16,8,512]{2,1,0:T(8,128)} %param.8) | copy-start | bytes 786436
  4.3 1.7 %copy-start.2 = (bf16[1664,768]{1,0:T(8,128)(2,1)S(1)}, bf16[1664,768]{1,0:T(8,128)(2,1)}, u32[]{:S(2)}) copy-start(bf16[1664,768]{1,0:T(8,128)(2,1)} %constant.33.clone.refs_3_) | copy-start | bytes 7667716
  6.0 0.7 %copy-start.5 = (bf16[3,64,16]{1,2,0:T(8,128)(2,1)S(1)}, bf16[3,64,16]{1,2,0:T(8,128)(2,1)}, u32[]{:S(2)}) copy-start(bf16[3,64,16]{1,2,0:T(8,128)(2,1)} %param.9) | copy-start | bytes 18436
  6.8 9.9 %copy-start.1 = (f32[16,8,512]{2,1,0:T(8,128)S(1)}, f32[16,8,512]{2,1,0:T(8,128)}, u32[]{:S(2)}) copy-start(f32[16,8,512]{2,1,0:T(8,128)} %param.8) | copy-start | bytes 786436
  8.5 9.1 %collective-permute-start.2 = (bf16[256,128]{1,0:T(8,128)(2,1)S(1)}, bf16[256,128]{1,0:T(8,128)(2,1)S(1)}, u32[]{:S(2)}, u32[]{:S(2)}) collective-permute-start(bf16[256,128]{1,0:T(8,128)(2,1)S(1)} %get-tuple-element.44), channel_id=1, source_target_pairs={{0,16},{16,0},{1,17},{17,1},{2,18},{18,2},{3,19},{19,3},{4,20},{20... | collective-permute-start | bytes 196616 | tf_op jit(solution)/shard_map/ppermute | solution.py:32
  11.6 6.0 %collective-permute-start = (bf16[128,128]{1,0:T(8,128)(2,1)S(1)}, bf16[128,128]{1,0:T(8,128)(2,1)S(1)}, u32[]{:S(2)}, u32[]{:S(2)}) collective-permute-start(bf16[128,128]{1,0:T(8,128)(2,1)S(1)} %get-tuple-element.42), channel_id=1, source_target_pairs={{0,1},{1,2},{2,3},{3,4},{4,5},{5,6},{6,7},{7,8},{8,9},{9,10},{10,1... | collective-permute-start | bytes 98312 | tf_op jit(solution)/shard_map/ppermute | solution.py:32
  11.6 6.0 %collective-permute-start.1 = (bf16[128,128]{1,0:T(8,128)(2,1)S(1)}, bf16[128,128]{1,0:T(8,128)(2,1)S(1)}, u32[]{:S(2)}, u32[]{:S(2)}) collective-permute-start(bf16[128,128]{1,0:T(8,128)(2,1)S(1)} %get-tuple-element.43), channel_id=1, source_target_pairs={{0,15},{1,0},{2,1},{3,2},{4,3},{5,4},{6,5},{7,6},{8,7},{9,8},{10,9... | collective-permute-start | bytes 98312 | tf_op jit(solution)/shard_map/ppermute | solution.py:32
  19.1 6.2 %collective-permute-start.5 = (bf16[256,128]{1,0:T(8,128)(2,1)S(1)}, bf16[256,128]{1,0:T(8,128)(2,1)S(1)}, u32[]{:S(2)}, u32[]{:S(2)}) collective-permute-start(bf16[256,128]{1,0:T(8,128)(2,1)S(1)} %get-tuple-element.55), channel_id=1, source_target_pairs={{0,16},{16,0},{1,17},{17,1},{2,18},{18,2},{3,19},{19,3},{4,20},{20... | collective-permute-start | bytes 196616 | tf_op jit(solution)/shard_map/ppermute | solution.py:32
  19.2 6.0 %collective-permute-start.3 = (bf16[128,128]{1,0:T(8,128)(2,1)S(1)}, bf16[128,128]{1,0:T(8,128)(2,1)S(1)}, u32[]{:S(2)}, u32[]{:S(2)}) collective-permute-start(bf16[128,128]{1,0:T(8,128)(2,1)S(1)} %get-tuple-element.53), channel_id=1, source_target_pairs={{0,1},{1,2},{2,3},{3,4},{4,5},{5,6},{6,7},{7,8},{8,9},{9,10},{10,1... | collective-permute-start | bytes 98312 | tf_op jit(solution)/shard_map/ppermute | solution.py:32
  19.2 6.1 %collective-permute-start.4 = (bf16[128,128]{1,0:T(8,128)(2,1)S(1)}, bf16[128,128]{1,0:T(8,128)(2,1)S(1)}, u32[]{:S(2)}, u32[]{:S(2)}) collective-permute-start(bf16[128,128]{1,0:T(8,128)(2,1)S(1)} %get-tuple-element.54), channel_id=1, source_target_pairs={{0,15},{1,0},{2,1},{3,2},{4,3},{5,4},{6,5},{7,6},{8,7},{9,8},{10,9... | collective-permute-start | bytes 98312 | tf_op jit(solution)/shard_map/ppermute | solution.py:32
  24.4 9.6 %copy-start.6 = (bf16[3,64,16]{1,2,0:T(8,128)(2,1)S(1)}, bf16[3,64,16]{1,2,0:T(8,128)(2,1)}, u32[]{:S(2)}) copy-start(bf16[3,64,16]{1,2,0:T(8,128)(2,1)} %param.9) | copy-start | bytes 18436
  27.6 8.6 %collective-permute-start.8 = (bf16[256,128]{1,0:T(8,128)(2,1)S(1)}, bf16[256,128]{1,0:T(8,128)(2,1)S(1)}, u32[]{:S(2)}, u32[]{:S(2)}) collective-permute-start(bf16[256,128]{1,0:T(8,128)(2,1)S(1)} %get-tuple-element.61), channel_id=1, source_target_pairs={{0,16},{16,0},{1,17},{17,1},{2,18},{18,2},{3,19},{19,3},{4,20},{20... | collective-permute-start | bytes 196616 | tf_op jit(solution)/shard_map/ppermute | solution.py:32
  29.5 6.6 %collective-permute-start.6 = (bf16[128,128]{1,0:T(8,128)(2,1)S(1)}, bf16[128,128]{1,0:T(8,128)(2,1)S(1)}, u32[]{:S(2)}, u32[]{:S(2)}) collective-permute-start(bf16[128,128]{1,0:T(8,128)(2,1)S(1)} %get-tuple-element.59), channel_id=1, source_target_pairs={{0,1},{1,2},{2,3},{3,4},{4,5},{5,6},{6,7},{7,8},{8,9},{9,10},{10,1... | collective-permute-start | bytes 98312 | tf_op jit(solution)/shard_map/ppermute | solution.py:32
  29.5 6.6 %collective-permute-start.7 = (bf16[128,128]{1,0:T(8,128)(2,1)S(1)}, bf16[128,128]{1,0:T(8,128)(2,1)S(1)}, u32[]{:S(2)}, u32[]{:S(2)}) collective-permute-start(bf16[128,128]{1,0:T(8,128)(2,1)S(1)} %get-tuple-element.60), channel_id=1, source_target_pairs={{0,15},{1,0},{2,1},{3,2},{4,3},{5,4},{6,5},{7,6},{8,7},{9,8},{10,9... | collective-permute-start | bytes 98312 | tf_op jit(solution)/shard_map/ppermute | solution.py:32
  35.3 0.9 %copy-start.4 = (f32[128,128]{1,0:T(8,128)}, f32[128,128]{1,0:T(8,128)S(1)}, u32[]{:S(2)}) copy-start(f32[128,128]{1,0:T(8,128)S(1)} %get-tuple-element.80.hinfo_ref) | copy-start | bytes 196612
  38.9 6.2 %collective-permute-start.11 = (bf16[256,128]{1,0:T(8,128)(2,1)S(1)}, bf16[256,128]{1,0:T(8,128)(2,1)S(1)}, u32[]{:S(2)}, u32[]{:S(2)}) collective-permute-start(bf16[256,128]{1,0:T(8,128)(2,1)S(1)} %get-tuple-element.70), channel_id=1, source_target_pairs={{0,16},{16,0},{1,17},{17,1},{2,18},{18,2},{3,19},{19,3},{4,20},{20... | collective-permute-start | bytes 196616 | tf_op jit(solution)/shard_map/ppermute | solution.py:32
  39.1 6.0 %collective-permute-start.9 = (bf16[128,128]{1,0:T(8,128)(2,1)S(1)}, bf16[128,128]{1,0:T(8,128)(2,1)S(1)}, u32[]{:S(2)}, u32[]{:S(2)}) collective-permute-start(bf16[128,128]{1,0:T(8,128)(2,1)S(1)} %get-tuple-element.68), channel_id=1, source_target_pairs={{0,1},{1,2},{2,3},{3,4},{4,5},{5,6},{6,7},{7,8},{8,9},{9,10},{10,1... | collective-permute-start | bytes 98312 | tf_op jit(solution)/shard_map/ppermute | solution.py:32
  39.1 6.0 %collective-permute-start.10 = (bf16[128,128]{1,0:T(8,128)(2,1)S(1)}, bf16[128,128]{1,0:T(8,128)(2,1)S(1)}, u32[]{:S(2)}, u32[]{:S(2)}) collective-permute-start(bf16[128,128]{1,0:T(8,128)(2,1)S(1)} %get-tuple-element.69), channel_id=1, source_target_pairs={{0,15},{1,0},{2,1},{3,2},{4,3},{5,4},{6,5},{7,6},{8,7},{9,8},{10,9... | collective-permute-start | bytes 98312 | tf_op jit(solution)/shard_map/ppermute | solution.py:32
  47.3 0.7 %copy-start.3 = (f32[128,512]{1,0:T(8,128)}, f32[128,512]{1,0:T(8,128)S(1)}, u32[]{:S(2)}) copy-start(f32[128,512]{1,0:T(8,128)S(1)} %get-tuple-element.77.home_ref) | copy-start | bytes 786436
  48.0 6.2 %collective-permute-start.12 = (f32[24,512]{1,0:T(8,128)S(1)}, f32[24,512]{1,0:T(8,128)S(1)}, u32[]{:S(2)}, u32[]{:S(2)}) collective-permute-start(f32[24,512]{1,0:T(8,128)S(1)} %get-tuple-element.78), channel_id=1, source_target_pairs={{0,1},{1,2},{2,3},{3,4},{4,5},{5,6},{6,7},{7,8},{8,9},{9,10},{10,1... | collective-permute-start | bytes 147464 | tf_op jit(solution)/shard_map/ppermute | solution.py:32
  48.0 6.2 %collective-permute-start.13 = (f32[24,512]{1,0:T(8,128)S(1)}, f32[24,512]{1,0:T(8,128)S(1)}, u32[]{:S(2)}, u32[]{:S(2)}) collective-permute-start(f32[24,512]{1,0:T(8,128)S(1)} %get-tuple-element.79), channel_id=1, source_target_pairs={{0,15},{1,0},{2,1},{3,2},{4,3},{5,4},{6,5},{7,6},{8,7},{9,8},{10,9... | collective-permute-start | bytes 147464 | tf_op jit(solution)/shard_map/ppermute | solution.py:32
  54.2 0.6 %copy-start.7 = (f32[24,512]{1,0:T(8,128)}, f32[24,512]{1,0:T(8,128)S(1)}, u32[]{:S(2)}) copy-start(f32[24,512]{1,0:T(8,128)S(1)} %collective-permute-done.12.from_l_ref) | copy-start | bytes 147460
  54.3 0.6 %copy-start.8 = (f32[24,512]{1,0:T(8,128)}, f32[24,512]{1,0:T(8,128)S(1)}, u32[]{:S(2)}) copy-start(f32[24,512]{1,0:T(8,128)S(1)} %collective-permute-done.13.from_r_ref) | copy-start | bytes 147460

commit v14 on v13

--- a/solution.py
+++ b/solution.py
@@ -495,8 +495,7 @@
     sw_out[...] = rep[:, 6:7]
 
 
-def late_kernel(local, fields, vt_ref, packed_ref, tab_ref, v3_out, m3_out, hinfo_out,
-                cnt_l_out, cnt_r_out, sel_l_out, sel_r_out):
+def late_kernel(local, fields, vt_ref, tab_ref, v3_out, m3_out):
     rows = local * fields
     views = table_views(tab_ref, rows, local)
     tm_ref = views["tm"]
@@ -510,6 +509,12 @@
         mvg.append((_dot(vt, tm_ref[0]) + _dot(vt, tm_ref[1])) + _dot(vt, tm_ref[2]))
     by_block = jnp.where(lanes < 2, mvg[0], jnp.where(lanes < 4, mvg[1], mvg[2]))
     m3_out[...] = _exact_right(bcast, jnp.minimum(sign * by_block, 0.0))
+
+
+def move_kernel(local, fields, packed_ref, tab_ref, hinfo_out, cnt_l_out, cnt_r_out, sel_l_out,
+                sel_r_out):
+    rows = local * fields
+    bcast = table_views(tab_ref, rows, local)["bcast"][...]
     eye16 = jnp.where(
         lax.broadcasted_iota(jnp.int32, (local, LANE), 0)
         == lax.broadcasted_iota(jnp.int32, (local, LANE), 1), 1.0, 0.0
@@ -702,6 +707,8 @@
     late_out = [
         jax.ShapeDtypeStruct((3, rows, P3**3), f32),
         jax.ShapeDtypeStruct((rows, 6 * LANE), f32),
+    ]
+    move_out = [
         jax.ShapeDtypeStruct((rows, LANE), f32),
         jax.ShapeDtypeStruct((8, LANE), f32),
         jax.ShapeDtypeStruct((8, LANE), f32),
@@ -730,13 +737,20 @@
         out_specs=[_vmem() for _ in near_out],
         compiler_params=pltpu.CompilerParams(vmem_limit_bytes=24 * 1024 * 1024),
     )(packed, table)
-    v3, m3, hinfo, cnt_l, cnt_r, sel_l, sel_r = pl.pallas_call(
+    v3, m3 = pl.pallas_call(
         functools.partial(late_kernel, local_count, field_count),
         out_shape=late_out,
-        in_specs=[_vmem() for _ in range(3)],
+        in_specs=[_vmem() for _ in range(2)],
         out_specs=[_vmem() for _ in late_out],
         compiler_params=pltpu.CompilerParams(vmem_limit_bytes=24 * 1024 * 1024),
-    )(vt, packed, table)
+    )(vt, table)
+    hinfo, cnt_l, cnt_r, sel_l, sel_r = pl.pallas_call(
+        functools.partial(move_kernel, local_count, field_count),
+        out_shape=move_out,
+        in_specs=[_vmem() for _ in range(2)],
+        out_specs=[_vmem() for _ in move_out],
+        compiler_params=pltpu.CompilerParams(vmem_limit_bytes=24 * 1024 * 1024),
+    )(packed, table)
     common = [p_local, p_remote, v7, m7, pre, stc, table]
     recv = exchange(sends)
     bulk_tabs = [v7, pre, stc, table]

time: 57.9 us -> 57.6 us (level)
  waiting for transfers between devices: 3.03 us -> 2.42 us
    pallas_call x0 -> x1, Pallas kernels: none -> 0.95 us  [per_device(): pl.pallas_call(functools.partial(move_kernel, local_count, field_count),...]
    pallas_call x1, Pallas kernels: 1.27 us -> 0.57 us  [per_device(): pl.pallas_call(functools.partial(late_kernel, local_count, field_count),...]
    ppermute x14, waiting for transfers between devices: 3.03 us -> 2.42 us  [shifted(): return lax.ppermute(value, axis, pairs)]
where the time goes in v14:
time: 57.6 us; the launch traced here: 57.3 us
  starting transfers between devices  27.6 us (48%)
  Pallas kernels  18.3 us (32%)
  local copies, waits for them, and re-layouts  6.75 us (12%)
  waiting for transfers between devices  2.42 us (4%)
  other arithmetic  1.37 us (2%)
  between operations  0.79 us (1%)
    ppermute x14, starting transfers between devices, shifted(): return lax.ppermute(value, axis, pairs)  27.6 us
    pallas_call x4, Pallas kernels, run_stage(): pl.pallas_call(kernel, out_shape=out_shapes, in_specs=[_vmem() for _ in i...  8.61 us
    unnamed x18, local copies, waits for them, and re-layouts  4.7 us
    pallas_call x4, Pallas kernels, run_bulk(): pl.pallas_call(functools.partial(bulk_kernel, coarse, local), out_shape=o...  3.07 us
    pallas_call x1, Pallas kernels, per_device(): pl.pallas_call(functools.partial(final_kernel, field_count, HOLD7), out_s...  2.74 us
    ppermute x14, waiting for transfers between devices, shifted(): return lax.ppermute(value, axis, pairs)  2.42 us
    pallas_call x1, Pallas kernels, per_device(): pl.pallas_call(functools.partial(setup_entry, local_count, field_count, l...  1.77 us
  transfers between devices with their start and end apart: 14, of which 5 were waited for; matrix products, arithmetic and copies ran while one was open for 1% of the time, Pallas kernels for 9%

profile of v14, /device:TPU:0, one launch (start us, length us, event | category | flops | bytes accessed | tf_op | source)
XLA Modules:
  0.0 57.3 jit_solution(6340106184783579845)
XLA Ops:
  0.6 0.7 %pad_bitcast_fusion = f32[1,16]{1,0:T(1,128)S(1)} fusion(f32[8]{0:T(128)} %param.11), kind=kLoop, calls=%fused_computation.9 | loop fusion | bytes 96 | tf_op jit(solution)/shard_map/stack | solution.py:640
  1.3 0.7 %convert_bitcast_fusion.1 = (f32[1,16]{1,0:T(1,128)S(1)}, f32[1,16]{1,0:T(1,128)S(1)}) fusion(s32[16]{0:T(128)} %param.14, s32[16]{0:T(128)} %param.13), kind=kLoop, calls=%fused_computation.8 | loop fusion | flops 32 | bytes 256 | tf_op jit(solution)/shard_map/stack | solution.py:640
  2.0 0.7 %convert_bitcast_fusion = f32[6,16]{1,0:T(8,128)S(1)} fusion(s32[16,6]{0,1:T(8,128)} %param.12, s32[]{:T(128)S(6)} %add.11), kind=kLoop, calls=%fused_computation.5 | loop fusion | flops 2016 | bytes 772 | tf_op jit(solution)/shard_map/transpose | solution.py:639
  2.7 0.7 %concatenate.3 = f32[10,16]{1,0:T(8,128)S(1)} concatenate(f32[6,16]{1,0:T(8,128)S(1)} %convert_bitcast_fusion, f32[1,16]{1,0:T(1,128)S(1)} %get-tuple-element.83, f32[1,16]{1,0:T(1,128)} %bitcast.19, f32[1,16]{1,0:T(1,128)S(1)} %pad_bitcast_fusion, f32[1,16]{1,0:T(1,128)S(1)} %get-tuple-element.82), dimensions={0} | concatenate | bytes 1280 | tf_op jit(solution)/shard_map/concatenate | solution.py:637
  3.4 0.9 %copy-done = f32[16,8,512]{2,1,0:T(8,128)S(1)} copy-done((f32[16,8,512]{2,1,0:T(8,128)S(1)}, f32[16,8,512]{2,1,0:T(8,128)}, u32[]{:S(2)}) %copy-start) | copy-done | bytes 262168
  4.3 1.7 %copy-done.2 = bf16[1664,768]{1,0:T(8,128)(2,1)S(1)} copy-done((bf16[1664,768]{1,0:T(8,128)(2,1)S(1)}, bf16[1664,768]{1,0:T(8,128)(2,1)}, u32[]{:S(2)}) %copy-start.2) | copy-done | bytes 2555928
  6.0 0.7 %copy-done.5 = bf16[3,64,16]{1,2,0:T(8,128)(2,1)S(1)} copy-done((bf16[3,64,16]{1,2,0:T(8,128)(2,1)S(1)}, bf16[3,64,16]{1,2,0:T(8,128)(2,1)}, u32[]{:S(2)}) %copy-start.5) | copy-done | bytes 6168
  6.8 1.8 %shard_map.95 = (bf16[3,128,512]{2,1,0:T(8,128)(2,1)S(1)}, f32[128,768]{1,0:T(8,128)S(1)}, f32[16,1]{1,0:T(8,128)S(1)}, f32[128,1]{1,0:T(8,128)S(1)}, bf16[128,1...) custom-call(f32[128,512]{1,0:T(8,128)S(1)} %bitcast.12, ...), custom_call_target="tpu_custom_call" | custom-call | tf_op jit(solution)/shard_map/pallas_call | solution.py:721
  8.5 3.0 %collective-permute-start.2 = (bf16[256,128]{1,0:T(8,128)(2,1)S(1)}, bf16[256,128]{1,0:T(8,128)(2,1)S(1)}, u32[]{:S(2)}, u32[]{:S(2)}) collective-permute-start(bf16[256,128]{1,0:T(8,128)(2,1)S(1)} %get-tuple-element.44), channel_id=1, source_target_pairs={{0,16},{16,0},{1,17},{17,1},{2,18},{18,2},{3,19},{19,3},{4,20},{20... | collective-permute-start | bytes 196616 | tf_op jit(solution)/shard_map/ppermute | solution.py:32
  11.6 4.4 %collective-permute-start.1 = (bf16[128,128]{1,0:T(8,128)(2,1)S(1)}, bf16[128,128]{1,0:T(8,128)(2,1)S(1)}, u32[]{:S(2)}, u32[]{:S(2)}) collective-permute-start(bf16[128,128]{1,0:T(8,128)(2,1)S(1)} %get-tuple-element.43), channel_id=1, source_target_pairs={{0,15},{1,0},{2,1},{3,2},{4,3},{5,4},{6,5},{7,6},{8,7},{9,8},{10,9... | collective-permute-start | bytes 98312 | tf_op jit(solution)/shard_map/ppermute | solution.py:32
  16.0 0.6 %shard_map.96 = (bf16[6,128,128]{2,1,0:T(8,128)(2,1)S(1)}, bf16[4,128,128]{2,1,0:T(8,128)(2,1)S(1)}, f32[128,1]{1,0:T(8,128)S(1)}) custom-call(f32[16,128]{1,0:T(8,128)S(1)} %pad.9.refs_2_.packed_ref, bf16[1664,768]{1,0:T(8,128)(2,1)S(1)} %get-tuple-element.45.tab_ref.refs_4_.refs_11_.refs_12_.refs_5_.refs_14_), custom_call_target="tpu_custom_call" | custom-call | tf_op jit(solution)/shard_map/pallas_call | solution.py:733
  16.6 0.7 %shard_map.97.refs_12_ = f32[128,512]{1,0:T(8,128)S(1)} custom-call(f32[128,512]{1,0:T(8,128)S(1)} %bitcast.13, bf16[3,128,512]{2,1,0:T(8,128)(2,1)S(1)} %get-tuple-element.48.refs_1_.refs_7_.refs_8_.refs_2_.refs_10_, f32[16,1]{1,0:T(8,128)S(1)} %get-tuple-element.50.refs_2_.refs_9_.refs_10_.refs_3_.refs_12_, ...), custom_call_target="tpu_custom_call" | custom-call | tf_op jit(solution)/shard_map/pallas_call | solution.py:420
  17.6 1.5 %shard_map.98 = (f32[128,512]{1,0:T(8,128)S(1)}, bf16[128,128]{1,0:T(8,128)(2,1)S(1)}, bf16[128,128]{1,0:T(8,128)(2,1)S(1)}, bf16[256,128]{1,0:T(8,128)(2,1)S(1)}) custom-call(f32[128,512]{1,0:T(8,128)S(1)} %bitcast.14, bf16[128,128]{1,0:T(8,128)(2,1)S(1)} %collective-permute-done.refs_1_, bf16[128,128]{1,0:T(8,128)(2,1)S(1)} %collective-permute-done.1.refs_2_, ...), custom_call_target="tpu_custom_call" | custom-call | tf_op jit(solution)/shard_map/pallas_call | solution.py:432
  19.2 4.5 %collective-permute-start.4 = (bf16[128,128]{1,0:T(8,128)(2,1)S(1)}, bf16[128,128]{1,0:T(8,128)(2,1)S(1)}, u32[]{:S(2)}, u32[]{:S(2)}) collective-permute-start(bf16[128,128]{1,0:T(8,128)(2,1)S(1)} %get-tuple-element.54), channel_id=1, source_target_pairs={{0,15},{1,0},{2,1},{3,2},{4,3},{5,4},{6,5},{7,6},{8,7},{9,8},{10,9... | collective-permute-start | bytes 98312 | tf_op jit(solution)/shard_map/ppermute | solution.py:32
  23.7 0.6 %shard_map.99.refs_14_ = f32[128,512]{1,0:T(8,128)S(1)} custom-call(f32[128,512]{1,0:T(8,128)S(1)} %get-tuple-element.52.refs_0_, bf16[3,128,512]{2,1,0:T(8,128)(2,1)S(1)} %get-tuple-element.48.refs_1_.refs_7_.refs_8_.refs_2_.refs_10_, f32[16,1]{1,0:T(8,128)S(1)} %get-tuple-element.50.refs_2_.refs_9_.refs_10_.refs_3_.refs_12_, ...), custom_call_target="tpu_custom_call" | custom-call | tf_op jit(solution)/shard_map/pallas_call | solution.py:420
  24.4 0.9 %collective-permute-done.3.refs_2_ = bf16[128,128]{1,0:T(8,128)(2,1)S(1)} collective-permute-done((bf16[128,128]{1,0:T(8,128)(2,1)S(1)}, bf16[128,128]{1,0:T(8,128)(2,1)S(1)}, u32[]{:S(2)}, u32[]{:S(2)}) %collective-permute-start.3) | collective-permute-done | bytes 32800 | tf_op jit(solution)/shard_map/ppermute | solution.py:32
  25.3 2.3 %shard_map.100 = (f32[128,512]{1,0:T(8,128)S(1)}, f32[128,64]{1,0:T(8,128)S(1)}, bf16[128,128]{1,0:T(8,128)(2,1)S(1)}, bf16[128,128]{1,0:T(8,128)(2,1)S(1)}, bf16[256,128]{1,0:T(8,128)(2,1)S(1)}) custom-call(f32[128,512]{1,0:T(8,128)S(1)} %get-tuple-element.52.refs_0_, f32[128,512]{1,0:T(8,128)S(1)} %bitcast.15, ...), custom_call_target="tpu_custom_call" | custom-call | tf_op jit(solution)/shard_map/pallas_call | solution.py:432
  27.6 2.0 %collective-permute-start.8 = (bf16[256,128]{1,0:T(8,128)(2,1)S(1)}, bf16[256,128]{1,0:T(8,128)(2,1)S(1)}, u32[]{:S(2)}, u32[]{:S(2)}) collective-permute-start(bf16[256,128]{1,0:T(8,128)(2,1)S(1)} %get-tuple-element.61), channel_id=1, source_target_pairs={{0,16},{16,0},{1,17},{17,1},{2,18},{18,2},{3,19},{19,3},{4,20},{20... | collective-permute-start | bytes 196616 | tf_op jit(solution)/shard_map/ppermute | solution.py:32
  29.5 4.4 %collective-permute-start.7 = (bf16[128,128]{1,0:T(8,128)(2,1)S(1)}, bf16[128,128]{1,0:T(8,128)(2,1)S(1)}, u32[]{:S(2)}, u32[]{:S(2)}) collective-permute-start(bf16[128,128]{1,0:T(8,128)(2,1)S(1)} %get-tuple-element.60), channel_id=1, source_target_pairs={{0,15},{1,0},{2,1},{3,2},{4,3},{5,4},{6,5},{7,6},{8,7},{9,8},{10,9... | collective-permute-start | bytes 98312 | tf_op jit(solution)/shard_map/ppermute | solution.py:32
  34.0 0.6 shard_map.101
  34.6 0.9 %shard_map.102 = (f32[128,512]{1,0:T(8,128)S(1)}, f32[128,64]{1,0:T(8,128)S(1)}) custom-call(f32[128,512]{1,0:T(8,128)S(1)} %get-tuple-element.57.refs_0_.refs_2_, f32[128,64]{1,0:T(8,128)S(1)} %get-tuple-element.58.refs_1_.refs_3_, bf16[3,128,512]{2,1,0:T(8,128)(2,1)S(1)} %get-tuple-element.48.refs_1_.refs_7_.refs_8_.refs_2_.refs_10_, ...), custom_call_target="tpu_custom_call" | custom-call | tf_op jit(solution)/shard_map/pallas_call | solution.py:420
  35.6 2.7 %shard_map.103 = (f32[128,512]{1,0:T(8,128)S(1)}, f32[128,64]{1,0:T(8,128)S(1)}, bf16[128,128]{1,0:T(8,128)(2,1)S(1)}, bf16[128,128]{1,0:T(8,128)(2,1)S(1)}, bf16[256,128]{1,0:T(8,128)(2,1)S(1)}) custom-call(f32[128,512]{1,0:T(8,128)S(1)} %get-tuple-element.57.refs_0_.refs_2_, f32[128,64]{1,0:T(8,128)S(1)} %get-tuple-element.58.refs_1_.refs_3_, ...), custom_call_target="tpu_custom_call" | custom-call | tf_op jit(solution)/shard_map/pallas_call | solution.py:432
  38.5 4.4 %collective-permute-start.10 = (bf16[128,128]{1,0:T(8,128)(2,1)S(1)}, bf16[128,128]{1,0:T(8,128)(2,1)S(1)}, u32[]{:S(2)}, u32[]{:S(2)}) collective-permute-start(bf16[128,128]{1,0:T(8,128)(2,1)S(1)} %get-tuple-element.69), channel_id=1, source_target_pairs={{0,15},{1,0},{2,1},{3,2},{4,3},{5,4},{6,5},{7,6},{8,7},{9,8},{10,9... | collective-permute-start | bytes 98312 | tf_op jit(solution)/shard_map/ppermute | solution.py:32
  42.9 1.0 %shard_map.104 = (f32[128,128]{1,0:T(8,128)S(1)}, f32[8,128]{1,0:T(8,128)S(1)}, f32[8,128]{1,0:T(8,128)S(1)}, bf16[16,128]{1,0:T(8,128)(2,1)S(1)}, bf16[16,128]{1,0:T(8,128)(2,1)S(1)}) custom-call(f32[16,128]{1,0:T(8,128)S(1)} %pad.9.refs_2_.packed_ref, bf16[1664,768]{1,0:T(8,128)(2,1)S(1)} %get-tuple-element.45.tab_ref.refs_4_.refs_11_.refs_12_.refs_5_.refs_14_), custom_call_target="tpu_custom_call" | custom-call | tf_op jit(solution)/shard_map/pallas_call | solution.py:747
  43.9 0.9 %shard_map.105 = (f32[128,512]{1,0:T(8,128)S(1)}, f32[128,64]{1,0:T(8,128)S(1)}) custom-call(f32[128,512]{1,0:T(8,128)S(1)} %get-tuple-element.66.refs_0_, f32[128,64]{1,0:T(8,128)S(1)} %get-tuple-element.67.refs_1_, bf16[3,128,512]{2,1,0:T(8,128)(2,1)S(1)} %get-tuple-element.48.refs_1_.refs_7_.refs_8_.refs_2_.refs_10_, ...), custom_call_target="tpu_custom_call" | custom-call | tf_op jit(solution)/shard_map/pallas_call | solution.py:420
  44.8 2.2 %shard_map.106 = (f32[128,512]{1,0:T(8,128)S(1)}, f32[128,64]{1,0:T(8,128)S(1)}, f32[24,512]{1,0:T(8,128)S(1)}, f32[24,512]{1,0:T(8,128)S(1)}) custom-call(f32[128,512]{1,0:T(8,128)S(1)} %get-tuple-element.66.refs_0_, f32[128,64]{1,0:T(8,128)S(1)} %get-tuple-element.67.refs_1_, f32[128,512]{1,0:T(8,128)S(1)} %get-tuple-element.57.refs_0_.refs_2_, ...), custom_call_target="tpu_custom_call" | custom-call | tf_op jit(solution)/shard_map/pallas_call | solution.py:432
  47.0 0.7 %copy-done.3 = f32[128,512]{1,0:T(8,128)} copy-done((f32[128,512]{1,0:T(8,128)}, f32[128,512]{1,0:T(8,128)S(1)}, u32[]{:S(2)}) %copy-start.3) | copy-done | bytes 262168
  47.7 4.4 %collective-permute-start.13 = (f32[24,512]{1,0:T(8,128)S(1)}, f32[24,512]{1,0:T(8,128)S(1)}, u32[]{:S(2)}, u32[]{:S(2)}) collective-permute-start(f32[24,512]{1,0:T(8,128)S(1)} %get-tuple-element.79), channel_id=1, source_target_pairs={{0,15},{1,0},{2,1},{3,2},{4,3},{5,4},{6,5},{7,6},{8,7},{9,8},{10,9... | collective-permute-start | bytes 147464 | tf_op jit(solution)/shard_map/ppermute | solution.py:32
  52.1 0.7 %reshape.15 = f32[16,512]{1,0:T(8,128)} reshape(f32[128,64]{1,0:T(8,128)S(1)} %get-tuple-element.81) | data formatting | bytes 65536 | tf_op jit(solution)/shard_map/reshape | solution.py:800
  52.8 1.1 %collective-permute-done.12.from_l_ref = f32[24,512]{1,0:T(8,128)S(1)} collective-permute-done((f32[24,512]{1,0:T(8,128)S(1)}, f32[24,512]{1,0:T(8,128)S(1)}, u32[]{:S(2)}, u32[]{:S(2)}) %collective-permute-start.12) | collective-permute-done | bytes 49184 | tf_op jit(solution)/shard_map/ppermute | solution.py:32
  53.9 0.6 %copy-done.7 = f32[24,512]{1,0:T(8,128)} copy-done((f32[24,512]{1,0:T(8,128)}, f32[24,512]{1,0:T(8,128)S(1)}, u32[]{:S(2)}) %copy-start.7) | copy-done | bytes 49176
  54.5 2.7 %shard_map.107 = f32[96,512]{1,0:T(8,128)} custom-call(f32[128,512]{1,0:T(8,128)} %copy-done.3, f32[24,512]{1,0:T(8,128)} %copy-done.7, f32[24,512]{1,0:T(8,128)} %copy-done.8, f32[128,128]{1,0:T(8,128)} %copy-done.4), custom_call_target="tpu_custom_call" | custom-call | tf_op jit(solution)/shard_map/pallas_call | solution.py:793
  (33 shorter events, 0.9 us)
Async XLA Ops:
  3.4 0.9 %copy-start = (f32[16,8,512]{2,1,0:T(8,128)S(1)}, f32[16,8,512]{2,1,0:T(8,128)}, u32[]{:S(2)}) copy-start(f32[16,8,512]{2,1,0:T(8,128)} %param.8) | copy-start | bytes 786436
  4.3 1.7 %copy-start.2 = (bf16[1664,768]{1,0:T(8,128)(2,1)S(1)}, bf16[1664,768]{1,0:T(8,128)(2,1)}, u32[]{:S(2)}) copy-start(bf16[1664,768]{1,0:T(8,128)(2,1)} %constant.33.clone.refs_3_) | copy-start | bytes 7667716
  6.0 0.7 %copy-start.5 = (bf16[3,64,16]{1,2,0:T(8,128)(2,1)S(1)}, bf16[3,64,16]{1,2,0:T(8,128)(2,1)}, u32[]{:S(2)}) copy-start(bf16[3,64,16]{1,2,0:T(8,128)(2,1)} %param.9) | copy-start | bytes 18436
  6.8 9.9 %copy-start.1 = (f32[16,8,512]{2,1,0:T(8,128)S(1)}, f32[16,8,512]{2,1,0:T(8,128)}, u32[]{:S(2)}) copy-start(f32[16,8,512]{2,1,0:T(8,128)} %param.8) | copy-start | bytes 786436
  8.5 9.1 %collective-permute-start.2 = (bf16[256,128]{1,0:T(8,128)(2,1)S(1)}, bf16[256,128]{1,0:T(8,128)(2,1)S(1)}, u32[]{:S(2)}, u32[]{:S(2)}) collective-permute-start(bf16[256,128]{1,0:T(8,128)(2,1)S(1)} %get-tuple-element.44), channel_id=1, source_target_pairs={{0,16},{16,0},{1,17},{17,1},{2,18},{18,2},{3,19},{19,3},{4,20},{20... | collective-permute-start | bytes 196616 | tf_op jit(solution)/shard_map/ppermute | solution.py:32
  11.6 6.0 %collective-permute-start = (bf16[128,128]{1,0:T(8,128)(2,1)S(1)}, bf16[128,128]{1,0:T(8,128)(2,1)S(1)}, u32[]{:S(2)}, u32[]{:S(2)}) collective-permute-start(bf16[128,128]{1,0:T(8,128)(2,1)S(1)} %get-tuple-element.42), channel_id=1, source_target_pairs={{0,1},{1,2},{2,3},{3,4},{4,5},{5,6},{6,7},{7,8},{8,9},{9,10},{10,1... | collective-permute-start | bytes 98312 | tf_op jit(solution)/shard_map/ppermute | solution.py:32
  11.6 6.0 %collective-permute-start.1 = (bf16[128,128]{1,0:T(8,128)(2,1)S(1)}, bf16[128,128]{1,0:T(8,128)(2,1)S(1)}, u32[]{:S(2)}, u32[]{:S(2)}) collective-permute-start(bf16[128,128]{1,0:T(8,128)(2,1)S(1)} %get-tuple-element.43), channel_id=1, source_target_pairs={{0,15},{1,0},{2,1},{3,2},{4,3},{5,4},{6,5},{7,6},{8,7},{9,8},{10,9... | collective-permute-start | bytes 98312 | tf_op jit(solution)/shard_map/ppermute | solution.py:32
  19.1 6.2 %collective-permute-start.5 = (bf16[256,128]{1,0:T(8,128)(2,1)S(1)}, bf16[256,128]{1,0:T(8,128)(2,1)S(1)}, u32[]{:S(2)}, u32[]{:S(2)}) collective-permute-start(bf16[256,128]{1,0:T(8,128)(2,1)S(1)} %get-tuple-element.55), channel_id=1, source_target_pairs={{0,16},{16,0},{1,17},{17,1},{2,18},{18,2},{3,19},{19,3},{4,20},{20... | collective-permute-start | bytes 196616 | tf_op jit(solution)/shard_map/ppermute | solution.py:32
  19.2 6.0 %collective-permute-start.3 = (bf16[128,128]{1,0:T(8,128)(2,1)S(1)}, bf16[128,128]{1,0:T(8,128)(2,1)S(1)}, u32[]{:S(2)}, u32[]{:S(2)}) collective-permute-start(bf16[128,128]{1,0:T(8,128)(2,1)S(1)} %get-tuple-element.53), channel_id=1, source_target_pairs={{0,1},{1,2},{2,3},{3,4},{4,5},{5,6},{6,7},{7,8},{8,9},{9,10},{10,1... | collective-permute-start | bytes 98312 | tf_op jit(solution)/shard_map/ppermute | solution.py:32
  19.2 6.1 %collective-permute-start.4 = (bf16[128,128]{1,0:T(8,128)(2,1)S(1)}, bf16[128,128]{1,0:T(8,128)(2,1)S(1)}, u32[]{:S(2)}, u32[]{:S(2)}) collective-permute-start(bf16[128,128]{1,0:T(8,128)(2,1)S(1)} %get-tuple-element.54), channel_id=1, source_target_pairs={{0,15},{1,0},{2,1},{3,2},{4,3},{5,4},{6,5},{7,6},{8,7},{9,8},{10,9... | collective-permute-start | bytes 98312 | tf_op jit(solution)/shard_map/ppermute | solution.py:32
  24.4 9.6 %copy-start.6 = (bf16[3,64,16]{1,2,0:T(8,128)(2,1)S(1)}, bf16[3,64,16]{1,2,0:T(8,128)(2,1)}, u32[]{:S(2)}) copy-start(bf16[3,64,16]{1,2,0:T(8,128)(2,1)} %param.9) | copy-start | bytes 18436
  27.6 8.0 %collective-permute-start.8 = (bf16[256,128]{1,0:T(8,128)(2,1)S(1)}, bf16[256,128]{1,0:T(8,128)(2,1)S(1)}, u32[]{:S(2)}, u32[]{:S(2)}) collective-permute-start(bf16[256,128]{1,0:T(8,128)(2,1)S(1)} %get-tuple-element.61), channel_id=1, source_target_pairs={{0,16},{16,0},{1,17},{17,1},{2,18},{18,2},{3,19},{19,3},{4,20},{20... | collective-permute-start | bytes 196616 | tf_op jit(solution)/shard_map/ppermute | solution.py:32
  29.5 6.0 %collective-permute-start.6 = (bf16[128,128]{1,0:T(8,128)(2,1)S(1)}, bf16[128,128]{1,0:T(8,128)(2,1)S(1)}, u32[]{:S(2)}, u32[]{:S(2)}) collective-permute-start(bf16[128,128]{1,0:T(8,128)(2,1)S(1)} %get-tuple-element.59), channel_id=1, source_target_pairs={{0,1},{1,2},{2,3},{3,4},{4,5},{5,6},{6,7},{7,8},{8,9},{9,10},{10,1... | collective-permute-start | bytes 98312 | tf_op jit(solution)/shard_map/ppermute | solution.py:32
  29.5 6.0 %collective-permute-start.7 = (bf16[128,128]{1,0:T(8,128)(2,1)S(1)}, bf16[128,128]{1,0:T(8,128)(2,1)S(1)}, u32[]{:S(2)}, u32[]{:S(2)}) collective-permute-start(bf16[128,128]{1,0:T(8,128)(2,1)S(1)} %get-tuple-element.60), channel_id=1, source_target_pairs={{0,15},{1,0},{2,1},{3,2},{4,3},{5,4},{6,5},{7,6},{8,7},{9,8},{10,9... | collective-permute-start | bytes 98312 | tf_op jit(solution)/shard_map/ppermute | solution.py:32
  38.3 6.5 %collective-permute-start.11 = (bf16[256,128]{1,0:T(8,128)(2,1)S(1)}, bf16[256,128]{1,0:T(8,128)(2,1)S(1)}, u32[]{:S(2)}, u32[]{:S(2)}) collective-permute-start(bf16[256,128]{1,0:T(8,128)(2,1)S(1)} %get-tuple-element.70), channel_id=1, source_target_pairs={{0,16},{16,0},{1,17},{17,1},{2,18},{18,2},{3,19},{19,3},{4,20},{20... | collective-permute-start | bytes 196616 | tf_op jit(solution)/shard_map/ppermute | solution.py:32
  38.5 6.3 %collective-permute-start.9 = (bf16[128,128]{1,0:T(8,128)(2,1)S(1)}, bf16[128,128]{1,0:T(8,128)(2,1)S(1)}, u32[]{:S(2)}, u32[]{:S(2)}) collective-permute-start(bf16[128,128]{1,0:T(8,128)(2,1)S(1)} %get-tuple-element.68), channel_id=1, source_target_pairs={{0,1},{1,2},{2,3},{3,4},{4,5},{5,6},{6,7},{7,8},{8,9},{9,10},{10,1... | collective-permute-start | bytes 98312 | tf_op jit(solution)/shard_map/ppermute | solution.py:32
  38.5 6.3 %collective-permute-start.10 = (bf16[128,128]{1,0:T(8,128)(2,1)S(1)}, bf16[128,128]{1,0:T(8,128)(2,1)S(1)}, u32[]{:S(2)}, u32[]{:S(2)}) collective-permute-start(bf16[128,128]{1,0:T(8,128)(2,1)S(1)} %get-tuple-element.69), channel_id=1, source_target_pairs={{0,15},{1,0},{2,1},{3,2},{4,3},{5,4},{6,5},{7,6},{8,7},{9,8},{10,9... | collective-permute-start | bytes 98312 | tf_op jit(solution)/shard_map/ppermute | solution.py:32
  43.9 3.1 %copy-start.4 = (f32[128,128]{1,0:T(8,128)}, f32[128,128]{1,0:T(8,128)S(1)}, u32[]{:S(2)}) copy-start(f32[128,128]{1,0:T(8,128)S(1)} %get-tuple-element.80.hinfo_ref) | copy-start | bytes 196612
  47.0 0.7 %copy-start.3 = (f32[128,512]{1,0:T(8,128)}, f32[128,512]{1,0:T(8,128)S(1)}, u32[]{:S(2)}) copy-start(f32[128,512]{1,0:T(8,128)S(1)} %get-tuple-element.77.home_ref) | copy-start | bytes 786436
  47.7 6.2 %collective-permute-start.12 = (f32[24,512]{1,0:T(8,128)S(1)}, f32[24,512]{1,0:T(8,128)S(1)}, u32[]{:S(2)}, u32[]{:S(2)}) collective-permute-start(f32[24,512]{1,0:T(8,128)S(1)} %get-tuple-element.78), channel_id=1, source_target_pairs={{0,1},{1,2},{2,3},{3,4},{4,5},{5,6},{6,7},{7,8},{8,9},{9,10},{10,1... | collective-permute-start | bytes 147464 | tf_op jit(solution)/shard_map/ppermute | solution.py:32
  47.7 6.2 %collective-permute-start.13 = (f32[24,512]{1,0:T(8,128)S(1)}, f32[24,512]{1,0:T(8,128)S(1)}, u32[]{:S(2)}, u32[]{:S(2)}) collective-permute-start(f32[24,512]{1,0:T(8,128)S(1)} %get-tuple-element.79), channel_id=1, source_target_pairs={{0,15},{1,0},{2,1},{3,2},{4,3},{5,4},{6,5},{7,6},{8,7},{9,8},{10,9... | collective-permute-start | bytes 147464 | tf_op jit(solution)/shard_map/ppermute | solution.py:32
  53.9 0.6 %copy-start.7 = (f32[24,512]{1,0:T(8,128)}, f32[24,512]{1,0:T(8,128)S(1)}, u32[]{:S(2)}) copy-start(f32[24,512]{1,0:T(8,128)S(1)} %collective-permute-done.12.from_l_ref) | copy-start | bytes 147460
  53.9 0.6 %copy-start.8 = (f32[24,512]{1,0:T(8,128)}, f32[24,512]{1,0:T(8,128)S(1)}, u32[]{:S(2)}) copy-start(f32[24,512]{1,0:T(8,128)S(1)} %collective-permute-done.13.from_r_ref) | copy-start | bytes 147460

commit v15 on v14

--- a/solution.py
+++ b/solution.py
@@ -303,6 +303,8 @@
         cnt_r_ref = take()
     res7_ref = take()
     res3_ref = take() if coarse else None
+    if project:
+        take()
     out_u = take()
     out_c = take() if (coarse or project) else None
     out_send = [take() for _ in range(3)] if sends else None
@@ -495,7 +497,7 @@
     sw_out[...] = rep[:, 6:7]
 
 
-def late_kernel(local, fields, vt_ref, tab_ref, v3_out, m3_out):
+def late_kernel(local, fields, vt_ref, tab_ref, after_ref, v3_out, m3_out):
     rows = local * fields
     views = table_views(tab_ref, rows, local)
     tm_ref = views["tm"]
@@ -737,13 +739,6 @@
         out_specs=[_vmem() for _ in near_out],
         compiler_params=pltpu.CompilerParams(vmem_limit_bytes=24 * 1024 * 1024),
     )(packed, table)
-    v3, m3 = pl.pallas_call(
-        functools.partial(late_kernel, local_count, field_count),
-        out_shape=late_out,
-        in_specs=[_vmem() for _ in range(2)],
-        out_specs=[_vmem() for _ in late_out],
-        compiler_params=pltpu.CompilerParams(vmem_limit_bytes=24 * 1024 * 1024),
-    )(vt, table)
     hinfo, cnt_l, cnt_r, sel_l, sel_r = pl.pallas_call(
         functools.partial(move_kernel, local_count, field_count),
         out_shape=move_out,
@@ -761,11 +756,18 @@
         [u_shape] + sends_shape,
     )
     first, sends = res[0], res[1:]
+    v3, m3 = pl.pallas_call(
+        functools.partial(late_kernel, local_count, field_count),
+        out_shape=late_out,
+        in_specs=[_vmem() for _ in range(3)],
+        out_specs=[_vmem() for _ in late_out],
+        compiler_params=pltpu.CompilerParams(vmem_limit_bytes=24 * 1024 * 1024),
+    )(vt, table, first)
     recv = exchange(sends)
     (bulk7,) = run_bulk(False, local_count, [first] + bulk_tabs, [u_shape])
     res = run_stage(
         (False, True, True, True, local_count),
-        [first, u0] + recv + common + [sw, bulk7],
+        [first, u0] + recv + common + [sw, bulk7, v3],
         [u_shape, c_shape] + sends_shape,
     )
     after, coarse, sends = res[0], res[1], res[2:]

time: 57.6 us -> 58.2 us (1.010)
  local copies, waits for them, and re-layouts: 6.75 us -> 7.36 us
    unnamed x18, local copies, waits for them, and re-layouts: 4.7 us -> 5.31 us
where the time goes in v15:
time: 58.2 us; the launch traced here: 57.9 us
  starting transfers between devices  27.6 us (47%)
  Pallas kernels  18.3 us (31%)
  local copies, waits for them, and re-layouts  7.36 us (13%)
  waiting for transfers between devices  2.45 us (4%)
  other arithmetic  1.37 us (2%)
  between operations  0.79 us (1%)
    ppermute x14, starting transfers between devices, shifted(): return lax.ppermute(value, axis, pairs)  27.6 us
    pallas_call x4, Pallas kernels, run_stage(): pl.pallas_call(kernel, out_shape=out_shapes, in_specs=[_vmem() for _ in i...  8.61 us
    unnamed x18, local copies, waits for them, and re-layouts  5.31 us
    pallas_call x4, Pallas kernels, run_bulk(): pl.pallas_call(functools.partial(bulk_kernel, coarse, local), out_shape=o...  3.07 us
    pallas_call x1, Pallas kernels, per_device(): pl.pallas_call(functools.partial(final_kernel, field_count, HOLD7), out_s...  2.74 us
    ppermute x14, waiting for transfers between devices, shifted(): return lax.ppermute(value, axis, pairs)  2.45 us
    pallas_call x1, Pallas kernels, per_device(): pl.pallas_call(functools.partial(setup_entry, local_count, field_count, l...  1.77 us
  transfers between devices with their start and end apart: 14, of which 5 were waited for; matrix products, arithmetic and copies ran while one was open for 1% of the time, Pallas kernels for 9%

profile of v15, /device:TPU:0, one launch (start us, length us, event | category | flops | bytes accessed | tf_op | source)
XLA Modules:
  0.0 57.9 jit_solution(3927727432386802976)
XLA Ops:
  0.6 0.7 %pad_bitcast_fusion = f32[1,16]{1,0:T(1,128)S(1)} fusion(f32[8]{0:T(128)} %param.11), kind=kLoop, calls=%fused_computation.9 | loop fusion | bytes 96 | tf_op jit(solution)/shard_map/stack | solution.py:642
  1.3 0.7 %convert_bitcast_fusion.1 = (f32[1,16]{1,0:T(1,128)S(1)}, f32[1,16]{1,0:T(1,128)S(1)}) fusion(s32[16]{0:T(128)} %param.14, s32[16]{0:T(128)} %param.13), kind=kLoop, calls=%fused_computation.8 | loop fusion | flops 32 | bytes 256 | tf_op jit(solution)/shard_map/stack | solution.py:642
  2.0 0.7 %convert_bitcast_fusion = f32[6,16]{1,0:T(8,128)S(1)} fusion(s32[16,6]{0,1:T(8,128)} %param.12, s32[]{:T(128)S(6)} %add.11), kind=kLoop, calls=%fused_computation.5 | loop fusion | flops 2016 | bytes 772 | tf_op jit(solution)/shard_map/transpose | solution.py:641
  2.7 0.7 %concatenate.3 = f32[10,16]{1,0:T(8,128)S(1)} concatenate(f32[6,16]{1,0:T(8,128)S(1)} %convert_bitcast_fusion, f32[1,16]{1,0:T(1,128)S(1)} %get-tuple-element.83, f32[1,16]{1,0:T(1,128)} %bitcast.19, f32[1,16]{1,0:T(1,128)S(1)} %pad_bitcast_fusion, f32[1,16]{1,0:T(1,128)S(1)} %get-tuple-element.82), dimensions={0} | concatenate | bytes 1280 | tf_op jit(solution)/shard_map/concatenate | solution.py:639
  3.4 0.9 %copy-done = f32[16,8,512]{2,1,0:T(8,128)S(1)} copy-done((f32[16,8,512]{2,1,0:T(8,128)S(1)}, f32[16,8,512]{2,1,0:T(8,128)}, u32[]{:S(2)}) %copy-start) | copy-done | bytes 262168
  4.3 1.7 %copy-done.2 = bf16[1664,768]{1,0:T(8,128)(2,1)S(1)} copy-done((bf16[1664,768]{1,0:T(8,128)(2,1)S(1)}, bf16[1664,768]{1,0:T(8,128)(2,1)}, u32[]{:S(2)}) %copy-start.2) | copy-done | bytes 2555928
  6.0 0.7 %copy-done.5 = bf16[3,64,16]{1,2,0:T(8,128)(2,1)S(1)} copy-done((bf16[3,64,16]{1,2,0:T(8,128)(2,1)S(1)}, bf16[3,64,16]{1,2,0:T(8,128)(2,1)}, u32[]{:S(2)}) %copy-start.5) | copy-done | bytes 6168
  6.8 1.8 %shard_map.95 = (bf16[3,128,512]{2,1,0:T(8,128)(2,1)S(1)}, f32[128,768]{1,0:T(8,128)S(1)}, f32[16,1]{1,0:T(8,128)S(1)}, f32[128,1]{1,0:T(8,128)S(1)}, bf16[128,1...) custom-call(f32[128,512]{1,0:T(8,128)S(1)} %bitcast.12, ...), custom_call_target="tpu_custom_call" | custom-call | tf_op jit(solution)/shard_map/pallas_call | solution.py:723
  8.5 3.0 %collective-permute-start.2 = (bf16[256,128]{1,0:T(8,128)(2,1)S(1)}, bf16[256,128]{1,0:T(8,128)(2,1)S(1)}, u32[]{:S(2)}, u32[]{:S(2)}) collective-permute-start(bf16[256,128]{1,0:T(8,128)(2,1)S(1)} %get-tuple-element.44), channel_id=1, source_target_pairs={{0,16},{16,0},{1,17},{17,1},{2,18},{18,2},{3,19},{19,3},{4,20},{20... | collective-permute-start | bytes 196616 | tf_op jit(solution)/shard_map/ppermute | solution.py:32
  11.6 4.4 %collective-permute-start.1 = (bf16[128,128]{1,0:T(8,128)(2,1)S(1)}, bf16[128,128]{1,0:T(8,128)(2,1)S(1)}, u32[]{:S(2)}, u32[]{:S(2)}) collective-permute-start(bf16[128,128]{1,0:T(8,128)(2,1)S(1)} %get-tuple-element.43), channel_id=1, source_target_pairs={{0,15},{1,0},{2,1},{3,2},{4,3},{5,4},{6,5},{7,6},{8,7},{9,8},{10,9... | collective-permute-start | bytes 98312 | tf_op jit(solution)/shard_map/ppermute | solution.py:32
  16.0 0.6 %shard_map.96 = (bf16[6,128,128]{2,1,0:T(8,128)(2,1)S(1)}, bf16[4,128,128]{2,1,0:T(8,128)(2,1)S(1)}, f32[128,1]{1,0:T(8,128)S(1)}) custom-call(f32[16,128]{1,0:T(8,128)S(1)} %pad.9.refs_2_.packed_ref, bf16[1664,768]{1,0:T(8,128)(2,1)S(1)} %get-tuple-element.45.tab_ref.refs_4_.refs_11_.refs_12_.refs_5_.refs_14_), custom_call_target="tpu_custom_call" | custom-call | tf_op jit(solution)/shard_map/pallas_call | solution.py:735
  16.6 0.7 %shard_map.97.refs_12_ = f32[128,512]{1,0:T(8,128)S(1)} custom-call(f32[128,512]{1,0:T(8,128)S(1)} %bitcast.13, bf16[3,128,512]{2,1,0:T(8,128)(2,1)S(1)} %get-tuple-element.48.refs_1_.refs_7_.refs_8_.refs_2_.refs_10_, f32[16,1]{1,0:T(8,128)S(1)} %get-tuple-element.50.refs_2_.refs_9_.refs_10_.refs_3_.refs_12_, ...), custom_call_target="tpu_custom_call" | custom-call | tf_op jit(solution)/shard_map/pallas_call | solution.py:422
  17.6 1.5 %shard_map.98 = (f32[128,512]{1,0:T(8,128)S(1)}, bf16[128,128]{1,0:T(8,128)(2,1)S(1)}, bf16[128,128]{1,0:T(8,128)(2,1)S(1)}, bf16[256,128]{1,0:T(8,128)(2,1)S(1)}) custom-call(f32[128,512]{1,0:T(8,128)S(1)} %bitcast.14, bf16[128,128]{1,0:T(8,128)(2,1)S(1)} %collective-permute-done.refs_1_, bf16[128,128]{1,0:T(8,128)(2,1)S(1)} %collective-permute-done.1.refs_2_, ...), custom_call_target="tpu_custom_call" | custom-call | tf_op jit(solution)/shard_map/pallas_call | solution.py:434
  19.2 4.5 %collective-permute-start.4 = (bf16[128,128]{1,0:T(8,128)(2,1)S(1)}, bf16[128,128]{1,0:T(8,128)(2,1)S(1)}, u32[]{:S(2)}, u32[]{:S(2)}) collective-permute-start(bf16[128,128]{1,0:T(8,128)(2,1)S(1)} %get-tuple-element.54), channel_id=1, source_target_pairs={{0,15},{1,0},{2,1},{3,2},{4,3},{5,4},{6,5},{7,6},{8,7},{9,8},{10,9... | collective-permute-start | bytes 98312 | tf_op jit(solution)/shard_map/ppermute | solution.py:32
  23.7 0.6 %shard_map.99.refs_14_ = f32[128,512]{1,0:T(8,128)S(1)} custom-call(f32[128,512]{1,0:T(8,128)S(1)} %get-tuple-element.52.refs_0_.after_ref, bf16[3,128,512]{2,1,0:T(8,128)(2,1)S(1)} %get-tuple-element.48.refs_1_.refs_7_.refs_8_.refs_2_.refs_10_, f32[16,1]{1,0:T(8,128)S(1)} %get-tuple-element.50.refs_2_.refs_9_.refs_10_.refs_3_.refs_12_, ...), custom_call_target="tpu_custom_call" | custom-call | tf_op jit(solution)/shard_map/pallas_call | solution.py:422
  25.3 2.3 %shard_map.101 = (f32[128,512]{1,0:T(8,128)S(1)}, f32[128,64]{1,0:T(8,128)S(1)}, bf16[128,128]{1,0:T(8,128)(2,1)S(1)}, bf16[128,128]{1,0:T(8,128)(2,1)S(1)}, bf16[256,128]{1,0:T(8,128)(2,1)S(1)}) custom-call(f32[128,512]{1,0:T(8,128)S(1)} %get-tuple-element.52.refs_0_.after_ref, f32[128,512]{1,0:T(8,128)S(1)} %bitcast.15, ...), custom_call_target="tpu_custom_call" | custom-call | tf_op jit(solution)/shard_map/pallas_call | solution.py:434
  27.6 2.0 %collective-permute-start.8 = (bf16[256,128]{1,0:T(8,128)(2,1)S(1)}, bf16[256,128]{1,0:T(8,128)(2,1)S(1)}, u32[]{:S(2)}, u32[]{:S(2)}) collective-permute-start(bf16[256,128]{1,0:T(8,128)(2,1)S(1)} %get-tuple-element.62), channel_id=1, source_target_pairs={{0,16},{16,0},{1,17},{17,1},{2,18},{18,2},{3,19},{19,3},{4,20},{20... | collective-permute-start | bytes 196616 | tf_op jit(solution)/shard_map/ppermute | solution.py:32
  29.6 4.4 %collective-permute-start.7 = (bf16[128,128]{1,0:T(8,128)(2,1)S(1)}, bf16[128,128]{1,0:T(8,128)(2,1)S(1)}, u32[]{:S(2)}, u32[]{:S(2)}) collective-permute-start(bf16[128,128]{1,0:T(8,128)(2,1)S(1)} %get-tuple-element.61), channel_id=1, source_target_pairs={{0,15},{1,0},{2,1},{3,2},{4,3},{5,4},{6,5},{7,6},{8,7},{9,8},{10,9... | collective-permute-start | bytes 98312 | tf_op jit(solution)/shard_map/ppermute | solution.py:32
  34.0 0.9 %shard_map.102 = (f32[128,512]{1,0:T(8,128)S(1)}, f32[128,64]{1,0:T(8,128)S(1)}) custom-call(f32[128,512]{1,0:T(8,128)S(1)} %get-tuple-element.58.refs_0_.refs_2_, f32[128,64]{1,0:T(8,128)S(1)} %get-tuple-element.59.refs_1_.refs_3_, bf16[3,128,512]{2,1,0:T(8,128)(2,1)S(1)} %get-tuple-element.48.refs_1_.refs_7_.refs_8_.refs_2_.refs_10_, ...), custom_call_target="tpu_custom_call" | custom-call | tf_op jit(solution)/shard_map/pallas_call | solution.py:422
  34.9 0.7 %collective-permute-done.6.refs_2_ = bf16[128,128]{1,0:T(8,128)(2,1)S(1)} collective-permute-done((bf16[128,128]{1,0:T(8,128)(2,1)S(1)}, bf16[128,128]{1,0:T(8,128)(2,1)S(1)}, u32[]{:S(2)}, u32[]{:S(2)}) %collective-permute-start.6) | collective-permute-done | bytes 32800 | tf_op jit(solution)/shard_map/ppermute | solution.py:32
  35.6 2.7 %shard_map.103 = (f32[128,512]{1,0:T(8,128)S(1)}, f32[128,64]{1,0:T(8,128)S(1)}, bf16[128,128]{1,0:T(8,128)(2,1)S(1)}, bf16[128,128]{1,0:T(8,128)(2,1)S(1)}, bf16[256,128]{1,0:T(8,128)(2,1)S(1)}) custom-call(f32[128,512]{1,0:T(8,128)S(1)} %get-tuple-element.58.refs_0_.refs_2_, f32[128,64]{1,0:T(8,128)S(1)} %get-tuple-element.59.refs_1_.refs_3_, ...), custom_call_target="tpu_custom_call" | custom-call | tf_op jit(solution)/shard_map/pallas_call | solution.py:434
  38.5 4.4 %collective-permute-start.10 = (bf16[128,128]{1,0:T(8,128)(2,1)S(1)}, bf16[128,128]{1,0:T(8,128)(2,1)S(1)}, u32[]{:S(2)}, u32[]{:S(2)}) collective-permute-start(bf16[128,128]{1,0:T(8,128)(2,1)S(1)} %get-tuple-element.69), channel_id=1, source_target_pairs={{0,15},{1,0},{2,1},{3,2},{4,3},{5,4},{6,5},{7,6},{8,7},{9,8},{10,9... | collective-permute-start | bytes 98312 | tf_op jit(solution)/shard_map/ppermute | solution.py:32
  43.0 1.0 %shard_map.104 = (f32[128,128]{1,0:T(8,128)S(1)}, f32[8,128]{1,0:T(8,128)S(1)}, f32[8,128]{1,0:T(8,128)S(1)}, bf16[16,128]{1,0:T(8,128)(2,1)S(1)}, bf16[16,128]{1,0:T(8,128)(2,1)S(1)}) custom-call(f32[16,128]{1,0:T(8,128)S(1)} %pad.9.refs_2_.packed_ref, bf16[1664,768]{1,0:T(8,128)(2,1)S(1)} %get-tuple-element.45.tab_ref.refs_4_.refs_11_.refs_12_.refs_5_.refs_14_), custom_call_target="tpu_custom_call" | custom-call | tf_op jit(solution)/shard_map/pallas_call | solution.py:742
  43.9 0.6 %copy-done.4 = f32[128,128]{1,0:T(8,128)} copy-done((f32[128,128]{1,0:T(8,128)}, f32[128,128]{1,0:T(8,128)S(1)}, u32[]{:S(2)}) %copy-start.4) | copy-done | bytes 65560
  44.5 0.9 %shard_map.105 = (f32[128,512]{1,0:T(8,128)S(1)}, f32[128,64]{1,0:T(8,128)S(1)}) custom-call(f32[128,512]{1,0:T(8,128)S(1)} %get-tuple-element.66.refs_0_, f32[128,64]{1,0:T(8,128)S(1)} %get-tuple-element.67.refs_1_, bf16[3,128,512]{2,1,0:T(8,128)(2,1)S(1)} %get-tuple-element.48.refs_1_.refs_7_.refs_8_.refs_2_.refs_10_, ...), custom_call_target="tpu_custom_call" | custom-call | tf_op jit(solution)/shard_map/pallas_call | solution.py:422
  45.5 2.2 %shard_map.106 = (f32[128,512]{1,0:T(8,128)S(1)}, f32[128,64]{1,0:T(8,128)S(1)}, f32[24,512]{1,0:T(8,128)S(1)}, f32[24,512]{1,0:T(8,128)S(1)}) custom-call(f32[128,512]{1,0:T(8,128)S(1)} %get-tuple-element.66.refs_0_, f32[128,64]{1,0:T(8,128)S(1)} %get-tuple-element.67.refs_1_, f32[128,512]{1,0:T(8,128)S(1)} %get-tuple-element.58.refs_0_.refs_2_, ...), custom_call_target="tpu_custom_call" | custom-call | tf_op jit(solution)/shard_map/pallas_call | solution.py:434
  47.7 0.7 %copy-done.3 = f32[128,512]{1,0:T(8,128)} copy-done((f32[128,512]{1,0:T(8,128)}, f32[128,512]{1,0:T(8,128)S(1)}, u32[]{:S(2)}) %copy-start.3) | copy-done | bytes 262168
  48.3 4.4 %collective-permute-start.13 = (f32[24,512]{1,0:T(8,128)S(1)}, f32[24,512]{1,0:T(8,128)S(1)}, u32[]{:S(2)}, u32[]{:S(2)}) collective-permute-start(f32[24,512]{1,0:T(8,128)S(1)} %get-tuple-element.79), channel_id=1, source_target_pairs={{0,15},{1,0},{2,1},{3,2},{4,3},{5,4},{6,5},{7,6},{8,7},{9,8},{10,9... | collective-permute-start | bytes 147464 | tf_op jit(solution)/shard_map/ppermute | solution.py:32
  52.8 0.7 %reshape.15 = f32[16,512]{1,0:T(8,128)} reshape(f32[128,64]{1,0:T(8,128)S(1)} %get-tuple-element.81) | data formatting | bytes 65536 | tf_op jit(solution)/shard_map/reshape | solution.py:802
  53.5 1.1 %collective-permute-done.12.from_l_ref = f32[24,512]{1,0:T(8,128)S(1)} collective-permute-done((f32[24,512]{1,0:T(8,128)S(1)}, f32[24,512]{1,0:T(8,128)S(1)}, u32[]{:S(2)}, u32[]{:S(2)}) %collective-permute-start.12) | collective-permute-done | bytes 49184 | tf_op jit(solution)/shard_map/ppermute | solution.py:32
  54.6 0.6 %copy-done.7 = f32[24,512]{1,0:T(8,128)} copy-done((f32[24,512]{1,0:T(8,128)}, f32[24,512]{1,0:T(8,128)S(1)}, u32[]{:S(2)}) %copy-start.7) | copy-done | bytes 49176
  55.2 2.7 %shard_map.107 = f32[96,512]{1,0:T(8,128)} custom-call(f32[128,512]{1,0:T(8,128)} %copy-done.3, f32[24,512]{1,0:T(8,128)} %copy-done.7, f32[24,512]{1,0:T(8,128)} %copy-done.8, f32[128,128]{1,0:T(8,128)} %copy-done.4), custom_call_target="tpu_custom_call" | custom-call | tf_op jit(solution)/shard_map/pallas_call | solution.py:795
  (33 shorter events, 1.6 us)
Async XLA Ops:
  3.4 0.9 %copy-start = (f32[16,8,512]{2,1,0:T(8,128)S(1)}, f32[16,8,512]{2,1,0:T(8,128)}, u32[]{:S(2)}) copy-start(f32[16,8,512]{2,1,0:T(8,128)} %param.8) | copy-start | bytes 786436
  4.3 1.7 %copy-start.2 = (bf16[1664,768]{1,0:T(8,128)(2,1)S(1)}, bf16[1664,768]{1,0:T(8,128)(2,1)}, u32[]{:S(2)}) copy-start(bf16[1664,768]{1,0:T(8,128)(2,1)} %constant.33.clone.refs_3_) | copy-start | bytes 7667716
  6.0 0.7 %copy-start.5 = (bf16[3,64,16]{1,2,0:T(8,128)(2,1)S(1)}, bf16[3,64,16]{1,2,0:T(8,128)(2,1)}, u32[]{:S(2)}) copy-start(bf16[3,64,16]{1,2,0:T(8,128)(2,1)} %param.9) | copy-start | bytes 18436
  6.8 9.9 %copy-start.1 = (f32[16,8,512]{2,1,0:T(8,128)S(1)}, f32[16,8,512]{2,1,0:T(8,128)}, u32[]{:S(2)}) copy-start(f32[16,8,512]{2,1,0:T(8,128)} %param.8) | copy-start | bytes 786436
  8.5 9.1 %collective-permute-start.2 = (bf16[256,128]{1,0:T(8,128)(2,1)S(1)}, bf16[256,128]{1,0:T(8,128)(2,1)S(1)}, u32[]{:S(2)}, u32[]{:S(2)}) collective-permute-start(bf16[256,128]{1,0:T(8,128)(2,1)S(1)} %get-tuple-element.44), channel_id=1, source_target_pairs={{0,16},{16,0},{1,17},{17,1},{2,18},{18,2},{3,19},{19,3},{4,20},{20... | collective-permute-start | bytes 196616 | tf_op jit(solution)/shard_map/ppermute | solution.py:32
  11.6 6.0 %collective-permute-start = (bf16[128,128]{1,0:T(8,128)(2,1)S(1)}, bf16[128,128]{1,0:T(8,128)(2,1)S(1)}, u32[]{:S(2)}, u32[]{:S(2)}) collective-permute-start(bf16[128,128]{1,0:T(8,128)(2,1)S(1)} %get-tuple-element.42), channel_id=1, source_target_pairs={{0,1},{1,2},{2,3},{3,4},{4,5},{5,6},{6,7},{7,8},{8,9},{9,10},{10,1... | collective-permute-start | bytes 98312 | tf_op jit(solution)/shard_map/ppermute | solution.py:32
  11.6 6.0 %collective-permute-start.1 = (bf16[128,128]{1,0:T(8,128)(2,1)S(1)}, bf16[128,128]{1,0:T(8,128)(2,1)S(1)}, u32[]{:S(2)}, u32[]{:S(2)}) collective-permute-start(bf16[128,128]{1,0:T(8,128)(2,1)S(1)} %get-tuple-element.43), channel_id=1, source_target_pairs={{0,15},{1,0},{2,1},{3,2},{4,3},{5,4},{6,5},{7,6},{8,7},{9,8},{10,9... | collective-permute-start | bytes 98312 | tf_op jit(solution)/shard_map/ppermute | solution.py:32
  19.1 5.3 %copy-start.6 = (bf16[3,64,16]{1,2,0:T(8,128)(2,1)S(1)}, bf16[3,64,16]{1,2,0:T(8,128)(2,1)}, u32[]{:S(2)}) copy-start(bf16[3,64,16]{1,2,0:T(8,128)(2,1)} %param.9) | copy-start | bytes 18436
  19.1 6.2 %collective-permute-start.5 = (bf16[256,128]{1,0:T(8,128)(2,1)S(1)}, bf16[256,128]{1,0:T(8,128)(2,1)S(1)}, u32[]{:S(2)}, u32[]{:S(2)}) collective-permute-start(bf16[256,128]{1,0:T(8,128)(2,1)S(1)} %get-tuple-element.55), channel_id=1, source_target_pairs={{0,16},{16,0},{1,17},{17,1},{2,18},{18,2},{3,19},{19,3},{4,20},{20... | collective-permute-start | bytes 196616 | tf_op jit(solution)/shard_map/ppermute | solution.py:32
  19.2 6.0 %collective-permute-start.3 = (bf16[128,128]{1,0:T(8,128)(2,1)S(1)}, bf16[128,128]{1,0:T(8,128)(2,1)S(1)}, u32[]{:S(2)}, u32[]{:S(2)}) collective-permute-start(bf16[128,128]{1,0:T(8,128)(2,1)S(1)} %get-tuple-element.53), channel_id=1, source_target_pairs={{0,1},{1,2},{2,3},{3,4},{4,5},{5,6},{6,7},{7,8},{8,9},{9,10},{10,1... | collective-permute-start | bytes 98312 | tf_op jit(solution)/shard_map/ppermute | solution.py:32
  19.2 6.1 %collective-permute-start.4 = (bf16[128,128]{1,0:T(8,128)(2,1)S(1)}, bf16[128,128]{1,0:T(8,128)(2,1)S(1)}, u32[]{:S(2)}, u32[]{:S(2)}) collective-permute-start(bf16[128,128]{1,0:T(8,128)(2,1)S(1)} %get-tuple-element.54), channel_id=1, source_target_pairs={{0,15},{1,0},{2,1},{3,2},{4,3},{5,4},{6,5},{7,6},{8,7},{9,8},{10,9... | collective-permute-start | bytes 98312 | tf_op jit(solution)/shard_map/ppermute | solution.py:32
  27.6 8.0 %collective-permute-start.8 = (bf16[256,128]{1,0:T(8,128)(2,1)S(1)}, bf16[256,128]{1,0:T(8,128)(2,1)S(1)}, u32[]{:S(2)}, u32[]{:S(2)}) collective-permute-start(bf16[256,128]{1,0:T(8,128)(2,1)S(1)} %get-tuple-element.62), channel_id=1, source_target_pairs={{0,16},{16,0},{1,17},{17,1},{2,18},{18,2},{3,19},{19,3},{4,20},{20... | collective-permute-start | bytes 196616 | tf_op jit(solution)/shard_map/ppermute | solution.py:32
  29.6 6.0 %collective-permute-start.6 = (bf16[128,128]{1,0:T(8,128)(2,1)S(1)}, bf16[128,128]{1,0:T(8,128)(2,1)S(1)}, u32[]{:S(2)}, u32[]{:S(2)}) collective-permute-start(bf16[128,128]{1,0:T(8,128)(2,1)S(1)} %get-tuple-element.60), channel_id=1, source_target_pairs={{0,1},{1,2},{2,3},{3,4},{4,5},{5,6},{6,7},{7,8},{8,9},{9,10},{10,1... | collective-permute-start | bytes 98312 | tf_op jit(solution)/shard_map/ppermute | solution.py:32
  29.6 6.0 %collective-permute-start.7 = (bf16[128,128]{1,0:T(8,128)(2,1)S(1)}, bf16[128,128]{1,0:T(8,128)(2,1)S(1)}, u32[]{:S(2)}, u32[]{:S(2)}) collective-permute-start(bf16[128,128]{1,0:T(8,128)(2,1)S(1)} %get-tuple-element.61), channel_id=1, source_target_pairs={{0,15},{1,0},{2,1},{3,2},{4,3},{5,4},{6,5},{7,6},{8,7},{9,8},{10,9... | collective-permute-start | bytes 98312 | tf_op jit(solution)/shard_map/ppermute | solution.py:32
  38.3 7.1 %collective-permute-start.11 = (bf16[256,128]{1,0:T(8,128)(2,1)S(1)}, bf16[256,128]{1,0:T(8,128)(2,1)S(1)}, u32[]{:S(2)}, u32[]{:S(2)}) collective-permute-start(bf16[256,128]{1,0:T(8,128)(2,1)S(1)} %get-tuple-element.70), channel_id=1, source_target_pairs={{0,16},{16,0},{1,17},{17,1},{2,18},{18,2},{3,19},{19,3},{4,20},{20... | collective-permute-start | bytes 196616 | tf_op jit(solution)/shard_map/ppermute | solution.py:32
  38.5 6.9 %collective-permute-start.9 = (bf16[128,128]{1,0:T(8,128)(2,1)S(1)}, bf16[128,128]{1,0:T(8,128)(2,1)S(1)}, u32[]{:S(2)}, u32[]{:S(2)}) collective-permute-start(bf16[128,128]{1,0:T(8,128)(2,1)S(1)} %get-tuple-element.68), channel_id=1, source_target_pairs={{0,1},{1,2},{2,3},{3,4},{4,5},{5,6},{6,7},{7,8},{8,9},{9,10},{10,1... | collective-permute-start | bytes 98312 | tf_op jit(solution)/shard_map/ppermute | solution.py:32
  38.5 6.9 %collective-permute-start.10 = (bf16[128,128]{1,0:T(8,128)(2,1)S(1)}, bf16[128,128]{1,0:T(8,128)(2,1)S(1)}, u32[]{:S(2)}, u32[]{:S(2)}) collective-permute-start(bf16[128,128]{1,0:T(8,128)(2,1)S(1)} %get-tuple-element.69), channel_id=1, source_target_pairs={{0,15},{1,0},{2,1},{3,2},{4,3},{5,4},{6,5},{7,6},{8,7},{9,8},{10,9... | collective-permute-start | bytes 98312 | tf_op jit(solution)/shard_map/ppermute | solution.py:32
  43.9 0.6 %copy-start.4 = (f32[128,128]{1,0:T(8,128)}, f32[128,128]{1,0:T(8,128)S(1)}, u32[]{:S(2)}) copy-start(f32[128,128]{1,0:T(8,128)S(1)} %get-tuple-element.80.hinfo_ref) | copy-start | bytes 196612
  47.6 0.7 %copy-start.3 = (f32[128,512]{1,0:T(8,128)}, f32[128,512]{1,0:T(8,128)S(1)}, u32[]{:S(2)}) copy-start(f32[128,512]{1,0:T(8,128)S(1)} %get-tuple-element.77.home_ref) | copy-start | bytes 786436
  48.3 6.2 %collective-permute-start.12 = (f32[24,512]{1,0:T(8,128)S(1)}, f32[24,512]{1,0:T(8,128)S(1)}, u32[]{:S(2)}, u32[]{:S(2)}) collective-permute-start(f32[24,512]{1,0:T(8,128)S(1)} %get-tuple-element.78), channel_id=1, source_target_pairs={{0,1},{1,2},{2,3},{3,4},{4,5},{5,6},{6,7},{7,8},{8,9},{9,10},{10,1... | collective-permute-start | bytes 147464 | tf_op jit(solution)/shard_map/ppermute | solution.py:32
  48.3 6.2 %collective-permute-start.13 = (f32[24,512]{1,0:T(8,128)S(1)}, f32[24,512]{1,0:T(8,128)S(1)}, u32[]{:S(2)}, u32[]{:S(2)}) collective-permute-start(f32[24,512]{1,0:T(8,128)S(1)} %get-tuple-element.79), channel_id=1, source_target_pairs={{0,15},{1,0},{2,1},{3,2},{4,3},{5,4},{6,5},{7,6},{8,7},{9,8},{10,9... | collective-permute-start | bytes 147464 | tf_op jit(solution)/shard_map/ppermute | solution.py:32
  54.5 0.6 %copy-start.7 = (f32[24,512]{1,0:T(8,128)}, f32[24,512]{1,0:T(8,128)S(1)}, u32[]{:S(2)}) copy-start(f32[24,512]{1,0:T(8,128)S(1)} %collective-permute-done.12.from_l_ref) | copy-start | bytes 147460
  54.5 0.6 %copy-start.8 = (f32[24,512]{1,0:T(8,128)}, f32[24,512]{1,0:T(8,128)S(1)}, u32[]{:S(2)}) copy-start(f32[24,512]{1,0:T(8,128)S(1)} %collective-permute-done.13.from_r_ref) | copy-start | bytes 147460
